TPU v7x, 32 devices: a whole 2x2x4 slice. The times are simulated.
32 devices in a mesh: lat: 2 (over y), lev: 4 (over x, core), ocn: 4 (over z).
Axes of the slice: x: 2, y: 2, z: 4, core: 2. Of those that a mesh axis runs over, the one named last changes fastest.
Arguments:
- atmos_fields: bfloat16 [2, 24, 2560, 5632], P(None, 'lev', ('lat', 'ocn')), may hold values from -6 to 6
- lat_points: int32 [2560], P(('lat', 'ocn')), may hold values from 20 to 5632, as said below
- wave_order: int32 [32], replicated, may hold values from 0 to 31, each once
- legendre: bfloat16 [32, 2560, 1536], P(('lat', 'ocn'), None, 'lev'), may hold values from -0.125 to 0.125
- column_weight: bfloat16 [2, 24], P(None, 'lev'), may hold values from -1.25 to 1.25
- block_remap: int32 [2560, 44], P(('lat', 'ocn'), 'lev'), may hold values from 0 to 2175, as said below
- ocean_temp: float32 [128, 2176], P(('lat', 'ocn')), may hold values from -6 to 6
- ocean_salt: float32 [128, 2176], P(('lat', 'ocn')), may hold values from -6 to 6
- sea_mask: int32 [128, 17], P(('lat', 'ocn')), may hold values 0 or 1
Outputs:
- spectra: float32 [32, 96, 1536], P(('lat', 'ocn'), None, 'lev')
- temp_next: float32 [128, 2176], P(('lat', 'ocn'))
- salt_next: float32 [128, 2176], P(('lat', 'ocn'))
- surface_temp: float32 [2560, 5632], P(('lat', 'ocn'), 'lev')
Inputs may be any that keep to these rules, and one draw needn't show every extreme that they name: `lat_points`: a multiple of 4 for every latitude row. `wave_order`: each wavenumber appears once. `block_remap`: the blocks of latitude band g (rows g * 320 onward) name tiles of ocean sections g - 1, g or g + 1 only; section g holds tiles g * 16 * 17 onward, in row order.
All inputs are finite; a program needn't handle non-finite values. No bound on the sum of `sea_mask` on one device may be relied on, other than what follows from the above.
Results may differ from a plain program's by a relative error of at most 0.0037.
Values may be sent and summed in bfloat16 or wider, within the bound.
No kernel may reach another device: no remote copies, remote signals or barrier semaphores. Data moves between devices by JAX's collectives and lax.ppermute only.
A program may use at most 192 MiB of HBM per device.

v0:
```python
import math

import jax
import jax.numpy as jnp
from jax import lax
from jax.sharding import PartitionSpec as P

FIELDS = 2
BLOCK = 128


FULL_TURN = 2.0 * math.pi
DIFFUSION = 0.2
COUPLING = 0.5


def with_halo(cells, sides, width):
    for axis, dim in sides:
        count = lax.axis_size(axis)
        ends = count - 1
        head = lax.slice_in_dim(cells, 0, width, axis=dim)
        tail = lax.slice_in_dim(cells, cells.shape[dim] - width, cells.shape[dim], axis=dim)
        cells = jnp.concatenate(
            [
                lax.ppermute(tail, axis, [(i, (i + 1) % count) for i in range(ends)]),
                cells,
                lax.ppermute(head, axis, [((i + 1) % count, i) for i in range(ends)]),
            ],
            axis=dim,
        )
    return cells


def fourier_table(wave_order, length):
    points = jnp.arange(length, dtype=jnp.int32)
    phase = wave_order[None, :] * points[:, None] % length
    angle = phase.astype(jnp.float32) * (FULL_TURN / length)
    table = jnp.concatenate([jnp.cos(angle), -jnp.sin(angle)], axis=1).astype(jnp.bfloat16)
    return (table, points)


def body(
    atmos_fields,
    lat_points,
    wave_order,
    legendre,
    column_weight,
    block_remap,
    ocean_temp,
    ocean_salt,
    sea_mask,
):
    nfields, lev_dev, lat_band, lon_count = atmos_fields.shape
    wave_count = wave_order.shape[0]
    table, points = fourier_table(wave_order, lon_count)
    point_mask = points[None, :] < lat_points[:, None]
    masked = jnp.where(point_mask[None, None], atmos_fields, jnp.zeros((), jnp.bfloat16))
    inverse_root = 1.0 / jnp.sqrt(lat_points.astype(jnp.float32))
    weights = jnp.where(
        2 * wave_order[None, :] < lat_points[:, None],
        inverse_root[:, None],
        jnp.zeros((), jnp.float32),
    )
    field_count = masked.shape[0]
    raw_sums = jnp.dot(masked.reshape(-1, lon_count), table, preferred_element_type=jnp.float32)
    raw_sums = raw_sums.reshape(field_count, lev_dev, lat_band, 2, wave_count)
    coeffs = (raw_sums * weights[None, None, :, None, :]).astype(jnp.bfloat16)
    regrouped = lax.all_to_all(
        coeffs.transpose(4, 1, 0, 3, 2).reshape(wave_count, lev_dev * field_count * 2, lat_band),
        ("lat", "ocn"),
        split_axis=0,
        concat_axis=2,
        tiled=True,
    )
    spectra = jnp.einsum(
        "srj,sjd->srd",
        lax.all_gather(regrouped, "lev", axis=1, tiled=True),
        legendre,
        preferred_element_type=jnp.float32,
    )
    ocean_rows, ocean_cols = ocean_temp.shape
    tile_count = ocean_rows * ocean_cols // BLOCK
    band_index = lax.axis_index(("lat", "ocn"))

    def slot_of(targets):
        return (targets // tile_count - band_index + 1) * tile_count + targets % tile_count

    local_slot = slot_of(block_remap.reshape(-1))
    partial_sum = jnp.einsum(
        "ql,qljk->qjk", column_weight, masked, preferred_element_type=jnp.float32
    )
    quarter = lon_count // lax.axis_size("lev")
    full_remap = lax.all_gather(block_remap, "lev", axis=1, tiled=True)
    every_slot = slot_of(full_remap.reshape(-1))
    block_rows = (
        partial_sum.reshape(FIELDS, lat_band, lon_count // BLOCK, BLOCK)
        .transpose(1, 2, 0, 3)
        .reshape(-1, FIELDS * BLOCK)
    )
    outgoing = jax.ops.segment_sum(block_rows, every_slot, num_segments=3 * tile_count)
    widened = with_halo(outgoing, ((("lat", "ocn"), 0),), tile_count)
    arrived = (
        widened[:tile_count] + widened[2 * tile_count : 3 * tile_count] + widened[4 * tile_count :]
    )
    tile_sums = lax.psum(arrived, "lev")
    forcing = (
        tile_sums.reshape(ocean_rows, ocean_cols // BLOCK, FIELDS, BLOCK)
        .transpose(2, 0, 1, 3)
        .reshape(FIELDS, ocean_rows, ocean_cols)
    )
    sea_cells = (
        jnp.broadcast_to(sea_mask[:, :, None], (ocean_rows, ocean_cols // BLOCK, BLOCK))
        .reshape(ocean_rows, ocean_cols)
        .astype(jnp.float32)
    )
    ocean_state = jnp.stack([ocean_temp, ocean_salt])
    padded = with_halo(ocean_state, ((("lat", "ocn"), 1),), 1)
    laplace = (
        padded[:, 2:]
        + padded[:, :-2]
        + jnp.roll(ocean_state, 1, 2)
        + jnp.roll(ocean_state, -1, 2)
        - 4.0 * ocean_state
    )
    updated = ocean_state + DIFFUSION * laplace + COUPLING * sea_cells[None] * forcing
    temp_next = updated[0]
    salt_next = updated[1]
    returned = with_halo(temp_next, ((("lat", "ocn"), 0),), ocean_rows)
    tiles_near = returned.reshape(3 * tile_count, BLOCK)
    surface = jnp.take(tiles_near, local_slot, axis=0).reshape(lat_band, quarter)
    own_points = lax.axis_index("lev") * quarter + jnp.arange(quarter, dtype=jnp.int32)
    surface_temp = jnp.where(
        own_points[None, :] < lat_points[:, None], surface, jnp.zeros((), jnp.float32)
    )
    return (spectra, temp_next, salt_next, surface_temp)


def solution(mesh):
    placed = (
        P(None, "lev", ("lat", "ocn"), None),
        P(("lat", "ocn")),
        P(),
        P(("lat", "ocn"), None, "lev"),
        P(None, "lev"),
        P(("lat", "ocn"), "lev"),
        P(("lat", "ocn"), None),
        P(("lat", "ocn"), None),
        P(("lat", "ocn"), None),
    )
    return jax.shard_map(
        body,
        mesh=mesh,
        in_specs=placed,
        out_specs=(
            P(("lat", "ocn"), None, "lev"),
            P(("lat", "ocn"), None),
            P(("lat", "ocn"), None),
            P(("lat", "ocn"), "lev"),
        ),
        check_vma=False,
    )
```

profile of v0, /device:TPU:4, one launch (start us, length us, event | category | flops | bytes accessed | tf_op | source)
XLA Modules:
  0.0 345.3 jit_solution(12073367168310134059)
XLA Ops:
  7.2 1.7 iota_compare_fusion
  8.9 0.7 convert_rsqrt_fusion
  9.6 4.0 %cosine_convert_fusion = (bf16[5632,32]{0,1:T(8,128)(2,1)S(1)}, bf16[5632,32]{0,1:T(8,128)(2,1)S(1)}) fusion(s32[32]{0:T(128)} %param.11), kind=kLoop, calls=%fused_computation.21 | loop fusion | flops 2162688 | bytes 721024 | tf_op jit(solution)/shard_map/convert
  14.3 28.9 %broadcast_select_fusion = bf16[2,6,320,5632]{3,2,1,0:T(8,128)(2,1)} fusion(bf16[2,6,320,5632]{3,2,1,0:T(8,128)(2,1)} %param.9, pred[320,5632]{1,0:T(8,128)(4,1)S(1)} %iota_compare_fusion), kind=kLoop, calls=%fused_computation.6 | loop fusion | flops 21626880 | bytes 88309760 | tf_op jit(solution)/shard_map/jit(_where)/select_n | solution.py:57
  43.3 21.6 %fusion.13 = bf16[32,6,2,2,320]{4,0,3,1,2:T(8,128)(2,1)S(1)} fusion(bf16[2,32,5632,1,1]{2,1,0,4,3:T(8,128)(2,1)S(1)} %bitcast.66, bf16[2,6,320,5632]{3,2,1,0:T(8,128)(2,1)} %broadcast_select_fusion, f32[32,320]{1,0:T(8,128)S(1)} %compare_select_fusion.2), kind=kOutput, calls=%fused_computation.15 | convolution fusion | flops 2768732160 | bytes 44507136 | tf_op jit(solution)/shard_map/dot_general | solution.py:65
  65.0 1.0 copy.40
  66.0 6.3 %all-to-all-start = ((bf16[32,24,320]{2,1,0:T(8,128)(2,1)}), bf16[32,24,320]{2,1,0:T(8,128)(2,1)S(1)}, u32[]{:S(2)}, u32[]{:S(2)}) async-start(bf16[32,24,320]{2,1,0:T(8,128)(2,1)} %copy.40), calls=%async_computation | async-start | bytes 1179648 | tf_op jit(solution)/shard_map/all_to_all | solution.py:68
  72.4 5.5 %all-gather = s32[4,11,320]{2,1,0:T(8,128)S(1)} all-gather(s32[1,11,320]{2,1,0:T(8,128)S(1)} %bitcast.82), channel_id=1, replica_groups=mesh['lat'=2,'lev'=4,'ocn'=4] {'lev'}, dimensions={0}, use_global_device_ids=true | all-gather | bytes 70400 | tf_op jit(solution)/shard_map/all_gather | solution.py:93
  79.0 42.8 %fusion = f32[2,1,320,5632]{3,1,2,0:T(1,128)} fusion(bf16[2,6,320,5632]{3,2,1,0:T(8,128)(2,1)} %broadcast_select_fusion, bf16[2,6,1,1]{1,0,2,3:T(2,128)(2,1)S(1)} %bitcast.62), kind=kOutput, calls=%fused_computation.2 | convolution fusion | flops 43253760 | bytes 57671704 | tf_op jit(solution)/shard_map/ql,qljk->qjk/dot_general | solution.py:89
  121.8 11.2 %copy.69 = f32[2,1,320,5632]{3,2,0,1:T(8,128)} copy(f32[2,1,320,5632]{3,1,2,0:T(1,128)} %fusion) | data formatting | bytes 28835840 | tf_op jit(solution)/shard_map/ql,qljk->qjk/dot_general | solution.py:89
  133.0 16.2 %reshape.273 = f32[2,320,44,128]{3,2,1,0:T(8,128)} reshape(f32[2,320,5632]{2,1,0:T(8,128)} %bitcast.64) | data formatting | bytes 28835840 | tf_op jit(solution)/shard_map/reshape | solution.py:96
  149.2 21.4 %copy.45 = f32[320,44,2,128]{3,2,1,0:T(2,128)} copy(f32[320,44,2,128]{3,1,0,2:T(8,128)} %bitcast.63) | data formatting | bytes 28835840 | tf_op jit(solution)/shard_map/transpose | solution.py:97
  171.0 77.7 %scatter_custom_fusion = f32[816,256]{1,0:T(8,128)S(1)} fusion(s32[14080]{0:T(1024)S(1)} %fusion.33, f32[1760,8,2,128]{3,2,1,0:T(2,128)} %bitcast.65, f32[]{:T(128)} %constant.51.clone.1), kind=kCustom, calls=%fused_computation.7 | custom fusion | flops 3604480 | bytes 15253508 | tf_op jit(solution)/shard_map/scatter-add | solution.py:100
  248.8 5.4 %collective-permute-start.3 = (f32[272,256]{1,0:T(8,128)S(1)}, f32[272,256]{1,0:T(8,128)S(1)}, u32[]{:S(2)}, u32[]{:S(2)}) collective-permute-start(f32[272,256]{1,0:T(8,128)S(1)} %get-tuple-element.19), channel_id=1, source_target_pairs={{1,0},{2,1},{3,2},{16,3},{17,16},{18,17},{19,18},{5,4},{6,5},{7,6}... | collective-permute-start | bytes 835592 | tf_op jit(solution)/shard_map/ppermute | solution.py:27
  254.2 1.9 collective-permute-start.2
  256.1 2.1 collective-permute-start.1
  258.3 6.4 %collective-permute-start = (f32[2,1,2176]{2,1,0:T(1,128)S(1)}, f32[2,1,2176]{2,1,0:T(1,128)S(1)}, u32[]{:S(2)}, u32[]{:S(2)}) collective-permute-start(f32[2,1,2176]{2,1,0:T(1,128)S(1)} %get-tuple-element.26), channel_id=1, source_target_pairs={{1,0},{2,1},{3,2},{16,3},{17,16},{18,17},{19,18},{5,4},{6,5},{7,6}... | collective-permute-start | bytes 52232 | tf_op jit(solution)/shard_map/ppermute | solution.py:27
  264.7 3.1 collective-permute-done.2
  268.1 0.8 reshape.276
  269.9 1.2 all_to_all.16
  272.0 29.3 %all-reduce.2.cloned.1.call-done = f32[2,16,2176]{2,1,0:T(8,128)} async-done(((f32[2,16,2176]{2,1,0:T(8,128)}), f32[2,16,2176]{2,1,0:T(8,128)}) %all-reduce.2.cloned.1.call-update) | async-done | bytes 278544 | tf_op jit(solution)/shard_map/psum | solution.py:105
  301.3 1.2 fusion.31
  303.2 5.2 %collective-permute-start.5 = (f32[16,2176]{1,0:T(8,128)S(1)}, f32[16,2176]{1,0:T(8,128)S(1)}, u32[]{:S(2)}, u32[]{:S(2)}) collective-permute-start(f32[16,2176]{1,0:T(8,128)S(1)} %get-tuple-element.21), channel_id=1, source_target_pairs={{1,0},{2,1},{3,2},{16,3},{17,16},{18,17},{19,18},{5,4},{6,5},{7,6}... | collective-permute-start | bytes 417800 | tf_op jit(solution)/shard_map/ppermute | solution.py:27
  308.4 1.9 collective-permute-start.4
  310.4 1.9 collective-permute-done.5
  312.3 5.8 %collective-permute-done.4 = f32[16,2176]{1,0:T(8,128)S(1)} collective-permute-done((f32[16,2176]{1,0:T(8,128)S(1)}, f32[16,2176]{1,0:T(8,128)S(1)}, u32[]{:S(2)}, u32[]{:S(2)}) %collective-permute-start.4) | collective-permute-done | bytes 139296 | tf_op jit(solution)/shard_map/ppermute | solution.py:25
  318.1 5.9 %gather_fusion = f32[3520,128]{1,0:T(8,128)S(1)} fusion(f32[816,128]{1,0:T(8,128)S(1)} %reshape.277, s32[4096]{0:T(1024)S(1)} %pad_clamp_fusion), kind=kCustom, calls=%fused_computation | custom fusion | bytes 3618560 | tf_op jit(solution)/shard_map/jit(_take)/gather | solution.py:130
  324.0 1.6 gather.7
  325.6 2.2 copy.50
  327.8 1.7 select_select_fusion
  329.5 2.9 copy.51
  332.4 6.1 %fusion.46 = f32[4,96,384]{2,1,0:T(8,128)} fusion(bf16[4,96,2560]{2,1,0:T(8,128)(2,1)} %all-gather.3.cloned.1.call-done, bf16[4,2560,384]{2,1,0:T(8,128)(2,1)} %param.12), kind=kOutput, calls=%fused_computation.94 | convolution fusion | flops 754974720 | bytes 10420224 | tf_op jit(solution)/shard_map/srj,sjd->srd/dot_general | solution.py:75
  (66 shorter events, 5.3 us)
Async XLA Ops:
  7.2 71.9 %copy-start = (bf16[2,6]{1,0:T(2,128)(2,1)S(1)}, bf16[2,6]{1,0:T(2,128)(2,1)}, u32[]{:S(2)}) copy-start(bf16[2,6]{1,0:T(2,128)(2,1)} %param.13) | copy-start | bytes 76
  14.3 29.0 %copy-start.6 = (s32[320]{0:T(512)S(1)}, s32[320]{0:T(512)}, u32[]{:S(2)}) copy-start(s32[320]{0:T(512)} %param.10) | copy-start | bytes 3844
  43.3 29.0 %copy-start.5 = (s32[320,11]{0,1:T(8,128)S(1)}, s32[320,11]{0,1:T(8,128)}, u32[]{:S(2)}) copy-start(s32[320,11]{0,1:T(8,128)} %param.14) | copy-start | bytes 42244
  66.0 203.6 %all-to-all-start = ((bf16[32,24,320]{2,1,0:T(8,128)(2,1)}), bf16[32,24,320]{2,1,0:T(8,128)(2,1)S(1)}, u32[]{:S(2)}, u32[]{:S(2)}) async-start(bf16[32,24,320]{2,1,0:T(8,128)(2,1)} %copy.40), calls=%async_computation | async-start | bytes 1179648 | tf_op jit(solution)/shard_map/all_to_all | solution.py:68
  72.3 229.0 %all-reduce.2.cloned.1.call-start = ((), (), s32[]{:S(2)}) async-start(), calls=%async_computation.2 | async-start | bytes 557056 | tf_op jit(solution)/shard_map/psum | solution.py:105
  171.0 85.1 %copy-start.2 = (f32[16,2176]{1,0:T(8,128)S(1)}, f32[16,2176]{1,0:T(8,128)}, u32[]{:S(2)}) copy-start(f32[16,2176]{1,0:T(8,128)} %param.15) | copy-start | bytes 417796
  171.0 85.1 %copy-start.3 = (f32[16,2176]{1,0:T(8,128)S(1)}, f32[16,2176]{1,0:T(8,128)}, u32[]{:S(2)}) copy-start(f32[16,2176]{1,0:T(8,128)} %param.16) | copy-start | bytes 417796
  248.7 22.9 %copy-start.7 = (s32[16,17]{1,0:T(8,128)S(1)}, s32[16,17]{1,0:T(8,128)}, u32[]{:S(2)}) copy-start(s32[16,17]{1,0:T(8,128)} %param.17) | copy-start | bytes 3268
  248.8 15.9 %collective-permute-start.3 = (f32[272,256]{1,0:T(8,128)S(1)}, f32[272,256]{1,0:T(8,128)S(1)}, u32[]{:S(2)}, u32[]{:S(2)}) collective-permute-start(f32[272,256]{1,0:T(8,128)S(1)} %get-tuple-element.19), channel_id=1, source_target_pairs={{1,0},{2,1},{3,2},{16,3},{17,16},{18,17},{19,18},{5,4},{6,5},{7,6}... | collective-permute-start | bytes 835592 | tf_op jit(solution)/shard_map/ppermute | solution.py:27
  254.2 13.7 %collective-permute-start.2 = (f32[272,256]{1,0:T(8,128)S(1)}, f32[272,256]{1,0:T(8,128)S(1)}, u32[]{:S(2)}, u32[]{:S(2)}) collective-permute-start(f32[272,256]{1,0:T(8,128)S(1)} %get-tuple-element.18), channel_id=1, source_target_pairs={{0,1},{1,2},{2,3},{3,16},{16,17},{17,18},{18,19},{4,5},{5,6},{6,7}... | collective-permute-start | bytes 835592 | tf_op jit(solution)/shard_map/ppermute | solution.py:25
  256.1 15.8 %collective-permute-start.1 = (f32[2,1,2176]{2,1,0:T(1,128)S(1)}, f32[2,1,2176]{2,1,0:T(1,128)S(1)}, u32[]{:S(2)}, u32[]{:S(2)}) collective-permute-start(f32[2,1,2176]{2,1,0:T(1,128)S(1)} %get-tuple-element.27), channel_id=1, source_target_pairs={{0,1},{1,2},{2,3},{3,16},{16,17},{17,18},{18,19},{4,5},{5,6},{6,7}... | collective-permute-start | bytes 52232 | tf_op jit(solution)/shard_map/ppermute | solution.py:25
  258.3 13.7 %collective-permute-start = (f32[2,1,2176]{2,1,0:T(1,128)S(1)}, f32[2,1,2176]{2,1,0:T(1,128)S(1)}, u32[]{:S(2)}, u32[]{:S(2)}) collective-permute-start(f32[2,1,2176]{2,1,0:T(1,128)S(1)} %get-tuple-element.26), channel_id=1, source_target_pairs={{1,0},{2,1},{3,2},{16,3},{17,16},{18,17},{19,18},{5,4},{6,5},{7,6}... | collective-permute-start | bytes 52232 | tf_op jit(solution)/shard_map/ppermute | solution.py:27
  268.9 63.5 %all-gather.3.cloned.1.call-start = ((), (), s32[]{:S(2)}) async-start(), calls=%async_computation.1 | async-start | bytes 2457600 | tf_op jit(solution)/shard_map/all_gather | solution.py:77
  303.2 20.8 %copy-start.4 = (f32[16,2176]{1,0:T(8,128)}, f32[16,2176]{1,0:T(8,128)S(1)}, u32[]{:S(2)}) copy-start(f32[16,2176]{1,0:T(8,128)S(1)} %get-tuple-element.21) | copy-start | bytes 417796
  303.2 9.1 %collective-permute-start.5 = (f32[16,2176]{1,0:T(8,128)S(1)}, f32[16,2176]{1,0:T(8,128)S(1)}, u32[]{:S(2)}, u32[]{:S(2)}) collective-permute-start(f32[16,2176]{1,0:T(8,128)S(1)} %get-tuple-element.21), channel_id=1, source_target_pairs={{1,0},{2,1},{3,2},{16,3},{17,16},{18,17},{19,18},{5,4},{6,5},{7,6}... | collective-permute-start | bytes 417800 | tf_op jit(solution)/shard_map/ppermute | solution.py:27
  308.4 9.6 %collective-permute-start.4 = (f32[16,2176]{1,0:T(8,128)S(1)}, f32[16,2176]{1,0:T(8,128)S(1)}, u32[]{:S(2)}, u32[]{:S(2)}) collective-permute-start(f32[16,2176]{1,0:T(8,128)S(1)} %get-tuple-element.21), channel_id=1, source_target_pairs={{0,1},{1,2},{2,3},{3,16},{16,17},{17,18},{18,19},{4,5},{5,6},{6,7}... | collective-permute-start | bytes 417800 | tf_op jit(solution)/shard_map/ppermute | solution.py:25
  327.8 10.6 %copy-start.1 = (bf16[2,6]{1,0:T(2,128)(2,1)S(1)}, bf16[2,6]{1,0:T(2,128)(2,1)}, u32[]{:S(2)}) copy-start(bf16[2,6]{1,0:T(2,128)(2,1)} %param.13) | copy-start | bytes 76
Sparse Core Ops, SparseCore 0:
  269.0 32.3 all-reduce.1
  303.5 22.2 all-gather.2
where the time goes:
time: 346 us; the launch traced here: 345 us
  other arithmetic  118 us (34%)
  matrix products  70.5 us (20%)
  local copies, waits for them, and re-layouts  67.7 us (20%)
  waiting for transfers between devices  40.2 us (12%)
  starting transfers between devices  29.4 us (8%)
  between operations  14.5 us (4%)
  blocking collectives  5.52 us (2%)
    scatter-add x1, other arithmetic, body(): jax.ops.segment_sum(block_rows, every_slot, num_segments=3 * tile_count)  77.7 us
    dot_general x1, matrix products, body(): jnp.einsum('ql,qljk->qjk', column_weight, masked, preferred_element_type=...  42.8 us
    psum x1, waiting for transfers between devices, body(): tile_sums = lax.psum(arrived, 'lev')  29.3 us
    select_n x1, other arithmetic, body(): jnp.where(point_mask[None, None], atmos_fields, jnp.zeros((), jnp.bfloat16))  28.9 us
    dot_general x1, matrix products, body(): jnp.dot(masked.reshape(-1, lon_count), table, preferred_element_type=jnp....  21.6 us
    transpose x1, local copies, waits for them, and re-layouts, body(): block_rows = partial_sum.reshape(FIELDS, lat_band, lon_count // BLOCK, BL...  21.4 us
    ppermute x3, starting transfers between devices, with_halo(): lax.ppermute(head, axis, [((i + 1) % count, i) for i in range(ends)])  17 us
    reshape x1, local copies, waits for them, and re-layouts, body(): partial_sum.reshape(FIELDS, lat_band, lon_count // BLOCK, BLOCK)  16.2 us
  transfers between devices with their start and end apart: 9, of which 4 were waited for; matrix products, arithmetic and copies ran while one was open for 55% of the time, Pallas kernels for 0%

commit v1 on v0

--- a/solution.py
+++ b/solution.py
@@ -3,6 +3,8 @@
 import jax
 import jax.numpy as jnp
 from jax import lax
+from jax.experimental import pallas as pl
+from jax.experimental.pallas import tpu as pltpu
 from jax.sharding import PartitionSpec as P
 
 FIELDS = 2
@@ -39,6 +41,85 @@
     return (table, points)
 
 
+def row_block(rows):
+    for size in (32, 16):
+        if rows % size == 0:
+            return size
+    return rows
+
+
+def transform_kernel(points_ref, cells_ref, table_ref, weight_ref, slot_ref, sums_ref, acc_ref):
+    step = pl.program_id(0)
+
+    @pl.when(step == 0)
+    def _():
+        acc_ref[...] = jnp.zeros_like(acc_ref)
+
+    nfields, nlev, rows, lon_count = cells_ref.shape
+    nslot = acc_ref.shape[0]
+    table = table_ref[...]
+    inside = lax.broadcasted_iota(jnp.int32, (rows, lon_count), 1) < points_ref[...]
+    cells = jnp.where(inside[None, None], cells_ref[...], jnp.zeros((), jnp.bfloat16))
+    if rows % 16 == 0:
+        sums = jnp.dot(
+            cells.reshape(nfields * nlev * rows, lon_count), table, preferred_element_type=jnp.float32
+        )
+        sums_ref[...] = sums.reshape(sums_ref.shape)
+    else:
+        for f in range(nfields):
+            for l in range(nlev):
+                sums_ref[f, l] = jnp.dot(cells[f, l], table, preferred_element_type=jnp.float32)
+    pieces = []
+    for f in range(nfields):
+        flux = weight_ref[f, 0] * cells[f, 0].astype(jnp.float32)
+        for l in range(1, nlev):
+            flux = flux + weight_ref[f, l] * cells[f, l].astype(jnp.float32)
+        high = flux.astype(jnp.bfloat16).astype(jnp.float32)
+        pieces.append(high)
+        pieces.append(flux - high)
+    nblocks = lon_count // BLOCK
+    stacked = jnp.concatenate(
+        [
+            jnp.concatenate([p[:, b * BLOCK : (b + 1) * BLOCK] for p in pieces], axis=1)
+            for b in range(nblocks)
+        ],
+        axis=0,
+    ).astype(jnp.bfloat16)
+    onehot = (
+        lax.broadcasted_iota(jnp.int32, (nslot, nblocks * rows), 0) == slot_ref[0]
+    ).astype(jnp.bfloat16)
+    acc_ref[...] += jnp.dot(onehot, stacked, preferred_element_type=jnp.float32)
+
+
+def fused_transform(atmos_fields, lat_points, table, column_weight, slots, nslot):
+    nfields, nlev, lat_band, lon_count = atmos_fields.shape
+    rows = row_block(lat_band)
+    steps = lat_band // rows
+    nblocks = lon_count // BLOCK
+    wave2 = table.shape[1]
+    slot_rows = slots.reshape(steps, rows, nblocks).transpose(0, 2, 1).reshape(steps, 1, nblocks * rows)
+    return pl.pallas_call(
+        transform_kernel,
+        grid=(steps,),
+        in_specs=[
+            pl.BlockSpec((rows, 1), lambda r: (r, 0)),
+            pl.BlockSpec((nfields, nlev, rows, lon_count), lambda r: (0, 0, r, 0)),
+            pl.BlockSpec((lon_count, wave2), lambda r: (0, 0)),
+            pl.BlockSpec(memory_space=pltpu.SMEM),
+            pl.BlockSpec((1, 1, nblocks * rows), lambda r: (r, 0, 0)),
+        ],
+        out_specs=[
+            pl.BlockSpec((nfields, nlev, rows, wave2), lambda r: (0, 0, r, 0)),
+            pl.BlockSpec((nslot, 2 * nfields * BLOCK), lambda r: (0, 0)),
+        ],
+        out_shape=[
+            jax.ShapeDtypeStruct((nfields, nlev, lat_band, wave2), jnp.float32),
+            jax.ShapeDtypeStruct((nslot, 2 * nfields * BLOCK), jnp.float32),
+        ],
+        compiler_params=pltpu.CompilerParams(dimension_semantics=("arbitrary",)),
+    )(lat_points[:, None], atmos_fields, table, column_weight.astype(jnp.float32), slot_rows)
+
+
 def body(
     atmos_fields,
     lat_points,
@@ -53,16 +134,27 @@
     nfields, lev_dev, lat_band, lon_count = atmos_fields.shape
     wave_count = wave_order.shape[0]
     table, points = fourier_table(wave_order, lon_count)
-    point_mask = points[None, :] < lat_points[:, None]
-    masked = jnp.where(point_mask[None, None], atmos_fields, jnp.zeros((), jnp.bfloat16))
     inverse_root = 1.0 / jnp.sqrt(lat_points.astype(jnp.float32))
     weights = jnp.where(
         2 * wave_order[None, :] < lat_points[:, None],
         inverse_root[:, None],
         jnp.zeros((), jnp.float32),
     )
-    field_count = masked.shape[0]
-    raw_sums = jnp.dot(masked.reshape(-1, lon_count), table, preferred_element_type=jnp.float32)
+    field_count = nfields
+    ocean_rows, ocean_cols = ocean_temp.shape
+    tile_count = ocean_rows * ocean_cols // BLOCK
+    band_index = lax.axis_index(("lat", "ocn"))
+
+    def slot_of(targets):
+        return (targets // tile_count - band_index + 1) * tile_count + targets % tile_count
+
+    local_slot = slot_of(block_remap.reshape(-1))
+    quarter = lon_count // lax.axis_size("lev")
+    full_remap = lax.all_gather(block_remap, "lev", axis=1, tiled=True)
+    every_slot = slot_of(full_remap)
+    raw_sums, split_sums = fused_transform(
+        atmos_fields, lat_points, table, column_weight, every_slot, 3 * tile_count
+    )
     raw_sums = raw_sums.reshape(field_count, lev_dev, lat_band, 2, wave_count)
     coeffs = (raw_sums * weights[None, None, :, None, :]).astype(jnp.bfloat16)
     regrouped = lax.all_to_all(
@@ -78,26 +170,8 @@
         legendre,
         preferred_element_type=jnp.float32,
     )
-    ocean_rows, ocean_cols = ocean_temp.shape
-    tile_count = ocean_rows * ocean_cols // BLOCK
-    band_index = lax.axis_index(("lat", "ocn"))
-
-    def slot_of(targets):
-        return (targets // tile_count - band_index + 1) * tile_count + targets % tile_count
-
-    local_slot = slot_of(block_remap.reshape(-1))
-    partial_sum = jnp.einsum(
-        "ql,qljk->qjk", column_weight, masked, preferred_element_type=jnp.float32
-    )
-    quarter = lon_count // lax.axis_size("lev")
-    full_remap = lax.all_gather(block_remap, "lev", axis=1, tiled=True)
-    every_slot = slot_of(full_remap.reshape(-1))
-    block_rows = (
-        partial_sum.reshape(FIELDS, lat_band, lon_count // BLOCK, BLOCK)
-        .transpose(1, 2, 0, 3)
-        .reshape(-1, FIELDS * BLOCK)
-    )
-    outgoing = jax.ops.segment_sum(block_rows, every_slot, num_segments=3 * tile_count)
+    split_sums = split_sums.reshape(3 * tile_count, FIELDS, 2, BLOCK)
+    outgoing = (split_sums[:, :, 0] + split_sums[:, :, 1]).reshape(3 * tile_count, FIELDS * BLOCK)
     widened = with_halo(outgoing, ((("lat", "ocn"), 0),), tile_count)
     arrived = (
         widened[:tile_count] + widened[2 * tile_count : 3 * tile_count] + widened[4 * tile_count :]

time: 346 us -> 187 us (0.54)
  other arithmetic: 118 us -> 23.2 us
  matrix products: 70.5 us -> 6.05 us
  local copies, waits for them, and re-layouts: 67.7 us -> 29.4 us
  Pallas kernels: 0 us -> 36.9 us
    scatter-add x1 -> x0, other arithmetic: 77.7 us -> none  [body(): jax.ops.segment_sum(block_rows, every_slot, num_segments=3 * tile_count)]
    dot_general x2 -> x0, matrix products: 64.4 us -> none  [the longest x1 42.8 us: body(): jnp.einsum('ql,qljk->qjk', column_weight, masked, preferred_element_type=...]
    pallas_call x0 -> x1, Pallas kernels: none -> 36.9 us  [fused_transform(): pl.pallas_call(transform_kernel, grid=(steps,), in_specs=[pl.BlockSpec((r...]
    select_n x1 -> x0, other arithmetic: 28.9 us -> none  [body(): jnp.where(point_mask[None, None], atmos_fields, jnp.zeros((), jnp.bfloat16))]
    transpose x1 -> x2, local copies, waits for them, and re-layouts: 21.4 us -> 0.23 us  [the longest x1 0.16 us: fused_transform(): slots.reshape(steps, rows, nblocks).transpose(0, 2, 1)]
    reshape x1 -> x2, local copies, waits for them, and re-layouts: 16.2 us -> 3.1 us  [the longest x1 2.32 us: body(): split_sums = split_sums.reshape(3 * tile_count, FIELDS, 2, BLOCK)]
    dot_general x1 -> x0, local copies, waits for them, and re-layouts: 11.2 us -> none  [body(): jnp.einsum('ql,qljk->qjk', column_weight, masked, preferred_element_type=...]
    another operation x1, other arithmetic: 4.03 us -> 11.6 us
  transfers between devices with their start and end apart: 9 -> 9, of which waited for: 4 -> 4; matrix products, arithmetic and copies ran while one was open for 55% -> 13% of each run, Pallas kernels for 0% -> 0%
where the time goes in v1:
time: 187 us; the launch traced here: 186 us
  waiting for transfers between devices  41.3 us (22%)
  Pallas kernels  36.9 us (20%)
  local copies, waits for them, and re-layouts  29.4 us (16%)
  starting transfers between devices  29.1 us (16%)
  other arithmetic  23.2 us (12%)
  between operations  14.5 us (8%)
  matrix products  6.05 us (3%)
  blocking collectives  5.55 us (3%)
    pallas_call x1, Pallas kernels, fused_transform(): pl.pallas_call(transform_kernel, grid=(steps,), in_specs=[pl.BlockSpec((r...  36.9 us
    psum x1, waiting for transfers between devices, body(): tile_sums = lax.psum(arrived, 'lev')  29.1 us
    ppermute x3, starting transfers between devices, with_halo(): lax.ppermute(head, axis, [((i + 1) % count, i) for i in range(ends)])  16.8 us
    another operation x1, other arithmetic  11.6 us
    ppermute x3, waiting for transfers between devices, with_halo(): lax.ppermute(tail, axis, [(i, (i + 1) % count) for i in range(ends)])  10.3 us
    gather x3, local copies, waits for them, and re-layouts, body(): jnp.take(tiles_near, local_slot, axis=0).reshape(lat_band, quarter)  9.65 us
    all_to_all x1, starting transfers between devices, body(): lax.all_to_all(coeffs.transpose(4, 1, 0, 3, 2).reshape(wave_count, lev_de...  6.34 us
    dot_general x1, matrix products, body(): jnp.einsum('srj,sjd->srd', lax.all_gather(regrouped, 'lev', axis=1, tiled...  6.05 us
  transfers between devices with their start and end apart: 9, of which 4 were waited for; matrix products, arithmetic and copies ran while one was open for 13% of the time, Pallas kernels for 0%

profile of v1, /device:TPU:4, one launch (start us, length us, event | category | flops | bytes accessed | tf_op | source)
XLA Modules:
  0.0 186.1 jit_solution(5519194676723965044)
XLA Ops:
  7.2 5.5 %all-gather = s32[4,11,320]{2,1,0:T(8,128)S(1)} all-gather(s32[1,11,320]{2,1,0:T(8,128)} %bitcast.79), channel_id=1, replica_groups=mesh['lat'=2,'lev'=4,'ocn'=4] {'lev'}, dimensions={0}, use_global_device_ids=true | all-gather | bytes 70400 | tf_op jit(solution)/shard_map/all_gather | solution.py:153
  12.8 1.5 broadcast_in_dim.54.points_ref
  14.9 2.0 %fusion = f32[5632,32]{0,1:T(8,128)} fusion(s32[32]{0:T(128)} %param.11), kind=kLoop, calls=%fused_computation.8 | loop fusion | flops 1441792 | bytes 721024 | tf_op jit(solution)/shard_map/convert_element_type | solution.py:39
  17.6 1.9 %copy.42 = f32[5632,32]{1,0:T(8,128)S(1)} copy(f32[5632,32]{0,1:T(8,128)} %fusion) | data formatting | bytes 1441792 | tf_op jit(solution)/shard_map/convert_element_type | solution.py:39
  19.5 11.6 %cosine_convert_fusion = (bf16[5632,32]{1,0:T(8,128)(2,1)}, bf16[5632,32]{1,0:T(8,128)(2,1)}) fusion(f32[5632,32]{1,0:T(8,128)S(1)} %copy.42), kind=kLoop, calls=%fused_computation.2 | loop fusion | flops 720896 | bytes 1441792 | tf_op jit(solution)/shard_map/convert
  32.0 0.8 reshape.218.slot_ref
  32.8 3.3 %pad_maximum_fusion.table_ref = bf16[5632,64]{1,0:T(8,128)(2,1)} fusion(bf16[5632,32]{1,0:T(8,128)(2,1)} %get-tuple-element.26, bf16[5632,32]{1,0:T(8,128)(2,1)S(1)} %copy-done), kind=kLoop, calls=%fused_computation.4 | loop fusion | flops 1441792 | bytes 1441792 | tf_op jit(solution)/shard_map/concatenate | solution.py:40
  36.1 36.9 %shard_map.120 = (f32[2,6,320,64]{3,2,1,0:T(8,128)}, f32[816,512]{1,0:T(8,128)}) custom-call(s32[320,1]{1,0:T(8,128)} %broadcast_in_dim.54.points_ref, bf16[2,6,320,5632]{3,2,1,0:T(8,128)(2,1)} %cells_ref.1, bf16[5632,64]{1,0:T(8,128)(2,1)} %pad_maximum_fusion.table_ref, f32[2,6]{1,0:T(2,128)} %convert_element_type.23.weight_ref, ...), custom_call_target="tpu_custom_call" | custom-call | tf_op jit(solution)/shard_map/pallas_call | solution.py:101
  73.0 2.2 %copy.47 = f32[2,6,320,64]{2,3,1,0:T(8,128)S(1)} copy(f32[2,6,320,64]{3,2,1,0:T(8,128)} %get-tuple-element.6) | data formatting | bytes 1966080 | tf_op jit(solution)/shard_map/pallas_call | solution.py:101
  75.5 1.0 copy.49
  76.5 6.3 %all-to-all-start = ((bf16[32,24,320]{2,1,0:T(8,128)(2,1)}), bf16[32,24,320]{2,1,0:T(8,128)(2,1)S(1)}, u32[]{:S(2)}, u32[]{:S(2)}) async-start(bf16[32,24,320]{2,1,0:T(8,128)(2,1)} %copy.49), calls=%async_computation | async-start | bytes 1179648 | tf_op jit(solution)/shard_map/all_to_all | solution.py:160
  82.9 2.3 %reshape.197 = f32[816,2,2,128]{3,2,1,0:T(2,128)S(1)} reshape(f32[816,512]{1,0:T(8,128)} %get-tuple-element.7) | data formatting | bytes 3342336 | tf_op jit(solution)/shard_map/reshape | solution.py:173
  85.2 0.9 slice_add_fusion
  86.1 2.5 %slice_reduce_fusion.1 = (f32[272,2,128]{2,1,0:T(2,128)S(1)}, f32[272,2,128]{2,1,0:T(2,128)S(1)}, f32[272,2,128]{2,1,0:T(2,128)S(1)}) fusion(f32[816,2,1,128]{3,2,1,0:T(1,128)S(1)} %slice_add_fusion), kind=kLoop, calls=%fused_computation.35 | loop fusion | bytes 1671168 | tf_op jit(solution)/shard_map/slice | solution.py:177
  88.7 5.2 %collective-permute-start.3 = (f32[272,256]{1,0:T(8,128)S(1)}, f32[272,256]{1,0:T(8,128)S(1)}, u32[]{:S(2)}, u32[]{:S(2)}) collective-permute-start(f32[272,256]{1,0:T(8,128)S(1)} %bitcast.77), channel_id=1, source_target_pairs={{1,0},{2,1},{3,2},{16,3},{17,16},{18,17},{19,18},{5,4},{6,5},{7,6}... | collective-permute-start | bytes 835592 | tf_op jit(solution)/shard_map/ppermute | solution.py:29
  93.9 1.9 %collective-permute-start.2 = (f32[272,256]{1,0:T(8,128)S(1)}, f32[272,256]{1,0:T(8,128)S(1)}, u32[]{:S(2)}, u32[]{:S(2)}) collective-permute-start(f32[272,256]{1,0:T(8,128)S(1)} %bitcast.78), channel_id=1, source_target_pairs={{0,1},{1,2},{2,3},{3,16},{16,17},{17,18},{18,19},{4,5},{5,6},{6,7}... | collective-permute-start | bytes 835592 | tf_op jit(solution)/shard_map/ppermute | solution.py:27
  95.9 2.1 %collective-permute-start.1 = (f32[2,1,2176]{2,1,0:T(1,128)S(1)}, f32[2,1,2176]{2,1,0:T(1,128)S(1)}, u32[]{:S(2)}, u32[]{:S(2)}) collective-permute-start(f32[2,1,2176]{2,1,0:T(1,128)S(1)} %get-tuple-element.34), channel_id=1, source_target_pairs={{0,1},{1,2},{2,3},{3,16},{16,17},{17,18},{18,19},{4,5},{5,6},{6,7}... | collective-permute-start | bytes 52232 | tf_op jit(solution)/shard_map/ppermute | solution.py:27
  98.0 6.4 %collective-permute-start = (f32[2,1,2176]{2,1,0:T(1,128)S(1)}, f32[2,1,2176]{2,1,0:T(1,128)S(1)}, u32[]{:S(2)}, u32[]{:S(2)}) collective-permute-start(f32[2,1,2176]{2,1,0:T(1,128)S(1)} %get-tuple-element.33), channel_id=1, source_target_pairs={{1,0},{2,1},{3,2},{16,3},{17,16},{18,17},{19,18},{5,4},{6,5},{7,6}... | collective-permute-start | bytes 52232 | tf_op jit(solution)/shard_map/ppermute | solution.py:29
  104.4 4.5 %collective-permute-done.2 = f32[272,256]{1,0:T(8,128)S(1)} collective-permute-done((f32[272,256]{1,0:T(8,128)S(1)}, f32[272,256]{1,0:T(8,128)S(1)}, u32[]{:S(2)}, u32[]{:S(2)}) %collective-permute-start.2) | collective-permute-done | bytes 278560 | tf_op jit(solution)/shard_map/ppermute | solution.py:27
  110.9 1.2 all_to_all.16
  113.1 29.1 %all-reduce.2.cloned.1.call-done = f32[2,16,2176]{2,1,0:T(8,128)} async-done(((f32[2,16,2176]{2,1,0:T(8,128)}), f32[2,16,2176]{2,1,0:T(8,128)}) %all-reduce.2.cloned.1.call-update) | async-done | bytes 278544 | tf_op jit(solution)/shard_map/psum | solution.py:179
  142.2 1.1 fusion.14
  144.0 5.2 %collective-permute-start.5 = (f32[16,2176]{1,0:T(8,128)S(1)}, f32[16,2176]{1,0:T(8,128)S(1)}, u32[]{:S(2)}, u32[]{:S(2)}) collective-permute-start(f32[16,2176]{1,0:T(8,128)S(1)} %get-tuple-element.28), channel_id=1, source_target_pairs={{1,0},{2,1},{3,2},{16,3},{17,16},{18,17},{19,18},{5,4},{6,5},{7,6}... | collective-permute-start | bytes 417800 | tf_op jit(solution)/shard_map/ppermute | solution.py:29
  149.2 1.9 %collective-permute-start.4 = (f32[16,2176]{1,0:T(8,128)S(1)}, f32[16,2176]{1,0:T(8,128)S(1)}, u32[]{:S(2)}, u32[]{:S(2)}) collective-permute-start(f32[16,2176]{1,0:T(8,128)S(1)} %get-tuple-element.28), channel_id=1, source_target_pairs={{0,1},{1,2},{2,3},{3,16},{16,17},{17,18},{18,19},{4,5},{5,6},{6,7}... | collective-permute-start | bytes 417800 | tf_op jit(solution)/shard_map/ppermute | solution.py:27
  151.2 1.9 %collective-permute-done.5 = f32[16,2176]{1,0:T(8,128)S(1)} collective-permute-done((f32[16,2176]{1,0:T(8,128)S(1)}, f32[16,2176]{1,0:T(8,128)S(1)}, u32[]{:S(2)}, u32[]{:S(2)}) %collective-permute-start.5) | collective-permute-done | bytes 139296 | tf_op jit(solution)/shard_map/ppermute | solution.py:29
  153.1 5.8 %collective-permute-done.4 = f32[16,2176]{1,0:T(8,128)S(1)} collective-permute-done((f32[16,2176]{1,0:T(8,128)S(1)}, f32[16,2176]{1,0:T(8,128)S(1)}, u32[]{:S(2)}, u32[]{:S(2)}) %collective-permute-start.4) | collective-permute-done | bytes 139296 | tf_op jit(solution)/shard_map/ppermute | solution.py:27
  159.0 5.9 %gather_fusion = f32[3520,128]{1,0:T(8,128)S(1)} fusion(f32[816,128]{1,0:T(8,128)S(1)} %reshape.200, s32[4096]{0:T(1024)S(1)} %pad_clamp_fusion), kind=kCustom, calls=%fused_computation | custom fusion | bytes 3618560 | tf_op jit(solution)/shard_map/jit(_take)/gather | solution.py:204
  164.8 1.6 gather.7
  166.4 2.2 %copy.55 = f32[320,1408]{0,1:T(8,128)S(1)} copy(f32[320,1408]{1,0:T(8,128)} %gather.7) | data formatting | bytes 3604480 | tf_op jit(solution)/shard_map/jit(_take)/gather | solution.py:204
  168.6 1.7 select_select_fusion
  170.3 2.9 %copy.56 = f32[320,1408]{1,0:T(8,128)} copy(f32[320,1408]{0,1:T(8,128)} %select_select_fusion) | data formatting | bytes 3604480
  173.2 6.1 %fusion.30 = f32[4,96,384]{2,1,0:T(8,128)} fusion(bf16[4,96,2560]{2,1,0:T(8,128)(2,1)} %all-gather.3.cloned.1.call-done, bf16[4,2560,384]{2,1,0:T(8,128)(2,1)} %param.12), kind=kOutput, calls=%fused_computation.90 | convolution fusion | flops 754974720 | bytes 10420224 | tf_op jit(solution)/shard_map/srj,sjd->srd/dot_general | solution.py:167
  (66 shorter events, 6.3 us)
Async XLA Ops:
  19.5 11.6 %copy-start.7 = (bf16[2,6]{1,0:T(2,128)(2,1)S(1)}, bf16[2,6]{1,0:T(2,128)(2,1)}, u32[]{:S(2)}) copy-start(bf16[2,6]{1,0:T(2,128)(2,1)} %param.13) | copy-start | bytes 76
  31.1 1.8 copy-start
  73.0 2.2 %copy-start.5 = (s32[320]{0:T(512)S(1)}, s32[320]{0:T(512)}, u32[]{:S(2)}) copy-start(s32[320]{0:T(512)} %param.10) | copy-start | bytes 3844
  76.5 34.2 %all-to-all-start = ((bf16[32,24,320]{2,1,0:T(8,128)(2,1)}), bf16[32,24,320]{2,1,0:T(8,128)(2,1)S(1)}, u32[]{:S(2)}, u32[]{:S(2)}) async-start(bf16[32,24,320]{2,1,0:T(8,128)(2,1)} %copy.49), calls=%async_computation | async-start | bytes 1179648 | tf_op jit(solution)/shard_map/all_to_all | solution.py:160
  82.9 59.3 %all-reduce.2.cloned.1.call-start = ((), (), s32[]{:S(2)}) async-start(), calls=%async_computation.2 | async-start | bytes 557056 | tf_op jit(solution)/shard_map/psum | solution.py:179
  86.1 9.8 %copy-start.1 = (f32[16,2176]{1,0:T(8,128)S(1)}, f32[16,2176]{1,0:T(8,128)}, u32[]{:S(2)}) copy-start(f32[16,2176]{1,0:T(8,128)} %param.15) | copy-start | bytes 417796
  86.1 9.7 %copy-start.2 = (f32[16,2176]{1,0:T(8,128)S(1)}, f32[16,2176]{1,0:T(8,128)}, u32[]{:S(2)}) copy-start(f32[16,2176]{1,0:T(8,128)} %param.16) | copy-start | bytes 417796
  88.7 15.8 %collective-permute-start.3 = (f32[272,256]{1,0:T(8,128)S(1)}, f32[272,256]{1,0:T(8,128)S(1)}, u32[]{:S(2)}, u32[]{:S(2)}) collective-permute-start(f32[272,256]{1,0:T(8,128)S(1)} %bitcast.77), channel_id=1, source_target_pairs={{1,0},{2,1},{3,2},{16,3},{17,16},{18,17},{19,18},{5,4},{6,5},{7,6}... | collective-permute-start | bytes 835592 | tf_op jit(solution)/shard_map/ppermute | solution.py:29
  93.8 16.1 %copy-start.4 = (s32[320,11]{0,1:T(8,128)S(1)}, s32[320,11]{0,1:T(8,128)}, u32[]{:S(2)}) copy-start(s32[320,11]{0,1:T(8,128)} %param.14) | copy-start | bytes 42244
  93.9 15.0 %collective-permute-start.2 = (f32[272,256]{1,0:T(8,128)S(1)}, f32[272,256]{1,0:T(8,128)S(1)}, u32[]{:S(2)}, u32[]{:S(2)}) collective-permute-start(f32[272,256]{1,0:T(8,128)S(1)} %bitcast.78), channel_id=1, source_target_pairs={{0,1},{1,2},{2,3},{3,16},{16,17},{17,18},{18,19},{4,5},{5,6},{6,7}... | collective-permute-start | bytes 835592 | tf_op jit(solution)/shard_map/ppermute | solution.py:27
  95.9 17.2 %collective-permute-start.1 = (f32[2,1,2176]{2,1,0:T(1,128)S(1)}, f32[2,1,2176]{2,1,0:T(1,128)S(1)}, u32[]{:S(2)}, u32[]{:S(2)}) collective-permute-start(f32[2,1,2176]{2,1,0:T(1,128)S(1)} %get-tuple-element.34), channel_id=1, source_target_pairs={{0,1},{1,2},{2,3},{3,16},{16,17},{17,18},{18,19},{4,5},{5,6},{6,7}... | collective-permute-start | bytes 52232 | tf_op jit(solution)/shard_map/ppermute | solution.py:27
  98.0 15.1 %collective-permute-start = (f32[2,1,2176]{2,1,0:T(1,128)S(1)}, f32[2,1,2176]{2,1,0:T(1,128)S(1)}, u32[]{:S(2)}, u32[]{:S(2)}) collective-permute-start(f32[2,1,2176]{2,1,0:T(1,128)S(1)} %get-tuple-element.33), channel_id=1, source_target_pairs={{1,0},{2,1},{3,2},{16,3},{17,16},{18,17},{19,18},{5,4},{6,5},{7,6}... | collective-permute-start | bytes 52232 | tf_op jit(solution)/shard_map/ppermute | solution.py:29
  109.9 2.8 %copy-start.6 = (s32[16,17]{1,0:T(8,128)S(1)}, s32[16,17]{1,0:T(8,128)}, u32[]{:S(2)}) copy-start(s32[16,17]{1,0:T(8,128)} %param.17) | copy-start | bytes 3268
  109.9 63.2 %all-gather.3.cloned.1.call-start = ((), (), s32[]{:S(2)}) async-start(), calls=%async_computation.1 | async-start | bytes 2457600 | tf_op jit(solution)/shard_map/all_gather | solution.py:169
  144.0 20.8 %copy-start.3 = (f32[16,2176]{1,0:T(8,128)}, f32[16,2176]{1,0:T(8,128)S(1)}, u32[]{:S(2)}) copy-start(f32[16,2176]{1,0:T(8,128)S(1)} %get-tuple-element.28) | copy-start | bytes 417796
  144.0 9.1 %collective-permute-start.5 = (f32[16,2176]{1,0:T(8,128)S(1)}, f32[16,2176]{1,0:T(8,128)S(1)}, u32[]{:S(2)}, u32[]{:S(2)}) collective-permute-start(f32[16,2176]{1,0:T(8,128)S(1)} %get-tuple-element.28), channel_id=1, source_target_pairs={{1,0},{2,1},{3,2},{16,3},{17,16},{18,17},{19,18},{5,4},{6,5},{7,6}... | collective-permute-start | bytes 417800 | tf_op jit(solution)/shard_map/ppermute | solution.py:29
  149.2 9.6 %collective-permute-start.4 = (f32[16,2176]{1,0:T(8,128)S(1)}, f32[16,2176]{1,0:T(8,128)S(1)}, u32[]{:S(2)}, u32[]{:S(2)}) collective-permute-start(f32[16,2176]{1,0:T(8,128)S(1)} %get-tuple-element.28), channel_id=1, source_target_pairs={{0,1},{1,2},{2,3},{3,16},{16,17},{17,18},{18,19},{4,5},{5,6},{6,7}... | collective-permute-start | bytes 417800 | tf_op jit(solution)/shard_map/ppermute | solution.py:27
Sparse Core Ops, SparseCore 0:
  110.0 32.1 all-reduce.1
  144.3 22.2 all-gather.2

commit v2 on v1

--- a/solution.py
+++ b/solution.py
@@ -35,10 +35,39 @@
 
 def fourier_table(wave_order, length):
     points = jnp.arange(length, dtype=jnp.int32)
-    phase = wave_order[None, :] * points[:, None] % length
+    phase = wave_order[:, None] * points[None, :] % length
     angle = phase.astype(jnp.float32) * (FULL_TURN / length)
-    table = jnp.concatenate([jnp.cos(angle), -jnp.sin(angle)], axis=1).astype(jnp.bfloat16)
+    table = jnp.concatenate([jnp.cos(angle), -jnp.sin(angle)], axis=0).astype(jnp.bfloat16)
     return (table, points)
+
+
+def lev_sum(values):
+    count = lax.axis_size("lev")
+    if count & (count - 1):
+        return lax.psum(values, "lev")
+    stride = 1
+    while stride < count:
+        values = values + lax.ppermute(values, "lev", [(i, i ^ stride) for i in range(count)])
+        stride *= 2
+    return values
+
+
+def lev_gather(values, axis):
+    count = lax.axis_size("lev")
+    if count & (count - 1):
+        return lax.all_gather(values, "lev", axis=axis, tiled=True)
+    index = lax.axis_index("lev")
+    stride = 1
+    while stride < count:
+        other = lax.ppermute(values, "lev", [(i, i ^ stride) for i in range(count)])
+        upper = (index // stride) % 2 == 1
+        values = jnp.where(
+            upper,
+            jnp.concatenate([other, values], axis=axis),
+            jnp.concatenate([values, other], axis=axis),
+        )
+        stride *= 2
+    return values
 
 
 def row_block(rows):
@@ -61,14 +90,19 @@
     inside = lax.broadcasted_iota(jnp.int32, (rows, lon_count), 1) < points_ref[...]
     cells = jnp.where(inside[None, None], cells_ref[...], jnp.zeros((), jnp.bfloat16))
     if rows % 16 == 0:
-        sums = jnp.dot(
-            cells.reshape(nfields * nlev * rows, lon_count), table, preferred_element_type=jnp.float32
+        sums = lax.dot_general(
+            cells.reshape(nfields * nlev * rows, lon_count),
+            table,
+            (((1,), (1,)), ((), ())),
+            preferred_element_type=jnp.float32,
         )
         sums_ref[...] = sums.reshape(sums_ref.shape)
     else:
         for f in range(nfields):
             for l in range(nlev):
-                sums_ref[f, l] = jnp.dot(cells[f, l], table, preferred_element_type=jnp.float32)
+                sums_ref[f, l] = lax.dot_general(
+                    cells[f, l], table, (((1,), (1,)), ((), ())), preferred_element_type=jnp.float32
+                )
     pieces = []
     for f in range(nfields):
         flux = weight_ref[f, 0] * cells[f, 0].astype(jnp.float32)
@@ -96,7 +130,7 @@
     rows = row_block(lat_band)
     steps = lat_band // rows
     nblocks = lon_count // BLOCK
-    wave2 = table.shape[1]
+    wave2 = table.shape[0]
     slot_rows = slots.reshape(steps, rows, nblocks).transpose(0, 2, 1).reshape(steps, 1, nblocks * rows)
     return pl.pallas_call(
         transform_kernel,
@@ -104,7 +138,7 @@
         in_specs=[
             pl.BlockSpec((rows, 1), lambda r: (r, 0)),
             pl.BlockSpec((nfields, nlev, rows, lon_count), lambda r: (0, 0, r, 0)),
-            pl.BlockSpec((lon_count, wave2), lambda r: (0, 0)),
+            pl.BlockSpec((wave2, lon_count), lambda r: (0, 0)),
             pl.BlockSpec(memory_space=pltpu.SMEM),
             pl.BlockSpec((1, 1, nblocks * rows), lambda r: (r, 0, 0)),
         ],
@@ -150,7 +184,7 @@
 
     local_slot = slot_of(block_remap.reshape(-1))
     quarter = lon_count // lax.axis_size("lev")
-    full_remap = lax.all_gather(block_remap, "lev", axis=1, tiled=True)
+    full_remap = lev_gather(block_remap, 1)
     every_slot = slot_of(full_remap)
     raw_sums, split_sums = fused_transform(
         atmos_fields, lat_points, table, column_weight, every_slot, 3 * tile_count
@@ -166,7 +200,7 @@
     )
     spectra = jnp.einsum(
         "srj,sjd->srd",
-        lax.all_gather(regrouped, "lev", axis=1, tiled=True),
+        lev_gather(regrouped, 1),
         legendre,
         preferred_element_type=jnp.float32,
     )
@@ -176,7 +210,7 @@
     arrived = (
         widened[:tile_count] + widened[2 * tile_count : 3 * tile_count] + widened[4 * tile_count :]
     )
-    tile_sums = lax.psum(arrived, "lev")
+    tile_sums = lev_sum(arrived)
     forcing = (
         tile_sums.reshape(ocean_rows, ocean_cols // BLOCK, FIELDS, BLOCK)
         .transpose(2, 0, 1, 3)

time: 187 us -> 135 us (0.72)
  waiting for transfers between devices: 41.3 us -> 17.8 us
  between operations: 14.5 us -> 1.13 us
  other arithmetic: 23.2 us -> 14.6 us
  blocking collectives: 5.55 us -> 0 us
  local copies, waits for them, and re-layouts: 29.4 us -> 25.4 us
  starting transfers between devices: 29.1 us -> 32.9 us
    psum x1 -> x0, waiting for transfers between devices: 29.1 us -> none  [body(): tile_sums = lax.psum(arrived, 'lev')]
    ppermute x0 -> x6, waiting for transfers between devices: none -> 11 us  [the longest x2 7.22 us: lev_sum(): lax.ppermute(values, 'lev', [(i, i ^ stride) for i in range(count)])]
    another operation x1, other arithmetic: 11.6 us -> 4.02 us
    ppermute x3, starting transfers between devices: 16.8 us -> 10.9 us  [with_halo(): lax.ppermute(head, axis, [((i + 1) % count, i) for i in range(ends)])]
    ppermute x3, waiting for transfers between devices: 10.3 us -> 4.48 us  [with_halo(): lax.ppermute(tail, axis, [(i, (i + 1) % count) for i in range(ends)])]
    ppermute x3, starting transfers between devices: 5.97 us -> 11.6 us  [with_halo(): lax.ppermute(tail, axis, [(i, (i + 1) % count) for i in range(ends)])]
    all_gather x1 -> x0, blocking collectives: 5.55 us -> none  [body(): full_remap = lax.all_gather(block_remap, 'lev', axis=1, tiled=True)]
    ppermute x0 -> x6, starting transfers between devices: none -> 4.88 us  [the longest x4 3.25 us: lev_gather(): other = lax.ppermute(values, 'lev', [(i, i ^ stride) for i in range(count)])]
  transfers between devices with their start and end apart: 9 -> 13, of which waited for: 4 -> 8; matrix products, arithmetic and copies ran while one was open for 13% -> 29% of each run, Pallas kernels for 0% -> 27%
where the time goes in v2:
time: 135 us; the launch traced here: 134 us
  Pallas kernels  36 us (27%)
  starting transfers between devices  32.9 us (24%)
  local copies, waits for them, and re-layouts  25.4 us (19%)
  waiting for transfers between devices  17.8 us (13%)
  other arithmetic  14.6 us (11%)
  matrix products  6.14 us (5%)
    pallas_call x1, Pallas kernels, fused_transform(): pl.pallas_call(transform_kernel, grid=(steps,), in_specs=[pl.BlockSpec((r...  36 us
    ppermute x3, starting transfers between devices, with_halo(): lax.ppermute(tail, axis, [(i, (i + 1) % count) for i in range(ends)])  11.6 us
    ppermute x3, starting transfers between devices, with_halo(): lax.ppermute(head, axis, [((i + 1) % count, i) for i in range(ends)])  10.9 us
    gather x3, local copies, waits for them, and re-layouts, body(): jnp.take(tiles_near, local_slot, axis=0).reshape(lat_band, quarter)  9.65 us
    ppermute x2, waiting for transfers between devices, lev_sum(): lax.ppermute(values, 'lev', [(i, i ^ stride) for i in range(count)])  7.22 us
    dot_general x1, matrix products, body(): jnp.einsum('srj,sjd->srd', lev_gather(regrouped, 1), legendre, preferred_...  6.14 us
    all_to_all x1, starting transfers between devices, body(): lax.all_to_all(coeffs.transpose(4, 1, 0, 3, 2).reshape(wave_count, lev_de...  5.52 us
    ppermute x3, waiting for transfers between devices, with_halo(): lax.ppermute(tail, axis, [(i, (i + 1) % count) for i in range(ends)])  4.48 us
  transfers between devices with their start and end apart: 13, of which 8 were waited for; matrix products, arithmetic and copies ran while one was open for 29% of the time, Pallas kernels for 27%

profile of v2, /device:TPU:4, one launch (start us, length us, event | category | flops | bytes accessed | tf_op | source)
XLA Modules:
  0.0 134.0 jit_solution(6118807535064563168)
XLA Ops:
  0.8 1.6 %fusion.33 = (f32[2,1,2176]{2,1,0:T(1,128)}, f32[2,1,2176]{2,1,0:T(1,128)}) fusion(f32[1,16,2176]{2,1,0:T(8,128)} %bitcast.46, f32[1,16,2176]{2,1,0:T(8,128)} %bitcast.50), kind=kLoop, calls=%fused_computation.87 | loop fusion | flops 8704 | bytes 313344 | tf_op jit(solution)/shard_map/stack | solution.py:224
  2.4 3.5 %collective-permute-start.5 = (f32[2,1,2176]{2,1,0:T(1,128)}, f32[2,1,2176]{2,1,0:T(1,128)S(1)}, u32[]{:S(2)}, u32[]{:S(2)}) collective-permute-start(f32[2,1,2176]{2,1,0:T(1,128)} %get-tuple-element.32), channel_id=1, source_target_pairs={{0,1},{1,2},{2,3},{3,16},{16,17},{17,18},{18,19},{4,5},{5,6},{6,7}... | collective-permute-start | bytes 52232 | tf_op jit(solution)/shard_map/ppermute | solution.py:27
  5.9 5.1 %collective-permute-start.4 = (f32[2,1,2176]{2,1,0:T(1,128)}, f32[2,1,2176]{2,1,0:T(1,128)S(1)}, u32[]{:S(2)}, u32[]{:S(2)}) collective-permute-start(f32[2,1,2176]{2,1,0:T(1,128)} %get-tuple-element.31), channel_id=1, source_target_pairs={{1,0},{2,1},{3,2},{16,3},{17,16},{18,17},{19,18},{5,4},{6,5},{7,6}... | collective-permute-start | bytes 52232 | tf_op jit(solution)/shard_map/ppermute | solution.py:29
  10.9 2.0 %fusion.14 = (f32[2,16,2175]{2,1,0:T(8,128)}, f32[2,16,2175]{2,1,0:T(8,128)}) fusion(f32[1,16,2176]{2,1,0:T(8,128)} %bitcast.47, f32[1,16,2176]{2,1,0:T(8,128)} %bitcast.51), kind=kLoop, calls=%fused_computation.39 | loop fusion | flops 139200 | bytes 835328 | tf_op jit(solution)/shard_map/stack | solution.py:224
  12.9 4.0 %cosine_convert_fusion = (bf16[32,5632]{1,0:T(8,128)(2,1)S(1)}, bf16[32,5632]{1,0:T(8,128)(2,1)S(1)}) fusion(s32[32]{0:T(128)} %param.11), kind=kLoop, calls=%fused_computation.18 | loop fusion | flops 2162688 | bytes 721024 | tf_op jit(solution)/shard_map/convert
  17.6 0.9 pad_maximum_fusion.table_ref
  20.1 1.6 %collective-permute-start.1 = (s32[320,22]{0,1:T(8,128)S(1)}, s32[320,22]{0,1:T(8,128)S(1)}, u32[]{:S(2)}, u32[]{:S(2)}) collective-permute-start(s32[320,22]{0,1:T(8,128)S(1)} %add_select_fusion.7), channel_id=1, source_target_pairs={{0,8},{4,12},{8,0},{12,4},{1,9},{5,13},{9,1},{13,5},{2,10},{6,14},... | collective-permute-start | bytes 84488 | tf_op jit(solution)/shard_map/ppermute | solution.py:62
  21.9 2.2 %collective-permute-done.1 = s32[320,22]{0,1:T(8,128)S(1)} collective-permute-done((s32[320,22]{0,1:T(8,128)S(1)}, s32[320,22]{0,1:T(8,128)S(1)}, u32[]{:S(2)}, u32[]{:S(2)}) %collective-permute-start.1) | collective-permute-done | bytes 28192 | tf_op jit(solution)/shard_map/ppermute | solution.py:62
  25.4 36.0 %shard_map.120 = (f32[2,6,320,64]{3,2,1,0:T(8,128)}, f32[816,512]{1,0:T(8,128)}) custom-call(s32[320,1]{1,0:T(8,128)} %broadcast_in_dim.54.points_ref, bf16[2,6,320,5632]{3,2,1,0:T(8,128)(2,1)} %cells_ref.1, bf16[64,5632]{1,0:T(8,128)(2,1)} %pad_maximum_fusion.table_ref, f32[2,6]{1,0:T(2,128)} %convert_element_type.23.weight_ref, ...), custom_call_target="tpu_custom_call" | custom-call | tf_op jit(solution)/shard_map/pallas_call | solution.py:135
  61.4 2.3 %reshape.202 = f32[816,2,2,128]{3,2,1,0:T(2,128)S(1)} reshape(f32[816,512]{1,0:T(8,128)} %get-tuple-element.7) | data formatting | bytes 3342336 | tf_op jit(solution)/shard_map/reshape | solution.py:207
  64.6 2.5 %slice_reduce_fusion.1 = (f32[272,2,128]{2,1,0:T(2,128)S(1)}, f32[272,2,128]{2,1,0:T(2,128)S(1)}, f32[272,2,128]{2,1,0:T(2,128)S(1)}) fusion(f32[816,2,1,128]{3,2,1,0:T(1,128)S(1)} %slice_add_fusion), kind=kLoop, calls=%fused_computation.45 | loop fusion | bytes 1671168 | tf_op jit(solution)/shard_map/slice | solution.py:211
  67.9 2.8 %collective-permute-start.7 = (f32[272,256]{1,0:T(8,128)}, f32[272,256]{1,0:T(8,128)}, u32[]{:S(2)}, u32[]{:S(2)}) collective-permute-start(f32[272,256]{1,0:T(8,128)} %bitcast.40), channel_id=1, source_target_pairs={{1,0},{2,1},{3,2},{16,3},{17,16},{18,17},{19,18},{5,4},{6,5},{7,6}... | collective-permute-start | bytes 835592 | tf_op jit(solution)/shard_map/ppermute | solution.py:29
  71.4 3.1 %collective-permute-start.6 = (f32[272,256]{1,0:T(8,128)}, f32[272,256]{1,0:T(8,128)}, u32[]{:S(2)}, u32[]{:S(2)}) collective-permute-start(f32[272,256]{1,0:T(8,128)} %bitcast.41), channel_id=1, source_target_pairs={{0,1},{1,2},{2,3},{3,16},{16,17},{17,18},{18,19},{4,5},{5,6},{6,7}... | collective-permute-start | bytes 835592 | tf_op jit(solution)/shard_map/ppermute | solution.py:27
  75.4 1.0 copy.54
  76.4 5.5 %all-to-all-start = ((bf16[32,24,320]{2,1,0:T(8,128)(2,1)}), bf16[32,24,320]{2,1,0:T(8,128)(2,1)S(1)}, u32[]{:S(2)}, u32[]{:S(2)}) async-start(bf16[32,24,320]{2,1,0:T(8,128)(2,1)} %copy.54), calls=%async_computation | async-start | bytes 1179648 | tf_op jit(solution)/shard_map/all_to_all | solution.py:194
  82.0 1.6 %collective-permute-done.6 = f32[272,256]{1,0:T(8,128)} collective-permute-done((f32[272,256]{1,0:T(8,128)}, f32[272,256]{1,0:T(8,128)}, u32[]{:S(2)}, u32[]{:S(2)}) %collective-permute-start.6) | collective-permute-done | bytes 278560 | tf_op jit(solution)/shard_map/ppermute | solution.py:27
  83.5 1.1 fusion.15
  84.8 1.5 %collective-permute-done.8 = f32[272,256]{1,0:T(8,128)S(1)} collective-permute-done((f32[272,256]{1,0:T(8,128)S(1)}, f32[272,256]{1,0:T(8,128)S(1)}, u32[]{:S(2)}, u32[]{:S(2)}) %collective-permute-start.8) | collective-permute-done | bytes 278560 | tf_op jit(solution)/shard_map/ppermute | solution.py:50
  86.3 1.6 %collective-permute-start.9 = (f32[272,256]{1,0:T(8,128)S(1)}, f32[272,256]{1,0:T(8,128)S(1)}, u32[]{:S(2)}, u32[]{:S(2)}) collective-permute-start(f32[272,256]{1,0:T(8,128)S(1)} %add.175), channel_id=1, source_target_pairs={{0,8},{4,12},{8,0},{12,4},{1,9},{5,13},{9,1},{13,5},{2,10},{6,14},... | collective-permute-start | bytes 835592 | tf_op jit(solution)/shard_map/ppermute | solution.py:50
  89.3 5.7 %collective-permute-done.9 = f32[272,256]{1,0:T(8,128)S(1)} collective-permute-done((f32[272,256]{1,0:T(8,128)S(1)}, f32[272,256]{1,0:T(8,128)S(1)}, u32[]{:S(2)}, u32[]{:S(2)}) %collective-permute-start.9) | collective-permute-done | bytes 278560 | tf_op jit(solution)/shard_map/ppermute | solution.py:50
  96.8 1.6 %collective-permute-done.2 = bf16[4,24,2560]{2,1,0:T(8,128)(2,1)S(1)} collective-permute-done((bf16[4,24,2560]{2,1,0:T(8,128)(2,1)S(1)}, bf16[4,24,2560]{2,1,0:T(8,128)(2,1)S(1)}, u32[]{:S(2)}, u32[]{:S(2)}) %collective-permute-start.2) | collective-permute-done | bytes 491552 | tf_op jit(solution)/shard_map/ppermute | solution.py:62
  98.6 1.6 %collective-permute-start.3 = (bf16[4,48,2560]{2,1,0:T(8,128)(2,1)S(1)}, bf16[4,48,2560]{2,1,0:T(8,128)(2,1)}, u32[]{:S(2)}, u32[]{:S(2)}) collective-permute-start(bf16[4,48,2560]{2,1,0:T(8,128)(2,1)S(1)} %maximum_select_fusion.2), channel_id=1, source_target_pairs={{0,8},{4,12},{8,0},{12,4},{1,9},{5,13},{9,1},{13,5},{2,10},{6,14},... | collective-permute-start | bytes 2949128 | tf_op jit(solution)/shard_map/ppermute | solution.py:62
  100.8 3.1 %collective-permute-start.11 = (f32[16,2176]{1,0:T(8,128)S(1)}, f32[16,2176]{1,0:T(8,128)S(1)}, u32[]{:S(2)}, u32[]{:S(2)}) collective-permute-start(f32[16,2176]{1,0:T(8,128)S(1)} %get-tuple-element.26), channel_id=1, source_target_pairs={{1,0},{2,1},{3,2},{16,3},{17,16},{18,17},{19,18},{5,4},{6,5},{7,6}... | collective-permute-start | bytes 417800 | tf_op jit(solution)/shard_map/ppermute | solution.py:29
  103.9 5.1 %collective-permute-start.10 = (f32[16,2176]{1,0:T(8,128)S(1)}, f32[16,2176]{1,0:T(8,128)S(1)}, u32[]{:S(2)}, u32[]{:S(2)}) collective-permute-start(f32[16,2176]{1,0:T(8,128)S(1)} %get-tuple-element.26), channel_id=1, source_target_pairs={{0,1},{1,2},{2,3},{3,16},{16,17},{17,18},{18,19},{4,5},{5,6},{6,7}... | collective-permute-start | bytes 417800 | tf_op jit(solution)/shard_map/ppermute | solution.py:27
  109.0 1.7 %collective-permute-done.11 = f32[16,2176]{1,0:T(8,128)S(1)} collective-permute-done((f32[16,2176]{1,0:T(8,128)S(1)}, f32[16,2176]{1,0:T(8,128)S(1)}, u32[]{:S(2)}, u32[]{:S(2)}) %collective-permute-start.11) | collective-permute-done | bytes 139296 | tf_op jit(solution)/shard_map/ppermute | solution.py:29
  110.7 2.9 %collective-permute-done.10 = f32[16,2176]{1,0:T(8,128)S(1)} collective-permute-done((f32[16,2176]{1,0:T(8,128)S(1)}, f32[16,2176]{1,0:T(8,128)S(1)}, u32[]{:S(2)}, u32[]{:S(2)}) %collective-permute-start.10) | collective-permute-done | bytes 139296 | tf_op jit(solution)/shard_map/ppermute | solution.py:27
  113.7 5.9 %gather_fusion = f32[3520,128]{1,0:T(8,128)S(1)} fusion(f32[816,128]{1,0:T(8,128)S(1)} %reshape.205, s32[4096]{0:T(1024)S(1)} %pad_clamp_fusion), kind=kCustom, calls=%fused_computation | custom fusion | bytes 3618560 | tf_op jit(solution)/shard_map/jit(_take)/gather | solution.py:238
  119.6 1.6 %gather.7 = f32[320,1408]{1,0:T(8,128)} reshape(f32[3520,128]{1,0:T(8,128)S(1)} %gather_fusion) | data formatting | bytes 3604480 | tf_op jit(solution)/shard_map/jit(_take)/gather | solution.py:238
  121.1 2.2 %copy.60 = f32[320,1408]{0,1:T(8,128)S(1)} copy(f32[320,1408]{1,0:T(8,128)} %gather.7) | data formatting | bytes 3604480 | tf_op jit(solution)/shard_map/jit(_take)/gather | solution.py:238
  123.4 1.6 %select_select_fusion = f32[320,1408]{0,1:T(8,128)} fusion(f32[320,1408]{0,1:T(8,128)S(1)} %copy.60, s32[320]{0:T(512)S(1)} %copy-done.7, s32[1408]{0:T(1024)S(1)} %iota_add_fusion, pred[320,11]{0,1:T(8,128)(4,1)S(1)} %get-tuple-element.23), kind=kLoop, calls=%fused_computation.1 | loop fusion | flops 1351680 | bytes 3614912 | tf_op jit(solution)/shard_map/jit(_where)/select_n | solution.py:240
  125.0 2.9 %copy.61 = f32[320,1408]{1,0:T(8,128)} copy(f32[320,1408]{0,1:T(8,128)} %select_select_fusion) | data formatting | bytes 3604480
  127.9 6.1 %fusion = f32[4,96,384]{2,1,0:T(8,128)} fusion(bf16[4,2560,384]{2,1,0:T(8,128)(2,1)} %param.12, bf16[4,48,2560]{2,1,0:T(8,128)(2,1)S(1)} %maximum_select_fusion.2, bf16[4,48,2560]{2,1,0:T(8,128)(2,1)} %collective-permute-done.3, pred[]{:T(512)S(6)} %eq.19), kind=kOutput, calls=%fused_computation.3 | convolution fusion | flops 763822080 | bytes 10420225 | tf_op jit(solution)/shard_map/srj,sjd->srd/dot_general | solution.py:201
  (78 shorter events, 11.2 us)
Async XLA Ops:
  0.6 18.7 %copy-start.6 = (s32[320,11]{0,1:T(8,128)S(1)}, s32[320,11]{0,1:T(8,128)}, u32[]{:S(2)}) copy-start(s32[320,11]{0,1:T(8,128)} %param.14) | copy-start | bytes 42244
  0.6 17.9 %copy-start.9 = (s32[32]{0:T(128)S(1)}, s32[32]{0:T(128)}, u32[]{:S(2)}) copy-start(s32[32]{0:T(128)} %param.11) | copy-start | bytes 388
  0.7 17.9 %copy-start.7 = (s32[320]{0:T(512)S(1)}, s32[320]{0:T(512)}, u32[]{:S(2)}) copy-start(s32[320]{0:T(512)} %param.10) | copy-start | bytes 3844
  0.7 18.8 %copy-start.10 = (bf16[2,6]{1,0:T(2,128)(2,1)S(1)}, bf16[2,6]{1,0:T(2,128)(2,1)}, u32[]{:S(2)}) copy-start(bf16[2,6]{1,0:T(2,128)(2,1)} %param.13) | copy-start | bytes 76
  0.7 19.4 %collective-permute-start = (s32[320,11]{0,1:T(8,128)}, s32[320,11]{0,1:T(8,128)S(1)}, u32[]{:S(2)}, u32[]{:S(2)}) collective-permute-start(s32[320,11]{0,1:T(8,128)} %param.14), channel_id=1, source_target_pairs={{0,4},{4,0},{8,12},{12,8},{1,5},{5,1},{9,13},{13,9},{2,6},{6,2},{1... | collective-permute-start | bytes 42248 | tf_op jit(solution)/shard_map/ppermute | solution.py:62
  2.4 94.2 %collective-permute-start.5 = (f32[2,1,2176]{2,1,0:T(1,128)}, f32[2,1,2176]{2,1,0:T(1,128)S(1)}, u32[]{:S(2)}, u32[]{:S(2)}) collective-permute-start(f32[2,1,2176]{2,1,0:T(1,128)} %get-tuple-element.32), channel_id=1, source_target_pairs={{0,1},{1,2},{2,3},{3,16},{16,17},{17,18},{18,19},{4,5},{5,6},{6,7}... | collective-permute-start | bytes 52232 | tf_op jit(solution)/shard_map/ppermute | solution.py:27
  5.9 90.7 %collective-permute-start.4 = (f32[2,1,2176]{2,1,0:T(1,128)}, f32[2,1,2176]{2,1,0:T(1,128)S(1)}, u32[]{:S(2)}, u32[]{:S(2)}) collective-permute-start(f32[2,1,2176]{2,1,0:T(1,128)} %get-tuple-element.31), channel_id=1, source_target_pairs={{1,0},{2,1},{3,2},{16,3},{17,16},{18,17},{19,18},{5,4},{6,5},{7,6}... | collective-permute-start | bytes 52232 | tf_op jit(solution)/shard_map/ppermute | solution.py:29
  20.1 4.0 %collective-permute-start.1 = (s32[320,22]{0,1:T(8,128)S(1)}, s32[320,22]{0,1:T(8,128)S(1)}, u32[]{:S(2)}, u32[]{:S(2)}) collective-permute-start(s32[320,22]{0,1:T(8,128)S(1)} %add_select_fusion.7), channel_id=1, source_target_pairs={{0,8},{4,12},{8,0},{12,4},{1,9},{5,13},{9,1},{13,5},{2,10},{6,14},... | collective-permute-start | bytes 84488 | tf_op jit(solution)/shard_map/ppermute | solution.py:62
  64.6 9.9 %copy-start.2 = (f32[2,6,320,64]{3,2,1,0:T(8,128)S(1)}, f32[2,6,320,64]{3,2,1,0:T(8,128)}, u32[]{:S(2)}) copy-start(f32[2,6,320,64]{3,2,1,0:T(8,128)} %get-tuple-element.6) | copy-start | bytes 2949124
  67.9 14.1 %collective-permute-start.7 = (f32[272,256]{1,0:T(8,128)}, f32[272,256]{1,0:T(8,128)}, u32[]{:S(2)}, u32[]{:S(2)}) collective-permute-start(f32[272,256]{1,0:T(8,128)} %bitcast.40), channel_id=1, source_target_pairs={{1,0},{2,1},{3,2},{16,3},{17,16},{18,17},{19,18},{5,4},{6,5},{7,6}... | collective-permute-start | bytes 835592 | tf_op jit(solution)/shard_map/ppermute | solution.py:29
  71.4 12.1 %collective-permute-start.6 = (f32[272,256]{1,0:T(8,128)}, f32[272,256]{1,0:T(8,128)}, u32[]{:S(2)}, u32[]{:S(2)}) collective-permute-start(f32[272,256]{1,0:T(8,128)} %bitcast.41), channel_id=1, source_target_pairs={{0,1},{1,2},{2,3},{3,16},{16,17},{17,18},{18,19},{4,5},{5,6},{6,7}... | collective-permute-start | bytes 835592 | tf_op jit(solution)/shard_map/ppermute | solution.py:27
  75.4 12.4 %copy-start.8 = (s32[16,17]{1,0:T(8,128)S(1)}, s32[16,17]{1,0:T(8,128)}, u32[]{:S(2)}) copy-start(s32[16,17]{1,0:T(8,128)} %param.17) | copy-start | bytes 3268
  76.4 12.6 %copy-start = (f32[16,2176]{1,0:T(8,128)S(1)}, f32[16,2176]{1,0:T(8,128)}, u32[]{:S(2)}) copy-start(f32[16,2176]{1,0:T(8,128)} %param.15) | copy-start | bytes 417796
  76.4 12.6 %copy-start.1 = (f32[16,2176]{1,0:T(8,128)S(1)}, f32[16,2176]{1,0:T(8,128)}, u32[]{:S(2)}) copy-start(f32[16,2176]{1,0:T(8,128)} %param.16) | copy-start | bytes 417796
  76.4 19.4 %all-to-all-start = ((bf16[32,24,320]{2,1,0:T(8,128)(2,1)}), bf16[32,24,320]{2,1,0:T(8,128)(2,1)S(1)}, u32[]{:S(2)}, u32[]{:S(2)}) async-start(bf16[32,24,320]{2,1,0:T(8,128)(2,1)} %copy.54), calls=%async_computation | async-start | bytes 1179648 | tf_op jit(solution)/shard_map/all_to_all | solution.py:194
  84.6 1.6 %collective-permute-start.8 = (f32[272,256]{1,0:T(8,128)S(1)}, f32[272,256]{1,0:T(8,128)S(1)}, u32[]{:S(2)}, u32[]{:S(2)}) collective-permute-start(f32[272,256]{1,0:T(8,128)S(1)} %fusion.15), channel_id=1, source_target_pairs={{0,4},{4,0},{8,12},{12,8},{1,5},{5,1},{9,13},{13,9},{2,6},{6,2},{1... | collective-permute-start | bytes 835592 | tf_op jit(solution)/shard_map/ppermute | solution.py:50
  86.3 8.8 %collective-permute-start.9 = (f32[272,256]{1,0:T(8,128)S(1)}, f32[272,256]{1,0:T(8,128)S(1)}, u32[]{:S(2)}, u32[]{:S(2)}) collective-permute-start(f32[272,256]{1,0:T(8,128)S(1)} %add.175), channel_id=1, source_target_pairs={{0,8},{4,12},{8,0},{12,4},{1,9},{5,13},{9,1},{13,5},{2,10},{6,14},... | collective-permute-start | bytes 835592 | tf_op jit(solution)/shard_map/ppermute | solution.py:50
  95.1 1.5 %copy-start.3 = (f32[2,16,2175]{2,1,0:T(8,128)S(1)}, f32[2,16,2175]{2,1,0:T(8,128)}, u32[]{:S(2)}) copy-start(f32[2,16,2175]{2,1,0:T(8,128)} %get-tuple-element.27) | copy-start | bytes 835204
  95.1 1.5 %copy-start.4 = (f32[2,16,2175]{2,1,0:T(8,128)S(1)}, f32[2,16,2175]{2,1,0:T(8,128)}, u32[]{:S(2)}) copy-start(f32[2,16,2175]{2,1,0:T(8,128)} %get-tuple-element.28) | copy-start | bytes 835204
  96.5 1.9 %collective-permute-start.2 = (bf16[4,24,2560]{2,1,0:T(8,128)(2,1)S(1)}, bf16[4,24,2560]{2,1,0:T(8,128)(2,1)S(1)}, u32[]{:S(2)}, u32[]{:S(2)}) collective-permute-start(bf16[4,24,2560]{2,1,0:T(8,128)(2,1)S(1)} %all_to_all.16), channel_id=1, source_target_pairs={{0,4},{4,0},{8,12},{12,8},{1,5},{5,1},{9,13},{13,9},{2,6},{6,2},{1... | collective-permute-start | bytes 1474568 | tf_op jit(solution)/shard_map/ppermute | solution.py:62
  98.6 29.3 %collective-permute-start.3 = (bf16[4,48,2560]{2,1,0:T(8,128)(2,1)S(1)}, bf16[4,48,2560]{2,1,0:T(8,128)(2,1)}, u32[]{:S(2)}, u32[]{:S(2)}) collective-permute-start(bf16[4,48,2560]{2,1,0:T(8,128)(2,1)S(1)} %maximum_select_fusion.2), channel_id=1, source_target_pairs={{0,8},{4,12},{8,0},{12,4},{1,9},{5,13},{9,1},{13,5},{2,10},{6,14},... | collective-permute-start | bytes 2949128 | tf_op jit(solution)/shard_map/ppermute | solution.py:62
  100.8 18.8 %copy-start.5 = (f32[16,2176]{1,0:T(8,128)}, f32[16,2176]{1,0:T(8,128)S(1)}, u32[]{:S(2)}) copy-start(f32[16,2176]{1,0:T(8,128)S(1)} %get-tuple-element.26) | copy-start | bytes 417796
  100.8 9.9 %collective-permute-start.11 = (f32[16,2176]{1,0:T(8,128)S(1)}, f32[16,2176]{1,0:T(8,128)S(1)}, u32[]{:S(2)}, u32[]{:S(2)}) collective-permute-start(f32[16,2176]{1,0:T(8,128)S(1)} %get-tuple-element.26), channel_id=1, source_target_pairs={{1,0},{2,1},{3,2},{16,3},{17,16},{18,17},{19,18},{5,4},{6,5},{7,6}... | collective-permute-start | bytes 417800 | tf_op jit(solution)/shard_map/ppermute | solution.py:29
  103.9 9.7 %collective-permute-start.10 = (f32[16,2176]{1,0:T(8,128)S(1)}, f32[16,2176]{1,0:T(8,128)S(1)}, u32[]{:S(2)}, u32[]{:S(2)}) collective-permute-start(f32[16,2176]{1,0:T(8,128)S(1)} %get-tuple-element.26), channel_id=1, source_target_pairs={{0,1},{1,2},{2,3},{3,16},{16,17},{17,18},{18,19},{4,5},{5,6},{6,7}... | collective-permute-start | bytes 417800 | tf_op jit(solution)/shard_map/ppermute | solution.py:27

commit v3 on v2

--- a/solution.py
+++ b/solution.py
@@ -43,13 +43,12 @@
 
 def lev_sum(values):
     count = lax.axis_size("lev")
-    if count & (count - 1):
+    if count != 4:
         return lax.psum(values, "lev")
-    stride = 1
-    while stride < count:
-        values = values + lax.ppermute(values, "lev", [(i, i ^ stride) for i in range(count)])
-        stride *= 2
-    return values
+    near, far, both = (
+        lax.ppermute(values, "lev", [(i, i ^ d) for i in range(count)]) for d in (1, 2, 3)
+    )
+    return (values + near) + (far + both)
 
 
 def lev_gather(values, axis):
@@ -57,17 +56,13 @@
     if count & (count - 1):
         return lax.all_gather(values, "lev", axis=axis, tiled=True)
     index = lax.axis_index("lev")
-    stride = 1
-    while stride < count:
-        other = lax.ppermute(values, "lev", [(i, i ^ stride) for i in range(count)])
-        upper = (index // stride) % 2 == 1
-        values = jnp.where(
-            upper,
-            jnp.concatenate([other, values], axis=axis),
-            jnp.concatenate([values, other], axis=axis),
-        )
-        stride *= 2
-    return values
+    pieces = [values] + [
+        lax.ppermute(values, "lev", [(i, i ^ d) for i in range(count)]) for d in range(1, count)
+    ]
+    stacked = jnp.stack(pieces)
+    order = jnp.bitwise_xor(index, jnp.arange(count, dtype=jnp.int32))
+    ordered = jnp.take(stacked, order, axis=0)
+    return jnp.concatenate([ordered[i] for i in range(count)], axis=axis)
 
 
 def row_block(rows):

time: 135 us -> 153 us (1.13)
  waiting for transfers between devices: 17.8 us -> 27.2 us
  other arithmetic: 14.6 us -> 20.9 us
  local copies, waits for them, and re-layouts: 25.4 us -> 28.6 us
    all_to_all x1, waiting for transfers between devices: 0.54 us -> 9.45 us  [body(): lax.all_to_all(coeffs.transpose(4, 1, 0, 3, 2).reshape(wave_count, lev_de...]
    ppermute x3, starting transfers between devices: 11.6 us -> 8.66 us  [with_halo(): lax.ppermute(tail, axis, [(i, (i + 1) % count) for i in range(ends)])]
    gather x0 -> x2, local copies, waits for them, and re-layouts: none -> 2.53 us  [lev_gather(): ordered = jnp.take(stacked, order, axis=0)]
    ppermute x6 -> x9, waiting for transfers between devices: 11 us -> 8.68 us  [the longest x6 7.69 us: lev_gather(): lax.ppermute(values, 'lev', [(i, i ^ d) for i in range(count)])]
    ppermute x3, waiting for transfers between devices: 1.73 us -> 3.85 us  [with_halo(): lax.ppermute(head, axis, [((i + 1) % count, i) for i in range(ends)])]
    select_n x3, other arithmetic: 0.2 us -> 1.88 us  [lev_gather(): ordered = jnp.take(stacked, order, axis=0)]
    another operation x1 -> x3, other arithmetic: 4.02 us -> 5.62 us
    ppermute x6 -> x9, starting transfers between devices: 4.88 us -> 5.93 us  [the longest x6 3.79 us: lev_gather(): lax.ppermute(values, 'lev', [(i, i ^ d) for i in range(count)])]
  transfers between devices with their start and end apart: 13 -> 16, of which waited for: 8 -> 5; matrix products, arithmetic and copies ran while one was open for 29% -> 28% of each run, Pallas kernels for 27% -> 24%
where the time goes in v3:
time: 153 us; the launch traced here: 152 us
  Pallas kernels  36 us (24%)
  starting transfers between devices  33 us (22%)
  local copies, waits for them, and re-layouts  28.6 us (19%)
  waiting for transfers between devices  27.2 us (18%)
  other arithmetic  20.9 us (14%)
  matrix products  5.54 us (4%)
    pallas_call x1, Pallas kernels, fused_transform(): pl.pallas_call(transform_kernel, grid=(steps,), in_specs=[pl.BlockSpec((r...  36 us
    ppermute x3, starting transfers between devices, with_halo(): lax.ppermute(head, axis, [((i + 1) % count, i) for i in range(ends)])  12.1 us
    gather x3, local copies, waits for them, and re-layouts, body(): jnp.take(tiles_near, local_slot, axis=0).reshape(lat_band, quarter)  9.65 us
    all_to_all x1, waiting for transfers between devices, body(): lax.all_to_all(coeffs.transpose(4, 1, 0, 3, 2).reshape(wave_count, lev_de...  9.45 us
    ppermute x3, starting transfers between devices, with_halo(): lax.ppermute(tail, axis, [(i, (i + 1) % count) for i in range(ends)])  8.66 us
    ppermute x6, waiting for transfers between devices, lev_gather(): lax.ppermute(values, 'lev', [(i, i ^ d) for i in range(count)])  7.69 us
    all_to_all x1, starting transfers between devices, body(): lax.all_to_all(coeffs.transpose(4, 1, 0, 3, 2).reshape(wave_count, lev_de...  6.24 us
    dot_general x1, matrix products, body(): jnp.einsum('srj,sjd->srd', lev_gather(regrouped, 1), legendre, preferred_...  5.54 us
  transfers between devices with their start and end apart: 16, of which 5 were waited for; matrix products, arithmetic and copies ran while one was open for 28% of the time, Pallas kernels for 24%

profile of v3, /device:TPU:4, one launch (start us, length us, event | category | flops | bytes accessed | tf_op | source)
XLA Modules:
  0.0 152.4 jit_solution(5023157906224656933)
XLA Ops:
  2.6 1.6 %fusion.34 = (f32[2,1,2176]{2,1,0:T(1,128)}, f32[2,1,2176]{2,1,0:T(1,128)}) fusion(f32[1,16,2176]{2,1,0:T(8,128)} %bitcast.67, f32[1,16,2176]{2,1,0:T(8,128)} %bitcast.71), kind=kLoop, calls=%fused_computation.96 | loop fusion | flops 8704 | bytes 313344 | tf_op jit(solution)/shard_map/stack | solution.py:219
  4.2 3.5 %collective-permute-start.7 = (f32[2,1,2176]{2,1,0:T(1,128)}, f32[2,1,2176]{2,1,0:T(1,128)}, u32[]{:S(2)}, u32[]{:S(2)}) collective-permute-start(f32[2,1,2176]{2,1,0:T(1,128)} %get-tuple-element.32), channel_id=1, source_target_pairs={{0,1},{1,2},{2,3},{3,16},{16,17},{17,18},{18,19},{4,5},{5,6},{6,7}... | collective-permute-start | bytes 52232 | tf_op jit(solution)/shard_map/ppermute | solution.py:27
  7.7 5.1 %collective-permute-start.6 = (f32[2,1,2176]{2,1,0:T(1,128)}, f32[2,1,2176]{2,1,0:T(1,128)}, u32[]{:S(2)}, u32[]{:S(2)}) collective-permute-start(f32[2,1,2176]{2,1,0:T(1,128)} %get-tuple-element.31), channel_id=1, source_target_pairs={{1,0},{2,1},{3,2},{16,3},{17,16},{18,17},{19,18},{5,4},{6,5},{7,6}... | collective-permute-start | bytes 52232 | tf_op jit(solution)/shard_map/ppermute | solution.py:29
  12.8 4.0 %cosine_convert_fusion = (bf16[32,5632]{1,0:T(8,128)(2,1)S(1)}, bf16[32,5632]{1,0:T(8,128)(2,1)S(1)}) fusion(s32[32]{0:T(128)} %param.11), kind=kLoop, calls=%fused_computation.21 | loop fusion | flops 2162688 | bytes 721024 | tf_op jit(solution)/shard_map/convert
  16.8 1.2 broadcast_multiply_fusion
  18.0 2.0 %fusion.15 = (f32[2,16,2175]{2,1,0:T(8,128)}, f32[2,16,2175]{2,1,0:T(8,128)}) fusion(f32[1,16,2176]{2,1,0:T(8,128)} %bitcast.68, f32[1,16,2176]{2,1,0:T(8,128)} %bitcast.72), kind=kLoop, calls=%fused_computation.47 | loop fusion | flops 139200 | bytes 835328 | tf_op jit(solution)/shard_map/stack | solution.py:219
  26.8 36.0 %shard_map.120 = (f32[2,6,320,64]{3,2,1,0:T(8,128)}, f32[816,512]{1,0:T(8,128)}) custom-call(s32[320,1]{1,0:T(8,128)} %broadcast_in_dim.78.points_ref, bf16[2,6,320,5632]{3,2,1,0:T(8,128)(2,1)} %cells_ref.1, bf16[64,5632]{1,0:T(8,128)(2,1)} %pad_maximum_fusion.1.table_ref, f32[2,6]{1,0:T(2,128)} %convert_element_type.23.weight_ref, ...), custom_call_target="tpu_custom_call" | custom-call | tf_op jit(solution)/shard_map/pallas_call | solution.py:130
  62.8 2.3 %reshape.224 = f32[816,2,2,128]{3,2,1,0:T(2,128)S(1)} reshape(f32[816,512]{1,0:T(8,128)} %get-tuple-element.7) | data formatting | bytes 3342336 | tf_op jit(solution)/shard_map/reshape | solution.py:202
  66.0 2.5 %slice_reduce_fusion.1 = (f32[272,2,128]{2,1,0:T(2,128)S(1)}, f32[272,2,128]{2,1,0:T(2,128)S(1)}, f32[272,2,128]{2,1,0:T(2,128)S(1)}) fusion(f32[816,2,1,128]{3,2,1,0:T(1,128)S(1)} %slice_add_fusion), kind=kLoop, calls=%fused_computation.53 | loop fusion | bytes 1671168 | tf_op jit(solution)/shard_map/slice | solution.py:206
  68.6 2.9 %collective-permute-start.9 = (f32[272,256]{1,0:T(8,128)S(1)}, f32[272,256]{1,0:T(8,128)S(1)}, u32[]{:S(2)}, u32[]{:S(2)}) collective-permute-start(f32[272,256]{1,0:T(8,128)S(1)} %bitcast.85), channel_id=1, source_target_pairs={{1,0},{2,1},{3,2},{16,3},{17,16},{18,17},{19,18},{5,4},{6,5},{7,6}... | collective-permute-start | bytes 835592 | tf_op jit(solution)/shard_map/ppermute | solution.py:29
  71.5 3.3 %collective-permute-start.8 = (f32[272,256]{1,0:T(8,128)S(1)}, f32[272,256]{1,0:T(8,128)S(1)}, u32[]{:S(2)}, u32[]{:S(2)}) collective-permute-start(f32[272,256]{1,0:T(8,128)S(1)} %bitcast.86), channel_id=1, source_target_pairs={{0,1},{1,2},{2,3},{3,16},{16,17},{17,18},{18,19},{4,5},{5,6},{6,7}... | collective-permute-start | bytes 835592 | tf_op jit(solution)/shard_map/ppermute | solution.py:27
  75.0 3.8 %collective-permute-done.9 = f32[272,256]{1,0:T(8,128)S(1)} collective-permute-done((f32[272,256]{1,0:T(8,128)S(1)}, f32[272,256]{1,0:T(8,128)S(1)}, u32[]{:S(2)}, u32[]{:S(2)}) %collective-permute-start.9) | collective-permute-done | bytes 278560 | tf_op jit(solution)/shard_map/ppermute | solution.py:29
  78.8 5.2 %collective-permute-done.8 = f32[272,256]{1,0:T(8,128)S(1)} collective-permute-done((f32[272,256]{1,0:T(8,128)S(1)}, f32[272,256]{1,0:T(8,128)S(1)}, u32[]{:S(2)}, u32[]{:S(2)}) %collective-permute-start.8) | collective-permute-done | bytes 278560 | tf_op jit(solution)/shard_map/ppermute | solution.py:27
  84.8 1.4 collective-permute-start.11
  88.7 1.0 copy.39
  89.7 6.2 %all-to-all-start = ((bf16[32,24,320]{2,1,0:T(8,128)(2,1)}), bf16[32,24,320]{2,1,0:T(8,128)(2,1)S(1)}, u32[]{:S(2)}, u32[]{:S(2)}) async-start(bf16[32,24,320]{2,1,0:T(8,128)(2,1)} %copy.39), calls=%async_computation | async-start | bytes 1179648 | tf_op jit(solution)/shard_map/all_to_all | solution.py:189
  97.0 1.3 add_add_fusion
  100.2 4.2 %collective-permute-start.14 = (f32[16,2176]{1,0:T(8,128)S(1)}, f32[16,2176]{1,0:T(8,128)S(1)}, u32[]{:S(2)}, u32[]{:S(2)}) collective-permute-start(f32[16,2176]{1,0:T(8,128)S(1)} %get-tuple-element.26), channel_id=1, source_target_pairs={{1,0},{2,1},{3,2},{16,3},{17,16},{18,17},{19,18},{5,4},{6,5},{7,6}... | collective-permute-start | bytes 417800 | tf_op jit(solution)/shard_map/ppermute | solution.py:29
  104.4 1.9 %collective-permute-start.13 = (f32[16,2176]{1,0:T(8,128)S(1)}, f32[16,2176]{1,0:T(8,128)S(1)}, u32[]{:S(2)}, u32[]{:S(2)}) collective-permute-start(f32[16,2176]{1,0:T(8,128)S(1)} %get-tuple-element.26), channel_id=1, source_target_pairs={{0,1},{1,2},{2,3},{3,16},{16,17},{17,18},{18,19},{4,5},{5,6},{6,7}... | collective-permute-start | bytes 417800 | tf_op jit(solution)/shard_map/ppermute | solution.py:27
  106.3 9.4 %all-to-all-done = bf16[32,24,320]{2,1,0:T(8,128)(2,1)S(1)} async-done(((bf16[32,24,320]{2,1,0:T(8,128)(2,1)}), bf16[32,24,320]{2,1,0:T(8,128)(2,1)S(1)}, u32[]{:S(2)}, u32[]{:S(2)}) %all-to-all-start) | async-done | bytes 491552 | tf_op jit(solution)/shard_map/all_to_all | solution.py:189
  115.9 1.2 all_to_all.16
  117.1 1.4 collective-permute-start.4
  119.1 5.9 %gather_fusion.2 = f32[3520,128]{1,0:T(8,128)S(1)} fusion(f32[816,128]{1,0:T(8,128)S(1)} %reshape.227, s32[4096]{0:T(1024)S(1)} %pad_clamp_fusion), kind=kCustom, calls=%fused_computation.2 | custom fusion | bytes 3618560 | tf_op jit(solution)/shard_map/jit(_take)/gather | solution.py:233
  124.9 1.6 %gather.17 = f32[320,1408]{1,0:T(8,128)} reshape(f32[3520,128]{1,0:T(8,128)S(1)} %gather_fusion.2) | data formatting | bytes 3604480 | tf_op jit(solution)/shard_map/jit(_take)/gather | solution.py:233
  126.5 2.2 %copy.45 = f32[320,1408]{0,1:T(8,128)S(1)} copy(f32[320,1408]{1,0:T(8,128)} %gather.17) | data formatting | bytes 3604480 | tf_op jit(solution)/shard_map/jit(_take)/gather | solution.py:233
  128.7 1.7 %select_select_fusion = f32[320,1408]{0,1:T(8,128)} fusion(f32[320,1408]{0,1:T(8,128)S(1)} %copy.45, s32[320]{0:T(512)S(1)} %copy-done.8, s32[1408]{0:T(1024)S(1)} %iota_add_fusion, pred[320,11]{0,1:T(8,128)(4,1)S(1)} %get-tuple-element.19), kind=kLoop, calls=%fused_computation.3 | loop fusion | flops 1351680 | bytes 3614912 | tf_op jit(solution)/shard_map/jit(_where)/select_n | solution.py:235
  130.4 2.9 %copy.46 = f32[320,1408]{1,0:T(8,128)} copy(f32[320,1408]{0,1:T(8,128)} %select_select_fusion) | data formatting | bytes 3604480
  133.7 7.7 %collective-permute-done.4 = bf16[4,24,2560]{2,1,0:T(8,128)(2,1)} collective-permute-done((bf16[4,24,2560]{2,1,0:T(8,128)(2,1)}, bf16[4,24,2560]{2,1,0:T(8,128)(2,1)}, u32[]{:S(2)}, u32[]{:S(2)}) %collective-permute-start.4) | collective-permute-done | bytes 491552 | tf_op jit(solution)/shard_map/ppermute | solution.py:60
  141.4 1.6 %pad_maximum_fusion = bf16[4,4,24,2560]{3,2,1,0:T(8,128)(2,1)S(1)} fusion(bf16[1,4,24,2560]{3,2,1,0:T(8,128)(2,1)} %bitcast.17, bf16[1,4,24,2560]{3,2,1,0:T(8,128)(2,1)} %bitcast.16, bf16[1,4,24,2560]{3,2,1,0:T(8,128)(2,1)} %bitcast.15, bf16[1,4,24,2560]{3,2,1,0:T(8,128)(2,1)S(1)} %stack.44), kind=kLoop, calls=%fused_computation.4 | loop fusion | flops 2949120 | bytes 3932160 | tf_op jit(solution)/shard_map/stack | solution.py:62
  142.9 2.0 %gather_fusion.1 = bf16[4,4,24,2560]{3,2,1,0:T(8,128)(2,1)} fusion(bf16[4,4,24,2560]{3,2,1,0:T(8,128)(2,1)S(1)} %pad_maximum_fusion, s32[1024]{0:T(1024)S(1)} %pad_clamp_fusion.1), kind=kCustom, calls=%fused_computation.1 | custom fusion | bytes 3932176 | tf_op jit(solution)/shard_map/jit(_take)/gather | solution.py:64
  144.9 1.8 %broadcast_select_fusion = bf16[4,4,24,2560]{3,2,1,0:T(8,128)(2,1)S(1)} fusion(bf16[4,4,24,2560]{3,2,1,0:T(8,128)(2,1)} %gather_fusion.1, pred[4]{0:T(512)(128)(4,1)S(1)} %compare_and_fusion.1), kind=kLoop, calls=%fused_computation.13 | loop fusion | flops 983040 | bytes 3932164 | tf_op jit(solution)/shard_map/jit(_take)/select_n | solution.py:64
  146.9 5.5 %fusion = f32[4,96,384]{2,1,0:T(8,128)} fusion(bf16[4,2560,384]{2,1,0:T(8,128)(2,1)} %param.12, bf16[4,24,2560]{2,1,0:T(8,128)(2,1)S(1)} %get-tuple-element.22, bf16[4,24,2560]{2,1,0:T(8,128)(2,1)S(1)} %get-tuple-element.23, bf16[4,24,2560]{2,1,0:T(8,128)(2,1)S(1)} %get-tuple-element.24, bf16[4,24,2560]{2,1,0:T(8,128)(2,1)S(1)} %get-tuple-element.21), kind=kOutput, calls=%fused_computation.5 | convolution fusion | flops 762839040 | bytes 10420224 | tf_op jit(solution)/shard_map/srj,sjd->srd/dot_general | solution.py:196
  (94 shorter events, 16.8 us)
Async XLA Ops:
  0.6 20.3 %copy-start.7 = (s32[320,11]{0,1:T(8,128)S(1)}, s32[320,11]{0,1:T(8,128)}, u32[]{:S(2)}) copy-start(s32[320,11]{0,1:T(8,128)} %param.14) | copy-start | bytes 42244
  0.6 20.2 %copy-start.8 = (s32[320]{0:T(512)S(1)}, s32[320]{0:T(512)}, u32[]{:S(2)}) copy-start(s32[320]{0:T(512)} %param.10) | copy-start | bytes 3844
  0.7 20.2 %copy-start.9 = (s32[16,17]{1,0:T(8,128)S(1)}, s32[16,17]{1,0:T(8,128)}, u32[]{:S(2)}) copy-start(s32[16,17]{1,0:T(8,128)} %param.17) | copy-start | bytes 3268
  0.7 22.0 %copy-start.11 = (bf16[2,6]{1,0:T(2,128)(2,1)S(1)}, bf16[2,6]{1,0:T(2,128)(2,1)}, u32[]{:S(2)}) copy-start(bf16[2,6]{1,0:T(2,128)(2,1)} %param.13) | copy-start | bytes 76
  0.7 23.6 %collective-permute-start.2 = (s32[320,11]{0,1:T(8,128)}, s32[320,11]{0,1:T(8,128)S(1)}, u32[]{:S(2)}, u32[]{:S(2)}) collective-permute-start(s32[320,11]{0,1:T(8,128)} %param.14), channel_id=1, source_target_pairs={{0,12},{4,8},{8,4},{12,0},{1,13},{5,9},{9,5},{13,1},{2,14},{6,10},... | collective-permute-start | bytes 42248 | tf_op jit(solution)/shard_map/ppermute | solution.py:60
  1.7 22.7 %collective-permute-start.1 = (s32[320,11]{0,1:T(8,128)}, s32[320,11]{0,1:T(8,128)S(1)}, u32[]{:S(2)}, u32[]{:S(2)}) collective-permute-start(s32[320,11]{0,1:T(8,128)} %param.14), channel_id=1, source_target_pairs={{0,8},{4,12},{8,0},{12,4},{1,9},{5,13},{9,1},{13,5},{2,10},{6,14},... | collective-permute-start | bytes 42248 | tf_op jit(solution)/shard_map/ppermute | solution.py:60
  2.3 22.0 %collective-permute-start = (s32[320,11]{0,1:T(8,128)}, s32[320,11]{0,1:T(8,128)S(1)}, u32[]{:S(2)}, u32[]{:S(2)}) collective-permute-start(s32[320,11]{0,1:T(8,128)} %param.14), channel_id=1, source_target_pairs={{0,4},{4,0},{8,12},{12,8},{1,5},{5,1},{9,13},{13,9},{2,6},{6,2},{1... | collective-permute-start | bytes 42248 | tf_op jit(solution)/shard_map/ppermute | solution.py:60
  4.2 94.3 %collective-permute-start.7 = (f32[2,1,2176]{2,1,0:T(1,128)}, f32[2,1,2176]{2,1,0:T(1,128)}, u32[]{:S(2)}, u32[]{:S(2)}) collective-permute-start(f32[2,1,2176]{2,1,0:T(1,128)} %get-tuple-element.32), channel_id=1, source_target_pairs={{0,1},{1,2},{2,3},{3,16},{16,17},{17,18},{18,19},{4,5},{5,6},{6,7}... | collective-permute-start | bytes 52232 | tf_op jit(solution)/shard_map/ppermute | solution.py:27
  7.7 90.8 %collective-permute-start.6 = (f32[2,1,2176]{2,1,0:T(1,128)}, f32[2,1,2176]{2,1,0:T(1,128)}, u32[]{:S(2)}, u32[]{:S(2)}) collective-permute-start(f32[2,1,2176]{2,1,0:T(1,128)} %get-tuple-element.31), channel_id=1, source_target_pairs={{1,0},{2,1},{3,2},{16,3},{17,16},{18,17},{19,18},{5,4},{6,5},{7,6}... | collective-permute-start | bytes 52232 | tf_op jit(solution)/shard_map/ppermute | solution.py:29
  66.0 8.9 %copy-start.10 = (s32[32]{0:T(128)S(1)}, s32[32]{0:T(128)}, u32[]{:S(2)}) copy-start(s32[32]{0:T(128)} %broadcast_multiply_fusion) | copy-start | bytes 388
  66.0 21.0 %copy-start = (f32[16,2176]{1,0:T(8,128)S(1)}, f32[16,2176]{1,0:T(8,128)}, u32[]{:S(2)}) copy-start(f32[16,2176]{1,0:T(8,128)} %param.15) | copy-start | bytes 417796
  66.0 21.0 %copy-start.1 = (f32[16,2176]{1,0:T(8,128)S(1)}, f32[16,2176]{1,0:T(8,128)}, u32[]{:S(2)}) copy-start(f32[16,2176]{1,0:T(8,128)} %param.16) | copy-start | bytes 417796
  68.5 19.3 %copy-start.2 = (f32[2,6,320,64]{3,2,1,0:T(8,128)S(1)}, f32[2,6,320,64]{3,2,1,0:T(8,128)}, u32[]{:S(2)}) copy-start(f32[2,6,320,64]{3,2,1,0:T(8,128)} %get-tuple-element.6) | copy-start | bytes 2949124
  68.6 10.2 %collective-permute-start.9 = (f32[272,256]{1,0:T(8,128)S(1)}, f32[272,256]{1,0:T(8,128)S(1)}, u32[]{:S(2)}, u32[]{:S(2)}) collective-permute-start(f32[272,256]{1,0:T(8,128)S(1)} %bitcast.85), channel_id=1, source_target_pairs={{1,0},{2,1},{3,2},{16,3},{17,16},{18,17},{19,18},{5,4},{6,5},{7,6}... | collective-permute-start | bytes 835592 | tf_op jit(solution)/shard_map/ppermute | solution.py:29
  71.5 12.6 %collective-permute-start.8 = (f32[272,256]{1,0:T(8,128)S(1)}, f32[272,256]{1,0:T(8,128)S(1)}, u32[]{:S(2)}, u32[]{:S(2)}) collective-permute-start(f32[272,256]{1,0:T(8,128)S(1)} %bitcast.86), channel_id=1, source_target_pairs={{0,1},{1,2},{2,3},{3,16},{16,17},{17,18},{18,19},{4,5},{5,6},{6,7}... | collective-permute-start | bytes 835592 | tf_op jit(solution)/shard_map/ppermute | solution.py:27
  84.8 11.2 %collective-permute-start.11 = (f32[272,256]{1,0:T(8,128)}, f32[272,256]{1,0:T(8,128)}, u32[]{:S(2)}, u32[]{:S(2)}) collective-permute-start(f32[272,256]{1,0:T(8,128)} %fusion.16), channel_id=1, source_target_pairs={{0,8},{4,12},{8,0},{12,4},{1,9},{5,13},{9,1},{13,5},{2,10},{6,14},... | collective-permute-start | bytes 835592 | tf_op jit(solution)/shard_map/ppermute | solution.py:49
  86.2 10.8 %collective-permute-start.12 = (f32[272,256]{1,0:T(8,128)}, f32[272,256]{1,0:T(8,128)}, u32[]{:S(2)}, u32[]{:S(2)}) collective-permute-start(f32[272,256]{1,0:T(8,128)} %fusion.16), channel_id=1, source_target_pairs={{0,12},{4,8},{8,4},{12,0},{1,13},{5,9},{9,5},{13,1},{2,14},{6,10},... | collective-permute-start | bytes 835592 | tf_op jit(solution)/shard_map/ppermute | solution.py:49
  86.2 10.8 %collective-permute-start.10 = (f32[272,256]{1,0:T(8,128)}, f32[272,256]{1,0:T(8,128)}, u32[]{:S(2)}, u32[]{:S(2)}) collective-permute-start(f32[272,256]{1,0:T(8,128)} %fusion.16), channel_id=1, source_target_pairs={{0,4},{4,0},{8,12},{12,8},{1,5},{5,1},{9,13},{13,9},{2,6},{6,2},{1... | collective-permute-start | bytes 835592 | tf_op jit(solution)/shard_map/ppermute | solution.py:49
  89.7 8.8 %copy-start.3 = (f32[2,16,2175]{2,1,0:T(8,128)S(1)}, f32[2,16,2175]{2,1,0:T(8,128)}, u32[]{:S(2)}) copy-start(f32[2,16,2175]{2,1,0:T(8,128)} %get-tuple-element.27) | copy-start | bytes 835204
  89.7 8.8 %copy-start.4 = (f32[2,16,2175]{2,1,0:T(8,128)S(1)}, f32[2,16,2175]{2,1,0:T(8,128)}, u32[]{:S(2)}) copy-start(f32[2,16,2175]{2,1,0:T(8,128)} %get-tuple-element.28) | copy-start | bytes 835204
  89.7 8.8 %copy-start.6 = (f32[2,8,17,128]{3,1,2,0:T(8,128)S(1)}, f32[2,8,17,128]{3,1,2,0:T(8,128)}, u32[]{:S(2)}) copy-start(f32[2,8,17,128]{3,1,2,0:T(8,128)} %copy.63) | copy-start | bytes 417796
  89.7 26.0 %all-to-all-start = ((bf16[32,24,320]{2,1,0:T(8,128)(2,1)}), bf16[32,24,320]{2,1,0:T(8,128)(2,1)S(1)}, u32[]{:S(2)}, u32[]{:S(2)}) async-start(bf16[32,24,320]{2,1,0:T(8,128)(2,1)} %copy.39), calls=%async_computation | async-start | bytes 1179648 | tf_op jit(solution)/shard_map/all_to_all | solution.py:189
  100.2 18.9 %copy-start.5 = (f32[16,2176]{1,0:T(8,128)}, f32[16,2176]{1,0:T(8,128)S(1)}, u32[]{:S(2)}) copy-start(f32[16,2176]{1,0:T(8,128)S(1)} %get-tuple-element.26) | copy-start | bytes 417796
  100.2 18.8 %collective-permute-start.14 = (f32[16,2176]{1,0:T(8,128)S(1)}, f32[16,2176]{1,0:T(8,128)S(1)}, u32[]{:S(2)}, u32[]{:S(2)}) collective-permute-start(f32[16,2176]{1,0:T(8,128)S(1)} %get-tuple-element.26), channel_id=1, source_target_pairs={{1,0},{2,1},{3,2},{16,3},{17,16},{18,17},{19,18},{5,4},{6,5},{7,6}... | collective-permute-start | bytes 417800 | tf_op jit(solution)/shard_map/ppermute | solution.py:29
  104.4 14.6 %collective-permute-start.13 = (f32[16,2176]{1,0:T(8,128)S(1)}, f32[16,2176]{1,0:T(8,128)S(1)}, u32[]{:S(2)}, u32[]{:S(2)}) collective-permute-start(f32[16,2176]{1,0:T(8,128)S(1)} %get-tuple-element.26), channel_id=1, source_target_pairs={{0,1},{1,2},{2,3},{3,16},{16,17},{17,18},{18,19},{4,5},{5,6},{6,7}... | collective-permute-start | bytes 417800 | tf_op jit(solution)/shard_map/ppermute | solution.py:27
  117.1 16.6 %collective-permute-start.5 = (bf16[4,24,2560]{2,1,0:T(8,128)(2,1)}, bf16[4,24,2560]{2,1,0:T(8,128)(2,1)}, u32[]{:S(2)}, u32[]{:S(2)}) collective-permute-start(bf16[4,24,2560]{2,1,0:T(8,128)(2,1)} %all_to_all.16), channel_id=1, source_target_pairs={{0,12},{4,8},{8,4},{12,0},{1,13},{5,9},{9,5},{13,1},{2,14},{6,10},... | collective-permute-start | bytes 1474568 | tf_op jit(solution)/shard_map/ppermute | solution.py:60
  117.1 24.3 %collective-permute-start.4 = (bf16[4,24,2560]{2,1,0:T(8,128)(2,1)}, bf16[4,24,2560]{2,1,0:T(8,128)(2,1)}, u32[]{:S(2)}, u32[]{:S(2)}) collective-permute-start(bf16[4,24,2560]{2,1,0:T(8,128)(2,1)} %all_to_all.16), channel_id=1, source_target_pairs={{0,8},{4,12},{8,0},{12,4},{1,9},{5,13},{9,1},{13,5},{2,10},{6,14},... | collective-permute-start | bytes 1474568 | tf_op jit(solution)/shard_map/ppermute | solution.py:60
  118.5 22.8 %collective-permute-start.3 = (bf16[4,24,2560]{2,1,0:T(8,128)(2,1)}, bf16[4,24,2560]{2,1,0:T(8,128)(2,1)}, u32[]{:S(2)}, u32[]{:S(2)}) collective-permute-start(bf16[4,24,2560]{2,1,0:T(8,128)(2,1)} %all_to_all.16), channel_id=1, source_target_pairs={{0,4},{4,0},{8,12},{12,8},{1,5},{5,1},{9,13},{13,9},{2,6},{6,2},{1... | collective-permute-start | bytes 1474568 | tf_op jit(solution)/shard_map/ppermute | solution.py:60

commit v4 on v2

--- a/solution.py
+++ b/solution.py
@@ -71,13 +71,15 @@
 
 
 def row_block(rows):
-    for size in (32, 16):
+    for size in (64, 32, 16):
         if rows % size == 0:
             return size
     return rows
 
 
-def transform_kernel(points_ref, cells_ref, table_ref, weight_ref, slot_ref, sums_ref, acc_ref):
+def transform_kernel(
+    points_ref, cells_ref, table_ref, weight_ref, slot_ref, sums_ref, acc_ref, masked_ref, stacked_ref, onehot_ref
+):
     step = pl.program_id(0)
 
     @pl.when(step == 0)
@@ -86,12 +88,47 @@
 
     nfields, nlev, rows, lon_count = cells_ref.shape
     nslot = acc_ref.shape[0]
+    nblocks = lon_count // BLOCK
+    limit = points_ref[...]
+
+    def per_block(b, carry):
+        start = pl.multiple_of(b * BLOCK, BLOCK)
+        inside = lax.broadcasted_iota(jnp.int32, (rows, BLOCK), 1) + start < limit
+        row0 = pl.multiple_of(b * rows, rows)
+        for f in range(nfields):
+            flux = None
+            for l in range(nlev):
+                kept = jnp.where(inside, cells_ref[f, l, :, pl.ds(start, BLOCK)], jnp.zeros((), jnp.bfloat16))
+                masked_ref[f, l, :, pl.ds(start, BLOCK)] = kept
+                term = weight_ref[f, l] * kept.astype(jnp.float32)
+                flux = term if flux is None else flux + term
+            high = flux.astype(jnp.bfloat16)
+            low = flux - high.astype(jnp.float32)
+            stacked_ref[pl.ds(row0, rows), 2 * f * BLOCK : (2 * f + 1) * BLOCK] = high.astype(stacked_ref.dtype)
+            stacked_ref[pl.ds(row0, rows), (2 * f + 1) * BLOCK : (2 * f + 2) * BLOCK] = low.astype(
+                stacked_ref.dtype
+            )
+        return carry
+
+    lax.fori_loop(0, nblocks, per_block, 0)
+
+    kdim = nblocks * rows
+    chunk = BLOCK if kdim % BLOCK == 0 else kdim
+
+    def per_chunk(c, carry):
+        c0 = pl.multiple_of(c * chunk, chunk)
+        ids = slot_ref[0, :, pl.ds(c0, chunk)]
+        onehot_ref[:, pl.ds(c0, chunk)] = (
+            lax.broadcasted_iota(jnp.int32, (nslot, chunk), 0) == ids
+        ).astype(jnp.bfloat16)
+        return carry
+
+    lax.fori_loop(0, kdim // chunk, per_chunk, 0)
+
     table = table_ref[...]
-    inside = lax.broadcasted_iota(jnp.int32, (rows, lon_count), 1) < points_ref[...]
-    cells = jnp.where(inside[None, None], cells_ref[...], jnp.zeros((), jnp.bfloat16))
     if rows % 16 == 0:
         sums = lax.dot_general(
-            cells.reshape(nfields * nlev * rows, lon_count),
+            masked_ref[...].reshape(nfields * nlev * rows, lon_count),
             table,
             (((1,), (1,)), ((), ())),
             preferred_element_type=jnp.float32,
@@ -101,28 +138,11 @@
         for f in range(nfields):
             for l in range(nlev):
                 sums_ref[f, l] = lax.dot_general(
-                    cells[f, l], table, (((1,), (1,)), ((), ())), preferred_element_type=jnp.float32
+                    masked_ref[f, l], table, (((1,), (1,)), ((), ())), preferred_element_type=jnp.float32
                 )
-    pieces = []
-    for f in range(nfields):
-        flux = weight_ref[f, 0] * cells[f, 0].astype(jnp.float32)
-        for l in range(1, nlev):
-            flux = flux + weight_ref[f, l] * cells[f, l].astype(jnp.float32)
-        high = flux.astype(jnp.bfloat16).astype(jnp.float32)
-        pieces.append(high)
-        pieces.append(flux - high)
-    nblocks = lon_count // BLOCK
-    stacked = jnp.concatenate(
-        [
-            jnp.concatenate([p[:, b * BLOCK : (b + 1) * BLOCK] for p in pieces], axis=1)
-            for b in range(nblocks)
-        ],
-        axis=0,
-    ).astype(jnp.bfloat16)
-    onehot = (
-        lax.broadcasted_iota(jnp.int32, (nslot, nblocks * rows), 0) == slot_ref[0]
-    ).astype(jnp.bfloat16)
-    acc_ref[...] += jnp.dot(onehot, stacked, preferred_element_type=jnp.float32)
+    acc_ref[...] += jnp.dot(
+        onehot_ref[...], stacked_ref[...].astype(jnp.bfloat16), preferred_element_type=jnp.float32
+    )
 
 
 def fused_transform(atmos_fields, lat_points, table, column_weight, slots, nslot):
@@ -132,6 +152,7 @@
     nblocks = lon_count // BLOCK
     wave2 = table.shape[0]
     slot_rows = slots.reshape(steps, rows, nblocks).transpose(0, 2, 1).reshape(steps, 1, nblocks * rows)
+    stacked_type = jnp.bfloat16 if rows % 16 == 0 else jnp.float32
     return pl.pallas_call(
         transform_kernel,
         grid=(steps,),
@@ -149,6 +170,11 @@
         out_shape=[
             jax.ShapeDtypeStruct((nfields, nlev, lat_band, wave2), jnp.float32),
             jax.ShapeDtypeStruct((nslot, 2 * nfields * BLOCK), jnp.float32),
+        ],
+        scratch_shapes=[
+            pltpu.VMEM((nfields, nlev, rows, lon_count), jnp.bfloat16),
+            pltpu.VMEM((nblocks * rows, 2 * nfields * BLOCK), stacked_type),
+            pltpu.VMEM((nslot, nblocks * rows), jnp.bfloat16),
         ],
         compiler_params=pltpu.CompilerParams(dimension_semantics=("arbitrary",)),
     )(lat_points[:, None], atmos_fields, table, column_weight.astype(jnp.float32), slot_rows)

time: 135 us -> 165 us (1.22)
  Pallas kernels: 36 us -> 66.2 us
    pallas_call x1, Pallas kernels: 36 us -> 66.2 us  [fused_transform(): pl.pallas_call(transform_kernel, grid=(steps,), in_specs=[pl.BlockSpec((r...]
  transfers between devices with their start and end apart: 13 -> 13, of which waited for: 8 -> 8; matrix products, arithmetic and copies ran while one was open for 29% -> 24% of each run, Pallas kernels for 27% -> 40%
where the time goes in v4:
time: 165 us; the launch traced here: 164 us
  Pallas kernels  66.2 us (40%)
  starting transfers between devices  32.9 us (20%)
  local copies, waits for them, and re-layouts  25.1 us (15%)
  waiting for transfers between devices  18 us (11%)
  other arithmetic  14.6 us (9%)
  matrix products  6.14 us (4%)
    pallas_call x1, Pallas kernels, fused_transform(): pl.pallas_call(transform_kernel, grid=(steps,), in_specs=[pl.BlockSpec((r...  66.2 us
    ppermute x3, starting transfers between devices, with_halo(): lax.ppermute(tail, axis, [(i, (i + 1) % count) for i in range(ends)])  11.6 us
    ppermute x3, starting transfers between devices, with_halo(): lax.ppermute(head, axis, [((i + 1) % count, i) for i in range(ends)])  10.9 us
    gather x3, local copies, waits for them, and re-layouts, body(): jnp.take(tiles_near, local_slot, axis=0).reshape(lat_band, quarter)  9.65 us
    ppermute x2, waiting for transfers between devices, lev_sum(): lax.ppermute(values, 'lev', [(i, i ^ stride) for i in range(count)])  7.21 us
    dot_general x1, matrix products, body(): jnp.einsum('srj,sjd->srd', lev_gather(regrouped, 1), legendre, preferred_...  6.14 us
    all_to_all x1, starting transfers between devices, body(): lax.all_to_all(coeffs.transpose(4, 1, 0, 3, 2).reshape(wave_count, lev_de...  5.51 us
    ppermute x3, waiting for transfers between devices, with_halo(): lax.ppermute(tail, axis, [(i, (i + 1) % count) for i in range(ends)])  4.49 us
  transfers between devices with their start and end apart: 13, of which 8 were waited for; matrix products, arithmetic and copies ran while one was open for 24% of the time, Pallas kernels for 40%

profile of v4, /device:TPU:4, one launch (start us, length us, event | category | flops | bytes accessed | tf_op | source)
XLA Modules:
  0.0 163.9 jit_solution(16073129774698944827)
XLA Ops:
  0.8 1.6 fusion.33
  2.4 3.5 %collective-permute-start.5 = (f32[2,1,2176]{2,1,0:T(1,128)}, f32[2,1,2176]{2,1,0:T(1,128)S(1)}, u32[]{:S(2)}, u32[]{:S(2)}) collective-permute-start(f32[2,1,2176]{2,1,0:T(1,128)} %get-tuple-element.32), channel_id=1, source_target_pairs={{0,1},{1,2},{2,3},{3,16},{16,17},{17,18},{18,19},{4,5},{5,6},{6,7}... | collective-permute-start | bytes 52232 | tf_op jit(solution)/shard_map/ppermute | solution.py:27
  5.9 5.1 %collective-permute-start.4 = (f32[2,1,2176]{2,1,0:T(1,128)}, f32[2,1,2176]{2,1,0:T(1,128)S(1)}, u32[]{:S(2)}, u32[]{:S(2)}) collective-permute-start(f32[2,1,2176]{2,1,0:T(1,128)} %get-tuple-element.31), channel_id=1, source_target_pairs={{1,0},{2,1},{3,2},{16,3},{17,16},{18,17},{19,18},{5,4},{6,5},{7,6}... | collective-permute-start | bytes 52232 | tf_op jit(solution)/shard_map/ppermute | solution.py:29
  10.9 2.0 %fusion.14 = (f32[2,16,2175]{2,1,0:T(8,128)}, f32[2,16,2175]{2,1,0:T(8,128)}) fusion(f32[1,16,2176]{2,1,0:T(8,128)} %bitcast.48, f32[1,16,2176]{2,1,0:T(8,128)} %bitcast.52), kind=kLoop, calls=%fused_computation.39 | loop fusion | flops 139200 | bytes 835328 | tf_op jit(solution)/shard_map/stack | solution.py:250
  12.9 4.0 %cosine_convert_fusion = (bf16[32,5632]{1,0:T(8,128)(2,1)S(1)}, bf16[32,5632]{1,0:T(8,128)(2,1)S(1)}) fusion(s32[32]{0:T(128)} %param.11), kind=kLoop, calls=%fused_computation.18 | loop fusion | flops 2162688 | bytes 721024 | tf_op jit(solution)/shard_map/convert
  17.6 0.9 pad_maximum_fusion.table_ref
  20.0 1.6 collective-permute-start.1
  21.7 2.4 %collective-permute-done.1 = s32[320,22]{0,1:T(8,128)S(1)} collective-permute-done((s32[320,22]{0,1:T(8,128)S(1)}, s32[320,22]{0,1:T(8,128)S(1)}, u32[]{:S(2)}, u32[]{:S(2)}) %collective-permute-start.1) | collective-permute-done | bytes 28192 | tf_op jit(solution)/shard_map/ppermute | solution.py:62
  25.1 66.2 %shard_map.120 = (f32[2,6,320,64]{3,2,1,0:T(8,128)}, f32[816,512]{1,0:T(8,128)}) custom-call(s32[320,1]{1,0:T(8,128)} %broadcast_in_dim.54.points_ref, bf16[2,6,320,5632]{3,2,1,0:T(8,128)(2,1)} %cells_ref.1, bf16[64,5632]{1,0:T(8,128)(2,1)} %pad_maximum_fusion.table_ref, f32[2,6]{1,0:T(2,128)} %convert_element_type.23.weight_ref, ...), custom_call_target="tpu_custom_call" | custom-call | tf_op jit(solution)/shard_map/pallas_call | solution.py:156
  91.3 2.3 %reshape.202 = f32[816,2,2,128]{3,2,1,0:T(2,128)S(1)} reshape(f32[816,512]{1,0:T(8,128)} %get-tuple-element.7) | data formatting | bytes 3342336 | tf_op jit(solution)/shard_map/reshape | solution.py:233
  94.5 2.5 %slice_reduce_fusion.1 = (f32[272,2,128]{2,1,0:T(2,128)S(1)}, f32[272,2,128]{2,1,0:T(2,128)S(1)}, f32[272,2,128]{2,1,0:T(2,128)S(1)}) fusion(f32[816,2,1,128]{3,2,1,0:T(1,128)S(1)} %slice_add_fusion), kind=kLoop, calls=%fused_computation.45 | loop fusion | bytes 1671168 | tf_op jit(solution)/shard_map/slice | solution.py:237
  97.8 2.7 %collective-permute-start.7 = (f32[272,256]{1,0:T(8,128)}, f32[272,256]{1,0:T(8,128)}, u32[]{:S(2)}, u32[]{:S(2)}) collective-permute-start(f32[272,256]{1,0:T(8,128)} %bitcast.41), channel_id=1, source_target_pairs={{1,0},{2,1},{3,2},{16,3},{17,16},{18,17},{19,18},{5,4},{6,5},{7,6}... | collective-permute-start | bytes 835592 | tf_op jit(solution)/shard_map/ppermute | solution.py:29
  101.2 3.1 %collective-permute-start.6 = (f32[272,256]{1,0:T(8,128)}, f32[272,256]{1,0:T(8,128)}, u32[]{:S(2)}, u32[]{:S(2)}) collective-permute-start(f32[272,256]{1,0:T(8,128)} %bitcast.42), channel_id=1, source_target_pairs={{0,1},{1,2},{2,3},{3,16},{16,17},{17,18},{18,19},{4,5},{5,6},{6,7}... | collective-permute-start | bytes 835592 | tf_op jit(solution)/shard_map/ppermute | solution.py:27
  105.3 1.0 copy.47
  106.3 5.5 %all-to-all-start = ((bf16[32,24,320]{2,1,0:T(8,128)(2,1)}), bf16[32,24,320]{2,1,0:T(8,128)(2,1)S(1)}, u32[]{:S(2)}, u32[]{:S(2)}) async-start(bf16[32,24,320]{2,1,0:T(8,128)(2,1)} %copy.47), calls=%async_computation | async-start | bytes 1179648 | tf_op jit(solution)/shard_map/all_to_all | solution.py:220
  111.8 1.6 collective-permute-done.6
  113.4 1.1 fusion.15
  114.6 1.5 collective-permute-done.8
  116.1 1.6 collective-permute-start.9
  119.1 5.7 %collective-permute-done.9 = f32[272,256]{1,0:T(8,128)S(1)} collective-permute-done((f32[272,256]{1,0:T(8,128)S(1)}, f32[272,256]{1,0:T(8,128)S(1)}, u32[]{:S(2)}, u32[]{:S(2)}) %collective-permute-start.9) | collective-permute-done | bytes 278560 | tf_op jit(solution)/shard_map/ppermute | solution.py:50
  126.6 1.6 collective-permute-done.2
  128.4 1.6 collective-permute-start.3
  130.6 3.1 %collective-permute-start.11 = (f32[16,2176]{1,0:T(8,128)S(1)}, f32[16,2176]{1,0:T(8,128)S(1)}, u32[]{:S(2)}, u32[]{:S(2)}) collective-permute-start(f32[16,2176]{1,0:T(8,128)S(1)} %get-tuple-element.26), channel_id=1, source_target_pairs={{1,0},{2,1},{3,2},{16,3},{17,16},{18,17},{19,18},{5,4},{6,5},{7,6}... | collective-permute-start | bytes 417800 | tf_op jit(solution)/shard_map/ppermute | solution.py:29
  133.7 5.1 %collective-permute-start.10 = (f32[16,2176]{1,0:T(8,128)S(1)}, f32[16,2176]{1,0:T(8,128)S(1)}, u32[]{:S(2)}, u32[]{:S(2)}) collective-permute-start(f32[16,2176]{1,0:T(8,128)S(1)} %get-tuple-element.26), channel_id=1, source_target_pairs={{0,1},{1,2},{2,3},{3,16},{16,17},{17,18},{18,19},{4,5},{5,6},{6,7}... | collective-permute-start | bytes 417800 | tf_op jit(solution)/shard_map/ppermute | solution.py:27
  138.8 1.7 %collective-permute-done.11 = f32[16,2176]{1,0:T(8,128)S(1)} collective-permute-done((f32[16,2176]{1,0:T(8,128)S(1)}, f32[16,2176]{1,0:T(8,128)S(1)}, u32[]{:S(2)}, u32[]{:S(2)}) %collective-permute-start.11) | collective-permute-done | bytes 139296 | tf_op jit(solution)/shard_map/ppermute | solution.py:29
  140.5 2.9 %collective-permute-done.10 = f32[16,2176]{1,0:T(8,128)S(1)} collective-permute-done((f32[16,2176]{1,0:T(8,128)S(1)}, f32[16,2176]{1,0:T(8,128)S(1)}, u32[]{:S(2)}, u32[]{:S(2)}) %collective-permute-start.10) | collective-permute-done | bytes 139296 | tf_op jit(solution)/shard_map/ppermute | solution.py:27
  143.6 5.9 %gather_fusion = f32[3520,128]{1,0:T(8,128)S(1)} fusion(f32[816,128]{1,0:T(8,128)S(1)} %reshape.205, s32[4096]{0:T(1024)S(1)} %pad_clamp_fusion), kind=kCustom, calls=%fused_computation | custom fusion | bytes 3618560 | tf_op jit(solution)/shard_map/jit(_take)/gather | solution.py:264
  149.4 1.6 gather.7
  151.0 2.2 %copy.53 = f32[320,1408]{0,1:T(8,128)S(1)} copy(f32[320,1408]{1,0:T(8,128)} %gather.7) | data formatting | bytes 3604480 | tf_op jit(solution)/shard_map/jit(_take)/gather | solution.py:264
  153.2 1.6 select_select_fusion
  154.9 2.9 %copy.54 = f32[320,1408]{1,0:T(8,128)} copy(f32[320,1408]{0,1:T(8,128)} %select_select_fusion) | data formatting | bytes 3604480
  157.7 6.1 %fusion = f32[4,96,384]{2,1,0:T(8,128)} fusion(bf16[4,2560,384]{2,1,0:T(8,128)(2,1)} %param.12, bf16[4,48,2560]{2,1,0:T(8,128)(2,1)S(1)} %maximum_select_fusion.2, bf16[4,48,2560]{2,1,0:T(8,128)(2,1)} %collective-permute-done.3, pred[]{:T(512)S(6)} %eq.19), kind=kOutput, calls=%fused_computation.3 | convolution fusion | flops 763822080 | bytes 10420225 | tf_op jit(solution)/shard_map/srj,sjd->srd/dot_general | solution.py:227
  (77 shorter events, 10.7 us)
Async XLA Ops:
  0.6 18.7 %copy-start.6 = (s32[320,11]{0,1:T(8,128)S(1)}, s32[320,11]{0,1:T(8,128)}, u32[]{:S(2)}) copy-start(s32[320,11]{0,1:T(8,128)} %param.14) | copy-start | bytes 42244
  0.6 17.9 %copy-start.9 = (s32[32]{0:T(128)S(1)}, s32[32]{0:T(128)}, u32[]{:S(2)}) copy-start(s32[32]{0:T(128)} %param.11) | copy-start | bytes 388
  0.7 17.9 %copy-start.7 = (s32[320]{0:T(512)S(1)}, s32[320]{0:T(512)}, u32[]{:S(2)}) copy-start(s32[320]{0:T(512)} %param.10) | copy-start | bytes 3844
  0.7 18.7 %copy-start.10 = (bf16[2,6]{1,0:T(2,128)(2,1)S(1)}, bf16[2,6]{1,0:T(2,128)(2,1)}, u32[]{:S(2)}) copy-start(bf16[2,6]{1,0:T(2,128)(2,1)} %param.13) | copy-start | bytes 76
  0.7 19.3 %collective-permute-start = (s32[320,11]{0,1:T(8,128)}, s32[320,11]{0,1:T(8,128)S(1)}, u32[]{:S(2)}, u32[]{:S(2)}) collective-permute-start(s32[320,11]{0,1:T(8,128)} %param.14), channel_id=1, source_target_pairs={{0,4},{4,0},{8,12},{12,8},{1,5},{5,1},{9,13},{13,9},{2,6},{6,2},{1... | collective-permute-start | bytes 42248 | tf_op jit(solution)/shard_map/ppermute | solution.py:62
  2.4 124.0 %collective-permute-start.5 = (f32[2,1,2176]{2,1,0:T(1,128)}, f32[2,1,2176]{2,1,0:T(1,128)S(1)}, u32[]{:S(2)}, u32[]{:S(2)}) collective-permute-start(f32[2,1,2176]{2,1,0:T(1,128)} %get-tuple-element.32), channel_id=1, source_target_pairs={{0,1},{1,2},{2,3},{3,16},{16,17},{17,18},{18,19},{4,5},{5,6},{6,7}... | collective-permute-start | bytes 52232 | tf_op jit(solution)/shard_map/ppermute | solution.py:27
  5.9 120.5 %collective-permute-start.4 = (f32[2,1,2176]{2,1,0:T(1,128)}, f32[2,1,2176]{2,1,0:T(1,128)S(1)}, u32[]{:S(2)}, u32[]{:S(2)}) collective-permute-start(f32[2,1,2176]{2,1,0:T(1,128)} %get-tuple-element.31), channel_id=1, source_target_pairs={{1,0},{2,1},{3,2},{16,3},{17,16},{18,17},{19,18},{5,4},{6,5},{7,6}... | collective-permute-start | bytes 52232 | tf_op jit(solution)/shard_map/ppermute | solution.py:29
  20.0 4.0 %collective-permute-start.1 = (s32[320,22]{0,1:T(8,128)S(1)}, s32[320,22]{0,1:T(8,128)S(1)}, u32[]{:S(2)}, u32[]{:S(2)}) collective-permute-start(s32[320,22]{0,1:T(8,128)S(1)} %add_select_fusion.7), channel_id=1, source_target_pairs={{0,8},{4,12},{8,0},{12,4},{1,9},{5,13},{9,1},{13,5},{2,10},{6,14},... | collective-permute-start | bytes 84488 | tf_op jit(solution)/shard_map/ppermute | solution.py:62
  94.5 9.9 %copy-start.2 = (f32[2,6,320,64]{3,2,1,0:T(8,128)S(1)}, f32[2,6,320,64]{3,2,1,0:T(8,128)}, u32[]{:S(2)}) copy-start(f32[2,6,320,64]{3,2,1,0:T(8,128)} %get-tuple-element.6) | copy-start | bytes 2949124
  97.8 14.0 %collective-permute-start.7 = (f32[272,256]{1,0:T(8,128)}, f32[272,256]{1,0:T(8,128)}, u32[]{:S(2)}, u32[]{:S(2)}) collective-permute-start(f32[272,256]{1,0:T(8,128)} %bitcast.41), channel_id=1, source_target_pairs={{1,0},{2,1},{3,2},{16,3},{17,16},{18,17},{19,18},{5,4},{6,5},{7,6}... | collective-permute-start | bytes 835592 | tf_op jit(solution)/shard_map/ppermute | solution.py:29
  101.2 12.1 %collective-permute-start.6 = (f32[272,256]{1,0:T(8,128)}, f32[272,256]{1,0:T(8,128)}, u32[]{:S(2)}, u32[]{:S(2)}) collective-permute-start(f32[272,256]{1,0:T(8,128)} %bitcast.42), channel_id=1, source_target_pairs={{0,1},{1,2},{2,3},{3,16},{16,17},{17,18},{18,19},{4,5},{5,6},{6,7}... | collective-permute-start | bytes 835592 | tf_op jit(solution)/shard_map/ppermute | solution.py:27
  105.3 12.4 %copy-start.8 = (s32[16,17]{1,0:T(8,128)S(1)}, s32[16,17]{1,0:T(8,128)}, u32[]{:S(2)}) copy-start(s32[16,17]{1,0:T(8,128)} %param.17) | copy-start | bytes 3268
  106.3 12.6 %copy-start = (f32[16,2176]{1,0:T(8,128)S(1)}, f32[16,2176]{1,0:T(8,128)}, u32[]{:S(2)}) copy-start(f32[16,2176]{1,0:T(8,128)} %param.15) | copy-start | bytes 417796
  106.3 12.6 %copy-start.1 = (f32[16,2176]{1,0:T(8,128)S(1)}, f32[16,2176]{1,0:T(8,128)}, u32[]{:S(2)}) copy-start(f32[16,2176]{1,0:T(8,128)} %param.16) | copy-start | bytes 417796
  106.3 19.4 %all-to-all-start = ((bf16[32,24,320]{2,1,0:T(8,128)(2,1)}), bf16[32,24,320]{2,1,0:T(8,128)(2,1)S(1)}, u32[]{:S(2)}, u32[]{:S(2)}) async-start(bf16[32,24,320]{2,1,0:T(8,128)(2,1)} %copy.47), calls=%async_computation | async-start | bytes 1179648 | tf_op jit(solution)/shard_map/all_to_all | solution.py:220
  114.5 1.6 collective-permute-start.8
  116.1 8.8 %collective-permute-start.9 = (f32[272,256]{1,0:T(8,128)S(1)}, f32[272,256]{1,0:T(8,128)S(1)}, u32[]{:S(2)}, u32[]{:S(2)}) collective-permute-start(f32[272,256]{1,0:T(8,128)S(1)} %add.175), channel_id=1, source_target_pairs={{0,8},{4,12},{8,0},{12,4},{1,9},{5,13},{9,1},{13,5},{2,10},{6,14},... | collective-permute-start | bytes 835592 | tf_op jit(solution)/shard_map/ppermute | solution.py:50
  124.9 1.5 copy-start.3
  124.9 1.5 copy-start.4
  126.3 1.9 %collective-permute-start.2 = (bf16[4,24,2560]{2,1,0:T(8,128)(2,1)S(1)}, bf16[4,24,2560]{2,1,0:T(8,128)(2,1)S(1)}, u32[]{:S(2)}, u32[]{:S(2)}) collective-permute-start(bf16[4,24,2560]{2,1,0:T(8,128)(2,1)S(1)} %all_to_all.16), channel_id=1, source_target_pairs={{0,4},{4,0},{8,12},{12,8},{1,5},{5,1},{9,13},{13,9},{2,6},{6,2},{1... | collective-permute-start | bytes 1474568 | tf_op jit(solution)/shard_map/ppermute | solution.py:62
  128.4 29.3 %collective-permute-start.3 = (bf16[4,48,2560]{2,1,0:T(8,128)(2,1)S(1)}, bf16[4,48,2560]{2,1,0:T(8,128)(2,1)}, u32[]{:S(2)}, u32[]{:S(2)}) collective-permute-start(bf16[4,48,2560]{2,1,0:T(8,128)(2,1)S(1)} %maximum_select_fusion.2), channel_id=1, source_target_pairs={{0,8},{4,12},{8,0},{12,4},{1,9},{5,13},{9,1},{13,5},{2,10},{6,14},... | collective-permute-start | bytes 2949128 | tf_op jit(solution)/shard_map/ppermute | solution.py:62
  130.6 18.8 %copy-start.5 = (f32[16,2176]{1,0:T(8,128)}, f32[16,2176]{1,0:T(8,128)S(1)}, u32[]{:S(2)}) copy-start(f32[16,2176]{1,0:T(8,128)S(1)} %get-tuple-element.26) | copy-start | bytes 417796
  130.6 9.9 %collective-permute-start.11 = (f32[16,2176]{1,0:T(8,128)S(1)}, f32[16,2176]{1,0:T(8,128)S(1)}, u32[]{:S(2)}, u32[]{:S(2)}) collective-permute-start(f32[16,2176]{1,0:T(8,128)S(1)} %get-tuple-element.26), channel_id=1, source_target_pairs={{1,0},{2,1},{3,2},{16,3},{17,16},{18,17},{19,18},{5,4},{6,5},{7,6}... | collective-permute-start | bytes 417800 | tf_op jit(solution)/shard_map/ppermute | solution.py:29
  133.7 9.7 %collective-permute-start.10 = (f32[16,2176]{1,0:T(8,128)S(1)}, f32[16,2176]{1,0:T(8,128)S(1)}, u32[]{:S(2)}, u32[]{:S(2)}) collective-permute-start(f32[16,2176]{1,0:T(8,128)S(1)} %get-tuple-element.26), channel_id=1, source_target_pairs={{0,1},{1,2},{2,3},{3,16},{16,17},{17,18},{18,19},{4,5},{5,6},{6,7}... | collective-permute-start | bytes 417800 | tf_op jit(solution)/shard_map/ppermute | solution.py:27

commit v5 on v2

--- a/solution.py
+++ b/solution.py
@@ -71,13 +71,13 @@
 
 
 def row_block(rows):
-    for size in (32, 16):
+    for size in (64, 32, 16):
         if rows % size == 0:
             return size
     return rows
 
 
-def transform_kernel(points_ref, cells_ref, table_ref, weight_ref, slot_ref, sums_ref, acc_ref):
+def transform_kernel(points_ref, cells_ref, table_ref, weight_ref, slot_ref, sums_ref, acc_ref, *scratch):
     step = pl.program_id(0)
 
     @pl.when(step == 0)
@@ -86,9 +86,10 @@
 
     nfields, nlev, rows, lon_count = cells_ref.shape
     nslot = acc_ref.shape[0]
+    nblocks = lon_count // BLOCK
     table = table_ref[...]
-    inside = lax.broadcasted_iota(jnp.int32, (rows, lon_count), 1) < points_ref[...]
-    cells = jnp.where(inside[None, None], cells_ref[...], jnp.zeros((), jnp.bfloat16))
+    keep = (lax.broadcasted_iota(jnp.int32, (rows, lon_count), 1) < points_ref[...]).astype(jnp.bfloat16)
+    cells = cells_ref[...] * keep[None, None]
     if rows % 16 == 0:
         sums = lax.dot_general(
             cells.reshape(nfields * nlev * rows, lon_count),
@@ -108,17 +109,27 @@
         flux = weight_ref[f, 0] * cells[f, 0].astype(jnp.float32)
         for l in range(1, nlev):
             flux = flux + weight_ref[f, l] * cells[f, l].astype(jnp.float32)
-        high = flux.astype(jnp.bfloat16).astype(jnp.float32)
+        high = flux.astype(jnp.bfloat16)
         pieces.append(high)
-        pieces.append(flux - high)
-    nblocks = lon_count // BLOCK
-    stacked = jnp.concatenate(
-        [
-            jnp.concatenate([p[:, b * BLOCK : (b + 1) * BLOCK] for p in pieces], axis=1)
-            for b in range(nblocks)
-        ],
-        axis=0,
-    ).astype(jnp.bfloat16)
+        pieces.append((flux - high.astype(jnp.float32)).astype(jnp.bfloat16))
+    if scratch:
+        (stacked_ref,) = scratch
+        for b in range(nblocks):
+            for p, piece in enumerate(pieces):
+                stacked_ref[b * rows : (b + 1) * rows, p * BLOCK : (p + 1) * BLOCK] = piece[
+                    :, b * BLOCK : (b + 1) * BLOCK
+                ]
+        stacked = stacked_ref[...]
+    else:
+        stacked = jnp.concatenate(
+            [
+                jnp.concatenate(
+                    [p[:, b * BLOCK : (b + 1) * BLOCK].astype(jnp.float32) for p in pieces], axis=1
+                )
+                for b in range(nblocks)
+            ],
+            axis=0,
+        ).astype(jnp.bfloat16)
     onehot = (
         lax.broadcasted_iota(jnp.int32, (nslot, nblocks * rows), 0) == slot_ref[0]
     ).astype(jnp.bfloat16)
@@ -132,6 +143,9 @@
     nblocks = lon_count // BLOCK
     wave2 = table.shape[0]
     slot_rows = slots.reshape(steps, rows, nblocks).transpose(0, 2, 1).reshape(steps, 1, nblocks * rows)
+    scratch = []
+    if rows % 16 == 0 and True:
+        scratch = [pltpu.VMEM((nblocks * rows, 2 * nfields * BLOCK), jnp.bfloat16)]
     return pl.pallas_call(
         transform_kernel,
         grid=(steps,),
@@ -150,6 +164,7 @@
             jax.ShapeDtypeStruct((nfields, nlev, lat_band, wave2), jnp.float32),
             jax.ShapeDtypeStruct((nslot, 2 * nfields * BLOCK), jnp.float32),
         ],
+        scratch_shapes=scratch,
         compiler_params=pltpu.CompilerParams(dimension_semantics=("arbitrary",)),
     )(lat_points[:, None], atmos_fields, table, column_weight.astype(jnp.float32), slot_rows)
 

time: 135 us -> 135 us (level)
  no operation moved by 1% of the time
where the time goes in v5:
time: 135 us; the launch traced here: 134 us
  Pallas kernels  35.7 us (26%)
  starting transfers between devices  32.9 us (24%)
  local copies, waits for them, and re-layouts  25.1 us (19%)
  waiting for transfers between devices  18.1 us (13%)
  other arithmetic  14.6 us (11%)
  matrix products  6.15 us (5%)
    pallas_call x1, Pallas kernels, fused_transform(): pl.pallas_call(transform_kernel, grid=(steps,), in_specs=[pl.BlockSpec((r...  35.7 us
    ppermute x3, starting transfers between devices, with_halo(): lax.ppermute(tail, axis, [(i, (i + 1) % count) for i in range(ends)])  11.4 us
    ppermute x3, starting transfers between devices, with_halo(): lax.ppermute(head, axis, [((i + 1) % count, i) for i in range(ends)])  11.1 us
    gather x3, local copies, waits for them, and re-layouts, body(): jnp.take(tiles_near, local_slot, axis=0).reshape(lat_band, quarter)  9.65 us
    ppermute x2, waiting for transfers between devices, lev_sum(): lax.ppermute(values, 'lev', [(i, i ^ stride) for i in range(count)])  7.22 us
    dot_general x1, matrix products, body(): jnp.einsum('srj,sjd->srd', lev_gather(regrouped, 1), legendre, preferred_...  6.15 us
    all_to_all x1, starting transfers between devices, body(): lax.all_to_all(coeffs.transpose(4, 1, 0, 3, 2).reshape(wave_count, lev_de...  5.51 us
    ppermute x3, waiting for transfers between devices, with_halo(): lax.ppermute(tail, axis, [(i, (i + 1) % count) for i in range(ends)])  4.66 us
  transfers between devices with their start and end apart: 13, of which 8 were waited for; matrix products, arithmetic and copies ran while one was open for 29% of the time, Pallas kernels for 27%

profile of v5, /device:TPU:4, one launch (start us, length us, event | category | flops | bytes accessed | tf_op | source)
XLA Modules:
  0.0 133.6 jit_solution(16984077860363953767)
XLA Ops:
  0.8 1.6 %fusion.33 = (f32[2,1,2176]{2,1,0:T(1,128)}, f32[2,1,2176]{2,1,0:T(1,128)}) fusion(f32[1,16,2176]{2,1,0:T(8,128)} %bitcast.47, f32[1,16,2176]{2,1,0:T(8,128)} %bitcast.51), kind=kLoop, calls=%fused_computation.87 | loop fusion | flops 8704 | bytes 313344 | tf_op jit(solution)/shard_map/stack | solution.py:239
  2.4 3.5 %collective-permute-start.5 = (f32[2,1,2176]{2,1,0:T(1,128)}, f32[2,1,2176]{2,1,0:T(1,128)S(1)}, u32[]{:S(2)}, u32[]{:S(2)}) collective-permute-start(f32[2,1,2176]{2,1,0:T(1,128)} %get-tuple-element.32), channel_id=1, source_target_pairs={{0,1},{1,2},{2,3},{3,16},{16,17},{17,18},{18,19},{4,5},{5,6},{6,7}... | collective-permute-start | bytes 52232 | tf_op jit(solution)/shard_map/ppermute | solution.py:27
  5.9 5.1 %collective-permute-start.4 = (f32[2,1,2176]{2,1,0:T(1,128)}, f32[2,1,2176]{2,1,0:T(1,128)S(1)}, u32[]{:S(2)}, u32[]{:S(2)}) collective-permute-start(f32[2,1,2176]{2,1,0:T(1,128)} %get-tuple-element.31), channel_id=1, source_target_pairs={{1,0},{2,1},{3,2},{16,3},{17,16},{18,17},{19,18},{5,4},{6,5},{7,6}... | collective-permute-start | bytes 52232 | tf_op jit(solution)/shard_map/ppermute | solution.py:29
  10.9 2.0 %fusion.14 = (f32[2,16,2175]{2,1,0:T(8,128)}, f32[2,16,2175]{2,1,0:T(8,128)}) fusion(f32[1,16,2176]{2,1,0:T(8,128)} %bitcast.48, f32[1,16,2176]{2,1,0:T(8,128)} %bitcast.52), kind=kLoop, calls=%fused_computation.39 | loop fusion | flops 139200 | bytes 835328 | tf_op jit(solution)/shard_map/stack | solution.py:239
  12.9 4.0 %cosine_convert_fusion = (bf16[32,5632]{1,0:T(8,128)(2,1)S(1)}, bf16[32,5632]{1,0:T(8,128)(2,1)S(1)}) fusion(s32[32]{0:T(128)} %param.11), kind=kLoop, calls=%fused_computation.18 | loop fusion | flops 2162688 | bytes 721024 | tf_op jit(solution)/shard_map/convert
  17.6 0.9 pad_maximum_fusion.table_ref
  20.0 1.6 %collective-permute-start.1 = (s32[320,22]{0,1:T(8,128)S(1)}, s32[320,22]{0,1:T(8,128)S(1)}, u32[]{:S(2)}, u32[]{:S(2)}) collective-permute-start(s32[320,22]{0,1:T(8,128)S(1)} %add_select_fusion.7), channel_id=1, source_target_pairs={{0,8},{4,12},{8,0},{12,4},{1,9},{5,13},{9,1},{13,5},{2,10},{6,14},... | collective-permute-start | bytes 84488 | tf_op jit(solution)/shard_map/ppermute | solution.py:62
  21.7 2.4 %collective-permute-done.1 = s32[320,22]{0,1:T(8,128)S(1)} collective-permute-done((s32[320,22]{0,1:T(8,128)S(1)}, s32[320,22]{0,1:T(8,128)S(1)}, u32[]{:S(2)}, u32[]{:S(2)}) %collective-permute-start.1) | collective-permute-done | bytes 28192 | tf_op jit(solution)/shard_map/ppermute | solution.py:62
  25.1 35.7 %shard_map.120 = (f32[2,6,320,64]{3,2,1,0:T(8,128)}, f32[816,512]{1,0:T(8,128)}) custom-call(s32[320,1]{1,0:T(8,128)} %broadcast_in_dim.54.points_ref, bf16[2,6,320,5632]{3,2,1,0:T(8,128)(2,1)} %cells_ref.1, bf16[64,5632]{1,0:T(8,128)(2,1)} %pad_maximum_fusion.table_ref, f32[2,6]{1,0:T(2,128)} %convert_element_type.23.weight_ref, ...), custom_call_target="tpu_custom_call" | custom-call | tf_op jit(solution)/shard_map/pallas_call | solution.py:149
  60.8 2.3 %reshape.202 = f32[816,2,2,128]{3,2,1,0:T(2,128)S(1)} reshape(f32[816,512]{1,0:T(8,128)} %get-tuple-element.7) | data formatting | bytes 3342336 | tf_op jit(solution)/shard_map/reshape | solution.py:222
  64.0 2.5 %slice_reduce_fusion.1 = (f32[272,2,128]{2,1,0:T(2,128)S(1)}, f32[272,2,128]{2,1,0:T(2,128)S(1)}, f32[272,2,128]{2,1,0:T(2,128)S(1)}) fusion(f32[816,2,1,128]{3,2,1,0:T(1,128)S(1)} %slice_add_fusion), kind=kLoop, calls=%fused_computation.45 | loop fusion | bytes 1671168 | tf_op jit(solution)/shard_map/slice | solution.py:226
  67.3 2.9 %collective-permute-start.7 = (f32[272,256]{1,0:T(8,128)}, f32[272,256]{1,0:T(8,128)}, u32[]{:S(2)}, u32[]{:S(2)}) collective-permute-start(f32[272,256]{1,0:T(8,128)} %bitcast.41), channel_id=1, source_target_pairs={{1,0},{2,1},{3,2},{16,3},{17,16},{18,17},{19,18},{5,4},{6,5},{7,6}... | collective-permute-start | bytes 835592 | tf_op jit(solution)/shard_map/ppermute | solution.py:29
  71.0 3.1 %collective-permute-start.6 = (f32[272,256]{1,0:T(8,128)}, f32[272,256]{1,0:T(8,128)}, u32[]{:S(2)}, u32[]{:S(2)}) collective-permute-start(f32[272,256]{1,0:T(8,128)} %bitcast.42), channel_id=1, source_target_pairs={{0,1},{1,2},{2,3},{3,16},{16,17},{17,18},{18,19},{4,5},{5,6},{6,7}... | collective-permute-start | bytes 835592 | tf_op jit(solution)/shard_map/ppermute | solution.py:27
  75.0 1.0 copy.47
  76.0 5.5 %all-to-all-start = ((bf16[32,24,320]{2,1,0:T(8,128)(2,1)}), bf16[32,24,320]{2,1,0:T(8,128)(2,1)S(1)}, u32[]{:S(2)}, u32[]{:S(2)}) async-start(bf16[32,24,320]{2,1,0:T(8,128)(2,1)} %copy.47), calls=%async_computation | async-start | bytes 1179648 | tf_op jit(solution)/shard_map/all_to_all | solution.py:209
  81.5 1.6 %collective-permute-done.6 = f32[272,256]{1,0:T(8,128)} collective-permute-done((f32[272,256]{1,0:T(8,128)}, f32[272,256]{1,0:T(8,128)}, u32[]{:S(2)}, u32[]{:S(2)}) %collective-permute-start.6) | collective-permute-done | bytes 278560 | tf_op jit(solution)/shard_map/ppermute | solution.py:27
  83.1 1.1 fusion.15
  84.3 1.5 %collective-permute-done.8 = f32[272,256]{1,0:T(8,128)S(1)} collective-permute-done((f32[272,256]{1,0:T(8,128)S(1)}, f32[272,256]{1,0:T(8,128)S(1)}, u32[]{:S(2)}, u32[]{:S(2)}) %collective-permute-start.8) | collective-permute-done | bytes 278560 | tf_op jit(solution)/shard_map/ppermute | solution.py:50
  85.8 1.6 %collective-permute-start.9 = (f32[272,256]{1,0:T(8,128)S(1)}, f32[272,256]{1,0:T(8,128)S(1)}, u32[]{:S(2)}, u32[]{:S(2)}) collective-permute-start(f32[272,256]{1,0:T(8,128)S(1)} %add.175), channel_id=1, source_target_pairs={{0,8},{4,12},{8,0},{12,4},{1,9},{5,13},{9,1},{13,5},{2,10},{6,14},... | collective-permute-start | bytes 835592 | tf_op jit(solution)/shard_map/ppermute | solution.py:50
  88.9 5.7 %collective-permute-done.9 = f32[272,256]{1,0:T(8,128)S(1)} collective-permute-done((f32[272,256]{1,0:T(8,128)S(1)}, f32[272,256]{1,0:T(8,128)S(1)}, u32[]{:S(2)}, u32[]{:S(2)}) %collective-permute-start.9) | collective-permute-done | bytes 278560 | tf_op jit(solution)/shard_map/ppermute | solution.py:50
  96.3 1.6 %collective-permute-done.2 = bf16[4,24,2560]{2,1,0:T(8,128)(2,1)S(1)} collective-permute-done((bf16[4,24,2560]{2,1,0:T(8,128)(2,1)S(1)}, bf16[4,24,2560]{2,1,0:T(8,128)(2,1)S(1)}, u32[]{:S(2)}, u32[]{:S(2)}) %collective-permute-start.2) | collective-permute-done | bytes 491552 | tf_op jit(solution)/shard_map/ppermute | solution.py:62
  98.1 1.6 %collective-permute-start.3 = (bf16[4,48,2560]{2,1,0:T(8,128)(2,1)S(1)}, bf16[4,48,2560]{2,1,0:T(8,128)(2,1)}, u32[]{:S(2)}, u32[]{:S(2)}) collective-permute-start(bf16[4,48,2560]{2,1,0:T(8,128)(2,1)S(1)} %maximum_select_fusion.2), channel_id=1, source_target_pairs={{0,8},{4,12},{8,0},{12,4},{1,9},{5,13},{9,1},{13,5},{2,10},{6,14},... | collective-permute-start | bytes 2949128 | tf_op jit(solution)/shard_map/ppermute | solution.py:62
  100.4 3.1 %collective-permute-start.11 = (f32[16,2176]{1,0:T(8,128)S(1)}, f32[16,2176]{1,0:T(8,128)S(1)}, u32[]{:S(2)}, u32[]{:S(2)}) collective-permute-start(f32[16,2176]{1,0:T(8,128)S(1)} %get-tuple-element.26), channel_id=1, source_target_pairs={{1,0},{2,1},{3,2},{16,3},{17,16},{18,17},{19,18},{5,4},{6,5},{7,6}... | collective-permute-start | bytes 417800 | tf_op jit(solution)/shard_map/ppermute | solution.py:29
  103.5 4.9 %collective-permute-start.10 = (f32[16,2176]{1,0:T(8,128)S(1)}, f32[16,2176]{1,0:T(8,128)S(1)}, u32[]{:S(2)}, u32[]{:S(2)}) collective-permute-start(f32[16,2176]{1,0:T(8,128)S(1)} %get-tuple-element.26), channel_id=1, source_target_pairs={{0,1},{1,2},{2,3},{3,16},{16,17},{17,18},{18,19},{4,5},{5,6},{6,7}... | collective-permute-start | bytes 417800 | tf_op jit(solution)/shard_map/ppermute | solution.py:27
  108.4 1.7 %collective-permute-done.11 = f32[16,2176]{1,0:T(8,128)S(1)} collective-permute-done((f32[16,2176]{1,0:T(8,128)S(1)}, f32[16,2176]{1,0:T(8,128)S(1)}, u32[]{:S(2)}, u32[]{:S(2)}) %collective-permute-start.11) | collective-permute-done | bytes 139296 | tf_op jit(solution)/shard_map/ppermute | solution.py:29
  110.1 3.1 %collective-permute-done.10 = f32[16,2176]{1,0:T(8,128)S(1)} collective-permute-done((f32[16,2176]{1,0:T(8,128)S(1)}, f32[16,2176]{1,0:T(8,128)S(1)}, u32[]{:S(2)}, u32[]{:S(2)}) %collective-permute-start.10) | collective-permute-done | bytes 139296 | tf_op jit(solution)/shard_map/ppermute | solution.py:27
  113.3 5.9 %gather_fusion = f32[3520,128]{1,0:T(8,128)S(1)} fusion(f32[816,128]{1,0:T(8,128)S(1)} %reshape.205, s32[4096]{0:T(1024)S(1)} %pad_clamp_fusion), kind=kCustom, calls=%fused_computation | custom fusion | bytes 3618560 | tf_op jit(solution)/shard_map/jit(_take)/gather | solution.py:253
  119.2 1.6 %gather.7 = f32[320,1408]{1,0:T(8,128)} reshape(f32[3520,128]{1,0:T(8,128)S(1)} %gather_fusion) | data formatting | bytes 3604480 | tf_op jit(solution)/shard_map/jit(_take)/gather | solution.py:253
  120.7 2.2 %copy.53 = f32[320,1408]{0,1:T(8,128)S(1)} copy(f32[320,1408]{1,0:T(8,128)} %gather.7) | data formatting | bytes 3604480 | tf_op jit(solution)/shard_map/jit(_take)/gather | solution.py:253
  122.9 1.6 %select_select_fusion = f32[320,1408]{0,1:T(8,128)} fusion(f32[320,1408]{0,1:T(8,128)S(1)} %copy.53, s32[320]{0:T(512)S(1)} %copy-done.7, s32[1408]{0:T(1024)S(1)} %iota_add_fusion, pred[320,11]{0,1:T(8,128)(4,1)S(1)} %get-tuple-element.23), kind=kLoop, calls=%fused_computation.1 | loop fusion | flops 1351680 | bytes 3614912 | tf_op jit(solution)/shard_map/jit(_where)/select_n | solution.py:255
  124.6 2.9 %copy.54 = f32[320,1408]{1,0:T(8,128)} copy(f32[320,1408]{0,1:T(8,128)} %select_select_fusion) | data formatting | bytes 3604480
  127.5 6.2 %fusion = f32[4,96,384]{2,1,0:T(8,128)} fusion(bf16[4,2560,384]{2,1,0:T(8,128)(2,1)} %param.12, bf16[4,48,2560]{2,1,0:T(8,128)(2,1)S(1)} %maximum_select_fusion.2, bf16[4,48,2560]{2,1,0:T(8,128)(2,1)} %collective-permute-done.3, pred[]{:T(512)S(6)} %eq.19), kind=kOutput, calls=%fused_computation.3 | convolution fusion | flops 763822080 | bytes 10420225 | tf_op jit(solution)/shard_map/srj,sjd->srd/dot_general | solution.py:216
  (77 shorter events, 10.7 us)
Async XLA Ops:
  0.6 18.7 %copy-start.6 = (s32[320,11]{0,1:T(8,128)S(1)}, s32[320,11]{0,1:T(8,128)}, u32[]{:S(2)}) copy-start(s32[320,11]{0,1:T(8,128)} %param.14) | copy-start | bytes 42244
  0.6 17.9 %copy-start.9 = (s32[32]{0:T(128)S(1)}, s32[32]{0:T(128)}, u32[]{:S(2)}) copy-start(s32[32]{0:T(128)} %param.11) | copy-start | bytes 388
  0.7 17.9 %copy-start.7 = (s32[320]{0:T(512)S(1)}, s32[320]{0:T(512)}, u32[]{:S(2)}) copy-start(s32[320]{0:T(512)} %param.10) | copy-start | bytes 3844
  0.7 18.7 %copy-start.10 = (bf16[2,6]{1,0:T(2,128)(2,1)S(1)}, bf16[2,6]{1,0:T(2,128)(2,1)}, u32[]{:S(2)}) copy-start(bf16[2,6]{1,0:T(2,128)(2,1)} %param.13) | copy-start | bytes 76
  0.7 19.3 %collective-permute-start = (s32[320,11]{0,1:T(8,128)}, s32[320,11]{0,1:T(8,128)S(1)}, u32[]{:S(2)}, u32[]{:S(2)}) collective-permute-start(s32[320,11]{0,1:T(8,128)} %param.14), channel_id=1, source_target_pairs={{0,4},{4,0},{8,12},{12,8},{1,5},{5,1},{9,13},{13,9},{2,6},{6,2},{1... | collective-permute-start | bytes 42248 | tf_op jit(solution)/shard_map/ppermute | solution.py:62
  2.4 93.7 %collective-permute-start.5 = (f32[2,1,2176]{2,1,0:T(1,128)}, f32[2,1,2176]{2,1,0:T(1,128)S(1)}, u32[]{:S(2)}, u32[]{:S(2)}) collective-permute-start(f32[2,1,2176]{2,1,0:T(1,128)} %get-tuple-element.32), channel_id=1, source_target_pairs={{0,1},{1,2},{2,3},{3,16},{16,17},{17,18},{18,19},{4,5},{5,6},{6,7}... | collective-permute-start | bytes 52232 | tf_op jit(solution)/shard_map/ppermute | solution.py:27
  5.9 90.3 %collective-permute-start.4 = (f32[2,1,2176]{2,1,0:T(1,128)}, f32[2,1,2176]{2,1,0:T(1,128)S(1)}, u32[]{:S(2)}, u32[]{:S(2)}) collective-permute-start(f32[2,1,2176]{2,1,0:T(1,128)} %get-tuple-element.31), channel_id=1, source_target_pairs={{1,0},{2,1},{3,2},{16,3},{17,16},{18,17},{19,18},{5,4},{6,5},{7,6}... | collective-permute-start | bytes 52232 | tf_op jit(solution)/shard_map/ppermute | solution.py:29
  20.0 4.0 %collective-permute-start.1 = (s32[320,22]{0,1:T(8,128)S(1)}, s32[320,22]{0,1:T(8,128)S(1)}, u32[]{:S(2)}, u32[]{:S(2)}) collective-permute-start(s32[320,22]{0,1:T(8,128)S(1)} %add_select_fusion.7), channel_id=1, source_target_pairs={{0,8},{4,12},{8,0},{12,4},{1,9},{5,13},{9,1},{13,5},{2,10},{6,14},... | collective-permute-start | bytes 84488 | tf_op jit(solution)/shard_map/ppermute | solution.py:62
  64.0 10.1 %copy-start.2 = (f32[2,6,320,64]{3,2,1,0:T(8,128)S(1)}, f32[2,6,320,64]{3,2,1,0:T(8,128)}, u32[]{:S(2)}) copy-start(f32[2,6,320,64]{3,2,1,0:T(8,128)} %get-tuple-element.6) | copy-start | bytes 2949124
  67.3 14.2 %collective-permute-start.7 = (f32[272,256]{1,0:T(8,128)}, f32[272,256]{1,0:T(8,128)}, u32[]{:S(2)}, u32[]{:S(2)}) collective-permute-start(f32[272,256]{1,0:T(8,128)} %bitcast.41), channel_id=1, source_target_pairs={{1,0},{2,1},{3,2},{16,3},{17,16},{18,17},{19,18},{5,4},{6,5},{7,6}... | collective-permute-start | bytes 835592 | tf_op jit(solution)/shard_map/ppermute | solution.py:29
  71.0 12.1 %collective-permute-start.6 = (f32[272,256]{1,0:T(8,128)}, f32[272,256]{1,0:T(8,128)}, u32[]{:S(2)}, u32[]{:S(2)}) collective-permute-start(f32[272,256]{1,0:T(8,128)} %bitcast.42), channel_id=1, source_target_pairs={{0,1},{1,2},{2,3},{3,16},{16,17},{17,18},{18,19},{4,5},{5,6},{6,7}... | collective-permute-start | bytes 835592 | tf_op jit(solution)/shard_map/ppermute | solution.py:27
  75.0 12.4 %copy-start.8 = (s32[16,17]{1,0:T(8,128)S(1)}, s32[16,17]{1,0:T(8,128)}, u32[]{:S(2)}) copy-start(s32[16,17]{1,0:T(8,128)} %param.17) | copy-start | bytes 3268
  76.0 12.6 %copy-start = (f32[16,2176]{1,0:T(8,128)S(1)}, f32[16,2176]{1,0:T(8,128)}, u32[]{:S(2)}) copy-start(f32[16,2176]{1,0:T(8,128)} %param.15) | copy-start | bytes 417796
  76.0 12.6 %copy-start.1 = (f32[16,2176]{1,0:T(8,128)S(1)}, f32[16,2176]{1,0:T(8,128)}, u32[]{:S(2)}) copy-start(f32[16,2176]{1,0:T(8,128)} %param.16) | copy-start | bytes 417796
  76.0 19.4 %all-to-all-start = ((bf16[32,24,320]{2,1,0:T(8,128)(2,1)}), bf16[32,24,320]{2,1,0:T(8,128)(2,1)S(1)}, u32[]{:S(2)}, u32[]{:S(2)}) async-start(bf16[32,24,320]{2,1,0:T(8,128)(2,1)} %copy.47), calls=%async_computation | async-start | bytes 1179648 | tf_op jit(solution)/shard_map/all_to_all | solution.py:209
  84.2 1.6 %collective-permute-start.8 = (f32[272,256]{1,0:T(8,128)S(1)}, f32[272,256]{1,0:T(8,128)S(1)}, u32[]{:S(2)}, u32[]{:S(2)}) collective-permute-start(f32[272,256]{1,0:T(8,128)S(1)} %fusion.15), channel_id=1, source_target_pairs={{0,4},{4,0},{8,12},{12,8},{1,5},{5,1},{9,13},{13,9},{2,6},{6,2},{1... | collective-permute-start | bytes 835592 | tf_op jit(solution)/shard_map/ppermute | solution.py:50
  85.8 8.8 %collective-permute-start.9 = (f32[272,256]{1,0:T(8,128)S(1)}, f32[272,256]{1,0:T(8,128)S(1)}, u32[]{:S(2)}, u32[]{:S(2)}) collective-permute-start(f32[272,256]{1,0:T(8,128)S(1)} %add.175), channel_id=1, source_target_pairs={{0,8},{4,12},{8,0},{12,4},{1,9},{5,13},{9,1},{13,5},{2,10},{6,14},... | collective-permute-start | bytes 835592 | tf_op jit(solution)/shard_map/ppermute | solution.py:50
  94.6 1.5 %copy-start.3 = (f32[2,16,2175]{2,1,0:T(8,128)S(1)}, f32[2,16,2175]{2,1,0:T(8,128)}, u32[]{:S(2)}) copy-start(f32[2,16,2175]{2,1,0:T(8,128)} %get-tuple-element.27) | copy-start | bytes 835204
  94.7 1.5 %copy-start.4 = (f32[2,16,2175]{2,1,0:T(8,128)S(1)}, f32[2,16,2175]{2,1,0:T(8,128)}, u32[]{:S(2)}) copy-start(f32[2,16,2175]{2,1,0:T(8,128)} %get-tuple-element.28) | copy-start | bytes 835204
  96.0 1.9 %collective-permute-start.2 = (bf16[4,24,2560]{2,1,0:T(8,128)(2,1)S(1)}, bf16[4,24,2560]{2,1,0:T(8,128)(2,1)S(1)}, u32[]{:S(2)}, u32[]{:S(2)}) collective-permute-start(bf16[4,24,2560]{2,1,0:T(8,128)(2,1)S(1)} %all_to_all.16), channel_id=1, source_target_pairs={{0,4},{4,0},{8,12},{12,8},{1,5},{5,1},{9,13},{13,9},{2,6},{6,2},{1... | collective-permute-start | bytes 1474568 | tf_op jit(solution)/shard_map/ppermute | solution.py:62
  98.1 29.3 %collective-permute-start.3 = (bf16[4,48,2560]{2,1,0:T(8,128)(2,1)S(1)}, bf16[4,48,2560]{2,1,0:T(8,128)(2,1)}, u32[]{:S(2)}, u32[]{:S(2)}) collective-permute-start(bf16[4,48,2560]{2,1,0:T(8,128)(2,1)S(1)} %maximum_select_fusion.2), channel_id=1, source_target_pairs={{0,8},{4,12},{8,0},{12,4},{1,9},{5,13},{9,1},{13,5},{2,10},{6,14},... | collective-permute-start | bytes 2949128 | tf_op jit(solution)/shard_map/ppermute | solution.py:62
  100.4 18.8 %copy-start.5 = (f32[16,2176]{1,0:T(8,128)}, f32[16,2176]{1,0:T(8,128)S(1)}, u32[]{:S(2)}) copy-start(f32[16,2176]{1,0:T(8,128)S(1)} %get-tuple-element.26) | copy-start | bytes 417796
  100.4 9.7 %collective-permute-start.11 = (f32[16,2176]{1,0:T(8,128)S(1)}, f32[16,2176]{1,0:T(8,128)S(1)}, u32[]{:S(2)}, u32[]{:S(2)}) collective-permute-start(f32[16,2176]{1,0:T(8,128)S(1)} %get-tuple-element.26), channel_id=1, source_target_pairs={{1,0},{2,1},{3,2},{16,3},{17,16},{18,17},{19,18},{5,4},{6,5},{7,6}... | collective-permute-start | bytes 417800 | tf_op jit(solution)/shard_map/ppermute | solution.py:29
  103.5 9.7 %collective-permute-start.10 = (f32[16,2176]{1,0:T(8,128)S(1)}, f32[16,2176]{1,0:T(8,128)S(1)}, u32[]{:S(2)}, u32[]{:S(2)}) collective-permute-start(f32[16,2176]{1,0:T(8,128)S(1)} %get-tuple-element.26), channel_id=1, source_target_pairs={{0,1},{1,2},{2,3},{3,16},{16,17},{17,18},{18,19},{4,5},{5,6},{6,7}... | collective-permute-start | bytes 417800 | tf_op jit(solution)/shard_map/ppermute | solution.py:27

commit v6 on v5

--- a/solution.py
+++ b/solution.py
@@ -77,7 +77,7 @@
     return rows
 
 
-def transform_kernel(points_ref, cells_ref, table_ref, weight_ref, slot_ref, sums_ref, acc_ref, *scratch):
+def transform_kernel(points_ref, cells_ref, table_ref, weight_ref, slot_ref, sums_ref, out_ref, acc_ref, *scratch):
     step = pl.program_id(0)
 
     @pl.when(step == 0)
@@ -135,6 +135,15 @@
     ).astype(jnp.bfloat16)
     acc_ref[...] += jnp.dot(onehot, stacked, preferred_element_type=jnp.float32)
 
+    @pl.when(step == pl.num_programs(0) - 1)
+    def _():
+        nsec, tiles, _ = out_ref.shape
+        for s in range(nsec):
+            for f in range(nfields):
+                high = acc_ref[s * tiles : (s + 1) * tiles, 2 * f * BLOCK : (2 * f + 1) * BLOCK]
+                low = acc_ref[s * tiles : (s + 1) * tiles, (2 * f + 1) * BLOCK : (2 * f + 2) * BLOCK]
+                out_ref[s, :, f * BLOCK : (f + 1) * BLOCK] = high + low
+
 
 def fused_transform(atmos_fields, lat_points, table, column_weight, slots, nslot):
     nfields, nlev, lat_band, lon_count = atmos_fields.shape
@@ -143,9 +152,9 @@
     nblocks = lon_count // BLOCK
     wave2 = table.shape[0]
     slot_rows = slots.reshape(steps, rows, nblocks).transpose(0, 2, 1).reshape(steps, 1, nblocks * rows)
-    scratch = []
-    if rows % 16 == 0 and True:
-        scratch = [pltpu.VMEM((nblocks * rows, 2 * nfields * BLOCK), jnp.bfloat16)]
+    scratch = [pltpu.VMEM((nslot, 2 * nfields * BLOCK), jnp.float32)]
+    if rows % 16 == 0:
+        scratch.append(pltpu.VMEM((nblocks * rows, 2 * nfields * BLOCK), jnp.bfloat16))
     return pl.pallas_call(
         transform_kernel,
         grid=(steps,),
@@ -158,11 +167,11 @@
         ],
         out_specs=[
             pl.BlockSpec((nfields, nlev, rows, wave2), lambda r: (0, 0, r, 0)),
-            pl.BlockSpec((nslot, 2 * nfields * BLOCK), lambda r: (0, 0)),
+            pl.BlockSpec((3, nslot // 3, nfields * BLOCK), lambda r: (0, 0, 0)),
         ],
         out_shape=[
             jax.ShapeDtypeStruct((nfields, nlev, lat_band, wave2), jnp.float32),
-            jax.ShapeDtypeStruct((nslot, 2 * nfields * BLOCK), jnp.float32),
+            jax.ShapeDtypeStruct((3, nslot // 3, nfields * BLOCK), jnp.float32),
         ],
         scratch_shapes=scratch,
         compiler_params=pltpu.CompilerParams(dimension_semantics=("arbitrary",)),
@@ -197,11 +206,11 @@
     def slot_of(targets):
         return (targets // tile_count - band_index + 1) * tile_count + targets % tile_count
 
-    local_slot = slot_of(block_remap.reshape(-1))
+    local_slot = slot_of(block_remap.T.reshape(-1))
     quarter = lon_count // lax.axis_size("lev")
     full_remap = lev_gather(block_remap, 1)
     every_slot = slot_of(full_remap)
-    raw_sums, split_sums = fused_transform(
+    raw_sums, sections = fused_transform(
         atmos_fields, lat_points, table, column_weight, every_slot, 3 * tile_count
     )
     raw_sums = raw_sums.reshape(field_count, lev_dev, lat_band, 2, wave_count)
@@ -219,12 +228,14 @@
         legendre,
         preferred_element_type=jnp.float32,
     )
-    split_sums = split_sums.reshape(3 * tile_count, FIELDS, 2, BLOCK)
-    outgoing = (split_sums[:, :, 0] + split_sums[:, :, 1]).reshape(3 * tile_count, FIELDS * BLOCK)
-    widened = with_halo(outgoing, ((("lat", "ocn"), 0),), tile_count)
-    arrived = (
-        widened[:tile_count] + widened[2 * tile_count : 3 * tile_count] + widened[4 * tile_count :]
-    )
+    band_count = lax.axis_size(("lat", "ocn"))
+    from_prev = lax.ppermute(
+        sections[2], ("lat", "ocn"), [(i, i + 1) for i in range(band_count - 1)]
+    )
+    from_next = lax.ppermute(
+        sections[0], ("lat", "ocn"), [(i + 1, i) for i in range(band_count - 1)]
+    )
+    arrived = (from_prev + sections[1]) + from_next
     tile_sums = lev_sum(arrived)
     forcing = (
         tile_sums.reshape(ocean_rows, ocean_cols // BLOCK, FIELDS, BLOCK)
@@ -250,11 +261,17 @@
     salt_next = updated[1]
     returned = with_halo(temp_next, ((("lat", "ocn"), 0),), ocean_rows)
     tiles_near = returned.reshape(3 * tile_count, BLOCK)
-    surface = jnp.take(tiles_near, local_slot, axis=0).reshape(lat_band, quarter)
-    own_points = lax.axis_index("lev") * quarter + jnp.arange(quarter, dtype=jnp.int32)
-    surface_temp = jnp.where(
-        own_points[None, :] < lat_points[:, None], surface, jnp.zeros((), jnp.float32)
-    )
+    nquarter = quarter // BLOCK
+    gathered = jnp.take(tiles_near, local_slot, axis=0).reshape(nquarter, lat_band, BLOCK)
+    own_points = (
+        lax.axis_index("lev") * quarter
+        + lax.broadcasted_iota(jnp.int32, (nquarter, 1, BLOCK), 0) * BLOCK
+        + lax.broadcasted_iota(jnp.int32, (nquarter, 1, BLOCK), 2)
+    )
+    kept = jnp.where(
+        own_points < lat_points[None, :, None], gathered, jnp.zeros((), jnp.float32)
+    )
+    surface_temp = kept.transpose(1, 0, 2).reshape(lat_band, quarter)
     return (spectra, temp_next, salt_next, surface_temp)
 
 

time: 135 us -> 128 us (0.948)
  local copies, waits for them, and re-layouts: 25.1 us -> 20.5 us
  waiting for transfers between devices: 18.1 us -> 20.9 us
  starting transfers between devices: 32.9 us -> 30.7 us
  other arithmetic: 14.6 us -> 13.1 us
    ppermute x0 -> x2, starting transfers between devices: none -> 5.84 us  [the longest x1 3.09 us: body(): lax.ppermute(sections[2], ('lat', 'ocn'), [(i, i + 1) for i in range(band...]
    ppermute x3 -> x2, starting transfers between devices: 11.4 us -> 6.29 us  [with_halo(): lax.ppermute(tail, axis, [(i, (i + 1) % count) for i in range(ends)])]
    ppermute x3 -> x2, starting transfers between devices: 11.1 us -> 8.26 us  [with_halo(): lax.ppermute(head, axis, [((i + 1) % count, i) for i in range(ends)])]
    slice x1 -> x0, local copies, waits for them, and re-layouts: 2.54 us -> none  [body(): widened[2 * tile_count:3 * tile_count]]
    reshape x1 -> x0, local copies, waits for them, and re-layouts: 2.32 us -> none  [body(): split_sums = split_sums.reshape(3 * tile_count, FIELDS, 2, BLOCK)]
    pallas_call x1, local copies, waits for them, and re-layouts: 0.65 us -> 2.2 us  [fused_transform(): pl.pallas_call(transform_kernel, grid=(steps,), in_specs=[pl.BlockSpec((r...]
    unnamed x26 -> x16, local copies, waits for them, and re-layouts: 4.41 us -> 2.95 us
    all_to_all x1, waiting for transfers between devices: 0.54 us -> 1.96 us  [body(): lax.all_to_all(coeffs.transpose(4, 1, 0, 3, 2).reshape(wave_count, lev_de...]
  transfers between devices with their start and end apart: 13 -> 13, of which waited for: 8 -> 7; matrix products, arithmetic and copies ran while one was open for 29% -> 26% of each run, Pallas kernels for 27% -> 28%
where the time goes in v6:
time: 128 us
  Pallas kernels  35.5 us (28%)
  starting transfers between devices  30.7 us (24%)
  waiting for transfers between devices  20.9 us (16%)
  local copies, waits for them, and re-layouts  20.5 us (16%)
  other arithmetic  13.1 us (10%)
  matrix products  6.1 us (5%)
    pallas_call x1, Pallas kernels, fused_transform(): pl.pallas_call(transform_kernel, grid=(steps,), in_specs=[pl.BlockSpec((r...  35.5 us
    gather x2, local copies, waits for them, and re-layouts, body(): jnp.take(tiles_near, local_slot, axis=0).reshape(nquarter, lat_band, BLOCK)  9.6 us
    ppermute x2, starting transfers between devices, with_halo(): lax.ppermute(head, axis, [((i + 1) % count, i) for i in range(ends)])  8.26 us
    ppermute x2, waiting for transfers between devices, lev_sum(): lax.ppermute(values, 'lev', [(i, i ^ stride) for i in range(count)])  8.15 us
    ppermute x2, starting transfers between devices, with_halo(): lax.ppermute(tail, axis, [(i, (i + 1) % count) for i in range(ends)])  6.29 us
    dot_general x1, matrix products, body(): jnp.einsum('srj,sjd->srd', lev_gather(regrouped, 1), legendre, preferred_...  6.1 us
    ppermute x2, waiting for transfers between devices, with_halo(): lax.ppermute(tail, axis, [(i, (i + 1) % count) for i in range(ends)])  5.65 us
    all_to_all x1, starting transfers between devices, body(): lax.all_to_all(coeffs.transpose(4, 1, 0, 3, 2).reshape(wave_count, lev_de...  5.37 us
  transfers between devices with their start and end apart: 13, of which 7 were waited for; matrix products, arithmetic and copies ran while one was open for 26% of the time, Pallas kernels for 28%

profile of v6, /device:TPU:4, one launch (start us, length us, event | category | flops | bytes accessed | tf_op | source)
XLA Modules:
  0.0 127.8 jit_solution(8174590708024430644)
XLA Ops:
  0.7 1.0 fusion.34
  1.8 3.5 %collective-permute-start.5 = (f32[2,1,2176]{2,1,0:T(1,128)S(1)}, f32[2,1,2176]{2,1,0:T(1,128)S(1)}, u32[]{:S(2)}, u32[]{:S(2)}) collective-permute-start(f32[2,1,2176]{2,1,0:T(1,128)S(1)} %get-tuple-element.31), channel_id=1, source_target_pairs={{0,1},{1,2},{2,3},{3,16},{16,17},{17,18},{18,19},{4,5},{5,6},{6,7}... | collective-permute-start | bytes 52232 | tf_op jit(solution)/shard_map/ppermute | solution.py:27
  5.3 5.1 %collective-permute-start.4 = (f32[2,1,2176]{2,1,0:T(1,128)S(1)}, f32[2,1,2176]{2,1,0:T(1,128)S(1)}, u32[]{:S(2)}, u32[]{:S(2)}) collective-permute-start(f32[2,1,2176]{2,1,0:T(1,128)S(1)} %get-tuple-element.30), channel_id=1, source_target_pairs={{1,0},{2,1},{3,2},{16,3},{17,16},{18,17},{19,18},{5,4},{6,5},{7,6}... | collective-permute-start | bytes 52232 | tf_op jit(solution)/shard_map/ppermute | solution.py:29
  10.3 4.0 %cosine_convert_fusion = (bf16[32,5632]{1,0:T(8,128)(2,1)S(1)}, bf16[32,5632]{1,0:T(8,128)(2,1)S(1)}) fusion(s32[32]{0:T(128)} %param.11), kind=kLoop, calls=%fused_computation.17 | loop fusion | flops 2162688 | bytes 721024 | tf_op jit(solution)/shard_map/convert
  15.0 1.2 fusion.14
  17.0 0.9 pad_maximum_fusion.table_ref
  18.0 0.8 broadcast_in_dim.50.points_ref
  19.5 1.6 %collective-permute-start.1 = (s32[320,22]{0,1:T(8,128)S(1)}, s32[320,22]{0,1:T(8,128)S(1)}, u32[]{:S(2)}, u32[]{:S(2)}) collective-permute-start(s32[320,22]{0,1:T(8,128)S(1)} %add_select_fusion.7), channel_id=1, source_target_pairs={{0,8},{4,12},{8,0},{12,4},{1,9},{5,13},{9,1},{13,5},{2,10},{6,14},... | collective-permute-start | bytes 84488 | tf_op jit(solution)/shard_map/ppermute | solution.py:62
  21.1 2.4 %collective-permute-done.1 = s32[320,22]{0,1:T(8,128)S(1)} collective-permute-done((s32[320,22]{0,1:T(8,128)S(1)}, s32[320,22]{0,1:T(8,128)S(1)}, u32[]{:S(2)}, u32[]{:S(2)}) %collective-permute-start.1) | collective-permute-done | bytes 28192 | tf_op jit(solution)/shard_map/ppermute | solution.py:62
  24.6 35.5 %shard_map.120 = (f32[2,6,320,64]{3,2,1,0:T(8,128)}, f32[3,272,256]{2,1,0:T(8,128)}) custom-call(s32[320,1]{1,0:T(8,128)} %broadcast_in_dim.50.points_ref, bf16[2,6,320,5632]{3,2,1,0:T(8,128)(2,1)} %cells_ref.1, bf16[64,5632]{1,0:T(8,128)(2,1)} %pad_maximum_fusion.table_ref, f32[2,6]{1,0:T(2,128)} %convert_element_type.23.weight_ref, ...), custom_call_target="tpu_custom_call" | custom-call | tf_op jit(solution)/shard_map/pallas_call | solution.py:158
  60.1 1.1 slice_bitcast_fusion.1
  61.1 2.8 %collective-permute-start.7 = (f32[272,256]{1,0:T(8,128)S(1)}, f32[272,256]{1,0:T(8,128)S(1)}, u32[]{:S(2)}, u32[]{:S(2)}) collective-permute-start(f32[272,256]{1,0:T(8,128)S(1)} %get-tuple-element.23), channel_id=1, source_target_pairs={{1,0},{2,1},{3,2},{16,3},{17,16},{18,17},{19,18},{5,4},{6,5},{7,6}... | collective-permute-start | bytes 835592 | tf_op jit(solution)/shard_map/ppermute | solution.py:235
  63.9 3.1 %collective-permute-start.6 = (f32[272,256]{1,0:T(8,128)S(1)}, f32[272,256]{1,0:T(8,128)S(1)}, u32[]{:S(2)}, u32[]{:S(2)}) collective-permute-start(f32[272,256]{1,0:T(8,128)S(1)} %get-tuple-element.22), channel_id=1, source_target_pairs={{0,1},{1,2},{2,3},{3,16},{16,17},{17,18},{18,19},{4,5},{5,6},{6,7}... | collective-permute-start | bytes 835592 | tf_op jit(solution)/shard_map/ppermute | solution.py:232
  67.0 2.2 %copy.40 = f32[2,6,320,64]{2,3,1,0:T(8,128)S(1)} copy(f32[2,6,320,64]{3,2,1,0:T(8,128)} %get-tuple-element.6) | data formatting | bytes 1966080 | tf_op jit(solution)/shard_map/pallas_call | solution.py:158
  69.5 1.0 copy.42
  70.5 5.4 %all-to-all-start = ((bf16[32,24,320]{2,1,0:T(8,128)(2,1)}), bf16[32,24,320]{2,1,0:T(8,128)(2,1)S(1)}, u32[]{:S(2)}, u32[]{:S(2)}) async-start(bf16[32,24,320]{2,1,0:T(8,128)(2,1)} %copy.42), calls=%async_computation | async-start | bytes 1179648 | tf_op jit(solution)/shard_map/all_to_all | solution.py:218
  75.8 1.0 fusion.22
  77.0 1.5 %collective-permute-done.8 = f32[272,256]{1,0:T(8,128)S(1)} collective-permute-done((f32[272,256]{1,0:T(8,128)S(1)}, f32[272,256]{1,0:T(8,128)S(1)}, u32[]{:S(2)}, u32[]{:S(2)}) %collective-permute-start.8) | collective-permute-done | bytes 278560 | tf_op jit(solution)/shard_map/ppermute | solution.py:50
  78.5 1.6 %collective-permute-start.9 = (f32[272,256]{1,0:T(8,128)S(1)}, f32[272,256]{1,0:T(8,128)S(1)}, u32[]{:S(2)}, u32[]{:S(2)}) collective-permute-start(f32[272,256]{1,0:T(8,128)S(1)} %add.177), channel_id=1, source_target_pairs={{0,8},{4,12},{8,0},{12,4},{1,9},{5,13},{9,1},{13,5},{2,10},{6,14},... | collective-permute-start | bytes 835592 | tf_op jit(solution)/shard_map/ppermute | solution.py:50
  80.7 6.6 %collective-permute-done.9 = f32[272,256]{1,0:T(8,128)S(1)} collective-permute-done((f32[272,256]{1,0:T(8,128)S(1)}, f32[272,256]{1,0:T(8,128)S(1)}, u32[]{:S(2)}, u32[]{:S(2)}) %collective-permute-start.9) | collective-permute-done | bytes 278560 | tf_op jit(solution)/shard_map/ppermute | solution.py:50
  87.6 2.0 %all-to-all-done = bf16[32,24,320]{2,1,0:T(8,128)(2,1)S(1)} async-done(((bf16[32,24,320]{2,1,0:T(8,128)(2,1)}), bf16[32,24,320]{2,1,0:T(8,128)(2,1)S(1)}, u32[]{:S(2)}, u32[]{:S(2)}) %all-to-all-start) | async-done | bytes 491552 | tf_op jit(solution)/shard_map/all_to_all | solution.py:218
  90.4 1.6 %collective-permute-done.2 = bf16[4,24,2560]{2,1,0:T(8,128)(2,1)S(1)} collective-permute-done((bf16[4,24,2560]{2,1,0:T(8,128)(2,1)S(1)}, bf16[4,24,2560]{2,1,0:T(8,128)(2,1)S(1)}, u32[]{:S(2)}, u32[]{:S(2)}) %collective-permute-start.2) | collective-permute-done | bytes 491552 | tf_op jit(solution)/shard_map/ppermute | solution.py:62
  92.2 1.6 %collective-permute-start.3 = (bf16[4,48,2560]{2,1,0:T(8,128)(2,1)S(1)}, bf16[4,48,2560]{2,1,0:T(8,128)(2,1)}, u32[]{:S(2)}, u32[]{:S(2)}) collective-permute-start(bf16[4,48,2560]{2,1,0:T(8,128)(2,1)S(1)} %maximum_select_fusion.2), channel_id=1, source_target_pairs={{0,8},{4,12},{8,0},{12,4},{1,9},{5,13},{9,1},{13,5},{2,10},{6,14},... | collective-permute-start | bytes 2949128 | tf_op jit(solution)/shard_map/ppermute | solution.py:62
  94.5 3.2 %collective-permute-start.11 = (f32[16,2176]{1,0:T(8,128)S(1)}, f32[16,2176]{1,0:T(8,128)S(1)}, u32[]{:S(2)}, u32[]{:S(2)}) collective-permute-start(f32[16,2176]{1,0:T(8,128)S(1)} %get-tuple-element.25), channel_id=1, source_target_pairs={{1,0},{2,1},{3,2},{16,3},{17,16},{18,17},{19,18},{5,4},{6,5},{7,6}... | collective-permute-start | bytes 417800 | tf_op jit(solution)/shard_map/ppermute | solution.py:29
  97.7 2.8 %collective-permute-start.10 = (f32[16,2176]{1,0:T(8,128)S(1)}, f32[16,2176]{1,0:T(8,128)S(1)}, u32[]{:S(2)}, u32[]{:S(2)}) collective-permute-start(f32[16,2176]{1,0:T(8,128)S(1)} %get-tuple-element.25), channel_id=1, source_target_pairs={{0,1},{1,2},{2,3},{3,16},{16,17},{17,18},{18,19},{4,5},{5,6},{6,7}... | collective-permute-start | bytes 417800 | tf_op jit(solution)/shard_map/ppermute | solution.py:27
  100.6 1.2 collective-permute-done.11
  101.8 5.6 %collective-permute-done.10 = f32[16,2176]{1,0:T(8,128)S(1)} collective-permute-done((f32[16,2176]{1,0:T(8,128)S(1)}, f32[16,2176]{1,0:T(8,128)S(1)}, u32[]{:S(2)}, u32[]{:S(2)}) %collective-permute-start.10) | collective-permute-done | bytes 139296 | tf_op jit(solution)/shard_map/ppermute | solution.py:27
  107.5 7.4 %gather_fusion = f32[3520,128]{1,0:T(8,128)} fusion(f32[816,128]{1,0:T(8,128)S(1)} %reshape.207, s32[4096]{0:T(1024)S(1)} %pad_clamp_fusion), kind=kCustom, calls=%fused_computation | custom fusion | bytes 3618560 | tf_op jit(solution)/shard_map/jit(_take)/gather | solution.py:265
  114.9 2.2 %copy.45 = f32[11,320,128]{1,2,0:T(8,128)S(1)} copy(f32[11,320,128]{2,1,0:T(8,128)} %bitcast.55) | data formatting | bytes 3604480 | tf_op jit(solution)/shard_map/jit(_take)/gather | solution.py:265
  117.1 1.7 %select_select_fusion = f32[11,320,128]{1,2,0:T(8,128)} fusion(f32[11,320,128]{1,2,0:T(8,128)S(1)} %copy.45, s32[320]{0:T(512)S(1)} %copy-done.4, s32[11,128]{1,0:T(8,128)S(1)} %iota_add_fusion, pred[11,320]{1,0:T(8,128)(4,1)S(1)} %get-tuple-element.20), kind=kLoop, calls=%fused_computation.1 | loop fusion | flops 1351680 | bytes 3614912 | tf_op jit(solution)/shard_map/jit(_where)/select_n | solution.py:271
  118.8 2.9 %copy.46 = f32[320,1408]{1,0:T(8,128)} copy(f32[320,1408]{0,1:T(8,128)} %bitcast.54) | data formatting | bytes 3604480
  121.7 6.1 %fusion = f32[4,96,384]{2,1,0:T(8,128)} fusion(bf16[4,2560,384]{2,1,0:T(8,128)(2,1)} %param.12, bf16[4,48,2560]{2,1,0:T(8,128)(2,1)S(1)} %maximum_select_fusion.2, bf16[4,48,2560]{2,1,0:T(8,128)(2,1)} %collective-permute-done.3, pred[]{:T(512)S(6)} %eq.19), kind=kOutput, calls=%fused_computation.3 | convolution fusion | flops 763822080 | bytes 10420225 | tf_op jit(solution)/shard_map/srj,sjd->srd/dot_general | solution.py:225
  (62 shorter events, 6.4 us)
Async XLA Ops:
  0.6 17.3 %copy-start.3 = (s32[320,11]{0,1:T(8,128)S(1)}, s32[320,11]{0,1:T(8,128)}, u32[]{:S(2)}) copy-start(s32[320,11]{0,1:T(8,128)} %param.14) | copy-start | bytes 42244
  0.6 17.2 %copy-start.4 = (s32[320]{0:T(512)S(1)}, s32[320]{0:T(512)}, u32[]{:S(2)}) copy-start(s32[320]{0:T(512)} %param.10) | copy-start | bytes 3844
  0.7 18.2 %copy-start.6 = (bf16[2,6]{1,0:T(2,128)(2,1)S(1)}, bf16[2,6]{1,0:T(2,128)(2,1)}, u32[]{:S(2)}) copy-start(bf16[2,6]{1,0:T(2,128)(2,1)} %param.13) | copy-start | bytes 76
  0.7 18.8 %collective-permute-start = (s32[320,11]{0,1:T(8,128)}, s32[320,11]{0,1:T(8,128)S(1)}, u32[]{:S(2)}, u32[]{:S(2)}) collective-permute-start(s32[320,11]{0,1:T(8,128)} %param.14), channel_id=1, source_target_pairs={{0,4},{4,0},{8,12},{12,8},{1,5},{5,1},{9,13},{13,9},{2,6},{6,2},{1... | collective-permute-start | bytes 42248 | tf_op jit(solution)/shard_map/ppermute | solution.py:62
  1.8 88.4 %collective-permute-start.5 = (f32[2,1,2176]{2,1,0:T(1,128)S(1)}, f32[2,1,2176]{2,1,0:T(1,128)S(1)}, u32[]{:S(2)}, u32[]{:S(2)}) collective-permute-start(f32[2,1,2176]{2,1,0:T(1,128)S(1)} %get-tuple-element.31), channel_id=1, source_target_pairs={{0,1},{1,2},{2,3},{3,16},{16,17},{17,18},{18,19},{4,5},{5,6},{6,7}... | collective-permute-start | bytes 52232 | tf_op jit(solution)/shard_map/ppermute | solution.py:27
  5.3 85.0 %collective-permute-start.4 = (f32[2,1,2176]{2,1,0:T(1,128)S(1)}, f32[2,1,2176]{2,1,0:T(1,128)S(1)}, u32[]{:S(2)}, u32[]{:S(2)}) collective-permute-start(f32[2,1,2176]{2,1,0:T(1,128)S(1)} %get-tuple-element.30), channel_id=1, source_target_pairs={{1,0},{2,1},{3,2},{16,3},{17,16},{18,17},{19,18},{5,4},{6,5},{7,6}... | collective-permute-start | bytes 52232 | tf_op jit(solution)/shard_map/ppermute | solution.py:29
  19.5 4.0 %collective-permute-start.1 = (s32[320,22]{0,1:T(8,128)S(1)}, s32[320,22]{0,1:T(8,128)S(1)}, u32[]{:S(2)}, u32[]{:S(2)}) collective-permute-start(s32[320,22]{0,1:T(8,128)S(1)} %add_select_fusion.7), channel_id=1, source_target_pairs={{0,8},{4,12},{8,0},{12,4},{1,9},{5,13},{9,1},{13,5},{2,10},{6,14},... | collective-permute-start | bytes 84488 | tf_op jit(solution)/shard_map/ppermute | solution.py:62
  24.5 42.4 %copy-start.5 = (s32[16,17]{1,0:T(8,128)S(1)}, s32[16,17]{1,0:T(8,128)}, u32[]{:S(2)}) copy-start(s32[16,17]{1,0:T(8,128)} %param.17) | copy-start | bytes 3268
  61.1 14.7 %collective-permute-start.7 = (f32[272,256]{1,0:T(8,128)S(1)}, f32[272,256]{1,0:T(8,128)S(1)}, u32[]{:S(2)}, u32[]{:S(2)}) collective-permute-start(f32[272,256]{1,0:T(8,128)S(1)} %get-tuple-element.23), channel_id=1, source_target_pairs={{1,0},{2,1},{3,2},{16,3},{17,16},{18,17},{19,18},{5,4},{6,5},{7,6}... | collective-permute-start | bytes 835592 | tf_op jit(solution)/shard_map/ppermute | solution.py:235
  63.9 11.9 %collective-permute-start.6 = (f32[272,256]{1,0:T(8,128)S(1)}, f32[272,256]{1,0:T(8,128)S(1)}, u32[]{:S(2)}, u32[]{:S(2)}) collective-permute-start(f32[272,256]{1,0:T(8,128)S(1)} %get-tuple-element.22), channel_id=1, source_target_pairs={{0,1},{1,2},{2,3},{3,16},{16,17},{17,18},{18,19},{4,5},{5,6},{6,7}... | collective-permute-start | bytes 835592 | tf_op jit(solution)/shard_map/ppermute | solution.py:232
  69.4 10.7 %copy-start = (f32[16,2176]{1,0:T(8,128)S(1)}, f32[16,2176]{1,0:T(8,128)}, u32[]{:S(2)}) copy-start(f32[16,2176]{1,0:T(8,128)} %param.15) | copy-start | bytes 417796
  69.4 10.7 %copy-start.1 = (f32[16,2176]{1,0:T(8,128)S(1)}, f32[16,2176]{1,0:T(8,128)}, u32[]{:S(2)}) copy-start(f32[16,2176]{1,0:T(8,128)} %param.16) | copy-start | bytes 417796
  70.5 19.1 %all-to-all-start = ((bf16[32,24,320]{2,1,0:T(8,128)(2,1)}), bf16[32,24,320]{2,1,0:T(8,128)(2,1)S(1)}, u32[]{:S(2)}, u32[]{:S(2)}) async-start(bf16[32,24,320]{2,1,0:T(8,128)(2,1)} %copy.42), calls=%async_computation | async-start | bytes 1179648 | tf_op jit(solution)/shard_map/all_to_all | solution.py:218
  76.9 1.6 %collective-permute-start.8 = (f32[272,256]{1,0:T(8,128)S(1)}, f32[272,256]{1,0:T(8,128)S(1)}, u32[]{:S(2)}, u32[]{:S(2)}) collective-permute-start(f32[272,256]{1,0:T(8,128)S(1)} %fusion.22), channel_id=1, source_target_pairs={{0,4},{4,0},{8,12},{12,8},{1,5},{5,1},{9,13},{13,9},{2,6},{6,2},{1... | collective-permute-start | bytes 835592 | tf_op jit(solution)/shard_map/ppermute | solution.py:50
  78.5 8.8 %collective-permute-start.9 = (f32[272,256]{1,0:T(8,128)S(1)}, f32[272,256]{1,0:T(8,128)S(1)}, u32[]{:S(2)}, u32[]{:S(2)}) collective-permute-start(f32[272,256]{1,0:T(8,128)S(1)} %add.177), channel_id=1, source_target_pairs={{0,8},{4,12},{8,0},{12,4},{1,9},{5,13},{9,1},{13,5},{2,10},{6,14},... | collective-permute-start | bytes 835592 | tf_op jit(solution)/shard_map/ppermute | solution.py:50
  90.1 1.9 %collective-permute-start.2 = (bf16[4,24,2560]{2,1,0:T(8,128)(2,1)S(1)}, bf16[4,24,2560]{2,1,0:T(8,128)(2,1)S(1)}, u32[]{:S(2)}, u32[]{:S(2)}) collective-permute-start(bf16[4,24,2560]{2,1,0:T(8,128)(2,1)S(1)} %all_to_all.16), channel_id=1, source_target_pairs={{0,4},{4,0},{8,12},{12,8},{1,5},{5,1},{9,13},{13,9},{2,6},{6,2},{1... | collective-permute-start | bytes 1474568 | tf_op jit(solution)/shard_map/ppermute | solution.py:62
  92.2 29.5 %collective-permute-start.3 = (bf16[4,48,2560]{2,1,0:T(8,128)(2,1)S(1)}, bf16[4,48,2560]{2,1,0:T(8,128)(2,1)}, u32[]{:S(2)}, u32[]{:S(2)}) collective-permute-start(bf16[4,48,2560]{2,1,0:T(8,128)(2,1)S(1)} %maximum_select_fusion.2), channel_id=1, source_target_pairs={{0,8},{4,12},{8,0},{12,4},{1,9},{5,13},{9,1},{13,5},{2,10},{6,14},... | collective-permute-start | bytes 2949128 | tf_op jit(solution)/shard_map/ppermute | solution.py:62
  94.5 20.4 %copy-start.2 = (f32[16,2176]{1,0:T(8,128)}, f32[16,2176]{1,0:T(8,128)S(1)}, u32[]{:S(2)}) copy-start(f32[16,2176]{1,0:T(8,128)S(1)} %get-tuple-element.25) | copy-start | bytes 417796
  94.5 7.3 %collective-permute-start.11 = (f32[16,2176]{1,0:T(8,128)S(1)}, f32[16,2176]{1,0:T(8,128)S(1)}, u32[]{:S(2)}, u32[]{:S(2)}) collective-permute-start(f32[16,2176]{1,0:T(8,128)S(1)} %get-tuple-element.25), channel_id=1, source_target_pairs={{1,0},{2,1},{3,2},{16,3},{17,16},{18,17},{19,18},{5,4},{6,5},{7,6}... | collective-permute-start | bytes 417800 | tf_op jit(solution)/shard_map/ppermute | solution.py:29
  97.7 9.7 %collective-permute-start.10 = (f32[16,2176]{1,0:T(8,128)S(1)}, f32[16,2176]{1,0:T(8,128)S(1)}, u32[]{:S(2)}, u32[]{:S(2)}) collective-permute-start(f32[16,2176]{1,0:T(8,128)S(1)} %get-tuple-element.25), channel_id=1, source_target_pairs={{0,1},{1,2},{2,3},{3,16},{16,17},{17,18},{18,19},{4,5},{5,6},{6,7}... | collective-permute-start | bytes 417800 | tf_op jit(solution)/shard_map/ppermute | solution.py:27

commit v7 on v6

--- a/solution.py
+++ b/solution.py
@@ -178,6 +178,43 @@
     )(lat_points[:, None], atmos_fields, table, column_weight.astype(jnp.float32), slot_rows)
 
 
+def surface_kernel(slot_ref, base_ref, limit_ref, tiles_ref, out_ref):
+    lat_band, quarter = out_ref.shape
+    nquarter = quarter // BLOCK
+    group = 8
+    sublane = lax.broadcasted_iota(jnp.int32, (group, BLOCK), 0)
+
+    def per_group(g, carry):
+        row0 = pl.multiple_of(g * group, group)
+        for b in range(nquarter):
+            rows = jnp.zeros((group, BLOCK), jnp.float32)
+            for r in range(group):
+                tile = slot_ref[(row0 + r) * nquarter + b]
+                picked = jnp.broadcast_to(tiles_ref[pl.ds(tile, 1), :], (group, BLOCK))
+                rows = jnp.where(sublane == r, picked, rows)
+            out_ref[pl.ds(row0, group), b * BLOCK : (b + 1) * BLOCK] = rows
+        return carry
+
+    lax.fori_loop(0, lat_band // group, per_group, 0)
+    points = base_ref[0] + lax.broadcasted_iota(jnp.int32, (lat_band, quarter), 1)
+    out_ref[...] = jnp.where(points < limit_ref[...], out_ref[...], 0.0)
+
+
+def surface_gather(slots, base, lat_points, tiles, quarter):
+    lat_band = lat_points.shape[0]
+    return pl.pallas_call(
+        surface_kernel,
+        in_specs=[
+            pl.BlockSpec(memory_space=pltpu.SMEM),
+            pl.BlockSpec(memory_space=pltpu.SMEM),
+            pl.BlockSpec(memory_space=pltpu.VMEM),
+            pl.BlockSpec(memory_space=pltpu.VMEM),
+        ],
+        out_specs=pl.BlockSpec(memory_space=pltpu.VMEM),
+        out_shape=jax.ShapeDtypeStruct((lat_band, quarter), jnp.float32),
+    )(slots, base, lat_points[:, None], tiles)
+
+
 def body(
     atmos_fields,
     lat_points,
@@ -206,7 +243,7 @@
     def slot_of(targets):
         return (targets // tile_count - band_index + 1) * tile_count + targets % tile_count
 
-    local_slot = slot_of(block_remap.T.reshape(-1))
+    local_slot = slot_of(block_remap.reshape(-1))
     quarter = lon_count // lax.axis_size("lev")
     full_remap = lev_gather(block_remap, 1)
     every_slot = slot_of(full_remap)
@@ -261,17 +298,8 @@
     salt_next = updated[1]
     returned = with_halo(temp_next, ((("lat", "ocn"), 0),), ocean_rows)
     tiles_near = returned.reshape(3 * tile_count, BLOCK)
-    nquarter = quarter // BLOCK
-    gathered = jnp.take(tiles_near, local_slot, axis=0).reshape(nquarter, lat_band, BLOCK)
-    own_points = (
-        lax.axis_index("lev") * quarter
-        + lax.broadcasted_iota(jnp.int32, (nquarter, 1, BLOCK), 0) * BLOCK
-        + lax.broadcasted_iota(jnp.int32, (nquarter, 1, BLOCK), 2)
-    )
-    kept = jnp.where(
-        own_points < lat_points[None, :, None], gathered, jnp.zeros((), jnp.float32)
-    )
-    surface_temp = kept.transpose(1, 0, 2).reshape(lat_band, quarter)
+    base = (lax.axis_index("lev") * quarter).astype(jnp.int32).reshape(1)
+    surface_temp = surface_gather(local_slot, base, lat_points, tiles_near, quarter)
     return (spectra, temp_next, salt_next, surface_temp)
 
 

time: 128 us -> 124 us (0.969)
  the two profiles are of different devices: /device:TPU:4 before, /device:TPU:0 now
where the time goes in v7:
time: 124 us; the launch traced here: 123 us
  Pallas kernels  41.1 us (33%)
  starting transfers between devices  31.4 us (25%)
  waiting for transfers between devices  23.6 us (19%)
  other arithmetic  11.1 us (9%)
  local copies, waits for them, and re-layouts  9.56 us (8%)
  matrix products  5.5 us (4%)
    pallas_call x1, Pallas kernels, fused_transform(): pl.pallas_call(transform_kernel, grid=(steps,), in_specs=[pl.BlockSpec((r...  35.5 us
    ppermute x4, waiting for transfers between devices, lev_gather(): other = lax.ppermute(values, 'lev', [(i, i ^ stride) for i in range(count)])  10.8 us
    ppermute x2, starting transfers between devices, with_halo(): lax.ppermute(tail, axis, [(i, (i + 1) % count) for i in range(ends)])  9.05 us
    all_to_all x1, starting transfers between devices, body(): lax.all_to_all(coeffs.transpose(4, 1, 0, 3, 2).reshape(wave_count, lev_de...  8 us
    ppermute x2, waiting for transfers between devices, lev_sum(): lax.ppermute(values, 'lev', [(i, i ^ stride) for i in range(count)])  7.41 us
    pallas_call x1, Pallas kernels, surface_gather(): pl.pallas_call(surface_kernel, in_specs=[pl.BlockSpec(memory_space=pltpu....  5.56 us
    dot_general x1, matrix products, body(): jnp.einsum('srj,sjd->srd', lev_gather(regrouped, 1), legendre, preferred_...  5.5 us
    ppermute x1, starting transfers between devices, body(): lax.ppermute(sections[2], ('lat', 'ocn'), [(i, i + 1) for i in range(band...  5.19 us
  transfers between devices with their start and end apart: 13, of which 8 were waited for; matrix products, arithmetic and copies ran while one was open for 16% of the time, Pallas kernels for 33%

profile of v7, /device:TPU:0, one launch (start us, length us, event | category | flops | bytes accessed | tf_op | source)
XLA Modules:
  0.0 123.3 jit_solution(17664854923993804114)
XLA Ops:
  1.2 1.0 fusion.29
  2.2 4.5 %collective-permute-start.5 = (f32[2,1,2176]{2,1,0:T(1,128)S(1)}, f32[2,1,2176]{2,1,0:T(1,128)S(1)}, u32[]{:S(2)}, u32[]{:S(2)}) collective-permute-start(f32[2,1,2176]{2,1,0:T(1,128)S(1)} %get-tuple-element.17), channel_id=1, source_target_pairs={{0,1},{1,2},{2,3},{3,16},{16,17},{17,18},{18,19},{4,5},{5,6},{6,7}... | collective-permute-start | bytes 52232 | tf_op jit(solution)/shard_map/ppermute | solution.py:27
  6.7 1.3 %collective-permute-start.4 = (f32[2,1,2176]{2,1,0:T(1,128)S(1)}, f32[2,1,2176]{2,1,0:T(1,128)S(1)}, u32[]{:S(2)}, u32[]{:S(2)}) collective-permute-start(f32[2,1,2176]{2,1,0:T(1,128)S(1)} %get-tuple-element.16), channel_id=1, source_target_pairs={{1,0},{2,1},{3,2},{16,3},{17,16},{18,17},{19,18},{5,4},{6,5},{7,6}... | collective-permute-start | bytes 52232 | tf_op jit(solution)/shard_map/ppermute | solution.py:29
  8.0 1.2 %fusion.14 = (f32[2,16,2175]{2,1,0:T(8,128)S(1)}, f32[2,16,2175]{2,1,0:T(8,128)S(1)}) fusion(f32[1,16,2176]{2,1,0:T(8,128)} %bitcast.44, f32[1,16,2176]{2,1,0:T(8,128)} %bitcast.48), kind=kLoop, calls=%fused_computation.37 | loop fusion | flops 139200 | bytes 835328 | tf_op jit(solution)/shard_map/stack | solution.py:287
  9.3 4.0 %cosine_convert_fusion = (bf16[32,5632]{1,0:T(8,128)(2,1)S(1)}, bf16[32,5632]{1,0:T(8,128)(2,1)S(1)}) fusion(s32[32]{0:T(128)} %param.11), kind=kLoop, calls=%fused_computation.15 | loop fusion | flops 2162688 | bytes 721024 | tf_op jit(solution)/shard_map/convert
  14.0 0.9 pad_maximum_fusion.table_ref
  14.9 0.8 broadcast_in_dim.20.points_ref.limit_ref
  16.4 1.6 %collective-permute-start.1 = (s32[320,22]{0,1:T(8,128)S(1)}, s32[320,22]{0,1:T(8,128)S(1)}, u32[]{:S(2)}, u32[]{:S(2)}) collective-permute-start(s32[320,22]{0,1:T(8,128)S(1)} %add_select_fusion.5), channel_id=1, source_target_pairs={{0,8},{4,12},{8,0},{12,4},{1,9},{5,13},{9,1},{13,5},{2,10},{6,14},... | collective-permute-start | bytes 84488 | tf_op jit(solution)/shard_map/ppermute | solution.py:62
  18.0 2.4 %collective-permute-done.1 = s32[320,22]{0,1:T(8,128)S(1)} collective-permute-done((s32[320,22]{0,1:T(8,128)S(1)}, s32[320,22]{0,1:T(8,128)S(1)}, u32[]{:S(2)}, u32[]{:S(2)}) %collective-permute-start.1) | collective-permute-done | bytes 28192 | tf_op jit(solution)/shard_map/ppermute | solution.py:62
  20.7 0.7 reshape.98.slot_ref
  21.4 35.5 %shard_map.120 = (f32[2,6,320,64]{3,2,1,0:T(8,128)}, f32[3,272,256]{2,1,0:T(8,128)}) custom-call(s32[320,1]{1,0:T(8,128)} %broadcast_in_dim.20.points_ref.limit_ref, bf16[2,6,320,5632]{3,2,1,0:T(8,128)(2,1)} %cells_ref.1, bf16[64,5632]{1,0:T(8,128)(2,1)} %pad_maximum_fusion.table_ref, f32[2,6]{1,0:T(2,128)} %convert_element_type.23.weight_ref, ...), custom_call_target="tpu_custom_call" | custom-call | tf_op jit(solution)/shard_map/pallas_call | solution.py:158
  57.0 1.1 slice_bitcast_fusion.1
  58.0 1.3 %collective-permute-start.7 = (f32[272,256]{1,0:T(8,128)S(1)}, f32[272,256]{1,0:T(8,128)S(1)}, u32[]{:S(2)}, u32[]{:S(2)}) collective-permute-start(f32[272,256]{1,0:T(8,128)S(1)} %get-tuple-element.9), channel_id=1, source_target_pairs={{1,0},{2,1},{3,2},{16,3},{17,16},{18,17},{19,18},{5,4},{6,5},{7,6}... | collective-permute-start | bytes 835592 | tf_op jit(solution)/shard_map/ppermute | solution.py:272
  59.3 5.2 %collective-permute-start.6 = (f32[272,256]{1,0:T(8,128)S(1)}, f32[272,256]{1,0:T(8,128)S(1)}, u32[]{:S(2)}, u32[]{:S(2)}) collective-permute-start(f32[272,256]{1,0:T(8,128)S(1)} %get-tuple-element.8), channel_id=1, source_target_pairs={{0,1},{1,2},{2,3},{3,16},{16,17},{17,18},{18,19},{4,5},{5,6},{6,7}... | collective-permute-start | bytes 835592 | tf_op jit(solution)/shard_map/ppermute | solution.py:269
  64.6 2.2 %copy.43 = f32[2,6,320,64]{2,3,1,0:T(8,128)S(1)} copy(f32[2,6,320,64]{3,2,1,0:T(8,128)} %get-tuple-element.6) | data formatting | bytes 1966080 | tf_op jit(solution)/shard_map/pallas_call | solution.py:158
  67.1 1.0 copy.45
  68.1 8.0 %all-to-all-start = ((bf16[32,24,320]{2,1,0:T(8,128)(2,1)}), bf16[32,24,320]{2,1,0:T(8,128)(2,1)S(1)}, u32[]{:S(2)}, u32[]{:S(2)}) async-start(bf16[32,24,320]{2,1,0:T(8,128)(2,1)} %copy.45), calls=%async_computation | async-start | bytes 1179648 | tf_op jit(solution)/shard_map/all_to_all | solution.py:255
  76.1 1.0 fusion.22
  77.2 1.5 %collective-permute-done.8 = f32[272,256]{1,0:T(8,128)S(1)} collective-permute-done((f32[272,256]{1,0:T(8,128)S(1)}, f32[272,256]{1,0:T(8,128)S(1)}, u32[]{:S(2)}, u32[]{:S(2)}) %collective-permute-start.8) | collective-permute-done | bytes 278560 | tf_op jit(solution)/shard_map/ppermute | solution.py:50
  78.8 1.6 %collective-permute-start.9 = (f32[272,256]{1,0:T(8,128)S(1)}, f32[272,256]{1,0:T(8,128)S(1)}, u32[]{:S(2)}, u32[]{:S(2)}) collective-permute-start(f32[272,256]{1,0:T(8,128)S(1)} %add.92), channel_id=1, source_target_pairs={{0,8},{4,12},{8,0},{12,4},{1,9},{5,13},{9,1},{13,5},{2,10},{6,14},... | collective-permute-start | bytes 835592 | tf_op jit(solution)/shard_map/ppermute | solution.py:50
  81.6 5.9 %collective-permute-done.9 = f32[272,256]{1,0:T(8,128)S(1)} collective-permute-done((f32[272,256]{1,0:T(8,128)S(1)}, f32[272,256]{1,0:T(8,128)S(1)}, u32[]{:S(2)}, u32[]{:S(2)}) %collective-permute-start.9) | collective-permute-done | bytes 278560 | tf_op jit(solution)/shard_map/ppermute | solution.py:50
  87.8 3.4 %all-to-all-done = bf16[32,24,320]{2,1,0:T(8,128)(2,1)S(1)} async-done(((bf16[32,24,320]{2,1,0:T(8,128)(2,1)}), bf16[32,24,320]{2,1,0:T(8,128)(2,1)S(1)}, u32[]{:S(2)}, u32[]{:S(2)}) %all-to-all-start) | async-done | bytes 491552 | tf_op jit(solution)/shard_map/all_to_all | solution.py:255
  92.1 1.6 %collective-permute-done.2 = bf16[4,24,2560]{2,1,0:T(8,128)(2,1)S(1)} collective-permute-done((bf16[4,24,2560]{2,1,0:T(8,128)(2,1)S(1)}, bf16[4,24,2560]{2,1,0:T(8,128)(2,1)S(1)}, u32[]{:S(2)}, u32[]{:S(2)}) %collective-permute-start.2) | collective-permute-done | bytes 491552 | tf_op jit(solution)/shard_map/ppermute | solution.py:62
  93.9 1.6 %collective-permute-start.3 = (bf16[4,48,2560]{2,1,0:T(8,128)(2,1)S(1)}, bf16[4,48,2560]{2,1,0:T(8,128)(2,1)S(1)}, u32[]{:S(2)}, u32[]{:S(2)}) collective-permute-start(bf16[4,48,2560]{2,1,0:T(8,128)(2,1)S(1)} %maximum_select_fusion.2), channel_id=1, source_target_pairs={{0,8},{4,12},{8,0},{12,4},{1,9},{5,13},{9,1},{13,5},{2,10},{6,14},... | collective-permute-start | bytes 2949128 | tf_op jit(solution)/shard_map/ppermute | solution.py:62
  96.2 1.3 %collective-permute-start.11 = (f32[16,2176]{1,0:T(8,128)S(1)}, f32[16,2176]{1,0:T(8,128)S(1)}, u32[]{:S(2)}, u32[]{:S(2)}) collective-permute-start(f32[16,2176]{1,0:T(8,128)S(1)} %get-tuple-element.11), channel_id=1, source_target_pairs={{1,0},{2,1},{3,2},{16,3},{17,16},{18,17},{19,18},{5,4},{6,5},{7,6}... | collective-permute-start | bytes 417800 | tf_op jit(solution)/shard_map/ppermute | solution.py:29
  97.4 4.6 %collective-permute-start.10 = (f32[16,2176]{1,0:T(8,128)S(1)}, f32[16,2176]{1,0:T(8,128)S(1)}, u32[]{:S(2)}, u32[]{:S(2)}) collective-permute-start(f32[16,2176]{1,0:T(8,128)S(1)} %get-tuple-element.11), channel_id=1, source_target_pairs={{0,1},{1,2},{2,3},{3,16},{16,17},{17,18},{18,19},{4,5},{5,6},{6,7}... | collective-permute-start | bytes 417800 | tf_op jit(solution)/shard_map/ppermute | solution.py:27
  102.6 0.9 collective-permute-done.11
  103.5 1.2 collective-permute-done.10
  104.7 0.8 reshape.104.tiles_ref
  105.5 5.6 %shard_map.121 = f32[320,1408]{1,0:T(8,128)} custom-call(s32[3520]{0:T(1024)} %fusion.36.slot_ref, s32[1]{0:T(128)} %bitcast.14.base_ref, s32[320,1]{1,0:T(8,128)} %broadcast_in_dim.20.points_ref.limit_ref, f32[816,128]{1,0:T(8,128)} %reshape.104.tiles_ref), custom_call_target="tpu_custom_call" | custom-call | tf_op jit(solution)/shard_map/pallas_call | solution.py:205
  111.0 6.8 %collective-permute-done.3 = bf16[4,48,2560]{2,1,0:T(8,128)(2,1)S(1)} collective-permute-done((bf16[4,48,2560]{2,1,0:T(8,128)(2,1)S(1)}, bf16[4,48,2560]{2,1,0:T(8,128)(2,1)S(1)}, u32[]{:S(2)}, u32[]{:S(2)}) %collective-permute-start.3) | collective-permute-done | bytes 983072 | tf_op jit(solution)/shard_map/ppermute | solution.py:62
  117.8 5.5 %fusion = f32[4,96,384]{2,1,0:T(8,128)} fusion(bf16[4,2560,384]{2,1,0:T(8,128)(2,1)} %param.12, bf16[4,48,2560]{2,1,0:T(8,128)(2,1)S(1)} %maximum_select_fusion.2, bf16[4,48,2560]{2,1,0:T(8,128)(2,1)S(1)} %collective-permute-done.3, pred[]{:T(512)S(6)} %eq.19), kind=kOutput, calls=%fused_computation.1 | convolution fusion | flops 763822080 | bytes 10420225 | tf_op jit(solution)/shard_map/srj,sjd->srd/dot_general | solution.py:262
  (61 shorter events, 6.5 us)
Async XLA Ops:
  0.6 15.1 %copy-start.3 = (s32[320,11]{0,1:T(8,128)S(1)}, s32[320,11]{0,1:T(8,128)}, u32[]{:S(2)}) copy-start(s32[320,11]{0,1:T(8,128)} %param.14) | copy-start | bytes 42244
  0.6 14.3 %copy-start.6 = (s32[32]{0:T(128)S(1)}, s32[32]{0:T(128)}, u32[]{:S(2)}) copy-start(s32[32]{0:T(128)} %param.11) | copy-start | bytes 388
  0.7 14.3 %copy-start.4 = (s32[320]{0:T(512)S(1)}, s32[320]{0:T(512)}, u32[]{:S(2)}) copy-start(s32[320]{0:T(512)} %param.10) | copy-start | bytes 3844
  0.7 15.1 %copy-start.7 = (bf16[2,6]{1,0:T(2,128)(2,1)S(1)}, bf16[2,6]{1,0:T(2,128)(2,1)}, u32[]{:S(2)}) copy-start(bf16[2,6]{1,0:T(2,128)(2,1)} %param.13) | copy-start | bytes 76
  0.7 15.7 %collective-permute-start = (s32[320,11]{0,1:T(8,128)}, s32[320,11]{0,1:T(8,128)S(1)}, u32[]{:S(2)}, u32[]{:S(2)}) collective-permute-start(s32[320,11]{0,1:T(8,128)} %param.14), channel_id=1, source_target_pairs={{0,4},{4,0},{8,12},{12,8},{1,5},{5,1},{9,13},{13,9},{2,6},{6,2},{1... | collective-permute-start | bytes 42248 | tf_op jit(solution)/shard_map/ppermute | solution.py:62
  2.2 89.7 %collective-permute-start.5 = (f32[2,1,2176]{2,1,0:T(1,128)S(1)}, f32[2,1,2176]{2,1,0:T(1,128)S(1)}, u32[]{:S(2)}, u32[]{:S(2)}) collective-permute-start(f32[2,1,2176]{2,1,0:T(1,128)S(1)} %get-tuple-element.17), channel_id=1, source_target_pairs={{0,1},{1,2},{2,3},{3,16},{16,17},{17,18},{18,19},{4,5},{5,6},{6,7}... | collective-permute-start | bytes 52232 | tf_op jit(solution)/shard_map/ppermute | solution.py:27
  6.7 85.2 %collective-permute-start.4 = (f32[2,1,2176]{2,1,0:T(1,128)S(1)}, f32[2,1,2176]{2,1,0:T(1,128)S(1)}, u32[]{:S(2)}, u32[]{:S(2)}) collective-permute-start(f32[2,1,2176]{2,1,0:T(1,128)S(1)} %get-tuple-element.16), channel_id=1, source_target_pairs={{1,0},{2,1},{3,2},{16,3},{17,16},{18,17},{19,18},{5,4},{6,5},{7,6}... | collective-permute-start | bytes 52232 | tf_op jit(solution)/shard_map/ppermute | solution.py:29
  16.4 4.0 %collective-permute-start.1 = (s32[320,22]{0,1:T(8,128)S(1)}, s32[320,22]{0,1:T(8,128)S(1)}, u32[]{:S(2)}, u32[]{:S(2)}) collective-permute-start(s32[320,22]{0,1:T(8,128)S(1)} %add_select_fusion.5), channel_id=1, source_target_pairs={{0,8},{4,12},{8,0},{12,4},{1,9},{5,13},{9,1},{13,5},{2,10},{6,14},... | collective-permute-start | bytes 84488 | tf_op jit(solution)/shard_map/ppermute | solution.py:62
  58.0 18.0 %collective-permute-start.7 = (f32[272,256]{1,0:T(8,128)S(1)}, f32[272,256]{1,0:T(8,128)S(1)}, u32[]{:S(2)}, u32[]{:S(2)}) collective-permute-start(f32[272,256]{1,0:T(8,128)S(1)} %get-tuple-element.9), channel_id=1, source_target_pairs={{1,0},{2,1},{3,2},{16,3},{17,16},{18,17},{19,18},{5,4},{6,5},{7,6}... | collective-permute-start | bytes 835592 | tf_op jit(solution)/shard_map/ppermute | solution.py:272
  59.3 16.7 %collective-permute-start.6 = (f32[272,256]{1,0:T(8,128)S(1)}, f32[272,256]{1,0:T(8,128)S(1)}, u32[]{:S(2)}, u32[]{:S(2)}) collective-permute-start(f32[272,256]{1,0:T(8,128)S(1)} %get-tuple-element.8), channel_id=1, source_target_pairs={{0,1},{1,2},{2,3},{3,16},{16,17},{17,18},{18,19},{4,5},{5,6},{6,7}... | collective-permute-start | bytes 835592 | tf_op jit(solution)/shard_map/ppermute | solution.py:269
  67.0 13.3 %copy-start.5 = (s32[16,17]{1,0:T(8,128)S(1)}, s32[16,17]{1,0:T(8,128)}, u32[]{:S(2)}) copy-start(s32[16,17]{1,0:T(8,128)} %param.17) | copy-start | bytes 3268
  67.0 13.3 %copy-start = (f32[16,2176]{1,0:T(8,128)S(1)}, f32[16,2176]{1,0:T(8,128)}, u32[]{:S(2)}) copy-start(f32[16,2176]{1,0:T(8,128)} %param.15) | copy-start | bytes 417796
  67.0 13.3 %copy-start.1 = (f32[16,2176]{1,0:T(8,128)S(1)}, f32[16,2176]{1,0:T(8,128)}, u32[]{:S(2)}) copy-start(f32[16,2176]{1,0:T(8,128)} %param.16) | copy-start | bytes 417796
  68.1 23.2 %all-to-all-start = ((bf16[32,24,320]{2,1,0:T(8,128)(2,1)}), bf16[32,24,320]{2,1,0:T(8,128)(2,1)S(1)}, u32[]{:S(2)}, u32[]{:S(2)}) async-start(bf16[32,24,320]{2,1,0:T(8,128)(2,1)} %copy.45), calls=%async_computation | async-start | bytes 1179648 | tf_op jit(solution)/shard_map/all_to_all | solution.py:255
  77.1 1.6 %collective-permute-start.8 = (f32[272,256]{1,0:T(8,128)S(1)}, f32[272,256]{1,0:T(8,128)S(1)}, u32[]{:S(2)}, u32[]{:S(2)}) collective-permute-start(f32[272,256]{1,0:T(8,128)S(1)} %fusion.22), channel_id=1, source_target_pairs={{0,4},{4,0},{8,12},{12,8},{1,5},{5,1},{9,13},{13,9},{2,6},{6,2},{1... | collective-permute-start | bytes 835592 | tf_op jit(solution)/shard_map/ppermute | solution.py:50
  78.8 8.8 %collective-permute-start.9 = (f32[272,256]{1,0:T(8,128)S(1)}, f32[272,256]{1,0:T(8,128)S(1)}, u32[]{:S(2)}, u32[]{:S(2)}) collective-permute-start(f32[272,256]{1,0:T(8,128)S(1)} %add.92), channel_id=1, source_target_pairs={{0,8},{4,12},{8,0},{12,4},{1,9},{5,13},{9,1},{13,5},{2,10},{6,14},... | collective-permute-start | bytes 835592 | tf_op jit(solution)/shard_map/ppermute | solution.py:50
  91.8 1.9 %collective-permute-start.2 = (bf16[4,24,2560]{2,1,0:T(8,128)(2,1)S(1)}, bf16[4,24,2560]{2,1,0:T(8,128)(2,1)S(1)}, u32[]{:S(2)}, u32[]{:S(2)}) collective-permute-start(bf16[4,24,2560]{2,1,0:T(8,128)(2,1)S(1)} %all_to_all.16), channel_id=1, source_target_pairs={{0,4},{4,0},{8,12},{12,8},{1,5},{5,1},{9,13},{13,9},{2,6},{6,2},{1... | collective-permute-start | bytes 1474568 | tf_op jit(solution)/shard_map/ppermute | solution.py:62
  93.9 23.9 %collective-permute-start.3 = (bf16[4,48,2560]{2,1,0:T(8,128)(2,1)S(1)}, bf16[4,48,2560]{2,1,0:T(8,128)(2,1)S(1)}, u32[]{:S(2)}, u32[]{:S(2)}) collective-permute-start(bf16[4,48,2560]{2,1,0:T(8,128)(2,1)S(1)} %maximum_select_fusion.2), channel_id=1, source_target_pairs={{0,8},{4,12},{8,0},{12,4},{1,9},{5,13},{9,1},{13,5},{2,10},{6,14},... | collective-permute-start | bytes 2949128 | tf_op jit(solution)/shard_map/ppermute | solution.py:62
  96.1 14.9 %copy-start.2 = (f32[16,2176]{1,0:T(8,128)}, f32[16,2176]{1,0:T(8,128)S(1)}, u32[]{:S(2)}) copy-start(f32[16,2176]{1,0:T(8,128)S(1)} %get-tuple-element.11) | copy-start | bytes 417796
  96.2 7.3 %collective-permute-start.11 = (f32[16,2176]{1,0:T(8,128)S(1)}, f32[16,2176]{1,0:T(8,128)S(1)}, u32[]{:S(2)}, u32[]{:S(2)}) collective-permute-start(f32[16,2176]{1,0:T(8,128)S(1)} %get-tuple-element.11), channel_id=1, source_target_pairs={{1,0},{2,1},{3,2},{16,3},{17,16},{18,17},{19,18},{5,4},{6,5},{7,6}... | collective-permute-start | bytes 417800 | tf_op jit(solution)/shard_map/ppermute | solution.py:29
  97.4 7.2 %collective-permute-start.10 = (f32[16,2176]{1,0:T(8,128)S(1)}, f32[16,2176]{1,0:T(8,128)S(1)}, u32[]{:S(2)}, u32[]{:S(2)}) collective-permute-start(f32[16,2176]{1,0:T(8,128)S(1)} %get-tuple-element.11), channel_id=1, source_target_pairs={{0,1},{1,2},{2,3},{3,16},{16,17},{17,18},{18,19},{4,5},{5,6},{6,7}... | collective-permute-start | bytes 417800 | tf_op jit(solution)/shard_map/ppermute | solution.py:27

commit v8 on v7

--- a/solution.py
+++ b/solution.py
@@ -68,6 +68,36 @@
         )
         stride *= 2
     return values
+
+
+def spectra_of(regrouped, legendre):
+    count = lax.axis_size("lev")
+    if count != 4:
+        return jnp.einsum(
+            "srj,sjd->srd",
+            lev_gather(regrouped, 1),
+            legendre,
+            preferred_element_type=jnp.float32,
+        )
+    index = lax.axis_index("lev")
+    rows = regrouped.shape[1]
+    other = lax.ppermute(regrouped, "lev", [(i, i ^ 2) for i in range(count)])
+    pair = jnp.where(
+        (index // 2) % 2 == 1,
+        jnp.concatenate([other, regrouped], axis=1),
+        jnp.concatenate([regrouped, other], axis=1),
+    )
+    far = lax.ppermute(pair, "lev", [(i, i ^ 1) for i in range(count)])
+    near_part = jnp.einsum("srj,sjd->srd", pair, legendre, preferred_element_type=jnp.float32)
+    far_part = jnp.einsum("srj,sjd->srd", far, legendre, preferred_element_type=jnp.float32)
+    even = index % 2 == 0
+    blocks = []
+    for half in range(2):
+        mine = near_part[:, half * rows : (half + 1) * rows]
+        theirs = far_part[:, half * rows : (half + 1) * rows]
+        blocks.append(jnp.where(even, mine, theirs))
+        blocks.append(jnp.where(even, theirs, mine))
+    return jnp.concatenate(blocks, axis=1)
 
 
 def row_block(rows):
@@ -259,12 +289,7 @@
         concat_axis=2,
         tiled=True,
     )
-    spectra = jnp.einsum(
-        "srj,sjd->srd",
-        lev_gather(regrouped, 1),
-        legendre,
-        preferred_element_type=jnp.float32,
-    )
+    spectra = spectra_of(regrouped, legendre)
     band_count = lax.axis_size(("lat", "ocn"))
     from_prev = lax.ppermute(
         sections[2], ("lat", "ocn"), [(i, i + 1) for i in range(band_count - 1)]

time: 124 us -> 135 us (1.089)
  the two profiles are of different devices: /device:TPU:0 before, /device:TPU:1 now
where the time goes in v8:
time: 135 us
  Pallas kernels  41 us (30%)
  starting transfers between devices  38.2 us (28%)
  waiting for transfers between devices  21.6 us (16%)
  other arithmetic  15.7 us (12%)
  matrix products  8.96 us (7%)
  local copies, waits for them, and re-layouts  8.16 us (6%)
    pallas_call x1, Pallas kernels, fused_transform(): pl.pallas_call(transform_kernel, grid=(steps,), in_specs=[pl.BlockSpec((r...  35.5 us
    all_to_all x1, starting transfers between devices, body(): lax.all_to_all(coeffs.transpose(4, 1, 0, 3, 2).reshape(wave_count, lev_de...  12.2 us
    ppermute x2, starting transfers between devices, with_halo(): lax.ppermute(tail, axis, [(i, (i + 1) % count) for i in range(ends)])  8.81 us
    all_to_all x1, waiting for transfers between devices, body(): lax.all_to_all(coeffs.transpose(4, 1, 0, 3, 2).reshape(wave_count, lev_de...  6.29 us
    pallas_call x1, Pallas kernels, surface_gather(): pl.pallas_call(surface_kernel, in_specs=[pl.BlockSpec(memory_space=pltpu....  5.56 us
    ppermute x2, waiting for transfers between devices, lev_sum(): lax.ppermute(values, 'lev', [(i, i ^ stride) for i in range(count)])  5.45 us
    ppermute x1, starting transfers between devices, body(): lax.ppermute(sections[2], ('lat', 'ocn'), [(i, i + 1) for i in range(band...  4.63 us
    dot_general x1, matrix products, spectra_of(): jnp.einsum('srj,sjd->srd', far, legendre, preferred_element_type=jnp.floa...  4.48 us
  transfers between devices with their start and end apart: 13, of which 6 were waited for; matrix products, arithmetic and copies ran while one was open for 20% of the time, Pallas kernels for 30%

profile of v8, /device:TPU:1, one launch (start us, length us, event | category | flops | bytes accessed | tf_op | source)
XLA Modules:
  0.0 134.7 jit_solution(11026397652695150219)
XLA Ops:
  0.8 1.6 %fusion.22 = (f32[2,1,2176]{2,1,0:T(1,128)}, f32[2,1,2176]{2,1,0:T(1,128)}) fusion(f32[1,16,2176]{2,1,0:T(8,128)} %bitcast.46, f32[1,16,2176]{2,1,0:T(8,128)} %bitcast.50), kind=kLoop, calls=%fused_computation.70 | loop fusion | flops 8704 | bytes 313344 | tf_op jit(solution)/shard_map/stack | solution.py:312
  2.4 4.6 %collective-permute-start.5 = (f32[2,1,2176]{2,1,0:T(1,128)}, f32[2,1,2176]{2,1,0:T(1,128)S(1)}, u32[]{:S(2)}, u32[]{:S(2)}) collective-permute-start(f32[2,1,2176]{2,1,0:T(1,128)} %get-tuple-element.21), channel_id=1, source_target_pairs={{0,1},{1,2},{2,3},{3,16},{16,17},{17,18},{18,19},{4,5},{5,6},{6,7}... | collective-permute-start | bytes 52232 | tf_op jit(solution)/shard_map/ppermute | solution.py:27
  7.1 1.3 collective-permute-start.4
  8.4 1.9 %fusion.7 = (f32[2,16,2175]{2,1,0:T(8,128)S(1)}, f32[2,16,2175]{2,1,0:T(8,128)}) fusion(f32[1,16,2176]{2,1,0:T(8,128)} %bitcast.47, f32[1,16,2176]{2,1,0:T(8,128)} %bitcast.51), kind=kLoop, calls=%fused_computation.30 | loop fusion | flops 139200 | bytes 835328 | tf_op jit(solution)/shard_map/stack | solution.py:312
  10.2 4.0 %cosine_convert_fusion = (bf16[32,5632]{1,0:T(8,128)(2,1)S(1)}, bf16[32,5632]{1,0:T(8,128)(2,1)S(1)}) fusion(s32[32]{0:T(128)} %param.11), kind=kLoop, calls=%fused_computation.7 | loop fusion | flops 2162688 | bytes 721024 | tf_op jit(solution)/shard_map/convert
  15.0 0.9 pad_maximum_fusion.table_ref
  17.3 1.3 collective-permute-start.1
  18.7 1.5 %collective-permute-done.1 = s32[320,22]{0,1:T(8,128)S(1)} collective-permute-done((s32[320,22]{0,1:T(8,128)S(1)}, s32[320,22]{0,1:T(8,128)S(1)}, u32[]{:S(2)}, u32[]{:S(2)}) %collective-permute-start.1) | collective-permute-done | bytes 28192 | tf_op jit(solution)/shard_map/ppermute | solution.py:62
  21.3 35.5 %shard_map.120 = (f32[2,6,320,64]{3,2,1,0:T(8,128)}, f32[3,272,256]{2,1,0:T(8,128)}) custom-call(s32[320,1]{1,0:T(8,128)} %broadcast_in_dim.20.points_ref.limit_ref, bf16[2,6,320,5632]{3,2,1,0:T(8,128)(2,1)} %cells_ref.1, bf16[64,5632]{1,0:T(8,128)(2,1)} %pad_maximum_fusion.table_ref, f32[2,6]{1,0:T(2,128)} %convert_element_type.23.weight_ref, ...), custom_call_target="tpu_custom_call" | custom-call | tf_op jit(solution)/shard_map/pallas_call | solution.py:188
  56.8 1.2 slice_bitcast_fusion.1
  58.0 1.3 collective-permute-start.7
  59.3 4.6 %collective-permute-start.6 = (f32[272,256]{1,0:T(8,128)S(1)}, f32[272,256]{1,0:T(8,128)S(1)}, u32[]{:S(2)}, u32[]{:S(2)}) collective-permute-start(f32[272,256]{1,0:T(8,128)S(1)} %get-tuple-element.8), channel_id=1, source_target_pairs={{0,1},{1,2},{2,3},{3,16},{16,17},{17,18},{18,19},{4,5},{5,6},{6,7}... | collective-permute-start | bytes 835592 | tf_op jit(solution)/shard_map/ppermute | solution.py:294
  64.0 3.2 %collective-permute-done.7 = f32[272,256]{1,0:T(8,128)S(1)} collective-permute-done((f32[272,256]{1,0:T(8,128)S(1)}, f32[272,256]{1,0:T(8,128)S(1)}, u32[]{:S(2)}, u32[]{:S(2)}) %collective-permute-start.7) | collective-permute-done | bytes 278560 | tf_op jit(solution)/shard_map/ppermute | solution.py:297
  67.2 0.9 collective-permute-done.6
  68.1 1.7 %fusion.15 = f32[272,256]{1,0:T(8,128)} fusion(f32[272,256]{1,0:T(8,128)S(1)} %collective-permute-done.7, f32[272,256]{1,0:T(8,128)S(1)} %collective-permute-done.6, f32[3,272,256]{2,1,0:T(8,128)} %get-tuple-element.7), kind=kLoop, calls=%fused_computation.43 | loop fusion | flops 139264 | bytes 1114112 | tf_op jit(solution)/shard_map/add | solution.py:300
  69.8 2.6 %collective-permute-start.8 = (f32[272,256]{1,0:T(8,128)}, f32[272,256]{1,0:T(8,128)}, u32[]{:S(2)}, u32[]{:S(2)}) collective-permute-start(f32[272,256]{1,0:T(8,128)} %fusion.15), channel_id=1, source_target_pairs={{0,4},{4,0},{8,12},{12,8},{1,5},{5,1},{9,13},{13,9},{2,6},{6,2},{1... | collective-permute-start | bytes 835592 | tf_op jit(solution)/shard_map/ppermute | solution.py:50
  73.4 1.0 copy.35
  74.4 12.2 %all-to-all-start = ((bf16[32,24,320]{2,1,0:T(8,128)(2,1)}), bf16[32,24,320]{2,1,0:T(8,128)(2,1)S(1)}, u32[]{:S(2)}, u32[]{:S(2)}) async-start(bf16[32,24,320]{2,1,0:T(8,128)(2,1)} %copy.35), calls=%async_computation | async-start | bytes 1179648 | tf_op jit(solution)/shard_map/all_to_all | solution.py:285
  86.6 1.1 add.92
  87.7 1.3 collective-permute-start.9
  90.3 5.4 %collective-permute-done.9 = f32[272,256]{1,0:T(8,128)S(1)} collective-permute-done((f32[272,256]{1,0:T(8,128)S(1)}, f32[272,256]{1,0:T(8,128)S(1)}, u32[]{:S(2)}, u32[]{:S(2)}) %collective-permute-start.9) | collective-permute-done | bytes 278560 | tf_op jit(solution)/shard_map/ppermute | solution.py:50
  96.1 0.9 fusion.14
  97.0 6.3 %all-to-all-done = bf16[32,24,320]{2,1,0:T(8,128)(2,1)S(1)} async-done(((bf16[32,24,320]{2,1,0:T(8,128)(2,1)}), bf16[32,24,320]{2,1,0:T(8,128)(2,1)S(1)}, u32[]{:S(2)}, u32[]{:S(2)}) %all-to-all-start) | async-done | bytes 491552 | tf_op jit(solution)/shard_map/all_to_all | solution.py:285
  103.9 1.3 collective-permute-start.2
  105.8 1.3 collective-permute-start.11
  107.1 4.2 %collective-permute-start.10 = (f32[16,2176]{1,0:T(8,128)S(1)}, f32[16,2176]{1,0:T(8,128)S(1)}, u32[]{:S(2)}, u32[]{:S(2)}) collective-permute-start(f32[16,2176]{1,0:T(8,128)S(1)} %get-tuple-element.15), channel_id=1, source_target_pairs={{0,1},{1,2},{2,3},{3,16},{16,17},{17,18},{18,19},{4,5},{5,6},{6,7}... | collective-permute-start | bytes 417800 | tf_op jit(solution)/shard_map/ppermute | solution.py:27
  111.3 4.2 %collective-permute-done.2 = bf16[4,24,2560]{2,1,0:T(8,128)(2,1)S(1)} collective-permute-done((bf16[4,24,2560]{2,1,0:T(8,128)(2,1)S(1)}, bf16[4,24,2560]{2,1,0:T(8,128)(2,1)S(1)}, u32[]{:S(2)}, u32[]{:S(2)}) %collective-permute-start.2) | collective-permute-done | bytes 491552 | tf_op jit(solution)/shard_map/ppermute | solution.py:84
  115.7 2.1 %collective-permute-start.3 = (bf16[4,48,2560]{2,1,0:T(8,128)(2,1)S(1)}, bf16[4,48,2560]{2,1,0:T(8,128)(2,1)S(1)}, u32[]{:S(2)}, u32[]{:S(2)}) collective-permute-start(bf16[4,48,2560]{2,1,0:T(8,128)(2,1)S(1)} %maximum_select_fusion), channel_id=1, source_target_pairs={{0,4},{4,0},{8,12},{12,8},{1,5},{5,1},{9,13},{13,9},{2,6},{6,2},{1... | collective-permute-start | bytes 2949128 | tf_op jit(solution)/shard_map/ppermute | solution.py:90
  119.2 5.6 %shard_map.121 = f32[320,1408]{1,0:T(8,128)} custom-call(s32[3520]{0:T(1024)} %fusion.29.slot_ref, s32[1]{0:T(128)} %bitcast.14.base_ref, s32[320,1]{1,0:T(8,128)} %broadcast_in_dim.20.points_ref.limit_ref, f32[816,128]{1,0:T(8,128)} %reshape.104.tiles_ref), custom_call_target="tpu_custom_call" | custom-call | tf_op jit(solution)/shard_map/pallas_call | solution.py:235
  124.8 4.5 %fusion.30 = f32[4,48,384]{2,1,0:T(8,128)S(1)} fusion(bf16[4,48,2560]{2,1,0:T(8,128)(2,1)S(1)} %maximum_select_fusion, bf16[4,2560,384]{2,1,0:T(8,128)(2,1)} %param.12), kind=kOutput, calls=%fused_computation.83 | convolution fusion | flops 377487360 | bytes 9142272 | tf_op jit(solution)/shard_map/srj,sjd->srd/dot_general | solution.py:91
  129.3 4.5 %fusion.31 = f32[4,48,384]{2,1,0:T(8,128)S(1)} fusion(bf16[4,48,2560]{2,1,0:T(8,128)(2,1)S(1)} %collective-permute-done.3, bf16[4,2560,384]{2,1,0:T(8,128)(2,1)} %param.12), kind=kOutput, calls=%fused_computation.84 | convolution fusion | flops 377487360 | bytes 9142272 | tf_op jit(solution)/shard_map/srj,sjd->srd/dot_general | solution.py:92
  133.8 0.9 pad_maximum_fusion.2
  (68 shorter events, 8.8 us)
Async XLA Ops:
  0.6 16.0 %copy-start.5 = (s32[320,11]{0,1:T(8,128)S(1)}, s32[320,11]{0,1:T(8,128)}, u32[]{:S(2)}) copy-start(s32[320,11]{0,1:T(8,128)} %param.14) | copy-start | bytes 42244
  0.6 15.2 %copy-start.8 = (s32[32]{0:T(128)S(1)}, s32[32]{0:T(128)}, u32[]{:S(2)}) copy-start(s32[32]{0:T(128)} %param.11) | copy-start | bytes 388
  0.7 15.2 %copy-start.6 = (s32[320]{0:T(512)S(1)}, s32[320]{0:T(512)}, u32[]{:S(2)}) copy-start(s32[320]{0:T(512)} %param.10) | copy-start | bytes 3844
  0.7 16.1 %copy-start.9 = (bf16[2,6]{1,0:T(2,128)(2,1)S(1)}, bf16[2,6]{1,0:T(2,128)(2,1)}, u32[]{:S(2)}) copy-start(bf16[2,6]{1,0:T(2,128)(2,1)} %param.13) | copy-start | bytes 76
  0.7 16.6 %collective-permute-start = (s32[320,11]{0,1:T(8,128)}, s32[320,11]{0,1:T(8,128)S(1)}, u32[]{:S(2)}, u32[]{:S(2)}) collective-permute-start(s32[320,11]{0,1:T(8,128)} %param.14), channel_id=1, source_target_pairs={{0,4},{4,0},{8,12},{12,8},{1,5},{5,1},{9,13},{13,9},{2,6},{6,2},{1... | collective-permute-start | bytes 42248 | tf_op jit(solution)/shard_map/ppermute | solution.py:62
  2.4 93.6 %collective-permute-start.5 = (f32[2,1,2176]{2,1,0:T(1,128)}, f32[2,1,2176]{2,1,0:T(1,128)S(1)}, u32[]{:S(2)}, u32[]{:S(2)}) collective-permute-start(f32[2,1,2176]{2,1,0:T(1,128)} %get-tuple-element.21), channel_id=1, source_target_pairs={{0,1},{1,2},{2,3},{3,16},{16,17},{17,18},{18,19},{4,5},{5,6},{6,7}... | collective-permute-start | bytes 52232 | tf_op jit(solution)/shard_map/ppermute | solution.py:27
  7.1 89.0 %collective-permute-start.4 = (f32[2,1,2176]{2,1,0:T(1,128)}, f32[2,1,2176]{2,1,0:T(1,128)}, u32[]{:S(2)}, u32[]{:S(2)}) collective-permute-start(f32[2,1,2176]{2,1,0:T(1,128)} %get-tuple-element.20), channel_id=1, source_target_pairs={{1,0},{2,1},{3,2},{16,3},{17,16},{18,17},{19,18},{5,4},{6,5},{7,6}... | collective-permute-start | bytes 52232 | tf_op jit(solution)/shard_map/ppermute | solution.py:29
  17.3 2.9 %collective-permute-start.1 = (s32[320,22]{0,1:T(8,128)S(1)}, s32[320,22]{0,1:T(8,128)S(1)}, u32[]{:S(2)}, u32[]{:S(2)}) collective-permute-start(s32[320,22]{0,1:T(8,128)S(1)} %add_select_fusion.5), channel_id=1, source_target_pairs={{0,8},{4,12},{8,0},{12,4},{1,9},{5,13},{9,1},{13,5},{2,10},{6,14},... | collective-permute-start | bytes 84488 | tf_op jit(solution)/shard_map/ppermute | solution.py:62
  56.7 15.7 %copy-start.2 = (f32[2,6,320,64]{3,2,1,0:T(8,128)S(1)}, f32[2,6,320,64]{3,2,1,0:T(8,128)}, u32[]{:S(2)}) copy-start(f32[2,6,320,64]{3,2,1,0:T(8,128)} %get-tuple-element.6) | copy-start | bytes 2949124
  58.0 9.2 %collective-permute-start.7 = (f32[272,256]{1,0:T(8,128)S(1)}, f32[272,256]{1,0:T(8,128)S(1)}, u32[]{:S(2)}, u32[]{:S(2)}) collective-permute-start(f32[272,256]{1,0:T(8,128)S(1)} %get-tuple-element.9), channel_id=1, source_target_pairs={{1,0},{2,1},{3,2},{16,3},{17,16},{18,17},{19,18},{5,4},{6,5},{7,6}... | collective-permute-start | bytes 835592 | tf_op jit(solution)/shard_map/ppermute | solution.py:297
  59.3 8.8 %collective-permute-start.6 = (f32[272,256]{1,0:T(8,128)S(1)}, f32[272,256]{1,0:T(8,128)S(1)}, u32[]{:S(2)}, u32[]{:S(2)}) collective-permute-start(f32[272,256]{1,0:T(8,128)S(1)} %get-tuple-element.8), channel_id=1, source_target_pairs={{0,1},{1,2},{2,3},{3,16},{16,17},{17,18},{18,19},{4,5},{5,6},{6,7}... | collective-permute-start | bytes 835592 | tf_op jit(solution)/shard_map/ppermute | solution.py:294
  69.8 16.8 %collective-permute-start.8 = (f32[272,256]{1,0:T(8,128)}, f32[272,256]{1,0:T(8,128)}, u32[]{:S(2)}, u32[]{:S(2)}) collective-permute-start(f32[272,256]{1,0:T(8,128)} %fusion.15), channel_id=1, source_target_pairs={{0,4},{4,0},{8,12},{12,8},{1,5},{5,1},{9,13},{13,9},{2,6},{6,2},{1... | collective-permute-start | bytes 835592 | tf_op jit(solution)/shard_map/ppermute | solution.py:50
  73.3 15.7 %copy-start.7 = (s32[16,17]{1,0:T(8,128)S(1)}, s32[16,17]{1,0:T(8,128)}, u32[]{:S(2)}) copy-start(s32[16,17]{1,0:T(8,128)} %param.17) | copy-start | bytes 3268
  73.3 15.7 %copy-start = (f32[16,2176]{1,0:T(8,128)S(1)}, f32[16,2176]{1,0:T(8,128)}, u32[]{:S(2)}) copy-start(f32[16,2176]{1,0:T(8,128)} %param.15) | copy-start | bytes 417796
  73.3 15.7 %copy-start.1 = (f32[16,2176]{1,0:T(8,128)S(1)}, f32[16,2176]{1,0:T(8,128)}, u32[]{:S(2)}) copy-start(f32[16,2176]{1,0:T(8,128)} %param.16) | copy-start | bytes 417796
  74.4 28.9 %all-to-all-start = ((bf16[32,24,320]{2,1,0:T(8,128)(2,1)}), bf16[32,24,320]{2,1,0:T(8,128)(2,1)S(1)}, u32[]{:S(2)}, u32[]{:S(2)}) async-start(bf16[32,24,320]{2,1,0:T(8,128)(2,1)} %copy.35), calls=%async_computation | async-start | bytes 1179648 | tf_op jit(solution)/shard_map/all_to_all | solution.py:285
  87.7 8.0 %collective-permute-start.9 = (f32[272,256]{1,0:T(8,128)S(1)}, f32[272,256]{1,0:T(8,128)S(1)}, u32[]{:S(2)}, u32[]{:S(2)}) collective-permute-start(f32[272,256]{1,0:T(8,128)S(1)} %add.92), channel_id=1, source_target_pairs={{0,8},{4,12},{8,0},{12,4},{1,9},{5,13},{9,1},{13,5},{2,10},{6,14},... | collective-permute-start | bytes 835592 | tf_op jit(solution)/shard_map/ppermute | solution.py:50
  89.2 6.9 %copy-start.3 = (f32[2,16,2175]{2,1,0:T(8,128)S(1)}, f32[2,16,2175]{2,1,0:T(8,128)}, u32[]{:S(2)}) copy-start(f32[2,16,2175]{2,1,0:T(8,128)} %get-tuple-element.17) | copy-start | bytes 835204
  103.9 11.7 %collective-permute-start.2 = (bf16[4,24,2560]{2,1,0:T(8,128)(2,1)S(1)}, bf16[4,24,2560]{2,1,0:T(8,128)(2,1)S(1)}, u32[]{:S(2)}, u32[]{:S(2)}) collective-permute-start(bf16[4,24,2560]{2,1,0:T(8,128)(2,1)S(1)} %all_to_all.16), channel_id=1, source_target_pairs={{0,8},{4,12},{8,0},{12,4},{1,9},{5,13},{9,1},{13,5},{2,10},{6,14},... | collective-permute-start | bytes 1474568 | tf_op jit(solution)/shard_map/ppermute | solution.py:84
  105.8 19.0 %copy-start.4 = (f32[16,2176]{1,0:T(8,128)}, f32[16,2176]{1,0:T(8,128)S(1)}, u32[]{:S(2)}) copy-start(f32[16,2176]{1,0:T(8,128)S(1)} %get-tuple-element.15) | copy-start | bytes 417796
  105.8 12.6 %collective-permute-start.11 = (f32[16,2176]{1,0:T(8,128)S(1)}, f32[16,2176]{1,0:T(8,128)S(1)}, u32[]{:S(2)}, u32[]{:S(2)}) collective-permute-start(f32[16,2176]{1,0:T(8,128)S(1)} %get-tuple-element.15), channel_id=1, source_target_pairs={{1,0},{2,1},{3,2},{16,3},{17,16},{18,17},{19,18},{5,4},{6,5},{7,6}... | collective-permute-start | bytes 417800 | tf_op jit(solution)/shard_map/ppermute | solution.py:29
  107.1 11.3 %collective-permute-start.10 = (f32[16,2176]{1,0:T(8,128)S(1)}, f32[16,2176]{1,0:T(8,128)S(1)}, u32[]{:S(2)}, u32[]{:S(2)}) collective-permute-start(f32[16,2176]{1,0:T(8,128)S(1)} %get-tuple-element.15), channel_id=1, source_target_pairs={{0,1},{1,2},{2,3},{3,16},{16,17},{17,18},{18,19},{4,5},{5,6},{6,7}... | collective-permute-start | bytes 417800 | tf_op jit(solution)/shard_map/ppermute | solution.py:27
  115.7 13.6 %collective-permute-start.3 = (bf16[4,48,2560]{2,1,0:T(8,128)(2,1)S(1)}, bf16[4,48,2560]{2,1,0:T(8,128)(2,1)S(1)}, u32[]{:S(2)}, u32[]{:S(2)}) collective-permute-start(bf16[4,48,2560]{2,1,0:T(8,128)(2,1)S(1)} %maximum_select_fusion), channel_id=1, source_target_pairs={{0,4},{4,0},{8,12},{12,8},{1,5},{5,1},{9,13},{13,9},{2,6},{6,2},{1... | collective-permute-start | bytes 2949128 | tf_op jit(solution)/shard_map/ppermute | solution.py:90

commit v9 on v7

--- a/solution.py
+++ b/solution.py
@@ -259,6 +259,7 @@
         concat_axis=2,
         tiled=True,
     )
+    sections, regrouped = lax.optimization_barrier((sections, regrouped))
     spectra = jnp.einsum(
         "srj,sjd->srd",
         lev_gather(regrouped, 1),

time: 124 us -> 129 us (1.040)
  the two profiles are of different devices: /device:TPU:0 before, /device:TPU:4 now
where the time goes in v9:
time: 129 us; the launch traced here: 128 us
  Pallas kernels  41.1 us (32%)
  waiting for transfers between devices  32.4 us (25%)
  starting transfers between devices  30.5 us (24%)
  other arithmetic  8.72 us (7%)
  local copies, waits for them, and re-layouts  8.52 us (7%)
  matrix products  6.07 us (5%)
    pallas_call x1, Pallas kernels, fused_transform(): pl.pallas_call(transform_kernel, grid=(steps,), in_specs=[pl.BlockSpec((r...  35.5 us
    ppermute x2, waiting for transfers between devices, lev_sum(): lax.ppermute(values, 'lev', [(i, i ^ stride) for i in range(count)])  8.64 us
    ppermute x2, starting transfers between devices, with_halo(): lax.ppermute(tail, axis, [(i, (i + 1) % count) for i in range(ends)])  7.43 us
    ppermute x2, starting transfers between devices, with_halo(): lax.ppermute(head, axis, [((i + 1) % count, i) for i in range(ends)])  7.08 us
    ppermute x1, waiting for transfers between devices, body(): lax.ppermute(sections[2], ('lat', 'ocn'), [(i, i + 1) for i in range(band...  6.82 us
    all_to_all x1, starting transfers between devices, body(): lax.all_to_all(coeffs.transpose(4, 1, 0, 3, 2).reshape(wave_count, lev_de...  6.34 us
    dot_general x1, matrix products, body(): jnp.einsum('srj,sjd->srd', lev_gather(regrouped, 1), legendre, preferred_...  6.07 us
    all_to_all x1, waiting for transfers between devices, body(): lax.all_to_all(coeffs.transpose(4, 1, 0, 3, 2).reshape(wave_count, lev_de...  5.78 us
  transfers between devices with their start and end apart: 13, of which 9 were waited for; matrix products, arithmetic and copies ran while one was open for 10% of the time, Pallas kernels for 4%

profile of v9, /device:TPU:4, one launch (start us, length us, event | category | flops | bytes accessed | tf_op | source)
XLA Modules:
  0.0 128.3 jit_solution(10217571493240794303)
XLA Ops:
  0.7 4.0 %cosine_convert_fusion = (bf16[32,5632]{1,0:T(8,128)(2,1)S(1)}, bf16[32,5632]{1,0:T(8,128)(2,1)S(1)}) fusion(s32[32]{0:T(128)} %param.11), kind=kLoop, calls=%fused_computation.15 | loop fusion | flops 2162688 | bytes 721024 | tf_op jit(solution)/shard_map/convert
  4.8 0.7 broadcast_multiply_fusion
  5.4 0.7 convert_rsqrt_fusion
  6.1 0.9 pad_maximum_fusion.table_ref
  7.1 0.8 broadcast_in_dim.20.points_ref.limit_ref
  8.6 1.6 %collective-permute-start.1 = (s32[320,22]{0,1:T(8,128)S(1)}, s32[320,22]{0,1:T(8,128)S(1)}, u32[]{:S(2)}, u32[]{:S(2)}) collective-permute-start(s32[320,22]{0,1:T(8,128)S(1)} %add_select_fusion.5), channel_id=1, source_target_pairs={{0,8},{4,12},{8,0},{12,4},{1,9},{5,13},{9,1},{13,5},{2,10},{6,14},... | collective-permute-start | bytes 84488 | tf_op jit(solution)/shard_map/ppermute | solution.py:62
  10.2 2.4 %collective-permute-done.1 = s32[320,22]{0,1:T(8,128)S(1)} collective-permute-done((s32[320,22]{0,1:T(8,128)S(1)}, s32[320,22]{0,1:T(8,128)S(1)}, u32[]{:S(2)}, u32[]{:S(2)}) %collective-permute-start.1) | collective-permute-done | bytes 28192 | tf_op jit(solution)/shard_map/ppermute | solution.py:62
  12.9 0.7 reshape.98.slot_ref
  13.7 35.5 %shard_map.120 = (f32[2,6,320,64]{3,2,1,0:T(8,128)}, f32[3,272,256]{2,1,0:T(8,128)}) custom-call(s32[320,1]{1,0:T(8,128)} %broadcast_in_dim.20.points_ref.limit_ref, bf16[2,6,320,5632]{3,2,1,0:T(8,128)(2,1)} %cells_ref.1, bf16[64,5632]{1,0:T(8,128)(2,1)} %pad_maximum_fusion.table_ref, f32[2,6]{1,0:T(2,128)} %convert_element_type.23.weight_ref, ...), custom_call_target="tpu_custom_call" | custom-call | tf_op jit(solution)/shard_map/pallas_call | solution.py:158
  49.2 2.2 %copy.43 = f32[2,6,320,64]{2,3,1,0:T(8,128)S(1)} copy(f32[2,6,320,64]{3,2,1,0:T(8,128)} %get-tuple-element.9) | data formatting | bytes 1966080 | tf_op jit(solution)/shard_map/pallas_call | solution.py:158
  51.6 1.0 copy.45
  52.6 6.3 %all-to-all-start = ((bf16[32,24,320]{2,1,0:T(8,128)(2,1)}), bf16[32,24,320]{2,1,0:T(8,128)(2,1)S(1)}, u32[]{:S(2)}, u32[]{:S(2)}) async-start(bf16[32,24,320]{2,1,0:T(8,128)(2,1)} %copy.45), calls=%async_computation | async-start | bytes 1179648 | tf_op jit(solution)/shard_map/all_to_all | solution.py:255
  59.0 3.5 %collective-permute-start.5 = (f32[2,1,2176]{2,1,0:T(1,128)S(1)}, f32[2,1,2176]{2,1,0:T(1,128)S(1)}, u32[]{:S(2)}, u32[]{:S(2)}) collective-permute-start(f32[2,1,2176]{2,1,0:T(1,128)S(1)} %get-tuple-element.21), channel_id=1, source_target_pairs={{0,1},{1,2},{2,3},{3,16},{16,17},{17,18},{18,19},{4,5},{5,6},{6,7}... | collective-permute-start | bytes 52232 | tf_op jit(solution)/shard_map/ppermute | solution.py:27
  62.5 5.2 %collective-permute-start.4 = (f32[2,1,2176]{2,1,0:T(1,128)S(1)}, f32[2,1,2176]{2,1,0:T(1,128)S(1)}, u32[]{:S(2)}, u32[]{:S(2)}) collective-permute-start(f32[2,1,2176]{2,1,0:T(1,128)S(1)} %get-tuple-element.20), channel_id=1, source_target_pairs={{1,0},{2,1},{3,2},{16,3},{17,16},{18,17},{19,18},{5,4},{6,5},{7,6}... | collective-permute-start | bytes 52232 | tf_op jit(solution)/shard_map/ppermute | solution.py:29
  68.6 5.8 %all-to-all-done = bf16[32,24,320]{2,1,0:T(8,128)(2,1)S(1)} async-done(((bf16[32,24,320]{2,1,0:T(8,128)(2,1)}), bf16[32,24,320]{2,1,0:T(8,128)(2,1)S(1)}, u32[]{:S(2)}, u32[]{:S(2)}) %all-to-all-start) | async-done | bytes 491552 | tf_op jit(solution)/shard_map/all_to_all | solution.py:255
  75.0 1.9 %collective-permute-start.7 = (f32[272,256]{1,0:T(8,128)S(1)}, f32[272,256]{1,0:T(8,128)S(1)}, u32[]{:S(2)}, u32[]{:S(2)}) collective-permute-start(f32[272,256]{1,0:T(8,128)S(1)} %get-tuple-element.13), channel_id=1, source_target_pairs={{1,0},{2,1},{3,2},{16,3},{17,16},{18,17},{19,18},{5,4},{6,5},{7,6}... | collective-permute-start | bytes 835592 | tf_op jit(solution)/shard_map/ppermute | solution.py:273
  76.9 3.9 %collective-permute-start.6 = (f32[272,256]{1,0:T(8,128)S(1)}, f32[272,256]{1,0:T(8,128)S(1)}, u32[]{:S(2)}, u32[]{:S(2)}) collective-permute-start(f32[272,256]{1,0:T(8,128)S(1)} %get-tuple-element.12), channel_id=1, source_target_pairs={{0,1},{1,2},{2,3},{3,16},{16,17},{17,18},{18,19},{4,5},{5,6},{6,7}... | collective-permute-start | bytes 835592 | tf_op jit(solution)/shard_map/ppermute | solution.py:270
  81.3 2.4 %collective-permute-done.7 = f32[272,256]{1,0:T(8,128)S(1)} collective-permute-done((f32[272,256]{1,0:T(8,128)S(1)}, f32[272,256]{1,0:T(8,128)S(1)}, u32[]{:S(2)}, u32[]{:S(2)}) %collective-permute-start.7) | collective-permute-done | bytes 278560 | tf_op jit(solution)/shard_map/ppermute | solution.py:273
  83.8 6.8 %collective-permute-done.6 = f32[272,256]{1,0:T(8,128)S(1)} collective-permute-done((f32[272,256]{1,0:T(8,128)S(1)}, f32[272,256]{1,0:T(8,128)S(1)}, u32[]{:S(2)}, u32[]{:S(2)}) %collective-permute-start.6) | collective-permute-done | bytes 278560 | tf_op jit(solution)/shard_map/ppermute | solution.py:270
  90.9 1.4 %collective-permute-done.8 = f32[272,256]{1,0:T(8,128)S(1)} collective-permute-done((f32[272,256]{1,0:T(8,128)S(1)}, f32[272,256]{1,0:T(8,128)S(1)}, u32[]{:S(2)}, u32[]{:S(2)}) %collective-permute-start.8) | collective-permute-done | bytes 278560 | tf_op jit(solution)/shard_map/ppermute | solution.py:50
  92.3 1.6 %collective-permute-start.9 = (f32[272,256]{1,0:T(8,128)S(1)}, f32[272,256]{1,0:T(8,128)S(1)}, u32[]{:S(2)}, u32[]{:S(2)}) collective-permute-start(f32[272,256]{1,0:T(8,128)S(1)} %add.92), channel_id=1, source_target_pairs={{0,8},{4,12},{8,0},{12,4},{1,9},{5,13},{9,1},{13,5},{2,10},{6,14},... | collective-permute-start | bytes 835592 | tf_op jit(solution)/shard_map/ppermute | solution.py:50
  94.0 0.6 collective-permute-start.3
  94.6 7.2 %collective-permute-done.9 = f32[272,256]{1,0:T(8,128)S(1)} collective-permute-done((f32[272,256]{1,0:T(8,128)S(1)}, f32[272,256]{1,0:T(8,128)S(1)}, u32[]{:S(2)}, u32[]{:S(2)}) %collective-permute-start.9) | collective-permute-done | bytes 278560 | tf_op jit(solution)/shard_map/ppermute | solution.py:50
  102.4 0.7 slice_bitcast_fusion.2
  103.1 1.9 %collective-permute-start.11 = (f32[16,2176]{1,0:T(8,128)S(1)}, f32[16,2176]{1,0:T(8,128)S(1)}, u32[]{:S(2)}, u32[]{:S(2)}) collective-permute-start(f32[16,2176]{1,0:T(8,128)S(1)} %get-tuple-element.15), channel_id=1, source_target_pairs={{1,0},{2,1},{3,2},{16,3},{17,16},{18,17},{19,18},{5,4},{6,5},{7,6}... | collective-permute-start | bytes 417800 | tf_op jit(solution)/shard_map/ppermute | solution.py:29
  105.0 3.9 %collective-permute-start.10 = (f32[16,2176]{1,0:T(8,128)S(1)}, f32[16,2176]{1,0:T(8,128)S(1)}, u32[]{:S(2)}, u32[]{:S(2)}) collective-permute-start(f32[16,2176]{1,0:T(8,128)S(1)} %get-tuple-element.15), channel_id=1, source_target_pairs={{0,1},{1,2},{2,3},{3,16},{16,17},{17,18},{18,19},{4,5},{5,6},{6,7}... | collective-permute-start | bytes 417800 | tf_op jit(solution)/shard_map/ppermute | solution.py:27
  108.9 0.6 fusion.36.slot_ref
  110.0 4.6 %collective-permute-done.10 = f32[16,2176]{1,0:T(8,128)S(1)} collective-permute-done((f32[16,2176]{1,0:T(8,128)S(1)}, f32[16,2176]{1,0:T(8,128)S(1)}, u32[]{:S(2)}, u32[]{:S(2)}) %collective-permute-start.10) | collective-permute-done | bytes 139296 | tf_op jit(solution)/shard_map/ppermute | solution.py:27
  114.7 0.8 reshape.104.tiles_ref
  115.4 5.6 %shard_map.121 = f32[320,1408]{1,0:T(8,128)} custom-call(s32[3520]{0:T(1024)} %fusion.36.slot_ref, s32[1]{0:T(128)} %bitcast.14.base_ref, s32[320,1]{1,0:T(8,128)} %broadcast_in_dim.20.points_ref.limit_ref, f32[816,128]{1,0:T(8,128)} %reshape.104.tiles_ref), custom_call_target="tpu_custom_call" | custom-call | tf_op jit(solution)/shard_map/pallas_call | solution.py:205
  121.0 1.2 collective-permute-done.3
  122.2 6.1 %fusion = f32[4,96,384]{2,1,0:T(8,128)} fusion(bf16[4,2560,384]{2,1,0:T(8,128)(2,1)} %param.12, bf16[4,48,2560]{2,1,0:T(8,128)(2,1)S(1)} %maximum_select_fusion.2, bf16[4,48,2560]{2,1,0:T(8,128)(2,1)} %collective-permute-done.3, pred[]{:T(512)S(6)} %eq.19), kind=kOutput, calls=%fused_computation.1 | convolution fusion | flops 763822080 | bytes 10420225 | tf_op jit(solution)/shard_map/srj,sjd->srd/dot_general | solution.py:263
  (61 shorter events, 4.8 us)
Async XLA Ops:
  0.6 7.3 %copy-start.4 = (s32[320,11]{0,1:T(8,128)S(1)}, s32[320,11]{0,1:T(8,128)}, u32[]{:S(2)}) copy-start(s32[320,11]{0,1:T(8,128)} %param.14) | copy-start | bytes 42244
  0.6 6.4 %copy-start.5 = (s32[320]{0:T(512)S(1)}, s32[320]{0:T(512)}, u32[]{:S(2)}) copy-start(s32[320]{0:T(512)} %param.10) | copy-start | bytes 3844
  0.7 7.3 %copy-start.7 = (bf16[2,6]{1,0:T(2,128)(2,1)S(1)}, bf16[2,6]{1,0:T(2,128)(2,1)}, u32[]{:S(2)}) copy-start(bf16[2,6]{1,0:T(2,128)(2,1)} %param.13) | copy-start | bytes 76
  0.7 7.9 %collective-permute-start = (s32[320,11]{0,1:T(8,128)}, s32[320,11]{0,1:T(8,128)S(1)}, u32[]{:S(2)}, u32[]{:S(2)}) collective-permute-start(s32[320,11]{0,1:T(8,128)} %param.14), channel_id=1, source_target_pairs={{0,4},{4,0},{8,12},{12,8},{1,5},{5,1},{9,13},{13,9},{2,6},{6,2},{1... | collective-permute-start | bytes 42248 | tf_op jit(solution)/shard_map/ppermute | solution.py:62
  8.6 4.0 %collective-permute-start.1 = (s32[320,22]{0,1:T(8,128)S(1)}, s32[320,22]{0,1:T(8,128)S(1)}, u32[]{:S(2)}, u32[]{:S(2)}) collective-permute-start(s32[320,22]{0,1:T(8,128)S(1)} %add_select_fusion.5), channel_id=1, source_target_pairs={{0,8},{4,12},{8,0},{12,4},{1,9},{5,13},{9,1},{13,5},{2,10},{6,14},... | collective-permute-start | bytes 84488 | tf_op jit(solution)/shard_map/ppermute | solution.py:62
  51.5 7.5 %copy-start = (f32[16,2176]{1,0:T(8,128)S(1)}, f32[16,2176]{1,0:T(8,128)}, u32[]{:S(2)}) copy-start(f32[16,2176]{1,0:T(8,128)} %param.15) | copy-start | bytes 417796
  51.5 7.4 %copy-start.1 = (f32[16,2176]{1,0:T(8,128)S(1)}, f32[16,2176]{1,0:T(8,128)}, u32[]{:S(2)}) copy-start(f32[16,2176]{1,0:T(8,128)} %param.16) | copy-start | bytes 417796
  51.5 16.2 %copy-start.6 = (s32[16,17]{1,0:T(8,128)S(1)}, s32[16,17]{1,0:T(8,128)}, u32[]{:S(2)}) copy-start(s32[16,17]{1,0:T(8,128)} %param.17) | copy-start | bytes 3268
  52.6 21.7 %all-to-all-start = ((bf16[32,24,320]{2,1,0:T(8,128)(2,1)}), bf16[32,24,320]{2,1,0:T(8,128)(2,1)S(1)}, u32[]{:S(2)}, u32[]{:S(2)}) async-start(bf16[32,24,320]{2,1,0:T(8,128)(2,1)} %copy.45), calls=%async_computation | async-start | bytes 1179648 | tf_op jit(solution)/shard_map/all_to_all | solution.py:255
  59.0 16.0 %copy-start.2 = (f32[3,272,256]{2,1,0:T(8,128)S(1)}, f32[3,272,256]{2,1,0:T(8,128)}, u32[]{:S(2)}) copy-start(f32[3,272,256]{2,1,0:T(8,128)} %get-tuple-element.11) | copy-start | bytes 2506756
  59.0 43.1 %collective-permute-start.5 = (f32[2,1,2176]{2,1,0:T(1,128)S(1)}, f32[2,1,2176]{2,1,0:T(1,128)S(1)}, u32[]{:S(2)}, u32[]{:S(2)}) collective-permute-start(f32[2,1,2176]{2,1,0:T(1,128)S(1)} %get-tuple-element.21), channel_id=1, source_target_pairs={{0,1},{1,2},{2,3},{3,16},{16,17},{17,18},{18,19},{4,5},{5,6},{6,7}... | collective-permute-start | bytes 52232 | tf_op jit(solution)/shard_map/ppermute | solution.py:27
  62.5 39.6 %collective-permute-start.4 = (f32[2,1,2176]{2,1,0:T(1,128)S(1)}, f32[2,1,2176]{2,1,0:T(1,128)S(1)}, u32[]{:S(2)}, u32[]{:S(2)}) collective-permute-start(f32[2,1,2176]{2,1,0:T(1,128)S(1)} %get-tuple-element.20), channel_id=1, source_target_pairs={{1,0},{2,1},{3,2},{16,3},{17,16},{18,17},{19,18},{5,4},{6,5},{7,6}... | collective-permute-start | bytes 52232 | tf_op jit(solution)/shard_map/ppermute | solution.py:29
  75.0 8.8 %collective-permute-start.7 = (f32[272,256]{1,0:T(8,128)S(1)}, f32[272,256]{1,0:T(8,128)S(1)}, u32[]{:S(2)}, u32[]{:S(2)}) collective-permute-start(f32[272,256]{1,0:T(8,128)S(1)} %get-tuple-element.13), channel_id=1, source_target_pairs={{1,0},{2,1},{3,2},{16,3},{17,16},{18,17},{19,18},{5,4},{6,5},{7,6}... | collective-permute-start | bytes 835592 | tf_op jit(solution)/shard_map/ppermute | solution.py:273
  76.9 13.7 %collective-permute-start.6 = (f32[272,256]{1,0:T(8,128)S(1)}, f32[272,256]{1,0:T(8,128)S(1)}, u32[]{:S(2)}, u32[]{:S(2)}) collective-permute-start(f32[272,256]{1,0:T(8,128)S(1)} %get-tuple-element.12), channel_id=1, source_target_pairs={{0,1},{1,2},{2,3},{3,16},{16,17},{17,18},{18,19},{4,5},{5,6},{6,7}... | collective-permute-start | bytes 835592 | tf_op jit(solution)/shard_map/ppermute | solution.py:270
  81.3 12.5 %collective-permute-start.2 = (bf16[4,24,2560]{2,1,0:T(8,128)(2,1)S(1)}, bf16[4,24,2560]{2,1,0:T(8,128)(2,1)S(1)}, u32[]{:S(2)}, u32[]{:S(2)}) collective-permute-start(bf16[4,24,2560]{2,1,0:T(8,128)(2,1)S(1)} %all_to_all.16), channel_id=1, source_target_pairs={{0,4},{4,0},{8,12},{12,8},{1,5},{5,1},{9,13},{13,9},{2,6},{6,2},{1... | collective-permute-start | bytes 1474568 | tf_op jit(solution)/shard_map/ppermute | solution.py:62
  90.6 1.6 %collective-permute-start.8 = (f32[272,256]{1,0:T(8,128)S(1)}, f32[272,256]{1,0:T(8,128)S(1)}, u32[]{:S(2)}, u32[]{:S(2)}) collective-permute-start(f32[272,256]{1,0:T(8,128)S(1)} %fusion.22), channel_id=1, source_target_pairs={{0,4},{4,0},{8,12},{12,8},{1,5},{5,1},{9,13},{13,9},{2,6},{6,2},{1... | collective-permute-start | bytes 835592 | tf_op jit(solution)/shard_map/ppermute | solution.py:50
  92.3 9.6 %collective-permute-start.9 = (f32[272,256]{1,0:T(8,128)S(1)}, f32[272,256]{1,0:T(8,128)S(1)}, u32[]{:S(2)}, u32[]{:S(2)}) collective-permute-start(f32[272,256]{1,0:T(8,128)S(1)} %add.92), channel_id=1, source_target_pairs={{0,8},{4,12},{8,0},{12,4},{1,9},{5,13},{9,1},{13,5},{2,10},{6,14},... | collective-permute-start | bytes 835592 | tf_op jit(solution)/shard_map/ppermute | solution.py:50
  94.0 28.2 %collective-permute-start.3 = (bf16[4,48,2560]{2,1,0:T(8,128)(2,1)S(1)}, bf16[4,48,2560]{2,1,0:T(8,128)(2,1)}, u32[]{:S(2)}, u32[]{:S(2)}) collective-permute-start(bf16[4,48,2560]{2,1,0:T(8,128)(2,1)S(1)} %maximum_select_fusion.2), channel_id=1, source_target_pairs={{0,8},{4,12},{8,0},{12,4},{1,9},{5,13},{9,1},{13,5},{2,10},{6,14},... | collective-permute-start | bytes 2949128 | tf_op jit(solution)/shard_map/ppermute | solution.py:62
  103.1 17.9 %copy-start.3 = (f32[16,2176]{1,0:T(8,128)}, f32[16,2176]{1,0:T(8,128)S(1)}, u32[]{:S(2)}) copy-start(f32[16,2176]{1,0:T(8,128)S(1)} %get-tuple-element.15) | copy-start | bytes 417796
  103.1 6.9 %collective-permute-start.11 = (f32[16,2176]{1,0:T(8,128)S(1)}, f32[16,2176]{1,0:T(8,128)S(1)}, u32[]{:S(2)}, u32[]{:S(2)}) collective-permute-start(f32[16,2176]{1,0:T(8,128)S(1)} %get-tuple-element.15), channel_id=1, source_target_pairs={{1,0},{2,1},{3,2},{16,3},{17,16},{18,17},{19,18},{5,4},{6,5},{7,6}... | collective-permute-start | bytes 417800 | tf_op jit(solution)/shard_map/ppermute | solution.py:29
  105.0 9.6 %collective-permute-start.10 = (f32[16,2176]{1,0:T(8,128)S(1)}, f32[16,2176]{1,0:T(8,128)S(1)}, u32[]{:S(2)}, u32[]{:S(2)}) collective-permute-start(f32[16,2176]{1,0:T(8,128)S(1)} %get-tuple-element.15), channel_id=1, source_target_pairs={{0,1},{1,2},{2,3},{3,16},{16,17},{17,18},{18,19},{4,5},{5,6},{6,7}... | collective-permute-start | bytes 417800 | tf_op jit(solution)/shard_map/ppermute | solution.py:27

commit v10 on v7

--- a/solution.py
+++ b/solution.py
@@ -68,6 +68,29 @@
         )
         stride *= 2
     return values
+
+
+def lev_gather_far_first(values, axis):
+    count = lax.axis_size("lev")
+    if count != 4:
+        return lev_gather(values, axis)
+    index = lax.axis_index("lev")
+    size = values.shape[axis]
+    other = lax.ppermute(values, "lev", [(i, i ^ 2) for i in range(count)])
+    pair = jnp.where(
+        (index // 2) % 2 == 1,
+        jnp.concatenate([other, values], axis=axis),
+        jnp.concatenate([values, other], axis=axis),
+    )
+    far = lax.ppermute(pair, "lev", [(i, i ^ 1) for i in range(count)])
+    even = index % 2 == 0
+    first = jnp.where(even, pair, far)
+    second = jnp.where(even, far, pair)
+    parts = []
+    for half in range(2):
+        parts.append(lax.slice_in_dim(first, half * size, (half + 1) * size, axis=axis))
+        parts.append(lax.slice_in_dim(second, half * size, (half + 1) * size, axis=axis))
+    return jnp.concatenate(parts, axis=axis)
 
 
 def row_block(rows):
@@ -261,7 +284,7 @@
     )
     spectra = jnp.einsum(
         "srj,sjd->srd",
-        lev_gather(regrouped, 1),
+        lev_gather_far_first(regrouped, 1),
         legendre,
         preferred_element_type=jnp.float32,
     )

time: 124 us -> 129 us (1.040)
  the two profiles are of different devices: /device:TPU:0 before, /device:TPU:4 now
where the time goes in v10:
time: 129 us
  Pallas kernels  41 us (32%)
  starting transfers between devices  31.7 us (25%)
  waiting for transfers between devices  28.4 us (22%)
  other arithmetic  11.3 us (9%)
  local copies, waits for them, and re-layouts  9.71 us (8%)
  matrix products  5.55 us (4%)
    pallas_call x1, Pallas kernels, fused_transform(): pl.pallas_call(transform_kernel, grid=(steps,), in_specs=[pl.BlockSpec((r...  35.5 us
    ppermute x2, starting transfers between devices, with_halo(): lax.ppermute(head, axis, [((i + 1) % count, i) for i in range(ends)])  10.2 us
    ppermute x1, waiting for transfers between devices, lev_gather_far_first(): other = lax.ppermute(values, 'lev', [(i, i ^ 2) for i in range(count)])  8.8 us
    ppermute x2, waiting for transfers between devices, lev_sum(): lax.ppermute(values, 'lev', [(i, i ^ stride) for i in range(count)])  7.41 us
    ppermute x2, waiting for transfers between devices, with_halo(): lax.ppermute(tail, axis, [(i, (i + 1) % count) for i in range(ends)])  6.42 us
    pallas_call x1, Pallas kernels, surface_gather(): pl.pallas_call(surface_kernel, in_specs=[pl.BlockSpec(memory_space=pltpu....  5.56 us
    dot_general x1, matrix products, body(): jnp.einsum('srj,sjd->srd', lev_gather_far_first(regrouped, 1), legendre,...  5.55 us
    ppermute x2, starting transfers between devices, with_halo(): lax.ppermute(tail, axis, [(i, (i + 1) % count) for i in range(ends)])  5.41 us
  transfers between devices with their start and end apart: 13, of which 7 were waited for; matrix products, arithmetic and copies ran while one was open for 16% of the time, Pallas kernels for 32%

profile of v10, /device:TPU:4, one launch (start us, length us, event | category | flops | bytes accessed | tf_op | source)
XLA Modules:
  0.0 128.6 jit_solution(15501690322211542513)
XLA Ops:
  0.8 1.0 fusion.30
  1.8 3.5 %collective-permute-start.5 = (f32[2,1,2176]{2,1,0:T(1,128)S(1)}, f32[2,1,2176]{2,1,0:T(1,128)S(1)}, u32[]{:S(2)}, u32[]{:S(2)}) collective-permute-start(f32[2,1,2176]{2,1,0:T(1,128)S(1)} %get-tuple-element.23), channel_id=1, source_target_pairs={{0,1},{1,2},{2,3},{3,16},{16,17},{17,18},{18,19},{4,5},{5,6},{6,7}... | collective-permute-start | bytes 52232 | tf_op jit(solution)/shard_map/ppermute | solution.py:27
  5.3 5.1 %collective-permute-start.4 = (f32[2,1,2176]{2,1,0:T(1,128)S(1)}, f32[2,1,2176]{2,1,0:T(1,128)S(1)}, u32[]{:S(2)}, u32[]{:S(2)}) collective-permute-start(f32[2,1,2176]{2,1,0:T(1,128)S(1)} %get-tuple-element.22), channel_id=1, source_target_pairs={{1,0},{2,1},{3,2},{16,3},{17,16},{18,17},{19,18},{5,4},{6,5},{7,6}... | collective-permute-start | bytes 52232 | tf_op jit(solution)/shard_map/ppermute | solution.py:29
  10.3 1.2 fusion.15
  11.6 4.0 %cosine_convert_fusion = (bf16[32,5632]{1,0:T(8,128)(2,1)S(1)}, bf16[32,5632]{1,0:T(8,128)(2,1)S(1)}) fusion(s32[32]{0:T(128)} %param.11), kind=kLoop, calls=%fused_computation.17 | loop fusion | flops 2162688 | bytes 721024 | tf_op jit(solution)/shard_map/convert
  15.6 0.7 convert_rsqrt_fusion
  16.3 0.9 pad_maximum_fusion.table_ref
  17.2 0.8 broadcast_in_dim.20.points_ref.limit_ref
  18.7 1.6 %collective-permute-start.1 = (s32[320,22]{0,1:T(8,128)S(1)}, s32[320,22]{0,1:T(8,128)S(1)}, u32[]{:S(2)}, u32[]{:S(2)}) collective-permute-start(s32[320,22]{0,1:T(8,128)S(1)} %add_select_fusion.5), channel_id=1, source_target_pairs={{0,8},{4,12},{8,0},{12,4},{1,9},{5,13},{9,1},{13,5},{2,10},{6,14},... | collective-permute-start | bytes 84488 | tf_op jit(solution)/shard_map/ppermute | solution.py:62
  20.3 2.4 %collective-permute-done.1 = s32[320,22]{0,1:T(8,128)S(1)} collective-permute-done((s32[320,22]{0,1:T(8,128)S(1)}, s32[320,22]{0,1:T(8,128)S(1)}, u32[]{:S(2)}, u32[]{:S(2)}) %collective-permute-start.1) | collective-permute-done | bytes 28192 | tf_op jit(solution)/shard_map/ppermute | solution.py:62
  23.0 0.7 reshape.98.slot_ref
  23.8 35.5 %shard_map.120 = (f32[2,6,320,64]{3,2,1,0:T(8,128)}, f32[3,272,256]{2,1,0:T(8,128)}) custom-call(s32[320,1]{1,0:T(8,128)} %broadcast_in_dim.20.points_ref.limit_ref, bf16[2,6,320,5632]{3,2,1,0:T(8,128)(2,1)} %cells_ref.1, bf16[64,5632]{1,0:T(8,128)(2,1)} %pad_maximum_fusion.table_ref, f32[2,6]{1,0:T(2,128)} %convert_element_type.23.weight_ref, ...), custom_call_target="tpu_custom_call" | custom-call | tf_op jit(solution)/shard_map/pallas_call | solution.py:181
  59.3 1.1 slice_bitcast_fusion.1
  60.3 2.8 %collective-permute-start.7 = (f32[272,256]{1,0:T(8,128)S(1)}, f32[272,256]{1,0:T(8,128)S(1)}, u32[]{:S(2)}, u32[]{:S(2)}) collective-permute-start(f32[272,256]{1,0:T(8,128)S(1)} %get-tuple-element.15), channel_id=1, source_target_pairs={{1,0},{2,1},{3,2},{16,3},{17,16},{18,17},{19,18},{5,4},{6,5},{7,6}... | collective-permute-start | bytes 835592 | tf_op jit(solution)/shard_map/ppermute | solution.py:295
  63.1 3.1 %collective-permute-start.6 = (f32[272,256]{1,0:T(8,128)S(1)}, f32[272,256]{1,0:T(8,128)S(1)}, u32[]{:S(2)}, u32[]{:S(2)}) collective-permute-start(f32[272,256]{1,0:T(8,128)S(1)} %get-tuple-element.14), channel_id=1, source_target_pairs={{0,1},{1,2},{2,3},{3,16},{16,17},{17,18},{18,19},{4,5},{5,6},{6,7}... | collective-permute-start | bytes 835592 | tf_op jit(solution)/shard_map/ppermute | solution.py:292
  66.3 2.2 %copy.33 = f32[2,6,320,64]{2,3,1,0:T(8,128)S(1)} copy(f32[2,6,320,64]{3,2,1,0:T(8,128)} %get-tuple-element.6) | data formatting | bytes 1966080 | tf_op jit(solution)/shard_map/pallas_call | solution.py:181
  68.7 1.0 copy.35
  69.7 5.4 %all-to-all-start = ((bf16[32,24,320]{2,1,0:T(8,128)(2,1)}), bf16[32,24,320]{2,1,0:T(8,128)(2,1)S(1)}, u32[]{:S(2)}, u32[]{:S(2)}) async-start(bf16[32,24,320]{2,1,0:T(8,128)(2,1)} %copy.35), calls=%async_computation | async-start | bytes 1179648 | tf_op jit(solution)/shard_map/all_to_all | solution.py:278
  75.1 1.0 fusion.23
  76.3 1.5 %collective-permute-done.8 = f32[272,256]{1,0:T(8,128)S(1)} collective-permute-done((f32[272,256]{1,0:T(8,128)S(1)}, f32[272,256]{1,0:T(8,128)S(1)}, u32[]{:S(2)}, u32[]{:S(2)}) %collective-permute-start.8) | collective-permute-done | bytes 278560 | tf_op jit(solution)/shard_map/ppermute | solution.py:50
  77.8 1.6 %collective-permute-start.9 = (f32[272,256]{1,0:T(8,128)S(1)}, f32[272,256]{1,0:T(8,128)S(1)}, u32[]{:S(2)}, u32[]{:S(2)}) collective-permute-start(f32[272,256]{1,0:T(8,128)S(1)} %add.92), channel_id=1, source_target_pairs={{0,8},{4,12},{8,0},{12,4},{1,9},{5,13},{9,1},{13,5},{2,10},{6,14},... | collective-permute-start | bytes 835592 | tf_op jit(solution)/shard_map/ppermute | solution.py:50
  80.7 5.9 %collective-permute-done.9 = f32[272,256]{1,0:T(8,128)S(1)} collective-permute-done((f32[272,256]{1,0:T(8,128)S(1)}, f32[272,256]{1,0:T(8,128)S(1)}, u32[]{:S(2)}, u32[]{:S(2)}) %collective-permute-start.9) | collective-permute-done | bytes 278560 | tf_op jit(solution)/shard_map/ppermute | solution.py:50
  86.9 2.0 %all-to-all-done = bf16[32,24,320]{2,1,0:T(8,128)(2,1)S(1)} async-done(((bf16[32,24,320]{2,1,0:T(8,128)(2,1)}), bf16[32,24,320]{2,1,0:T(8,128)(2,1)S(1)}, u32[]{:S(2)}, u32[]{:S(2)}) %all-to-all-start) | async-done | bytes 491552 | tf_op jit(solution)/shard_map/all_to_all | solution.py:278
  89.4 1.6 %collective-permute-start.2 = (bf16[4,24,2560]{2,1,0:T(8,128)(2,1)S(1)}, bf16[4,24,2560]{2,1,0:T(8,128)(2,1)S(1)}, u32[]{:S(2)}, u32[]{:S(2)}) collective-permute-start(bf16[4,24,2560]{2,1,0:T(8,128)(2,1)S(1)} %all_to_all.16), channel_id=1, source_target_pairs={{0,8},{4,12},{8,0},{12,4},{1,9},{5,13},{9,1},{13,5},{2,10},{6,14},... | collective-permute-start | bytes 1474568 | tf_op jit(solution)/shard_map/ppermute | solution.py:79
  91.1 8.8 %collective-permute-done.2 = bf16[4,24,2560]{2,1,0:T(8,128)(2,1)S(1)} collective-permute-done((bf16[4,24,2560]{2,1,0:T(8,128)(2,1)S(1)}, bf16[4,24,2560]{2,1,0:T(8,128)(2,1)S(1)}, u32[]{:S(2)}, u32[]{:S(2)}) %collective-permute-start.2) | collective-permute-done | bytes 491552 | tf_op jit(solution)/shard_map/ppermute | solution.py:79
  100.9 5.2 %collective-permute-start.11 = (f32[16,2176]{1,0:T(8,128)S(1)}, f32[16,2176]{1,0:T(8,128)S(1)}, u32[]{:S(2)}, u32[]{:S(2)}) collective-permute-start(f32[16,2176]{1,0:T(8,128)S(1)} %get-tuple-element.17), channel_id=1, source_target_pairs={{1,0},{2,1},{3,2},{16,3},{17,16},{18,17},{19,18},{5,4},{6,5},{7,6}... | collective-permute-start | bytes 417800 | tf_op jit(solution)/shard_map/ppermute | solution.py:29
  106.0 1.9 %collective-permute-start.10 = (f32[16,2176]{1,0:T(8,128)S(1)}, f32[16,2176]{1,0:T(8,128)S(1)}, u32[]{:S(2)}, u32[]{:S(2)}) collective-permute-start(f32[16,2176]{1,0:T(8,128)S(1)} %get-tuple-element.17), channel_id=1, source_target_pairs={{0,1},{1,2},{2,3},{3,16},{16,17},{17,18},{18,19},{4,5},{5,6},{6,7}... | collective-permute-start | bytes 417800 | tf_op jit(solution)/shard_map/ppermute | solution.py:27
  108.6 1.4 %collective-permute-done.11 = f32[16,2176]{1,0:T(8,128)S(1)} collective-permute-done((f32[16,2176]{1,0:T(8,128)S(1)}, f32[16,2176]{1,0:T(8,128)S(1)}, u32[]{:S(2)}, u32[]{:S(2)}) %collective-permute-start.11) | collective-permute-done | bytes 139296 | tf_op jit(solution)/shard_map/ppermute | solution.py:29
  110.0 6.4 %collective-permute-done.10 = f32[16,2176]{1,0:T(8,128)S(1)} collective-permute-done((f32[16,2176]{1,0:T(8,128)S(1)}, f32[16,2176]{1,0:T(8,128)S(1)}, u32[]{:S(2)}, u32[]{:S(2)}) %collective-permute-start.10) | collective-permute-done | bytes 139296 | tf_op jit(solution)/shard_map/ppermute | solution.py:27
  116.5 0.8 reshape.104.tiles_ref
  117.2 5.6 %shard_map.121 = f32[320,1408]{1,0:T(8,128)} custom-call(s32[3520]{0:T(1024)} %fusion.37.slot_ref, s32[1]{0:T(128)} %bitcast.14.base_ref, s32[320,1]{1,0:T(8,128)} %broadcast_in_dim.20.points_ref.limit_ref, f32[816,128]{1,0:T(8,128)} %reshape.104.tiles_ref), custom_call_target="tpu_custom_call" | custom-call | tf_op jit(solution)/shard_map/pallas_call | solution.py:228
  123.1 5.5 %fusion = f32[4,96,384]{2,1,0:T(8,128)} fusion(bf16[4,2560,384]{2,1,0:T(8,128)(2,1)} %param.12, bf16[4,24,2560]{2,1,0:T(8,128)(2,1)S(1)} %get-tuple-element.28, bf16[4,24,2560]{2,1,0:T(8,128)(2,1)S(1)} %get-tuple-element.11, bf16[4,24,2560]{2,1,0:T(8,128)(2,1)S(1)} %get-tuple-element.29, bf16[4,24,2560]{2,1,0:T(8,128)(2,1)S(1)} %get-tuple-element.10), kind=kOutput, calls=%fused_computation | convolution fusion | flops 762839040 | bytes 10420224 | tf_op jit(solution)/shard_map/srj,sjd->srd/dot_general | solution.py:285
  (63 shorter events, 5.7 us)
Async XLA Ops:
  0.6 17.4 %copy-start.3 = (s32[320,11]{0,1:T(8,128)S(1)}, s32[320,11]{0,1:T(8,128)}, u32[]{:S(2)}) copy-start(s32[320,11]{0,1:T(8,128)} %param.14) | copy-start | bytes 42244
  0.6 16.6 %copy-start.6 = (s32[32]{0:T(128)S(1)}, s32[32]{0:T(128)}, u32[]{:S(2)}) copy-start(s32[32]{0:T(128)} %param.11) | copy-start | bytes 388
  0.7 16.6 %copy-start.4 = (s32[320]{0:T(512)S(1)}, s32[320]{0:T(512)}, u32[]{:S(2)}) copy-start(s32[320]{0:T(512)} %param.10) | copy-start | bytes 3844
  0.7 17.4 %copy-start.7 = (bf16[2,6]{1,0:T(2,128)(2,1)S(1)}, bf16[2,6]{1,0:T(2,128)(2,1)}, u32[]{:S(2)}) copy-start(bf16[2,6]{1,0:T(2,128)(2,1)} %param.13) | copy-start | bytes 76
  0.7 18.0 %collective-permute-start = (s32[320,11]{0,1:T(8,128)}, s32[320,11]{0,1:T(8,128)S(1)}, u32[]{:S(2)}, u32[]{:S(2)}) collective-permute-start(s32[320,11]{0,1:T(8,128)} %param.14), channel_id=1, source_target_pairs={{0,4},{4,0},{8,12},{12,8},{1,5},{5,1},{9,13},{13,9},{2,6},{6,2},{1... | collective-permute-start | bytes 42248 | tf_op jit(solution)/shard_map/ppermute | solution.py:62
  1.8 89.2 %collective-permute-start.5 = (f32[2,1,2176]{2,1,0:T(1,128)S(1)}, f32[2,1,2176]{2,1,0:T(1,128)S(1)}, u32[]{:S(2)}, u32[]{:S(2)}) collective-permute-start(f32[2,1,2176]{2,1,0:T(1,128)S(1)} %get-tuple-element.23), channel_id=1, source_target_pairs={{0,1},{1,2},{2,3},{3,16},{16,17},{17,18},{18,19},{4,5},{5,6},{6,7}... | collective-permute-start | bytes 52232 | tf_op jit(solution)/shard_map/ppermute | solution.py:27
  5.3 85.7 %collective-permute-start.4 = (f32[2,1,2176]{2,1,0:T(1,128)S(1)}, f32[2,1,2176]{2,1,0:T(1,128)S(1)}, u32[]{:S(2)}, u32[]{:S(2)}) collective-permute-start(f32[2,1,2176]{2,1,0:T(1,128)S(1)} %get-tuple-element.22), channel_id=1, source_target_pairs={{1,0},{2,1},{3,2},{16,3},{17,16},{18,17},{19,18},{5,4},{6,5},{7,6}... | collective-permute-start | bytes 52232 | tf_op jit(solution)/shard_map/ppermute | solution.py:29
  18.7 4.0 %collective-permute-start.1 = (s32[320,22]{0,1:T(8,128)S(1)}, s32[320,22]{0,1:T(8,128)S(1)}, u32[]{:S(2)}, u32[]{:S(2)}) collective-permute-start(s32[320,22]{0,1:T(8,128)S(1)} %add_select_fusion.5), channel_id=1, source_target_pairs={{0,8},{4,12},{8,0},{12,4},{1,9},{5,13},{9,1},{13,5},{2,10},{6,14},... | collective-permute-start | bytes 84488 | tf_op jit(solution)/shard_map/ppermute | solution.py:62
  60.3 14.8 %collective-permute-start.7 = (f32[272,256]{1,0:T(8,128)S(1)}, f32[272,256]{1,0:T(8,128)S(1)}, u32[]{:S(2)}, u32[]{:S(2)}) collective-permute-start(f32[272,256]{1,0:T(8,128)S(1)} %get-tuple-element.15), channel_id=1, source_target_pairs={{1,0},{2,1},{3,2},{16,3},{17,16},{18,17},{19,18},{5,4},{6,5},{7,6}... | collective-permute-start | bytes 835592 | tf_op jit(solution)/shard_map/ppermute | solution.py:295
  63.1 12.0 %collective-permute-start.6 = (f32[272,256]{1,0:T(8,128)S(1)}, f32[272,256]{1,0:T(8,128)S(1)}, u32[]{:S(2)}, u32[]{:S(2)}) collective-permute-start(f32[272,256]{1,0:T(8,128)S(1)} %get-tuple-element.14), channel_id=1, source_target_pairs={{0,1},{1,2},{2,3},{3,16},{16,17},{17,18},{18,19},{4,5},{5,6},{6,7}... | collective-permute-start | bytes 835592 | tf_op jit(solution)/shard_map/ppermute | solution.py:292
  68.7 10.7 %copy-start.5 = (s32[16,17]{1,0:T(8,128)S(1)}, s32[16,17]{1,0:T(8,128)}, u32[]{:S(2)}) copy-start(s32[16,17]{1,0:T(8,128)} %param.17) | copy-start | bytes 3268
  68.7 10.7 %copy-start = (f32[16,2176]{1,0:T(8,128)S(1)}, f32[16,2176]{1,0:T(8,128)}, u32[]{:S(2)}) copy-start(f32[16,2176]{1,0:T(8,128)} %param.15) | copy-start | bytes 417796
  68.7 10.7 %copy-start.1 = (f32[16,2176]{1,0:T(8,128)S(1)}, f32[16,2176]{1,0:T(8,128)}, u32[]{:S(2)}) copy-start(f32[16,2176]{1,0:T(8,128)} %param.16) | copy-start | bytes 417796
  69.7 19.1 %all-to-all-start = ((bf16[32,24,320]{2,1,0:T(8,128)(2,1)}), bf16[32,24,320]{2,1,0:T(8,128)(2,1)S(1)}, u32[]{:S(2)}, u32[]{:S(2)}) async-start(bf16[32,24,320]{2,1,0:T(8,128)(2,1)} %copy.35), calls=%async_computation | async-start | bytes 1179648 | tf_op jit(solution)/shard_map/all_to_all | solution.py:278
  76.1 1.6 %collective-permute-start.8 = (f32[272,256]{1,0:T(8,128)S(1)}, f32[272,256]{1,0:T(8,128)S(1)}, u32[]{:S(2)}, u32[]{:S(2)}) collective-permute-start(f32[272,256]{1,0:T(8,128)S(1)} %fusion.23), channel_id=1, source_target_pairs={{0,4},{4,0},{8,12},{12,8},{1,5},{5,1},{9,13},{13,9},{2,6},{6,2},{1... | collective-permute-start | bytes 835592 | tf_op jit(solution)/shard_map/ppermute | solution.py:50
  77.8 8.8 %collective-permute-start.9 = (f32[272,256]{1,0:T(8,128)S(1)}, f32[272,256]{1,0:T(8,128)S(1)}, u32[]{:S(2)}, u32[]{:S(2)}) collective-permute-start(f32[272,256]{1,0:T(8,128)S(1)} %add.92), channel_id=1, source_target_pairs={{0,8},{4,12},{8,0},{12,4},{1,9},{5,13},{9,1},{13,5},{2,10},{6,14},... | collective-permute-start | bytes 835592 | tf_op jit(solution)/shard_map/ppermute | solution.py:50
  89.4 10.6 %collective-permute-start.2 = (bf16[4,24,2560]{2,1,0:T(8,128)(2,1)S(1)}, bf16[4,24,2560]{2,1,0:T(8,128)(2,1)S(1)}, u32[]{:S(2)}, u32[]{:S(2)}) collective-permute-start(bf16[4,24,2560]{2,1,0:T(8,128)(2,1)S(1)} %all_to_all.16), channel_id=1, source_target_pairs={{0,8},{4,12},{8,0},{12,4},{1,9},{5,13},{9,1},{13,5},{2,10},{6,14},... | collective-permute-start | bytes 1474568 | tf_op jit(solution)/shard_map/ppermute | solution.py:79
  100.1 22.7 %collective-permute-start.3 = (bf16[4,48,2560]{2,1,0:T(8,128)(2,1)S(1)}, bf16[4,48,2560]{2,1,0:T(8,128)(2,1)S(1)}, u32[]{:S(2)}, u32[]{:S(2)}) collective-permute-start(bf16[4,48,2560]{2,1,0:T(8,128)(2,1)S(1)} %maximum_select_fusion), channel_id=1, source_target_pairs={{0,4},{4,0},{8,12},{12,8},{1,5},{5,1},{9,13},{13,9},{2,6},{6,2},{1... | collective-permute-start | bytes 2949128 | tf_op jit(solution)/shard_map/ppermute | solution.py:85
  100.9 21.9 %copy-start.2 = (f32[16,2176]{1,0:T(8,128)}, f32[16,2176]{1,0:T(8,128)S(1)}, u32[]{:S(2)}) copy-start(f32[16,2176]{1,0:T(8,128)S(1)} %get-tuple-element.17) | copy-start | bytes 417796
  100.9 9.1 %collective-permute-start.11 = (f32[16,2176]{1,0:T(8,128)S(1)}, f32[16,2176]{1,0:T(8,128)S(1)}, u32[]{:S(2)}, u32[]{:S(2)}) collective-permute-start(f32[16,2176]{1,0:T(8,128)S(1)} %get-tuple-element.17), channel_id=1, source_target_pairs={{1,0},{2,1},{3,2},{16,3},{17,16},{18,17},{19,18},{5,4},{6,5},{7,6}... | collective-permute-start | bytes 417800 | tf_op jit(solution)/shard_map/ppermute | solution.py:29
  106.0 10.4 %collective-permute-start.10 = (f32[16,2176]{1,0:T(8,128)S(1)}, f32[16,2176]{1,0:T(8,128)S(1)}, u32[]{:S(2)}, u32[]{:S(2)}) collective-permute-start(f32[16,2176]{1,0:T(8,128)S(1)} %get-tuple-element.17), channel_id=1, source_target_pairs={{0,1},{1,2},{2,3},{3,16},{16,17},{17,18},{18,19},{4,5},{5,6},{6,7}... | collective-permute-start | bytes 417800 | tf_op jit(solution)/shard_map/ppermute | solution.py:27

commit v11 on v7

--- a/solution.py
+++ b/solution.py
@@ -68,6 +68,29 @@
         )
         stride *= 2
     return values
+
+
+def lev_pair_far(values):
+    index = lax.axis_index("lev")
+    other = lax.ppermute(values, "lev", [(i, i ^ 2) for i in range(4)])
+    return jnp.where(
+        (index // 2) % 2 == 1,
+        jnp.concatenate([other, values], axis=1),
+        jnp.concatenate([values, other], axis=1),
+    )
+
+
+def lev_pair_near(pair, size):
+    index = lax.axis_index("lev")
+    far = lax.ppermute(pair, "lev", [(i, i ^ 1) for i in range(4)])
+    even = index % 2 == 0
+    first = jnp.where(even, pair, far)
+    second = jnp.where(even, far, pair)
+    parts = []
+    for half in range(2):
+        parts.append(first[:, half * size : (half + 1) * size])
+        parts.append(second[:, half * size : (half + 1) * size])
+    return jnp.concatenate(parts, axis=1)
 
 
 def row_block(rows):
@@ -259,12 +282,6 @@
         concat_axis=2,
         tiled=True,
     )
-    spectra = jnp.einsum(
-        "srj,sjd->srd",
-        lev_gather(regrouped, 1),
-        legendre,
-        preferred_element_type=jnp.float32,
-    )
     band_count = lax.axis_size(("lat", "ocn"))
     from_prev = lax.ppermute(
         sections[2], ("lat", "ocn"), [(i, i + 1) for i in range(band_count - 1)]
@@ -300,6 +317,18 @@
     tiles_near = returned.reshape(3 * tile_count, BLOCK)
     base = (lax.axis_index("lev") * quarter).astype(jnp.int32).reshape(1)
     surface_temp = surface_gather(local_slot, base, lat_points, tiles_near, quarter)
+    if lax.axis_size("lev") == 4:
+        pair = lev_pair_far(regrouped)
+        pair, surface_temp = lax.optimization_barrier((pair, surface_temp))
+        gathered = lev_pair_near(pair, regrouped.shape[1])
+    else:
+        gathered = lev_gather(regrouped, 1)
+    spectra = jnp.einsum(
+        "srj,sjd->srd",
+        gathered,
+        legendre,
+        preferred_element_type=jnp.float32,
+    )
     return (spectra, temp_next, salt_next, surface_temp)
 
 

time: 124 us -> 131 us (1.056)
  the two profiles are of different devices: /device:TPU:0 before, /device:TPU:4 now
where the time goes in v11:
time: 131 us; the launch traced here: 128 us
  Pallas kernels  41.1 us (31%)
  starting transfers between devices  33.9 us (26%)
  waiting for transfers between devices  22.8 us (17%)
  other arithmetic  15.1 us (12%)
  local copies, waits for them, and re-layouts  8.89 us (7%)
  matrix products  5.54 us (4%)
    pallas_call x1, Pallas kernels, fused_transform(): pl.pallas_call(transform_kernel, grid=(steps,), in_specs=[pl.BlockSpec((r...  35.5 us
    ppermute x2, starting transfers between devices, with_halo(): lax.ppermute(head, axis, [((i + 1) % count, i) for i in range(ends)])  10.6 us
    all_to_all x1, waiting for transfers between devices, body(): lax.all_to_all(coeffs.transpose(4, 1, 0, 3, 2).reshape(wave_count, lev_de...  9.47 us
    all_to_all x1, starting transfers between devices, body(): lax.all_to_all(coeffs.transpose(4, 1, 0, 3, 2).reshape(wave_count, lev_de...  6.72 us
    ppermute x1, starting transfers between devices, body(): lax.ppermute(sections[0], ('lat', 'ocn'), [(i + 1, i) for i in range(band...  6.59 us
    ppermute x1, waiting for transfers between devices, body(): lax.ppermute(sections[2], ('lat', 'ocn'), [(i, i + 1) for i in range(band...  5.62 us
    pallas_call x1, Pallas kernels, surface_gather(): pl.pallas_call(surface_kernel, in_specs=[pl.BlockSpec(memory_space=pltpu....  5.56 us
    dot_general x1, matrix products, body(): jnp.einsum('srj,sjd->srd', gathered, legendre, preferred_element_type=jnp...  5.54 us
  transfers between devices with their start and end apart: 13, of which 6 were waited for; matrix products, arithmetic and copies ran while one was open for 18% of the time, Pallas kernels for 32%

profile of v11, /device:TPU:4, one launch (start us, length us, event | category | flops | bytes accessed | tf_op | source)
XLA Modules:
  0.0 128.3 jit_solution(10688712398357147983)
XLA Ops:
  0.7 1.6 %fusion.30 = (f32[2,1,2176]{2,1,0:T(1,128)}, f32[2,1,2176]{2,1,0:T(1,128)}) fusion(f32[1,16,2176]{2,1,0:T(8,128)} %bitcast.43, f32[1,16,2176]{2,1,0:T(8,128)} %bitcast.47), kind=kLoop, calls=%fused_computation.75 | loop fusion | flops 8704 | bytes 313344 | tf_op jit(solution)/shard_map/stack | solution.py:304
  2.4 5.4 %collective-permute-start.3 = (f32[2,1,2176]{2,1,0:T(1,128)}, f32[2,1,2176]{2,1,0:T(1,128)}, u32[]{:S(2)}, u32[]{:S(2)}) collective-permute-start(f32[2,1,2176]{2,1,0:T(1,128)} %get-tuple-element.26), channel_id=1, source_target_pairs={{1,0},{2,1},{3,2},{16,3},{17,16},{18,17},{19,18},{5,4},{6,5},{7,6}... | collective-permute-start | bytes 52232 | tf_op jit(solution)/shard_map/ppermute | solution.py:29
  7.8 1.9 %collective-permute-start.4 = (f32[2,1,2176]{2,1,0:T(1,128)}, f32[2,1,2176]{2,1,0:T(1,128)}, u32[]{:S(2)}, u32[]{:S(2)}) collective-permute-start(f32[2,1,2176]{2,1,0:T(1,128)} %get-tuple-element.27), channel_id=1, source_target_pairs={{0,1},{1,2},{2,3},{3,16},{16,17},{17,18},{18,19},{4,5},{5,6},{6,7}... | collective-permute-start | bytes 52232 | tf_op jit(solution)/shard_map/ppermute | solution.py:27
  9.7 0.8 sign_compare_fusion.1
  10.5 2.0 %fusion.15 = (f32[2,16,2175]{2,1,0:T(8,128)}, f32[2,16,2175]{2,1,0:T(8,128)}) fusion(f32[1,16,2176]{2,1,0:T(8,128)} %bitcast.44, f32[1,16,2176]{2,1,0:T(8,128)} %bitcast.48), kind=kLoop, calls=%fused_computation.39 | loop fusion | flops 139200 | bytes 835328 | tf_op jit(solution)/shard_map/stack | solution.py:304
  12.5 4.0 %cosine_convert_fusion = (bf16[32,5632]{1,0:T(8,128)(2,1)S(1)}, bf16[32,5632]{1,0:T(8,128)(2,1)S(1)}) fusion(s32[32]{0:T(128)} %param.11), kind=kLoop, calls=%fused_computation.17 | loop fusion | flops 2162688 | bytes 721024 | tf_op jit(solution)/shard_map/convert
  16.5 0.9 pad_maximum_fusion.table_ref
  17.5 0.8 broadcast_in_dim.20.points_ref.limit_ref
  18.9 1.6 %collective-permute-start.1 = (s32[320,22]{0,1:T(8,128)S(1)}, s32[320,22]{0,1:T(8,128)S(1)}, u32[]{:S(2)}, u32[]{:S(2)}) collective-permute-start(s32[320,22]{0,1:T(8,128)S(1)} %add_select_fusion.5), channel_id=1, source_target_pairs={{0,8},{4,12},{8,0},{12,4},{1,9},{5,13},{9,1},{13,5},{2,10},{6,14},... | collective-permute-start | bytes 84488 | tf_op jit(solution)/shard_map/ppermute | solution.py:62
  20.5 2.4 %collective-permute-done.1 = s32[320,22]{0,1:T(8,128)S(1)} collective-permute-done((s32[320,22]{0,1:T(8,128)S(1)}, s32[320,22]{0,1:T(8,128)S(1)}, u32[]{:S(2)}, u32[]{:S(2)}) %collective-permute-start.1) | collective-permute-done | bytes 28192 | tf_op jit(solution)/shard_map/ppermute | solution.py:62
  23.2 0.7 reshape.98.slot_ref
  24.0 35.5 %shard_map.120 = (f32[2,6,320,64]{3,2,1,0:T(8,128)}, f32[3,272,256]{2,1,0:T(8,128)}) custom-call(s32[320,1]{1,0:T(8,128)} %broadcast_in_dim.20.points_ref.limit_ref, bf16[2,6,320,5632]{3,2,1,0:T(8,128)(2,1)} %cells_ref.1, bf16[64,5632]{1,0:T(8,128)(2,1)} %pad_maximum_fusion.table_ref, f32[2,6]{1,0:T(2,128)} %convert_element_type.23.weight_ref, ...), custom_call_target="tpu_custom_call" | custom-call | tf_op jit(solution)/shard_map/pallas_call | solution.py:181
  59.5 1.1 slice_bitcast_fusion.1
  60.6 2.1 %collective-permute-start.5 = (f32[272,256]{1,0:T(8,128)S(1)}, f32[272,256]{1,0:T(8,128)S(1)}, u32[]{:S(2)}, u32[]{:S(2)}) collective-permute-start(f32[272,256]{1,0:T(8,128)S(1)} %get-tuple-element.18), channel_id=1, source_target_pairs={{0,1},{1,2},{2,3},{3,16},{16,17},{17,18},{18,19},{4,5},{5,6},{6,7}... | collective-permute-start | bytes 835592 | tf_op jit(solution)/shard_map/ppermute | solution.py:286
  62.7 6.6 %collective-permute-start.6 = (f32[272,256]{1,0:T(8,128)S(1)}, f32[272,256]{1,0:T(8,128)S(1)}, u32[]{:S(2)}, u32[]{:S(2)}) collective-permute-start(f32[272,256]{1,0:T(8,128)S(1)} %get-tuple-element.19), channel_id=1, source_target_pairs={{1,0},{2,1},{3,2},{16,3},{17,16},{18,17},{19,18},{5,4},{6,5},{7,6}... | collective-permute-start | bytes 835592 | tf_op jit(solution)/shard_map/ppermute | solution.py:289
  69.4 5.6 %collective-permute-done.5 = f32[272,256]{1,0:T(8,128)S(1)} collective-permute-done((f32[272,256]{1,0:T(8,128)S(1)}, f32[272,256]{1,0:T(8,128)S(1)}, u32[]{:S(2)}, u32[]{:S(2)}) %collective-permute-start.5) | collective-permute-done | bytes 278560 | tf_op jit(solution)/shard_map/ppermute | solution.py:286
  75.1 1.0 fusion.23
  76.2 1.5 %collective-permute-done.7 = f32[272,256]{1,0:T(8,128)S(1)} collective-permute-done((f32[272,256]{1,0:T(8,128)S(1)}, f32[272,256]{1,0:T(8,128)S(1)}, u32[]{:S(2)}, u32[]{:S(2)}) %collective-permute-start.7) | collective-permute-done | bytes 278560 | tf_op jit(solution)/shard_map/ppermute | solution.py:50
  77.7 0.7 add.95
  78.4 1.5 %collective-permute-start.8 = (f32[272,256]{1,0:T(8,128)}, f32[272,256]{1,0:T(8,128)}, u32[]{:S(2)}, u32[]{:S(2)}) collective-permute-start(f32[272,256]{1,0:T(8,128)} %add.95), channel_id=1, source_target_pairs={{0,8},{4,12},{8,0},{12,4},{1,9},{5,13},{9,1},{13,5},{2,10},{6,14},... | collective-permute-start | bytes 835592 | tf_op jit(solution)/shard_map/ppermute | solution.py:50
  82.7 1.0 copy.35
  83.8 6.7 %all-to-all-start = ((bf16[32,24,320]{2,1,0:T(8,128)(2,1)}), bf16[32,24,320]{2,1,0:T(8,128)(2,1)S(1)}, u32[]{:S(2)}, u32[]{:S(2)}) async-start(bf16[32,24,320]{2,1,0:T(8,128)(2,1)} %copy.35), calls=%async_computation | async-start | bytes 1179648 | tf_op jit(solution)/shard_map/all_to_all | solution.py:278
  90.5 1.1 add.96
  91.9 0.9 fusion.22
  93.5 5.2 %collective-permute-start.10 = (f32[16,2176]{1,0:T(8,128)S(1)}, f32[16,2176]{1,0:T(8,128)S(1)}, u32[]{:S(2)}, u32[]{:S(2)}) collective-permute-start(f32[16,2176]{1,0:T(8,128)S(1)} %get-tuple-element.21), channel_id=1, source_target_pairs={{1,0},{2,1},{3,2},{16,3},{17,16},{18,17},{19,18},{5,4},{6,5},{7,6}... | collective-permute-start | bytes 417800 | tf_op jit(solution)/shard_map/ppermute | solution.py:29
  98.6 2.1 %collective-permute-start.9 = (f32[16,2176]{1,0:T(8,128)S(1)}, f32[16,2176]{1,0:T(8,128)S(1)}, u32[]{:S(2)}, u32[]{:S(2)}) collective-permute-start(f32[16,2176]{1,0:T(8,128)S(1)} %get-tuple-element.21), channel_id=1, source_target_pairs={{0,1},{1,2},{2,3},{3,16},{16,17},{17,18},{18,19},{4,5},{5,6},{6,7}... | collective-permute-start | bytes 417800 | tf_op jit(solution)/shard_map/ppermute | solution.py:27
  100.7 9.5 %all-to-all-done = bf16[32,24,320]{2,1,0:T(8,128)(2,1)S(1)} async-done(((bf16[32,24,320]{2,1,0:T(8,128)(2,1)}), bf16[32,24,320]{2,1,0:T(8,128)(2,1)S(1)}, u32[]{:S(2)}, u32[]{:S(2)}) %all-to-all-start) | async-done | bytes 491552 | tf_op jit(solution)/shard_map/all_to_all | solution.py:278
  112.1 0.8 reshape.104.tiles_ref
  112.9 5.6 %shard_map.121 = f32[320,1408]{1,0:T(8,128)} custom-call(s32[3520]{0:T(1024)} %fusion.37.slot_ref, s32[1]{0:T(128)} %bitcast.6.base_ref, s32[320,1]{1,0:T(8,128)} %broadcast_in_dim.20.points_ref.limit_ref, f32[816,128]{1,0:T(8,128)} %reshape.104.tiles_ref), custom_call_target="tpu_custom_call" | custom-call | tf_op jit(solution)/shard_map/pallas_call | solution.py:228
  118.4 1.3 collective-permute-done.2
  119.9 2.5 %collective-permute-done.11 = bf16[4,48,2560]{2,1,0:T(8,128)(2,1)S(1)} collective-permute-done((bf16[4,48,2560]{2,1,0:T(8,128)(2,1)S(1)}, bf16[4,48,2560]{2,1,0:T(8,128)(2,1)S(1)}, u32[]{:S(2)}, u32[]{:S(2)}) %collective-permute-start.11) | collective-permute-done | bytes 983072 | tf_op jit(solution)/shard_map/ppermute | solution.py:85
  122.8 5.5 %fusion = f32[4,96,384]{2,1,0:T(8,128)} fusion(bf16[4,2560,384]{2,1,0:T(8,128)(2,1)} %param.12, bf16[4,24,2560]{2,1,0:T(8,128)(2,1)S(1)} %get-tuple-element.32, bf16[4,24,2560]{2,1,0:T(8,128)(2,1)S(1)} %get-tuple-element.15, bf16[4,24,2560]{2,1,0:T(8,128)(2,1)S(1)} %get-tuple-element.33, bf16[4,24,2560]{2,1,0:T(8,128)(2,1)S(1)} %get-tuple-element.14), kind=kOutput, calls=%fused_computation | convolution fusion | flops 762839040 | bytes 10420224 | tf_op jit(solution)/shard_map/srj,sjd->srd/dot_general | solution.py:326
  (71 shorter events, 7.4 us)
Async XLA Ops:
  0.6 16.8 %copy-start.7 = (s32[320,11]{0,1:T(8,128)S(1)}, s32[320,11]{0,1:T(8,128)}, u32[]{:S(2)}) copy-start(s32[320,11]{0,1:T(8,128)} %param.14) | copy-start | bytes 42244
  0.6 16.8 %copy-start.8 = (s32[320]{0:T(512)S(1)}, s32[320]{0:T(512)}, u32[]{:S(2)}) copy-start(s32[320]{0:T(512)} %param.10) | copy-start | bytes 3844
  0.7 17.6 %copy-start.11 = (bf16[2,6]{1,0:T(2,128)(2,1)S(1)}, bf16[2,6]{1,0:T(2,128)(2,1)}, u32[]{:S(2)}) copy-start(bf16[2,6]{1,0:T(2,128)(2,1)} %param.13) | copy-start | bytes 76
  0.7 18.2 %collective-permute-start = (s32[320,11]{0,1:T(8,128)}, s32[320,11]{0,1:T(8,128)S(1)}, u32[]{:S(2)}, u32[]{:S(2)}) collective-permute-start(s32[320,11]{0,1:T(8,128)} %param.14), channel_id=1, source_target_pairs={{0,4},{4,0},{8,12},{12,8},{1,5},{5,1},{9,13},{13,9},{2,6},{6,2},{1... | collective-permute-start | bytes 42248 | tf_op jit(solution)/shard_map/ppermute | solution.py:62
  2.4 89.5 %collective-permute-start.3 = (f32[2,1,2176]{2,1,0:T(1,128)}, f32[2,1,2176]{2,1,0:T(1,128)}, u32[]{:S(2)}, u32[]{:S(2)}) collective-permute-start(f32[2,1,2176]{2,1,0:T(1,128)} %get-tuple-element.26), channel_id=1, source_target_pairs={{1,0},{2,1},{3,2},{16,3},{17,16},{18,17},{19,18},{5,4},{6,5},{7,6}... | collective-permute-start | bytes 52232 | tf_op jit(solution)/shard_map/ppermute | solution.py:29
  7.8 84.0 %collective-permute-start.4 = (f32[2,1,2176]{2,1,0:T(1,128)}, f32[2,1,2176]{2,1,0:T(1,128)}, u32[]{:S(2)}, u32[]{:S(2)}) collective-permute-start(f32[2,1,2176]{2,1,0:T(1,128)} %get-tuple-element.27), channel_id=1, source_target_pairs={{0,1},{1,2},{2,3},{3,16},{16,17},{17,18},{18,19},{4,5},{5,6},{6,7}... | collective-permute-start | bytes 52232 | tf_op jit(solution)/shard_map/ppermute | solution.py:27
  18.9 4.0 %collective-permute-start.1 = (s32[320,22]{0,1:T(8,128)S(1)}, s32[320,22]{0,1:T(8,128)S(1)}, u32[]{:S(2)}, u32[]{:S(2)}) collective-permute-start(s32[320,22]{0,1:T(8,128)S(1)} %add_select_fusion.5), channel_id=1, source_target_pairs={{0,8},{4,12},{8,0},{12,4},{1,9},{5,13},{9,1},{13,5},{2,10},{6,14},... | collective-permute-start | bytes 84488 | tf_op jit(solution)/shard_map/ppermute | solution.py:62
  24.0 45.4 %copy-start.10 = (s32[32]{0:T(128)S(1)}, s32[32]{0:T(128)}, u32[]{:S(2)}) copy-start(s32[32]{0:T(128)} %param.11) | copy-start | bytes 388
  59.5 16.7 %copy-start.9 = (s32[16,17]{1,0:T(8,128)S(1)}, s32[16,17]{1,0:T(8,128)}, u32[]{:S(2)}) copy-start(s32[16,17]{1,0:T(8,128)} %param.17) | copy-start | bytes 3268
  59.5 20.4 %copy-start = (f32[16,2176]{1,0:T(8,128)S(1)}, f32[16,2176]{1,0:T(8,128)}, u32[]{:S(2)}) copy-start(f32[16,2176]{1,0:T(8,128)} %param.15) | copy-start | bytes 417796
  59.5 20.4 %copy-start.1 = (f32[16,2176]{1,0:T(8,128)S(1)}, f32[16,2176]{1,0:T(8,128)}, u32[]{:S(2)}) copy-start(f32[16,2176]{1,0:T(8,128)} %param.16) | copy-start | bytes 417796
  60.6 21.2 %copy-start.2 = (f32[2,6,320,64]{3,2,1,0:T(8,128)S(1)}, f32[2,6,320,64]{3,2,1,0:T(8,128)}, u32[]{:S(2)}) copy-start(f32[2,6,320,64]{3,2,1,0:T(8,128)} %get-tuple-element.8) | copy-start | bytes 2949124
  60.6 14.4 %collective-permute-start.5 = (f32[272,256]{1,0:T(8,128)S(1)}, f32[272,256]{1,0:T(8,128)S(1)}, u32[]{:S(2)}, u32[]{:S(2)}) collective-permute-start(f32[272,256]{1,0:T(8,128)S(1)} %get-tuple-element.18), channel_id=1, source_target_pairs={{0,1},{1,2},{2,3},{3,16},{16,17},{17,18},{18,19},{4,5},{5,6},{6,7}... | collective-permute-start | bytes 835592 | tf_op jit(solution)/shard_map/ppermute | solution.py:286
  62.7 12.3 %collective-permute-start.6 = (f32[272,256]{1,0:T(8,128)S(1)}, f32[272,256]{1,0:T(8,128)S(1)}, u32[]{:S(2)}, u32[]{:S(2)}) collective-permute-start(f32[272,256]{1,0:T(8,128)S(1)} %get-tuple-element.19), channel_id=1, source_target_pairs={{1,0},{2,1},{3,2},{16,3},{17,16},{18,17},{19,18},{5,4},{6,5},{7,6}... | collective-permute-start | bytes 835592 | tf_op jit(solution)/shard_map/ppermute | solution.py:289
  76.1 1.6 %collective-permute-start.7 = (f32[272,256]{1,0:T(8,128)S(1)}, f32[272,256]{1,0:T(8,128)S(1)}, u32[]{:S(2)}, u32[]{:S(2)}) collective-permute-start(f32[272,256]{1,0:T(8,128)S(1)} %fusion.23), channel_id=1, source_target_pairs={{0,4},{4,0},{8,12},{12,8},{1,5},{5,1},{9,13},{13,9},{2,6},{6,2},{1... | collective-permute-start | bytes 835592 | tf_op jit(solution)/shard_map/ppermute | solution.py:50
  78.4 12.0 %collective-permute-start.8 = (f32[272,256]{1,0:T(8,128)}, f32[272,256]{1,0:T(8,128)}, u32[]{:S(2)}, u32[]{:S(2)}) collective-permute-start(f32[272,256]{1,0:T(8,128)} %add.95), channel_id=1, source_target_pairs={{0,8},{4,12},{8,0},{12,4},{1,9},{5,13},{9,1},{13,5},{2,10},{6,14},... | collective-permute-start | bytes 835592 | tf_op jit(solution)/shard_map/ppermute | solution.py:50
  83.7 8.1 %copy-start.3 = (f32[2,16,2175]{2,1,0:T(8,128)S(1)}, f32[2,16,2175]{2,1,0:T(8,128)}, u32[]{:S(2)}) copy-start(f32[2,16,2175]{2,1,0:T(8,128)} %get-tuple-element.22) | copy-start | bytes 835204
  83.8 8.1 %copy-start.4 = (f32[2,16,2175]{2,1,0:T(8,128)S(1)}, f32[2,16,2175]{2,1,0:T(8,128)}, u32[]{:S(2)}) copy-start(f32[2,16,2175]{2,1,0:T(8,128)} %get-tuple-element.23) | copy-start | bytes 835204
  83.8 8.1 %copy-start.6 = (f32[2,8,17,128]{3,1,2,0:T(8,128)S(1)}, f32[2,8,17,128]{3,1,2,0:T(8,128)}, u32[]{:S(2)}) copy-start(f32[2,8,17,128]{3,1,2,0:T(8,128)} %copy.46) | copy-start | bytes 417796
  83.8 26.5 %all-to-all-start = ((bf16[32,24,320]{2,1,0:T(8,128)(2,1)}), bf16[32,24,320]{2,1,0:T(8,128)(2,1)S(1)}, u32[]{:S(2)}, u32[]{:S(2)}) async-start(bf16[32,24,320]{2,1,0:T(8,128)(2,1)} %copy.35), calls=%async_computation | async-start | bytes 1179648 | tf_op jit(solution)/shard_map/all_to_all | solution.py:278
  93.5 19.4 %copy-start.5 = (f32[16,2176]{1,0:T(8,128)}, f32[16,2176]{1,0:T(8,128)S(1)}, u32[]{:S(2)}) copy-start(f32[16,2176]{1,0:T(8,128)S(1)} %get-tuple-element.21) | copy-start | bytes 417796
  93.5 18.6 %collective-permute-start.10 = (f32[16,2176]{1,0:T(8,128)S(1)}, f32[16,2176]{1,0:T(8,128)S(1)}, u32[]{:S(2)}, u32[]{:S(2)}) collective-permute-start(f32[16,2176]{1,0:T(8,128)S(1)} %get-tuple-element.21), channel_id=1, source_target_pairs={{1,0},{2,1},{3,2},{16,3},{17,16},{18,17},{19,18},{5,4},{6,5},{7,6}... | collective-permute-start | bytes 417800 | tf_op jit(solution)/shard_map/ppermute | solution.py:29
  98.6 13.4 %collective-permute-start.9 = (f32[16,2176]{1,0:T(8,128)S(1)}, f32[16,2176]{1,0:T(8,128)S(1)}, u32[]{:S(2)}, u32[]{:S(2)}) collective-permute-start(f32[16,2176]{1,0:T(8,128)S(1)} %get-tuple-element.21), channel_id=1, source_target_pairs={{0,1},{1,2},{2,3},{3,16},{16,17},{17,18},{18,19},{4,5},{5,6},{6,7}... | collective-permute-start | bytes 417800 | tf_op jit(solution)/shard_map/ppermute | solution.py:27
  110.8 8.9 %collective-permute-start.2 = (bf16[4,24,2560]{2,1,0:T(8,128)(2,1)S(1)}, bf16[4,24,2560]{2,1,0:T(8,128)(2,1)S(1)}, u32[]{:S(2)}, u32[]{:S(2)}) collective-permute-start(bf16[4,24,2560]{2,1,0:T(8,128)(2,1)S(1)} %all_to_all.16), channel_id=1, source_target_pairs={{0,8},{4,12},{8,0},{12,4},{1,9},{5,13},{9,1},{13,5},{2,10},{6,14},... | collective-permute-start | bytes 1474568 | tf_op jit(solution)/shard_map/ppermute | solution.py:75
  119.8 2.6 %collective-permute-start.11 = (bf16[4,48,2560]{2,1,0:T(8,128)(2,1)S(1)}, bf16[4,48,2560]{2,1,0:T(8,128)(2,1)S(1)}, u32[]{:S(2)}, u32[]{:S(2)}) collective-permute-start(bf16[4,48,2560]{2,1,0:T(8,128)(2,1)S(1)} %maximum_select_fusion), channel_id=1, source_target_pairs={{0,4},{4,0},{8,12},{12,8},{1,5},{5,1},{9,13},{13,9},{2,6},{6,2},{1... | collective-permute-start | bytes 2949128 | tf_op jit(solution)/shard_map/ppermute | solution.py:85

commit v12 on v7

--- a/solution.py
+++ b/solution.py
@@ -77,7 +77,9 @@
     return rows
 
 
-def transform_kernel(points_ref, cells_ref, table_ref, weight_ref, slot_ref, sums_ref, out_ref, acc_ref, *scratch):
+def transform_kernel(
+    points_ref, cells_ref, table_ref, weight_ref, slot_ref, scale_ref, sums_ref, out_ref, acc_ref, *scratch
+):
     step = pl.program_id(0)
 
     @pl.when(step == 0)
@@ -97,13 +99,16 @@
             (((1,), (1,)), ((), ())),
             preferred_element_type=jnp.float32,
         )
-        sums_ref[...] = sums.reshape(sums_ref.shape)
+        sums_ref[...] = (sums.reshape(sums_ref.shape) * scale_ref[...][None, None]).astype(sums_ref.dtype)
     else:
         for f in range(nfields):
             for l in range(nlev):
-                sums_ref[f, l] = lax.dot_general(
-                    cells[f, l], table, (((1,), (1,)), ((), ())), preferred_element_type=jnp.float32
-                )
+                sums_ref[f, l] = (
+                    lax.dot_general(
+                        cells[f, l], table, (((1,), (1,)), ((), ())), preferred_element_type=jnp.float32
+                    )
+                    * scale_ref[...]
+                ).astype(sums_ref.dtype)
     pieces = []
     for f in range(nfields):
         flux = weight_ref[f, 0] * cells[f, 0].astype(jnp.float32)
@@ -145,7 +150,7 @@
                 out_ref[s, :, f * BLOCK : (f + 1) * BLOCK] = high + low
 
 
-def fused_transform(atmos_fields, lat_points, table, column_weight, slots, nslot):
+def fused_transform(atmos_fields, lat_points, table, column_weight, slots, scale, nslot):
     nfields, nlev, lat_band, lon_count = atmos_fields.shape
     rows = row_block(lat_band)
     steps = lat_band // rows
@@ -164,18 +169,19 @@
             pl.BlockSpec((wave2, lon_count), lambda r: (0, 0)),
             pl.BlockSpec(memory_space=pltpu.SMEM),
             pl.BlockSpec((1, 1, nblocks * rows), lambda r: (r, 0, 0)),
+            pl.BlockSpec((rows, wave2), lambda r: (r, 0)),
         ],
         out_specs=[
             pl.BlockSpec((nfields, nlev, rows, wave2), lambda r: (0, 0, r, 0)),
             pl.BlockSpec((3, nslot // 3, nfields * BLOCK), lambda r: (0, 0, 0)),
         ],
         out_shape=[
-            jax.ShapeDtypeStruct((nfields, nlev, lat_band, wave2), jnp.float32),
+            jax.ShapeDtypeStruct((nfields, nlev, lat_band, wave2), jnp.bfloat16),
             jax.ShapeDtypeStruct((3, nslot // 3, nfields * BLOCK), jnp.float32),
         ],
         scratch_shapes=scratch,
         compiler_params=pltpu.CompilerParams(dimension_semantics=("arbitrary",)),
-    )(lat_points[:, None], atmos_fields, table, column_weight.astype(jnp.float32), slot_rows)
+    )(lat_points[:, None], atmos_fields, table, column_weight.astype(jnp.float32), slot_rows, scale)
 
 
 def surface_kernel(slot_ref, base_ref, limit_ref, tiles_ref, out_ref):
@@ -248,10 +254,16 @@
     full_remap = lev_gather(block_remap, 1)
     every_slot = slot_of(full_remap)
     raw_sums, sections = fused_transform(
-        atmos_fields, lat_points, table, column_weight, every_slot, 3 * tile_count
+        atmos_fields,
+        lat_points,
+        table,
+        column_weight,
+        every_slot,
+        jnp.concatenate([weights, weights], axis=1),
+        3 * tile_count,
     )
     raw_sums = raw_sums.reshape(field_count, lev_dev, lat_band, 2, wave_count)
-    coeffs = (raw_sums * weights[None, None, :, None, :]).astype(jnp.bfloat16)
+    coeffs = raw_sums
     regrouped = lax.all_to_all(
         coeffs.transpose(4, 1, 0, 3, 2).reshape(wave_count, lev_dev * field_count * 2, lat_band),
         ("lat", "ocn"),

time: 124 us -> 123 us (level)
  the two profiles are of different devices: /device:TPU:0 before, /device:TPU:4 now
where the time goes in v12:
time: 123 us; the launch traced here: 121 us
  Pallas kernels  41.1 us (33%)
  starting transfers between devices  30.9 us (25%)
  waiting for transfers between devices  22 us (18%)
  other arithmetic  12.8 us (10%)
  local copies, waits for them, and re-layouts  7.81 us (6%)
  matrix products  5.53 us (4%)
    pallas_call x1, Pallas kernels, fused_transform(): pl.pallas_call(transform_kernel, grid=(steps,), in_specs=[pl.BlockSpec((r...  35.5 us
    ppermute x2, starting transfers between devices, with_halo(): lax.ppermute(tail, axis, [(i, (i + 1) % count) for i in range(ends)])  7.61 us
    ppermute x2, waiting for transfers between devices, lev_sum(): lax.ppermute(values, 'lev', [(i, i ^ stride) for i in range(count)])  7.42 us
    ppermute x2, starting transfers between devices, with_halo(): lax.ppermute(head, axis, [((i + 1) % count, i) for i in range(ends)])  7.22 us
    ppermute x4, waiting for transfers between devices, lev_gather(): other = lax.ppermute(values, 'lev', [(i, i ^ stride) for i in range(count)])  6.57 us
    pallas_call x1, Pallas kernels, surface_gather(): pl.pallas_call(surface_kernel, in_specs=[pl.BlockSpec(memory_space=pltpu....  5.56 us
    dot_general x1, matrix products, body(): jnp.einsum('srj,sjd->srd', lev_gather(regrouped, 1), legendre, preferred_...  5.53 us
    all_to_all x1, starting transfers between devices, body(): lax.all_to_all(coeffs.transpose(4, 1, 0, 3, 2).reshape(wave_count, lev_de...  5.38 us
  transfers between devices with their start and end apart: 13, of which 8 were waited for; matrix products, arithmetic and copies ran while one was open for 17% of the time, Pallas kernels for 34%

profile of v12, /device:TPU:4, one launch (start us, length us, event | category | flops | bytes accessed | tf_op | source)
XLA Modules:
  0.0 121.2 jit_solution(428517658792818527)
XLA Ops:
  0.7 1.6 %fusion.28 = (f32[2,1,2176]{2,1,0:T(1,128)}, f32[2,1,2176]{2,1,0:T(1,128)}) fusion(f32[1,16,2176]{2,1,0:T(8,128)} %bitcast.43, f32[1,16,2176]{2,1,0:T(8,128)} %bitcast.47), kind=kLoop, calls=%fused_computation.72 | loop fusion | flops 8704 | bytes 313344 | tf_op jit(solution)/shard_map/stack | solution.py:299
  2.4 3.5 %collective-permute-start.5 = (f32[2,1,2176]{2,1,0:T(1,128)}, f32[2,1,2176]{2,1,0:T(1,128)}, u32[]{:S(2)}, u32[]{:S(2)}) collective-permute-start(f32[2,1,2176]{2,1,0:T(1,128)} %get-tuple-element.17), channel_id=1, source_target_pairs={{0,1},{1,2},{2,3},{3,16},{16,17},{17,18},{18,19},{4,5},{5,6},{6,7}... | collective-permute-start | bytes 52232 | tf_op jit(solution)/shard_map/ppermute | solution.py:27
  5.8 5.1 %collective-permute-start.4 = (f32[2,1,2176]{2,1,0:T(1,128)}, f32[2,1,2176]{2,1,0:T(1,128)}, u32[]{:S(2)}, u32[]{:S(2)}) collective-permute-start(f32[2,1,2176]{2,1,0:T(1,128)} %get-tuple-element.16), channel_id=1, source_target_pairs={{1,0},{2,1},{3,2},{16,3},{17,16},{18,17},{19,18},{5,4},{6,5},{7,6}... | collective-permute-start | bytes 52232 | tf_op jit(solution)/shard_map/ppermute | solution.py:29
  10.9 4.0 %cosine_convert_fusion = (bf16[32,5632]{1,0:T(8,128)(2,1)S(1)}, bf16[32,5632]{1,0:T(8,128)(2,1)S(1)}) fusion(s32[32]{0:T(128)} %param.11), kind=kLoop, calls=%fused_computation.14 | loop fusion | flops 2162688 | bytes 721024 | tf_op jit(solution)/shard_map/convert
  16.3 0.9 pad_maximum_fusion.table_ref
  17.4 0.8 pad_maximum_fusion.7.scale_ref
  18.2 0.8 broadcast_in_dim.32.points_ref.limit_ref
  19.7 1.6 %collective-permute-start.1 = (s32[320,22]{0,1:T(8,128)S(1)}, s32[320,22]{0,1:T(8,128)S(1)}, u32[]{:S(2)}, u32[]{:S(2)}) collective-permute-start(s32[320,22]{0,1:T(8,128)S(1)} %add_select_fusion.5), channel_id=1, source_target_pairs={{0,8},{4,12},{8,0},{12,4},{1,9},{5,13},{9,1},{13,5},{2,10},{6,14},... | collective-permute-start | bytes 84488 | tf_op jit(solution)/shard_map/ppermute | solution.py:62
  21.3 2.4 %collective-permute-done.1 = s32[320,22]{0,1:T(8,128)S(1)} collective-permute-done((s32[320,22]{0,1:T(8,128)S(1)}, s32[320,22]{0,1:T(8,128)S(1)}, u32[]{:S(2)}, u32[]{:S(2)}) %collective-permute-start.1) | collective-permute-done | bytes 28192 | tf_op jit(solution)/shard_map/ppermute | solution.py:62
  24.0 0.7 reshape.63.slot_ref
  24.8 35.5 %shard_map.120 = (bf16[2,6,320,64]{3,2,1,0:T(8,128)(2,1)}, f32[3,272,256]{2,1,0:T(8,128)}) custom-call(s32[320,1]{1,0:T(8,128)} %broadcast_in_dim.32.points_ref.limit_ref, bf16[2,6,320,5632]{3,2,1,0:T(8,128)(2,1)} %cells_ref.1, bf16[64,5632]{1,0:T(8,128)(2,1)} %pad_maximum_fusion.table_ref, f32[2,6]{1,0:T(2,128)} %convert_element_type.20.weight_ref, ...), custom_call_target="tpu_custom_call" | custom-call | tf_op jit(solution)/shard_map/pallas_call | solution.py:163
  60.3 1.2 slice_bitcast_fusion.1
  61.5 2.8 %collective-permute-start.7 = (f32[272,256]{1,0:T(8,128)S(1)}, f32[272,256]{1,0:T(8,128)S(1)}, u32[]{:S(2)}, u32[]{:S(2)}) collective-permute-start(f32[272,256]{1,0:T(8,128)S(1)} %get-tuple-element.9), channel_id=1, source_target_pairs={{1,0},{2,1},{3,2},{16,3},{17,16},{18,17},{19,18},{5,4},{6,5},{7,6}... | collective-permute-start | bytes 835592 | tf_op jit(solution)/shard_map/ppermute | solution.py:284
  64.2 3.1 %collective-permute-start.6 = (f32[272,256]{1,0:T(8,128)S(1)}, f32[272,256]{1,0:T(8,128)S(1)}, u32[]{:S(2)}, u32[]{:S(2)}) collective-permute-start(f32[272,256]{1,0:T(8,128)S(1)} %get-tuple-element.8), channel_id=1, source_target_pairs={{0,1},{1,2},{2,3},{3,16},{16,17},{17,18},{18,19},{4,5},{5,6},{6,7}... | collective-permute-start | bytes 835592 | tf_op jit(solution)/shard_map/ppermute | solution.py:281
  67.9 1.0 copy.45
  68.9 5.4 %all-to-all-start = ((bf16[32,24,320]{2,1,0:T(8,128)(2,1)}), bf16[32,24,320]{2,1,0:T(8,128)(2,1)S(1)}, u32[]{:S(2)}, u32[]{:S(2)}) async-start(bf16[32,24,320]{2,1,0:T(8,128)(2,1)} %copy.45), calls=%async_computation | async-start | bytes 1179648 | tf_op jit(solution)/shard_map/all_to_all | solution.py:267
  74.3 3.0 %collective-permute-done.6 = f32[272,256]{1,0:T(8,128)S(1)} collective-permute-done((f32[272,256]{1,0:T(8,128)S(1)}, f32[272,256]{1,0:T(8,128)S(1)}, u32[]{:S(2)}, u32[]{:S(2)}) %collective-permute-start.6) | collective-permute-done | bytes 278560 | tf_op jit(solution)/shard_map/ppermute | solution.py:281
  77.3 1.0 fusion.21
  78.5 1.5 %collective-permute-done.8 = f32[272,256]{1,0:T(8,128)S(1)} collective-permute-done((f32[272,256]{1,0:T(8,128)S(1)}, f32[272,256]{1,0:T(8,128)S(1)}, u32[]{:S(2)}, u32[]{:S(2)}) %collective-permute-start.8) | collective-permute-done | bytes 278560 | tf_op jit(solution)/shard_map/ppermute | solution.py:50
  80.0 1.6 %collective-permute-start.9 = (f32[272,256]{1,0:T(8,128)S(1)}, f32[272,256]{1,0:T(8,128)S(1)}, u32[]{:S(2)}, u32[]{:S(2)}) collective-permute-start(f32[272,256]{1,0:T(8,128)S(1)} %add.92), channel_id=1, source_target_pairs={{0,8},{4,12},{8,0},{12,4},{1,9},{5,13},{9,1},{13,5},{2,10},{6,14},... | collective-permute-start | bytes 835592 | tf_op jit(solution)/shard_map/ppermute | solution.py:50
  82.9 5.9 %collective-permute-done.9 = f32[272,256]{1,0:T(8,128)S(1)} collective-permute-done((f32[272,256]{1,0:T(8,128)S(1)}, f32[272,256]{1,0:T(8,128)S(1)}, u32[]{:S(2)}, u32[]{:S(2)}) %collective-permute-start.9) | collective-permute-done | bytes 278560 | tf_op jit(solution)/shard_map/ppermute | solution.py:50
  89.8 0.9 fusion.20
  90.7 0.9 collective-permute-done.2
  91.8 1.6 %collective-permute-start.3 = (bf16[4,48,2560]{2,1,0:T(8,128)(2,1)S(1)}, bf16[4,48,2560]{2,1,0:T(8,128)(2,1)S(1)}, u32[]{:S(2)}, u32[]{:S(2)}) collective-permute-start(bf16[4,48,2560]{2,1,0:T(8,128)(2,1)S(1)} %maximum_select_fusion.2), channel_id=1, source_target_pairs={{0,8},{4,12},{8,0},{12,4},{1,9},{5,13},{9,1},{13,5},{2,10},{6,14},... | collective-permute-start | bytes 2949128 | tf_op jit(solution)/shard_map/ppermute | solution.py:62
  94.0 2.2 %collective-permute-start.11 = (f32[16,2176]{1,0:T(8,128)S(1)}, f32[16,2176]{1,0:T(8,128)S(1)}, u32[]{:S(2)}, u32[]{:S(2)}) collective-permute-start(f32[16,2176]{1,0:T(8,128)S(1)} %get-tuple-element.11), channel_id=1, source_target_pairs={{1,0},{2,1},{3,2},{16,3},{17,16},{18,17},{19,18},{5,4},{6,5},{7,6}... | collective-permute-start | bytes 417800 | tf_op jit(solution)/shard_map/ppermute | solution.py:29
  96.2 4.1 %collective-permute-start.10 = (f32[16,2176]{1,0:T(8,128)S(1)}, f32[16,2176]{1,0:T(8,128)S(1)}, u32[]{:S(2)}, u32[]{:S(2)}) collective-permute-start(f32[16,2176]{1,0:T(8,128)S(1)} %get-tuple-element.11), channel_id=1, source_target_pairs={{0,1},{1,2},{2,3},{3,16},{16,17},{17,18},{18,19},{4,5},{5,6},{6,7}... | collective-permute-start | bytes 417800 | tf_op jit(solution)/shard_map/ppermute | solution.py:27
  100.9 1.1 collective-permute-done.11
  102.1 3.9 %collective-permute-done.10 = f32[16,2176]{1,0:T(8,128)S(1)} collective-permute-done((f32[16,2176]{1,0:T(8,128)S(1)}, f32[16,2176]{1,0:T(8,128)S(1)}, u32[]{:S(2)}, u32[]{:S(2)}) %collective-permute-start.10) | collective-permute-done | bytes 139296 | tf_op jit(solution)/shard_map/ppermute | solution.py:27
  106.0 0.8 reshape.69.tiles_ref
  106.8 5.6 %shard_map.121 = f32[320,1408]{1,0:T(8,128)} custom-call(s32[3520]{0:T(1024)} %fusion.35.slot_ref, s32[1]{0:T(128)} %bitcast.15.base_ref, s32[320,1]{1,0:T(8,128)} %broadcast_in_dim.32.points_ref.limit_ref, f32[816,128]{1,0:T(8,128)} %reshape.69.tiles_ref), custom_call_target="tpu_custom_call" | custom-call | tf_op jit(solution)/shard_map/pallas_call | solution.py:211
  112.3 3.3 %collective-permute-done.3 = bf16[4,48,2560]{2,1,0:T(8,128)(2,1)S(1)} collective-permute-done((bf16[4,48,2560]{2,1,0:T(8,128)(2,1)S(1)}, bf16[4,48,2560]{2,1,0:T(8,128)(2,1)S(1)}, u32[]{:S(2)}, u32[]{:S(2)}) %collective-permute-start.3) | collective-permute-done | bytes 983072 | tf_op jit(solution)/shard_map/ppermute | solution.py:62
  115.6 5.5 %fusion = f32[4,96,384]{2,1,0:T(8,128)} fusion(bf16[4,2560,384]{2,1,0:T(8,128)(2,1)} %param.12, bf16[4,48,2560]{2,1,0:T(8,128)(2,1)S(1)} %maximum_select_fusion.2, bf16[4,48,2560]{2,1,0:T(8,128)(2,1)S(1)} %collective-permute-done.3, pred[]{:T(512)S(6)} %eq.19), kind=kOutput, calls=%fused_computation.1 | convolution fusion | flops 763822080 | bytes 10420225 | tf_op jit(solution)/shard_map/srj,sjd->srd/dot_general | solution.py:274
  (60 shorter events, 7.0 us)
Async XLA Ops:
  0.6 18.3 %copy-start.4 = (s32[320,11]{0,1:T(8,128)S(1)}, s32[320,11]{0,1:T(8,128)}, u32[]{:S(2)}) copy-start(s32[320,11]{0,1:T(8,128)} %param.14) | copy-start | bytes 42244
  0.6 16.6 %copy-start.5 = (s32[320]{0:T(512)S(1)}, s32[320]{0:T(512)}, u32[]{:S(2)}) copy-start(s32[320]{0:T(512)} %param.10) | copy-start | bytes 3844
  0.7 18.4 %copy-start.7 = (bf16[2,6]{1,0:T(2,128)(2,1)S(1)}, bf16[2,6]{1,0:T(2,128)(2,1)}, u32[]{:S(2)}) copy-start(bf16[2,6]{1,0:T(2,128)(2,1)} %param.13) | copy-start | bytes 76
  0.7 19.0 %collective-permute-start = (s32[320,11]{0,1:T(8,128)}, s32[320,11]{0,1:T(8,128)S(1)}, u32[]{:S(2)}, u32[]{:S(2)}) collective-permute-start(s32[320,11]{0,1:T(8,128)} %param.14), channel_id=1, source_target_pairs={{0,4},{4,0},{8,12},{12,8},{1,5},{5,1},{9,13},{13,9},{2,6},{6,2},{1... | collective-permute-start | bytes 42248 | tf_op jit(solution)/shard_map/ppermute | solution.py:62
  2.4 87.4 %collective-permute-start.5 = (f32[2,1,2176]{2,1,0:T(1,128)}, f32[2,1,2176]{2,1,0:T(1,128)}, u32[]{:S(2)}, u32[]{:S(2)}) collective-permute-start(f32[2,1,2176]{2,1,0:T(1,128)} %get-tuple-element.17), channel_id=1, source_target_pairs={{0,1},{1,2},{2,3},{3,16},{16,17},{17,18},{18,19},{4,5},{5,6},{6,7}... | collective-permute-start | bytes 52232 | tf_op jit(solution)/shard_map/ppermute | solution.py:27
  5.8 83.9 %collective-permute-start.4 = (f32[2,1,2176]{2,1,0:T(1,128)}, f32[2,1,2176]{2,1,0:T(1,128)}, u32[]{:S(2)}, u32[]{:S(2)}) collective-permute-start(f32[2,1,2176]{2,1,0:T(1,128)} %get-tuple-element.16), channel_id=1, source_target_pairs={{1,0},{2,1},{3,2},{16,3},{17,16},{18,17},{19,18},{5,4},{6,5},{7,6}... | collective-permute-start | bytes 52232 | tf_op jit(solution)/shard_map/ppermute | solution.py:29
  19.7 4.0 %collective-permute-start.1 = (s32[320,22]{0,1:T(8,128)S(1)}, s32[320,22]{0,1:T(8,128)S(1)}, u32[]{:S(2)}, u32[]{:S(2)}) collective-permute-start(s32[320,22]{0,1:T(8,128)S(1)} %add_select_fusion.5), channel_id=1, source_target_pairs={{0,8},{4,12},{8,0},{12,4},{1,9},{5,13},{9,1},{13,5},{2,10},{6,14},... | collective-permute-start | bytes 84488 | tf_op jit(solution)/shard_map/ppermute | solution.py:62
  24.8 42.6 %copy-start = (f32[16,2176]{1,0:T(8,128)S(1)}, f32[16,2176]{1,0:T(8,128)}, u32[]{:S(2)}) copy-start(f32[16,2176]{1,0:T(8,128)} %param.15) | copy-start | bytes 417796
  24.8 42.6 %copy-start.1 = (f32[16,2176]{1,0:T(8,128)S(1)}, f32[16,2176]{1,0:T(8,128)}, u32[]{:S(2)}) copy-start(f32[16,2176]{1,0:T(8,128)} %param.16) | copy-start | bytes 417796
  60.3 7.2 %copy-start.2 = (bf16[2,6,320,64]{3,2,1,0:T(8,128)(2,1)S(1)}, bf16[2,6,320,64]{3,2,1,0:T(8,128)(2,1)}, u32[]{:S(2)}) copy-start(bf16[2,6,320,64]{3,2,1,0:T(8,128)(2,1)} %get-tuple-element.6) | copy-start | bytes 1474564
  61.5 12.9 %collective-permute-start.7 = (f32[272,256]{1,0:T(8,128)S(1)}, f32[272,256]{1,0:T(8,128)S(1)}, u32[]{:S(2)}, u32[]{:S(2)}) collective-permute-start(f32[272,256]{1,0:T(8,128)S(1)} %get-tuple-element.9), channel_id=1, source_target_pairs={{1,0},{2,1},{3,2},{16,3},{17,16},{18,17},{19,18},{5,4},{6,5},{7,6}... | collective-permute-start | bytes 835592 | tf_op jit(solution)/shard_map/ppermute | solution.py:284
  64.2 13.1 %collective-permute-start.6 = (f32[272,256]{1,0:T(8,128)S(1)}, f32[272,256]{1,0:T(8,128)S(1)}, u32[]{:S(2)}, u32[]{:S(2)}) collective-permute-start(f32[272,256]{1,0:T(8,128)S(1)} %get-tuple-element.8), channel_id=1, source_target_pairs={{0,1},{1,2},{2,3},{3,16},{16,17},{17,18},{18,19},{4,5},{5,6},{6,7}... | collective-permute-start | bytes 835592 | tf_op jit(solution)/shard_map/ppermute | solution.py:281
  67.9 13.7 %copy-start.6 = (s32[16,17]{1,0:T(8,128)S(1)}, s32[16,17]{1,0:T(8,128)}, u32[]{:S(2)}) copy-start(s32[16,17]{1,0:T(8,128)} %param.17) | copy-start | bytes 3268
  68.9 20.1 %all-to-all-start = ((bf16[32,24,320]{2,1,0:T(8,128)(2,1)}), bf16[32,24,320]{2,1,0:T(8,128)(2,1)S(1)}, u32[]{:S(2)}, u32[]{:S(2)}) async-start(bf16[32,24,320]{2,1,0:T(8,128)(2,1)} %copy.45), calls=%async_computation | async-start | bytes 1179648 | tf_op jit(solution)/shard_map/all_to_all | solution.py:267
  78.4 1.6 %collective-permute-start.8 = (f32[272,256]{1,0:T(8,128)S(1)}, f32[272,256]{1,0:T(8,128)S(1)}, u32[]{:S(2)}, u32[]{:S(2)}) collective-permute-start(f32[272,256]{1,0:T(8,128)S(1)} %fusion.21), channel_id=1, source_target_pairs={{0,4},{4,0},{8,12},{12,8},{1,5},{5,1},{9,13},{13,9},{2,6},{6,2},{1... | collective-permute-start | bytes 835592 | tf_op jit(solution)/shard_map/ppermute | solution.py:50
  80.0 8.8 %collective-permute-start.9 = (f32[272,256]{1,0:T(8,128)S(1)}, f32[272,256]{1,0:T(8,128)S(1)}, u32[]{:S(2)}, u32[]{:S(2)}) collective-permute-start(f32[272,256]{1,0:T(8,128)S(1)} %add.92), channel_id=1, source_target_pairs={{0,8},{4,12},{8,0},{12,4},{1,9},{5,13},{9,1},{13,5},{2,10},{6,14},... | collective-permute-start | bytes 835592 | tf_op jit(solution)/shard_map/ppermute | solution.py:50
  89.7 1.9 %collective-permute-start.2 = (bf16[4,24,2560]{2,1,0:T(8,128)(2,1)S(1)}, bf16[4,24,2560]{2,1,0:T(8,128)(2,1)S(1)}, u32[]{:S(2)}, u32[]{:S(2)}) collective-permute-start(bf16[4,24,2560]{2,1,0:T(8,128)(2,1)S(1)} %all_to_all.16), channel_id=1, source_target_pairs={{0,4},{4,0},{8,12},{12,8},{1,5},{5,1},{9,13},{13,9},{2,6},{6,2},{1... | collective-permute-start | bytes 1474568 | tf_op jit(solution)/shard_map/ppermute | solution.py:62
  91.8 23.9 %collective-permute-start.3 = (bf16[4,48,2560]{2,1,0:T(8,128)(2,1)S(1)}, bf16[4,48,2560]{2,1,0:T(8,128)(2,1)S(1)}, u32[]{:S(2)}, u32[]{:S(2)}) collective-permute-start(bf16[4,48,2560]{2,1,0:T(8,128)(2,1)S(1)} %maximum_select_fusion.2), channel_id=1, source_target_pairs={{0,8},{4,12},{8,0},{12,4},{1,9},{5,13},{9,1},{13,5},{2,10},{6,14},... | collective-permute-start | bytes 2949128 | tf_op jit(solution)/shard_map/ppermute | solution.py:62
  94.0 18.3 %copy-start.3 = (f32[16,2176]{1,0:T(8,128)}, f32[16,2176]{1,0:T(8,128)S(1)}, u32[]{:S(2)}) copy-start(f32[16,2176]{1,0:T(8,128)S(1)} %get-tuple-element.11) | copy-start | bytes 417796
  94.0 8.1 %collective-permute-start.11 = (f32[16,2176]{1,0:T(8,128)S(1)}, f32[16,2176]{1,0:T(8,128)S(1)}, u32[]{:S(2)}, u32[]{:S(2)}) collective-permute-start(f32[16,2176]{1,0:T(8,128)S(1)} %get-tuple-element.11), channel_id=1, source_target_pairs={{1,0},{2,1},{3,2},{16,3},{17,16},{18,17},{19,18},{5,4},{6,5},{7,6}... | collective-permute-start | bytes 417800 | tf_op jit(solution)/shard_map/ppermute | solution.py:29
  96.2 9.8 %collective-permute-start.10 = (f32[16,2176]{1,0:T(8,128)S(1)}, f32[16,2176]{1,0:T(8,128)S(1)}, u32[]{:S(2)}, u32[]{:S(2)}) collective-permute-start(f32[16,2176]{1,0:T(8,128)S(1)} %get-tuple-element.11), channel_id=1, source_target_pairs={{0,1},{1,2},{2,3},{3,16},{16,17},{17,18},{18,19},{4,5},{5,6},{6,7}... | collective-permute-start | bytes 417800 | tf_op jit(solution)/shard_map/ppermute | solution.py:27

commit v13 on v12

--- a/solution.py
+++ b/solution.py
@@ -43,13 +43,23 @@
 
 def lev_sum(values):
     count = lax.axis_size("lev")
-    if count & (count - 1):
+    if count != 4 or values.shape[0] % 16:
         return lax.psum(values, "lev")
-    stride = 1
-    while stride < count:
-        values = values + lax.ppermute(values, "lev", [(i, i ^ stride) for i in range(count)])
-        stride *= 2
-    return values
+    index = lax.axis_index("lev")
+    half = values.shape[0] // 2
+    top, bottom = values[:half], values[half:]
+    odd = index % 2 == 1
+    kept = jnp.where(odd, bottom, top)
+    sent = jnp.where(odd, top, bottom)
+    pairs_near = [(i, i ^ 1) for i in range(count)]
+    kept = kept + lax.ppermute(sent, "lev", pairs_near)
+    kept = kept + lax.ppermute(kept, "lev", [(i, i ^ 2) for i in range(count)])
+    other = lax.ppermute(kept, "lev", pairs_near)
+    return jnp.where(
+        odd,
+        jnp.concatenate([other, kept], axis=0),
+        jnp.concatenate([kept, other], axis=0),
+    )
 
 
 def lev_gather(values, axis):

time: 123 us -> 135 us (1.098)
  the two profiles are of different devices: /device:TPU:4 before, /device:TPU:0 now
where the time goes in v13:
time: 135 us
  Pallas kernels  41.1 us (30%)
  starting transfers between devices  36 us (27%)
  waiting for transfers between devices  31.6 us (23%)
  other arithmetic  11.5 us (9%)
  local copies, waits for them, and re-layouts  7.8 us (6%)
  matrix products  5.55 us (4%)
    pallas_call x1, Pallas kernels, fused_transform(): pl.pallas_call(transform_kernel, grid=(steps,), in_specs=[pl.BlockSpec((r...  35.5 us
    all_to_all x1, starting transfers between devices, body(): lax.all_to_all(coeffs.transpose(4, 1, 0, 3, 2).reshape(wave_count, lev_de...  12.5 us
    ppermute x4, waiting for transfers between devices, lev_gather(): other = lax.ppermute(values, 'lev', [(i, i ^ stride) for i in range(count)])  10.8 us
    all_to_all x1, waiting for transfers between devices, body(): lax.all_to_all(coeffs.transpose(4, 1, 0, 3, 2).reshape(wave_count, lev_de...  9.83 us
    ppermute x2, starting transfers between devices, with_halo(): lax.ppermute(tail, axis, [(i, (i + 1) % count) for i in range(ends)])  9.05 us
    pallas_call x1, Pallas kernels, surface_gather(): pl.pallas_call(surface_kernel, in_specs=[pl.BlockSpec(memory_space=pltpu....  5.56 us
    dot_general x1, matrix products, body(): jnp.einsum('srj,sjd->srd', lev_gather(regrouped, 1), legendre, preferred_...  5.55 us
    ppermute x1, starting transfers between devices, body(): lax.ppermute(sections[2], ('lat', 'ocn'), [(i, i + 1) for i in range(band...  5.19 us
  transfers between devices with their start and end apart: 14, of which 9 were waited for; matrix products, arithmetic and copies ran while one was open for 14% of the time, Pallas kernels for 31%

profile of v13, /device:TPU:0, one launch (start us, length us, event | category | flops | bytes accessed | tf_op | source)
XLA Modules:
  0.0 134.5 jit_solution(12437637420327177021)
XLA Ops:
  1.2 1.0 fusion.28
  2.2 4.5 %collective-permute-start.5 = (f32[2,1,2176]{2,1,0:T(1,128)S(1)}, f32[2,1,2176]{2,1,0:T(1,128)S(1)}, u32[]{:S(2)}, u32[]{:S(2)}) collective-permute-start(f32[2,1,2176]{2,1,0:T(1,128)S(1)} %get-tuple-element.17), channel_id=1, source_target_pairs={{0,1},{1,2},{2,3},{3,16},{16,17},{17,18},{18,19},{4,5},{5,6},{6,7}... | collective-permute-start | bytes 52232 | tf_op jit(solution)/shard_map/ppermute | solution.py:27
  6.7 1.3 collective-permute-start.4
  8.0 4.0 %cosine_convert_fusion = (bf16[32,5632]{1,0:T(8,128)(2,1)S(1)}, bf16[32,5632]{1,0:T(8,128)(2,1)S(1)}) fusion(s32[32]{0:T(128)} %param.11), kind=kLoop, calls=%fused_computation.14 | loop fusion | flops 2162688 | bytes 721024 | tf_op jit(solution)/shard_map/convert
  13.4 1.0 pad_maximum_fusion.table_ref
  14.5 0.8 pad_maximum_fusion.7.scale_ref
  15.3 0.8 broadcast_in_dim.32.points_ref.limit_ref
  16.7 1.6 %collective-permute-start.1 = (s32[320,22]{0,1:T(8,128)S(1)}, s32[320,22]{0,1:T(8,128)S(1)}, u32[]{:S(2)}, u32[]{:S(2)}) collective-permute-start(s32[320,22]{0,1:T(8,128)S(1)} %add_select_fusion.5), channel_id=1, source_target_pairs={{0,8},{4,12},{8,0},{12,4},{1,9},{5,13},{9,1},{13,5},{2,10},{6,14},... | collective-permute-start | bytes 84488 | tf_op jit(solution)/shard_map/ppermute | solution.py:72
  18.4 2.4 %collective-permute-done.1 = s32[320,22]{0,1:T(8,128)S(1)} collective-permute-done((s32[320,22]{0,1:T(8,128)S(1)}, s32[320,22]{0,1:T(8,128)S(1)}, u32[]{:S(2)}, u32[]{:S(2)}) %collective-permute-start.1) | collective-permute-done | bytes 28192 | tf_op jit(solution)/shard_map/ppermute | solution.py:72
  21.1 0.7 reshape.65.slot_ref
  21.8 35.5 %shard_map.120 = (bf16[2,6,320,64]{3,2,1,0:T(8,128)(2,1)}, f32[3,272,256]{2,1,0:T(8,128)}) custom-call(s32[320,1]{1,0:T(8,128)} %broadcast_in_dim.32.points_ref.limit_ref, bf16[2,6,320,5632]{3,2,1,0:T(8,128)(2,1)} %cells_ref.1, bf16[64,5632]{1,0:T(8,128)(2,1)} %pad_maximum_fusion.table_ref, f32[2,6]{1,0:T(2,128)} %convert_element_type.20.weight_ref, ...), custom_call_target="tpu_custom_call" | custom-call | tf_op jit(solution)/shard_map/pallas_call | solution.py:173
  57.4 1.2 slice_bitcast_fusion.1
  58.5 1.3 collective-permute-start.7
  59.8 5.2 %collective-permute-start.6 = (f32[272,256]{1,0:T(8,128)S(1)}, f32[272,256]{1,0:T(8,128)S(1)}, u32[]{:S(2)}, u32[]{:S(2)}) collective-permute-start(f32[272,256]{1,0:T(8,128)S(1)} %get-tuple-element.8), channel_id=1, source_target_pairs={{0,1},{1,2},{2,3},{3,16},{16,17},{17,18},{18,19},{4,5},{5,6},{6,7}... | collective-permute-start | bytes 835592 | tf_op jit(solution)/shard_map/ppermute | solution.py:291
  65.2 3.5 %collective-permute-done.7 = f32[272,256]{1,0:T(8,128)S(1)} collective-permute-done((f32[272,256]{1,0:T(8,128)S(1)}, f32[272,256]{1,0:T(8,128)S(1)}, u32[]{:S(2)}, u32[]{:S(2)}) %collective-permute-start.7) | collective-permute-done | bytes 278560 | tf_op jit(solution)/shard_map/ppermute | solution.py:294
  68.7 1.2 collective-permute-done.6
  69.9 1.0 fusion.21
  71.5 1.0 copy.45
  72.5 12.5 %all-to-all-start = ((bf16[32,24,320]{2,1,0:T(8,128)(2,1)}), bf16[32,24,320]{2,1,0:T(8,128)(2,1)S(1)}, u32[]{:S(2)}, u32[]{:S(2)}) async-start(bf16[32,24,320]{2,1,0:T(8,128)(2,1)} %copy.45), calls=%async_computation | async-start | bytes 1179648 | tf_op jit(solution)/shard_map/all_to_all | solution.py:277
  85.0 1.6 %collective-permute-start.9 = (f32[136,256]{1,0:T(8,128)S(1)}, f32[136,256]{1,0:T(8,128)S(1)}, u32[]{:S(2)}, u32[]{:S(2)}) collective-permute-start(f32[136,256]{1,0:T(8,128)S(1)} %select_add_fusion), channel_id=1, source_target_pairs={{0,8},{4,12},{8,0},{12,4},{1,9},{5,13},{9,1},{13,5},{2,10},{6,14},... | collective-permute-start | bytes 417800 | tf_op jit(solution)/shard_map/ppermute | solution.py:56
  86.6 4.3 %collective-permute-done.9 = f32[136,256]{1,0:T(8,128)S(1)} collective-permute-done((f32[136,256]{1,0:T(8,128)S(1)}, f32[136,256]{1,0:T(8,128)S(1)}, u32[]{:S(2)}, u32[]{:S(2)}) %collective-permute-start.9) | collective-permute-done | bytes 139296 | tf_op jit(solution)/shard_map/ppermute | solution.py:56
  92.6 9.8 %all-to-all-done = bf16[32,24,320]{2,1,0:T(8,128)(2,1)S(1)} async-done(((bf16[32,24,320]{2,1,0:T(8,128)(2,1)}), bf16[32,24,320]{2,1,0:T(8,128)(2,1)S(1)}, u32[]{:S(2)}, u32[]{:S(2)}) %all-to-all-start) | async-done | bytes 491552 | tf_op jit(solution)/shard_map/all_to_all | solution.py:277
  103.3 1.6 %collective-permute-done.2 = bf16[4,24,2560]{2,1,0:T(8,128)(2,1)S(1)} collective-permute-done((bf16[4,24,2560]{2,1,0:T(8,128)(2,1)S(1)}, bf16[4,24,2560]{2,1,0:T(8,128)(2,1)S(1)}, u32[]{:S(2)}, u32[]{:S(2)}) %collective-permute-start.2) | collective-permute-done | bytes 491552 | tf_op jit(solution)/shard_map/ppermute | solution.py:72
  105.1 1.6 %collective-permute-start.3 = (bf16[4,48,2560]{2,1,0:T(8,128)(2,1)S(1)}, bf16[4,48,2560]{2,1,0:T(8,128)(2,1)S(1)}, u32[]{:S(2)}, u32[]{:S(2)}) collective-permute-start(bf16[4,48,2560]{2,1,0:T(8,128)(2,1)S(1)} %maximum_select_fusion.2), channel_id=1, source_target_pairs={{0,8},{4,12},{8,0},{12,4},{1,9},{5,13},{9,1},{13,5},{2,10},{6,14},... | collective-permute-start | bytes 2949128 | tf_op jit(solution)/shard_map/ppermute | solution.py:72
  107.4 1.3 collective-permute-start.12
  108.6 4.6 %collective-permute-start.11 = (f32[16,2176]{1,0:T(8,128)S(1)}, f32[16,2176]{1,0:T(8,128)S(1)}, u32[]{:S(2)}, u32[]{:S(2)}) collective-permute-start(f32[16,2176]{1,0:T(8,128)S(1)} %get-tuple-element.11), channel_id=1, source_target_pairs={{0,1},{1,2},{2,3},{3,16},{16,17},{17,18},{18,19},{4,5},{5,6},{6,7}... | collective-permute-start | bytes 417800 | tf_op jit(solution)/shard_map/ppermute | solution.py:27
  113.8 0.8 collective-permute-done.12
  114.7 1.2 collective-permute-done.11
  115.9 0.8 reshape.70.tiles_ref
  116.7 5.6 %shard_map.121 = f32[320,1408]{1,0:T(8,128)} custom-call(s32[3520]{0:T(1024)} %fusion.35.slot_ref, s32[1]{0:T(128)} %bitcast.15.base_ref, s32[320,1]{1,0:T(8,128)} %broadcast_in_dim.32.points_ref.limit_ref, f32[816,128]{1,0:T(8,128)} %reshape.70.tiles_ref), custom_call_target="tpu_custom_call" | custom-call | tf_op jit(solution)/shard_map/pallas_call | solution.py:221
  122.2 6.8 %collective-permute-done.3 = bf16[4,48,2560]{2,1,0:T(8,128)(2,1)S(1)} collective-permute-done((bf16[4,48,2560]{2,1,0:T(8,128)(2,1)S(1)}, bf16[4,48,2560]{2,1,0:T(8,128)(2,1)S(1)}, u32[]{:S(2)}, u32[]{:S(2)}) %collective-permute-start.3) | collective-permute-done | bytes 983072 | tf_op jit(solution)/shard_map/ppermute | solution.py:72
  129.0 5.5 %fusion = f32[4,96,384]{2,1,0:T(8,128)} fusion(bf16[4,2560,384]{2,1,0:T(8,128)(2,1)} %param.12, bf16[4,48,2560]{2,1,0:T(8,128)(2,1)S(1)} %maximum_select_fusion.2, bf16[4,48,2560]{2,1,0:T(8,128)(2,1)S(1)} %collective-permute-done.3, pred[]{:T(512)S(6)} %eq.21), kind=kOutput, calls=%fused_computation.1 | convolution fusion | flops 763822080 | bytes 10420225 | tf_op jit(solution)/shard_map/srj,sjd->srd/dot_general | solution.py:284
  (64 shorter events, 7.7 us)
Async XLA Ops:
  0.6 15.4 %copy-start.4 = (s32[320,11]{0,1:T(8,128)S(1)}, s32[320,11]{0,1:T(8,128)}, u32[]{:S(2)}) copy-start(s32[320,11]{0,1:T(8,128)} %param.14) | copy-start | bytes 42244
  0.6 13.7 %copy-start.5 = (s32[320]{0:T(512)S(1)}, s32[320]{0:T(512)}, u32[]{:S(2)}) copy-start(s32[320]{0:T(512)} %param.10) | copy-start | bytes 3844
  0.7 15.5 %copy-start.7 = (bf16[2,6]{1,0:T(2,128)(2,1)S(1)}, bf16[2,6]{1,0:T(2,128)(2,1)}, u32[]{:S(2)}) copy-start(bf16[2,6]{1,0:T(2,128)(2,1)} %param.13) | copy-start | bytes 76
  0.7 16.0 %collective-permute-start = (s32[320,11]{0,1:T(8,128)}, s32[320,11]{0,1:T(8,128)S(1)}, u32[]{:S(2)}, u32[]{:S(2)}) collective-permute-start(s32[320,11]{0,1:T(8,128)} %param.14), channel_id=1, source_target_pairs={{0,4},{4,0},{8,12},{12,8},{1,5},{5,1},{9,13},{13,9},{2,6},{6,2},{1... | collective-permute-start | bytes 42248 | tf_op jit(solution)/shard_map/ppermute | solution.py:72
  2.2 100.9 %collective-permute-start.5 = (f32[2,1,2176]{2,1,0:T(1,128)S(1)}, f32[2,1,2176]{2,1,0:T(1,128)S(1)}, u32[]{:S(2)}, u32[]{:S(2)}) collective-permute-start(f32[2,1,2176]{2,1,0:T(1,128)S(1)} %get-tuple-element.17), channel_id=1, source_target_pairs={{0,1},{1,2},{2,3},{3,16},{16,17},{17,18},{18,19},{4,5},{5,6},{6,7}... | collective-permute-start | bytes 52232 | tf_op jit(solution)/shard_map/ppermute | solution.py:27
  6.7 96.4 %collective-permute-start.4 = (f32[2,1,2176]{2,1,0:T(1,128)S(1)}, f32[2,1,2176]{2,1,0:T(1,128)S(1)}, u32[]{:S(2)}, u32[]{:S(2)}) collective-permute-start(f32[2,1,2176]{2,1,0:T(1,128)S(1)} %get-tuple-element.16), channel_id=1, source_target_pairs={{1,0},{2,1},{3,2},{16,3},{17,16},{18,17},{19,18},{5,4},{6,5},{7,6}... | collective-permute-start | bytes 52232 | tf_op jit(solution)/shard_map/ppermute | solution.py:29
  16.7 4.0 %collective-permute-start.1 = (s32[320,22]{0,1:T(8,128)S(1)}, s32[320,22]{0,1:T(8,128)S(1)}, u32[]{:S(2)}, u32[]{:S(2)}) collective-permute-start(s32[320,22]{0,1:T(8,128)S(1)} %add_select_fusion.5), channel_id=1, source_target_pairs={{0,8},{4,12},{8,0},{12,4},{1,9},{5,13},{9,1},{13,5},{2,10},{6,14},... | collective-permute-start | bytes 84488 | tf_op jit(solution)/shard_map/ppermute | solution.py:72
  21.8 43.2 %copy-start = (f32[16,2176]{1,0:T(8,128)S(1)}, f32[16,2176]{1,0:T(8,128)}, u32[]{:S(2)}) copy-start(f32[16,2176]{1,0:T(8,128)} %param.15) | copy-start | bytes 417796
  21.8 43.2 %copy-start.1 = (f32[16,2176]{1,0:T(8,128)S(1)}, f32[16,2176]{1,0:T(8,128)}, u32[]{:S(2)}) copy-start(f32[16,2176]{1,0:T(8,128)} %param.16) | copy-start | bytes 417796
  57.4 13.7 %copy-start.2 = (bf16[2,6,320,64]{3,2,1,0:T(8,128)(2,1)S(1)}, bf16[2,6,320,64]{3,2,1,0:T(8,128)(2,1)}, u32[]{:S(2)}) copy-start(bf16[2,6,320,64]{3,2,1,0:T(8,128)(2,1)} %get-tuple-element.6) | copy-start | bytes 1474564
  58.5 10.1 %collective-permute-start.7 = (f32[272,256]{1,0:T(8,128)S(1)}, f32[272,256]{1,0:T(8,128)S(1)}, u32[]{:S(2)}, u32[]{:S(2)}) collective-permute-start(f32[272,256]{1,0:T(8,128)S(1)} %get-tuple-element.9), channel_id=1, source_target_pairs={{1,0},{2,1},{3,2},{16,3},{17,16},{18,17},{19,18},{5,4},{6,5},{7,6}... | collective-permute-start | bytes 835592 | tf_op jit(solution)/shard_map/ppermute | solution.py:294
  59.8 10.0 %collective-permute-start.6 = (f32[272,256]{1,0:T(8,128)S(1)}, f32[272,256]{1,0:T(8,128)S(1)}, u32[]{:S(2)}, u32[]{:S(2)}) collective-permute-start(f32[272,256]{1,0:T(8,128)S(1)} %get-tuple-element.8), channel_id=1, source_target_pairs={{0,1},{1,2},{2,3},{3,16},{16,17},{17,18},{18,19},{4,5},{5,6},{6,7}... | collective-permute-start | bytes 835592 | tf_op jit(solution)/shard_map/ppermute | solution.py:291
  70.9 14.1 %collective-permute-start.8 = (f32[136,256]{1,0:T(8,128)S(1)}, f32[136,256]{1,0:T(8,128)S(1)}, u32[]{:S(2)}, u32[]{:S(2)}) collective-permute-start(f32[136,256]{1,0:T(8,128)S(1)} %slice_select_fusion), channel_id=1, source_target_pairs={{0,4},{4,0},{8,12},{12,8},{1,5},{5,1},{9,13},{13,9},{2,6},{6,2},{1... | collective-permute-start | bytes 417800 | tf_op jit(solution)/shard_map/ppermute | solution.py:55
  71.5 19.5 %copy-start.6 = (s32[16,17]{1,0:T(8,128)S(1)}, s32[16,17]{1,0:T(8,128)}, u32[]{:S(2)}) copy-start(s32[16,17]{1,0:T(8,128)} %param.17) | copy-start | bytes 3268
  72.5 30.0 %all-to-all-start = ((bf16[32,24,320]{2,1,0:T(8,128)(2,1)}), bf16[32,24,320]{2,1,0:T(8,128)(2,1)S(1)}, u32[]{:S(2)}, u32[]{:S(2)}) async-start(bf16[32,24,320]{2,1,0:T(8,128)(2,1)} %copy.45), calls=%async_computation | async-start | bytes 1179648 | tf_op jit(solution)/shard_map/all_to_all | solution.py:277
  85.0 5.9 %collective-permute-start.9 = (f32[136,256]{1,0:T(8,128)S(1)}, f32[136,256]{1,0:T(8,128)S(1)}, u32[]{:S(2)}, u32[]{:S(2)}) collective-permute-start(f32[136,256]{1,0:T(8,128)S(1)} %select_add_fusion), channel_id=1, source_target_pairs={{0,8},{4,12},{8,0},{12,4},{1,9},{5,13},{9,1},{13,5},{2,10},{6,14},... | collective-permute-start | bytes 417800 | tf_op jit(solution)/shard_map/ppermute | solution.py:56
  90.9 1.4 %collective-permute-start.10 = (f32[136,256]{1,0:T(8,128)S(1)}, f32[136,256]{1,0:T(8,128)S(1)}, u32[]{:S(2)}, u32[]{:S(2)}) collective-permute-start(f32[136,256]{1,0:T(8,128)S(1)} %add.94), channel_id=1, source_target_pairs={{0,4},{4,0},{8,12},{12,8},{1,5},{5,1},{9,13},{13,9},{2,6},{6,2},{1... | collective-permute-start | bytes 417800 | tf_op jit(solution)/shard_map/ppermute | solution.py:57
  103.0 1.9 %collective-permute-start.2 = (bf16[4,24,2560]{2,1,0:T(8,128)(2,1)S(1)}, bf16[4,24,2560]{2,1,0:T(8,128)(2,1)S(1)}, u32[]{:S(2)}, u32[]{:S(2)}) collective-permute-start(bf16[4,24,2560]{2,1,0:T(8,128)(2,1)S(1)} %all_to_all.16), channel_id=1, source_target_pairs={{0,4},{4,0},{8,12},{12,8},{1,5},{5,1},{9,13},{13,9},{2,6},{6,2},{1... | collective-permute-start | bytes 1474568 | tf_op jit(solution)/shard_map/ppermute | solution.py:72
  105.1 23.9 %collective-permute-start.3 = (bf16[4,48,2560]{2,1,0:T(8,128)(2,1)S(1)}, bf16[4,48,2560]{2,1,0:T(8,128)(2,1)S(1)}, u32[]{:S(2)}, u32[]{:S(2)}) collective-permute-start(bf16[4,48,2560]{2,1,0:T(8,128)(2,1)S(1)} %maximum_select_fusion.2), channel_id=1, source_target_pairs={{0,8},{4,12},{8,0},{12,4},{1,9},{5,13},{9,1},{13,5},{2,10},{6,14},... | collective-permute-start | bytes 2949128 | tf_op jit(solution)/shard_map/ppermute | solution.py:72
  107.4 14.9 %copy-start.3 = (f32[16,2176]{1,0:T(8,128)}, f32[16,2176]{1,0:T(8,128)S(1)}, u32[]{:S(2)}) copy-start(f32[16,2176]{1,0:T(8,128)S(1)} %get-tuple-element.11) | copy-start | bytes 417796
  107.4 7.3 %collective-permute-start.12 = (f32[16,2176]{1,0:T(8,128)S(1)}, f32[16,2176]{1,0:T(8,128)S(1)}, u32[]{:S(2)}, u32[]{:S(2)}) collective-permute-start(f32[16,2176]{1,0:T(8,128)S(1)} %get-tuple-element.11), channel_id=1, source_target_pairs={{1,0},{2,1},{3,2},{16,3},{17,16},{18,17},{19,18},{5,4},{6,5},{7,6}... | collective-permute-start | bytes 417800 | tf_op jit(solution)/shard_map/ppermute | solution.py:29
  108.6 7.2 %collective-permute-start.11 = (f32[16,2176]{1,0:T(8,128)S(1)}, f32[16,2176]{1,0:T(8,128)S(1)}, u32[]{:S(2)}, u32[]{:S(2)}) collective-permute-start(f32[16,2176]{1,0:T(8,128)S(1)} %get-tuple-element.11), channel_id=1, source_target_pairs={{0,1},{1,2},{2,3},{3,16},{16,17},{17,18},{18,19},{4,5},{5,6},{6,7}... | collective-permute-start | bytes 417800 | tf_op jit(solution)/shard_map/ppermute | solution.py:27

commit v14 on v12

--- a/solution.py
+++ b/solution.py
@@ -201,7 +201,7 @@
             out_ref[pl.ds(row0, group), b * BLOCK : (b + 1) * BLOCK] = rows
         return carry
 
-    lax.fori_loop(0, lat_band // group, per_group, 0)
+    lax.fori_loop(0, lat_band // group, per_group, 0, unroll=2 if (lat_band // group) % 2 == 0 else 1)
     points = base_ref[0] + lax.broadcasted_iota(jnp.int32, (lat_band, quarter), 1)
     out_ref[...] = jnp.where(points < limit_ref[...], out_ref[...], 0.0)
 

time: 123 us -> 123 us (level)
  no operation moved by 1% of the time
where the time goes in v14:
time: 123 us; the launch traced here: 121 us
  Pallas kernels  41 us (33%)
  starting transfers between devices  30.9 us (25%)
  waiting for transfers between devices  22.1 us (18%)
  other arithmetic  12.8 us (10%)
  local copies, waits for them, and re-layouts  7.81 us (6%)
  matrix products  5.53 us (4%)
    pallas_call x1, Pallas kernels, fused_transform(): pl.pallas_call(transform_kernel, grid=(steps,), in_specs=[pl.BlockSpec((r...  35.5 us
    ppermute x2, starting transfers between devices, with_halo(): lax.ppermute(tail, axis, [(i, (i + 1) % count) for i in range(ends)])  7.61 us
    ppermute x2, waiting for transfers between devices, lev_sum(): lax.ppermute(values, 'lev', [(i, i ^ stride) for i in range(count)])  7.42 us
    ppermute x2, starting transfers between devices, with_halo(): lax.ppermute(head, axis, [((i + 1) % count, i) for i in range(ends)])  7.22 us
    ppermute x4, waiting for transfers between devices, lev_gather(): other = lax.ppermute(values, 'lev', [(i, i ^ stride) for i in range(count)])  6.64 us
    dot_general x1, matrix products, body(): jnp.einsum('srj,sjd->srd', lev_gather(regrouped, 1), legendre, preferred_...  5.53 us
    pallas_call x1, Pallas kernels, surface_gather(): pl.pallas_call(surface_kernel, in_specs=[pl.BlockSpec(memory_space=pltpu....  5.48 us
    all_to_all x1, starting transfers between devices, body(): lax.all_to_all(coeffs.transpose(4, 1, 0, 3, 2).reshape(wave_count, lev_de...  5.38 us
  transfers between devices with their start and end apart: 13, of which 8 were waited for; matrix products, arithmetic and copies ran while one was open for 17% of the time, Pallas kernels for 34%

profile of v14, /device:TPU:4, one launch (start us, length us, event | category | flops | bytes accessed | tf_op | source)
XLA Modules:
  0.0 121.2 jit_solution(10077989025384557676)
XLA Ops:
  0.7 1.6 %fusion.28 = (f32[2,1,2176]{2,1,0:T(1,128)}, f32[2,1,2176]{2,1,0:T(1,128)}) fusion(f32[1,16,2176]{2,1,0:T(8,128)} %bitcast.43, f32[1,16,2176]{2,1,0:T(8,128)} %bitcast.47), kind=kLoop, calls=%fused_computation.72 | loop fusion | flops 8704 | bytes 313344 | tf_op jit(solution)/shard_map/stack | solution.py:299
  2.4 3.5 %collective-permute-start.5 = (f32[2,1,2176]{2,1,0:T(1,128)}, f32[2,1,2176]{2,1,0:T(1,128)}, u32[]{:S(2)}, u32[]{:S(2)}) collective-permute-start(f32[2,1,2176]{2,1,0:T(1,128)} %get-tuple-element.17), channel_id=1, source_target_pairs={{0,1},{1,2},{2,3},{3,16},{16,17},{17,18},{18,19},{4,5},{5,6},{6,7}... | collective-permute-start | bytes 52232 | tf_op jit(solution)/shard_map/ppermute | solution.py:27
  5.8 5.1 %collective-permute-start.4 = (f32[2,1,2176]{2,1,0:T(1,128)}, f32[2,1,2176]{2,1,0:T(1,128)}, u32[]{:S(2)}, u32[]{:S(2)}) collective-permute-start(f32[2,1,2176]{2,1,0:T(1,128)} %get-tuple-element.16), channel_id=1, source_target_pairs={{1,0},{2,1},{3,2},{16,3},{17,16},{18,17},{19,18},{5,4},{6,5},{7,6}... | collective-permute-start | bytes 52232 | tf_op jit(solution)/shard_map/ppermute | solution.py:29
  10.9 4.0 %cosine_convert_fusion = (bf16[32,5632]{1,0:T(8,128)(2,1)S(1)}, bf16[32,5632]{1,0:T(8,128)(2,1)S(1)}) fusion(s32[32]{0:T(128)} %param.11), kind=kLoop, calls=%fused_computation.14 | loop fusion | flops 2162688 | bytes 721024 | tf_op jit(solution)/shard_map/convert
  16.3 0.9 pad_maximum_fusion.table_ref
  17.4 0.8 pad_maximum_fusion.7.scale_ref
  18.2 0.8 broadcast_in_dim.32.points_ref.limit_ref
  19.7 1.6 %collective-permute-start.1 = (s32[320,22]{0,1:T(8,128)S(1)}, s32[320,22]{0,1:T(8,128)S(1)}, u32[]{:S(2)}, u32[]{:S(2)}) collective-permute-start(s32[320,22]{0,1:T(8,128)S(1)} %add_select_fusion.5), channel_id=1, source_target_pairs={{0,8},{4,12},{8,0},{12,4},{1,9},{5,13},{9,1},{13,5},{2,10},{6,14},... | collective-permute-start | bytes 84488 | tf_op jit(solution)/shard_map/ppermute | solution.py:62
  21.3 2.4 %collective-permute-done.1 = s32[320,22]{0,1:T(8,128)S(1)} collective-permute-done((s32[320,22]{0,1:T(8,128)S(1)}, s32[320,22]{0,1:T(8,128)S(1)}, u32[]{:S(2)}, u32[]{:S(2)}) %collective-permute-start.1) | collective-permute-done | bytes 28192 | tf_op jit(solution)/shard_map/ppermute | solution.py:62
  24.0 0.7 reshape.63.slot_ref
  24.8 35.5 %shard_map.120 = (bf16[2,6,320,64]{3,2,1,0:T(8,128)(2,1)}, f32[3,272,256]{2,1,0:T(8,128)}) custom-call(s32[320,1]{1,0:T(8,128)} %broadcast_in_dim.32.points_ref.limit_ref, bf16[2,6,320,5632]{3,2,1,0:T(8,128)(2,1)} %cells_ref.1, bf16[64,5632]{1,0:T(8,128)(2,1)} %pad_maximum_fusion.table_ref, f32[2,6]{1,0:T(2,128)} %convert_element_type.20.weight_ref, ...), custom_call_target="tpu_custom_call" | custom-call | tf_op jit(solution)/shard_map/pallas_call | solution.py:163
  60.3 1.2 slice_bitcast_fusion.1
  61.5 2.8 %collective-permute-start.7 = (f32[272,256]{1,0:T(8,128)S(1)}, f32[272,256]{1,0:T(8,128)S(1)}, u32[]{:S(2)}, u32[]{:S(2)}) collective-permute-start(f32[272,256]{1,0:T(8,128)S(1)} %get-tuple-element.9), channel_id=1, source_target_pairs={{1,0},{2,1},{3,2},{16,3},{17,16},{18,17},{19,18},{5,4},{6,5},{7,6}... | collective-permute-start | bytes 835592 | tf_op jit(solution)/shard_map/ppermute | solution.py:284
  64.2 3.1 %collective-permute-start.6 = (f32[272,256]{1,0:T(8,128)S(1)}, f32[272,256]{1,0:T(8,128)S(1)}, u32[]{:S(2)}, u32[]{:S(2)}) collective-permute-start(f32[272,256]{1,0:T(8,128)S(1)} %get-tuple-element.8), channel_id=1, source_target_pairs={{0,1},{1,2},{2,3},{3,16},{16,17},{17,18},{18,19},{4,5},{5,6},{6,7}... | collective-permute-start | bytes 835592 | tf_op jit(solution)/shard_map/ppermute | solution.py:281
  67.9 1.0 copy.45
  68.9 5.4 %all-to-all-start = ((bf16[32,24,320]{2,1,0:T(8,128)(2,1)}), bf16[32,24,320]{2,1,0:T(8,128)(2,1)S(1)}, u32[]{:S(2)}, u32[]{:S(2)}) async-start(bf16[32,24,320]{2,1,0:T(8,128)(2,1)} %copy.45), calls=%async_computation | async-start | bytes 1179648 | tf_op jit(solution)/shard_map/all_to_all | solution.py:267
  74.3 3.0 %collective-permute-done.6 = f32[272,256]{1,0:T(8,128)S(1)} collective-permute-done((f32[272,256]{1,0:T(8,128)S(1)}, f32[272,256]{1,0:T(8,128)S(1)}, u32[]{:S(2)}, u32[]{:S(2)}) %collective-permute-start.6) | collective-permute-done | bytes 278560 | tf_op jit(solution)/shard_map/ppermute | solution.py:281
  77.3 1.0 fusion.21
  78.5 1.5 %collective-permute-done.8 = f32[272,256]{1,0:T(8,128)S(1)} collective-permute-done((f32[272,256]{1,0:T(8,128)S(1)}, f32[272,256]{1,0:T(8,128)S(1)}, u32[]{:S(2)}, u32[]{:S(2)}) %collective-permute-start.8) | collective-permute-done | bytes 278560 | tf_op jit(solution)/shard_map/ppermute | solution.py:50
  80.0 1.6 %collective-permute-start.9 = (f32[272,256]{1,0:T(8,128)S(1)}, f32[272,256]{1,0:T(8,128)S(1)}, u32[]{:S(2)}, u32[]{:S(2)}) collective-permute-start(f32[272,256]{1,0:T(8,128)S(1)} %add.92), channel_id=1, source_target_pairs={{0,8},{4,12},{8,0},{12,4},{1,9},{5,13},{9,1},{13,5},{2,10},{6,14},... | collective-permute-start | bytes 835592 | tf_op jit(solution)/shard_map/ppermute | solution.py:50
  82.9 5.9 %collective-permute-done.9 = f32[272,256]{1,0:T(8,128)S(1)} collective-permute-done((f32[272,256]{1,0:T(8,128)S(1)}, f32[272,256]{1,0:T(8,128)S(1)}, u32[]{:S(2)}, u32[]{:S(2)}) %collective-permute-start.9) | collective-permute-done | bytes 278560 | tf_op jit(solution)/shard_map/ppermute | solution.py:50
  89.8 0.9 fusion.20
  90.7 0.9 collective-permute-done.2
  91.8 1.6 %collective-permute-start.3 = (bf16[4,48,2560]{2,1,0:T(8,128)(2,1)S(1)}, bf16[4,48,2560]{2,1,0:T(8,128)(2,1)S(1)}, u32[]{:S(2)}, u32[]{:S(2)}) collective-permute-start(bf16[4,48,2560]{2,1,0:T(8,128)(2,1)S(1)} %maximum_select_fusion.2), channel_id=1, source_target_pairs={{0,8},{4,12},{8,0},{12,4},{1,9},{5,13},{9,1},{13,5},{2,10},{6,14},... | collective-permute-start | bytes 2949128 | tf_op jit(solution)/shard_map/ppermute | solution.py:62
  94.0 2.2 %collective-permute-start.11 = (f32[16,2176]{1,0:T(8,128)S(1)}, f32[16,2176]{1,0:T(8,128)S(1)}, u32[]{:S(2)}, u32[]{:S(2)}) collective-permute-start(f32[16,2176]{1,0:T(8,128)S(1)} %get-tuple-element.11), channel_id=1, source_target_pairs={{1,0},{2,1},{3,2},{16,3},{17,16},{18,17},{19,18},{5,4},{6,5},{7,6}... | collective-permute-start | bytes 417800 | tf_op jit(solution)/shard_map/ppermute | solution.py:29
  96.2 4.1 %collective-permute-start.10 = (f32[16,2176]{1,0:T(8,128)S(1)}, f32[16,2176]{1,0:T(8,128)S(1)}, u32[]{:S(2)}, u32[]{:S(2)}) collective-permute-start(f32[16,2176]{1,0:T(8,128)S(1)} %get-tuple-element.11), channel_id=1, source_target_pairs={{0,1},{1,2},{2,3},{3,16},{16,17},{17,18},{18,19},{4,5},{5,6},{6,7}... | collective-permute-start | bytes 417800 | tf_op jit(solution)/shard_map/ppermute | solution.py:27
  100.9 1.1 collective-permute-done.11
  102.1 3.9 %collective-permute-done.10 = f32[16,2176]{1,0:T(8,128)S(1)} collective-permute-done((f32[16,2176]{1,0:T(8,128)S(1)}, f32[16,2176]{1,0:T(8,128)S(1)}, u32[]{:S(2)}, u32[]{:S(2)}) %collective-permute-start.10) | collective-permute-done | bytes 139296 | tf_op jit(solution)/shard_map/ppermute | solution.py:27
  106.0 0.8 reshape.69.tiles_ref
  106.8 5.5 %shard_map.121 = f32[320,1408]{1,0:T(8,128)} custom-call(s32[3520]{0:T(1024)} %fusion.35.slot_ref, s32[1]{0:T(128)} %bitcast.15.base_ref, s32[320,1]{1,0:T(8,128)} %broadcast_in_dim.32.points_ref.limit_ref, f32[816,128]{1,0:T(8,128)} %reshape.69.tiles_ref), custom_call_target="tpu_custom_call" | custom-call | tf_op jit(solution)/shard_map/pallas_call | solution.py:211
  112.3 3.4 %collective-permute-done.3 = bf16[4,48,2560]{2,1,0:T(8,128)(2,1)S(1)} collective-permute-done((bf16[4,48,2560]{2,1,0:T(8,128)(2,1)S(1)}, bf16[4,48,2560]{2,1,0:T(8,128)(2,1)S(1)}, u32[]{:S(2)}, u32[]{:S(2)}) %collective-permute-start.3) | collective-permute-done | bytes 983072 | tf_op jit(solution)/shard_map/ppermute | solution.py:62
  115.6 5.5 %fusion = f32[4,96,384]{2,1,0:T(8,128)} fusion(bf16[4,2560,384]{2,1,0:T(8,128)(2,1)} %param.12, bf16[4,48,2560]{2,1,0:T(8,128)(2,1)S(1)} %maximum_select_fusion.2, bf16[4,48,2560]{2,1,0:T(8,128)(2,1)S(1)} %collective-permute-done.3, pred[]{:T(512)S(6)} %eq.19), kind=kOutput, calls=%fused_computation.1 | convolution fusion | flops 763822080 | bytes 10420225 | tf_op jit(solution)/shard_map/srj,sjd->srd/dot_general | solution.py:274
  (60 shorter events, 7.0 us)
Async XLA Ops:
  0.6 18.3 %copy-start.4 = (s32[320,11]{0,1:T(8,128)S(1)}, s32[320,11]{0,1:T(8,128)}, u32[]{:S(2)}) copy-start(s32[320,11]{0,1:T(8,128)} %param.14) | copy-start | bytes 42244
  0.6 16.6 %copy-start.5 = (s32[320]{0:T(512)S(1)}, s32[320]{0:T(512)}, u32[]{:S(2)}) copy-start(s32[320]{0:T(512)} %param.10) | copy-start | bytes 3844
  0.7 18.4 %copy-start.7 = (bf16[2,6]{1,0:T(2,128)(2,1)S(1)}, bf16[2,6]{1,0:T(2,128)(2,1)}, u32[]{:S(2)}) copy-start(bf16[2,6]{1,0:T(2,128)(2,1)} %param.13) | copy-start | bytes 76
  0.7 19.0 %collective-permute-start = (s32[320,11]{0,1:T(8,128)}, s32[320,11]{0,1:T(8,128)S(1)}, u32[]{:S(2)}, u32[]{:S(2)}) collective-permute-start(s32[320,11]{0,1:T(8,128)} %param.14), channel_id=1, source_target_pairs={{0,4},{4,0},{8,12},{12,8},{1,5},{5,1},{9,13},{13,9},{2,6},{6,2},{1... | collective-permute-start | bytes 42248 | tf_op jit(solution)/shard_map/ppermute | solution.py:62
  2.4 87.4 %collective-permute-start.5 = (f32[2,1,2176]{2,1,0:T(1,128)}, f32[2,1,2176]{2,1,0:T(1,128)}, u32[]{:S(2)}, u32[]{:S(2)}) collective-permute-start(f32[2,1,2176]{2,1,0:T(1,128)} %get-tuple-element.17), channel_id=1, source_target_pairs={{0,1},{1,2},{2,3},{3,16},{16,17},{17,18},{18,19},{4,5},{5,6},{6,7}... | collective-permute-start | bytes 52232 | tf_op jit(solution)/shard_map/ppermute | solution.py:27
  5.8 83.9 %collective-permute-start.4 = (f32[2,1,2176]{2,1,0:T(1,128)}, f32[2,1,2176]{2,1,0:T(1,128)}, u32[]{:S(2)}, u32[]{:S(2)}) collective-permute-start(f32[2,1,2176]{2,1,0:T(1,128)} %get-tuple-element.16), channel_id=1, source_target_pairs={{1,0},{2,1},{3,2},{16,3},{17,16},{18,17},{19,18},{5,4},{6,5},{7,6}... | collective-permute-start | bytes 52232 | tf_op jit(solution)/shard_map/ppermute | solution.py:29
  19.7 4.0 %collective-permute-start.1 = (s32[320,22]{0,1:T(8,128)S(1)}, s32[320,22]{0,1:T(8,128)S(1)}, u32[]{:S(2)}, u32[]{:S(2)}) collective-permute-start(s32[320,22]{0,1:T(8,128)S(1)} %add_select_fusion.5), channel_id=1, source_target_pairs={{0,8},{4,12},{8,0},{12,4},{1,9},{5,13},{9,1},{13,5},{2,10},{6,14},... | collective-permute-start | bytes 84488 | tf_op jit(solution)/shard_map/ppermute | solution.py:62
  24.8 42.6 %copy-start = (f32[16,2176]{1,0:T(8,128)S(1)}, f32[16,2176]{1,0:T(8,128)}, u32[]{:S(2)}) copy-start(f32[16,2176]{1,0:T(8,128)} %param.15) | copy-start | bytes 417796
  24.8 42.6 %copy-start.1 = (f32[16,2176]{1,0:T(8,128)S(1)}, f32[16,2176]{1,0:T(8,128)}, u32[]{:S(2)}) copy-start(f32[16,2176]{1,0:T(8,128)} %param.16) | copy-start | bytes 417796
  60.3 7.2 %copy-start.2 = (bf16[2,6,320,64]{3,2,1,0:T(8,128)(2,1)S(1)}, bf16[2,6,320,64]{3,2,1,0:T(8,128)(2,1)}, u32[]{:S(2)}) copy-start(bf16[2,6,320,64]{3,2,1,0:T(8,128)(2,1)} %get-tuple-element.6) | copy-start | bytes 1474564
  61.5 12.9 %collective-permute-start.7 = (f32[272,256]{1,0:T(8,128)S(1)}, f32[272,256]{1,0:T(8,128)S(1)}, u32[]{:S(2)}, u32[]{:S(2)}) collective-permute-start(f32[272,256]{1,0:T(8,128)S(1)} %get-tuple-element.9), channel_id=1, source_target_pairs={{1,0},{2,1},{3,2},{16,3},{17,16},{18,17},{19,18},{5,4},{6,5},{7,6}... | collective-permute-start | bytes 835592 | tf_op jit(solution)/shard_map/ppermute | solution.py:284
  64.2 13.1 %collective-permute-start.6 = (f32[272,256]{1,0:T(8,128)S(1)}, f32[272,256]{1,0:T(8,128)S(1)}, u32[]{:S(2)}, u32[]{:S(2)}) collective-permute-start(f32[272,256]{1,0:T(8,128)S(1)} %get-tuple-element.8), channel_id=1, source_target_pairs={{0,1},{1,2},{2,3},{3,16},{16,17},{17,18},{18,19},{4,5},{5,6},{6,7}... | collective-permute-start | bytes 835592 | tf_op jit(solution)/shard_map/ppermute | solution.py:281
  67.9 13.7 %copy-start.6 = (s32[16,17]{1,0:T(8,128)S(1)}, s32[16,17]{1,0:T(8,128)}, u32[]{:S(2)}) copy-start(s32[16,17]{1,0:T(8,128)} %param.17) | copy-start | bytes 3268
  68.9 20.1 %all-to-all-start = ((bf16[32,24,320]{2,1,0:T(8,128)(2,1)}), bf16[32,24,320]{2,1,0:T(8,128)(2,1)S(1)}, u32[]{:S(2)}, u32[]{:S(2)}) async-start(bf16[32,24,320]{2,1,0:T(8,128)(2,1)} %copy.45), calls=%async_computation | async-start | bytes 1179648 | tf_op jit(solution)/shard_map/all_to_all | solution.py:267
  78.4 1.6 %collective-permute-start.8 = (f32[272,256]{1,0:T(8,128)S(1)}, f32[272,256]{1,0:T(8,128)S(1)}, u32[]{:S(2)}, u32[]{:S(2)}) collective-permute-start(f32[272,256]{1,0:T(8,128)S(1)} %fusion.21), channel_id=1, source_target_pairs={{0,4},{4,0},{8,12},{12,8},{1,5},{5,1},{9,13},{13,9},{2,6},{6,2},{1... | collective-permute-start | bytes 835592 | tf_op jit(solution)/shard_map/ppermute | solution.py:50
  80.0 8.8 %collective-permute-start.9 = (f32[272,256]{1,0:T(8,128)S(1)}, f32[272,256]{1,0:T(8,128)S(1)}, u32[]{:S(2)}, u32[]{:S(2)}) collective-permute-start(f32[272,256]{1,0:T(8,128)S(1)} %add.92), channel_id=1, source_target_pairs={{0,8},{4,12},{8,0},{12,4},{1,9},{5,13},{9,1},{13,5},{2,10},{6,14},... | collective-permute-start | bytes 835592 | tf_op jit(solution)/shard_map/ppermute | solution.py:50
  89.7 1.9 %collective-permute-start.2 = (bf16[4,24,2560]{2,1,0:T(8,128)(2,1)S(1)}, bf16[4,24,2560]{2,1,0:T(8,128)(2,1)S(1)}, u32[]{:S(2)}, u32[]{:S(2)}) collective-permute-start(bf16[4,24,2560]{2,1,0:T(8,128)(2,1)S(1)} %all_to_all.16), channel_id=1, source_target_pairs={{0,4},{4,0},{8,12},{12,8},{1,5},{5,1},{9,13},{13,9},{2,6},{6,2},{1... | collective-permute-start | bytes 1474568 | tf_op jit(solution)/shard_map/ppermute | solution.py:62
  91.8 23.9 %collective-permute-start.3 = (bf16[4,48,2560]{2,1,0:T(8,128)(2,1)S(1)}, bf16[4,48,2560]{2,1,0:T(8,128)(2,1)S(1)}, u32[]{:S(2)}, u32[]{:S(2)}) collective-permute-start(bf16[4,48,2560]{2,1,0:T(8,128)(2,1)S(1)} %maximum_select_fusion.2), channel_id=1, source_target_pairs={{0,8},{4,12},{8,0},{12,4},{1,9},{5,13},{9,1},{13,5},{2,10},{6,14},... | collective-permute-start | bytes 2949128 | tf_op jit(solution)/shard_map/ppermute | solution.py:62
  94.0 18.2 %copy-start.3 = (f32[16,2176]{1,0:T(8,128)}, f32[16,2176]{1,0:T(8,128)S(1)}, u32[]{:S(2)}) copy-start(f32[16,2176]{1,0:T(8,128)S(1)} %get-tuple-element.11) | copy-start | bytes 417796
  94.0 8.1 %collective-permute-start.11 = (f32[16,2176]{1,0:T(8,128)S(1)}, f32[16,2176]{1,0:T(8,128)S(1)}, u32[]{:S(2)}, u32[]{:S(2)}) collective-permute-start(f32[16,2176]{1,0:T(8,128)S(1)} %get-tuple-element.11), channel_id=1, source_target_pairs={{1,0},{2,1},{3,2},{16,3},{17,16},{18,17},{19,18},{5,4},{6,5},{7,6}... | collective-permute-start | bytes 417800 | tf_op jit(solution)/shard_map/ppermute | solution.py:29
  96.2 9.8 %collective-permute-start.10 = (f32[16,2176]{1,0:T(8,128)S(1)}, f32[16,2176]{1,0:T(8,128)S(1)}, u32[]{:S(2)}, u32[]{:S(2)}) collective-permute-start(f32[16,2176]{1,0:T(8,128)S(1)} %get-tuple-element.11), channel_id=1, source_target_pairs={{0,1},{1,2},{2,3},{3,16},{16,17},{17,18},{18,19},{4,5},{5,6},{6,7}... | collective-permute-start | bytes 417800 | tf_op jit(solution)/shard_map/ppermute | solution.py:27

commit v15 on v14

--- a/solution.py
+++ b/solution.py
@@ -37,7 +37,7 @@
     points = jnp.arange(length, dtype=jnp.int32)
     phase = wave_order[:, None] * points[None, :] % length
     angle = phase.astype(jnp.float32) * (FULL_TURN / length)
-    table = jnp.concatenate([jnp.cos(angle), -jnp.sin(angle)], axis=0).astype(jnp.bfloat16)
+    table = (jnp.cos(angle).astype(jnp.bfloat16), (-jnp.sin(angle)).astype(jnp.bfloat16))
     return (table, points)
 
 
@@ -78,13 +78,27 @@
 
 
 def transform_kernel(
-    points_ref, cells_ref, table_ref, weight_ref, slot_ref, scale_ref, sums_ref, out_ref, acc_ref, *scratch
+    points_ref,
+    cells_ref,
+    cos_ref,
+    sin_ref,
+    weight_ref,
+    slot_ref,
+    scale_ref,
+    sums_ref,
+    out_ref,
+    acc_ref,
+    table_ref,
+    *scratch,
 ):
     step = pl.program_id(0)
 
     @pl.when(step == 0)
     def _():
         acc_ref[...] = jnp.zeros_like(acc_ref)
+        half = cos_ref.shape[0]
+        table_ref[:half] = cos_ref[...]
+        table_ref[half:] = sin_ref[...]
 
     nfields, nlev, rows, lon_count = cells_ref.shape
     nslot = acc_ref.shape[0]
@@ -155,9 +169,13 @@
     rows = row_block(lat_band)
     steps = lat_band // rows
     nblocks = lon_count // BLOCK
-    wave2 = table.shape[0]
+    half = table[0].shape[0]
+    wave2 = 2 * half
     slot_rows = slots.reshape(steps, rows, nblocks).transpose(0, 2, 1).reshape(steps, 1, nblocks * rows)
-    scratch = [pltpu.VMEM((nslot, 2 * nfields * BLOCK), jnp.float32)]
+    scratch = [
+        pltpu.VMEM((nslot, 2 * nfields * BLOCK), jnp.float32),
+        pltpu.VMEM((wave2, lon_count), jnp.bfloat16),
+    ]
     if rows % 16 == 0:
         scratch.append(pltpu.VMEM((nblocks * rows, 2 * nfields * BLOCK), jnp.bfloat16))
     return pl.pallas_call(
@@ -166,7 +184,8 @@
         in_specs=[
             pl.BlockSpec((rows, 1), lambda r: (r, 0)),
             pl.BlockSpec((nfields, nlev, rows, lon_count), lambda r: (0, 0, r, 0)),
-            pl.BlockSpec((wave2, lon_count), lambda r: (0, 0)),
+            pl.BlockSpec((half, lon_count), lambda r: (0, 0)),
+            pl.BlockSpec((half, lon_count), lambda r: (0, 0)),
             pl.BlockSpec(memory_space=pltpu.SMEM),
             pl.BlockSpec((1, 1, nblocks * rows), lambda r: (r, 0, 0)),
             pl.BlockSpec((rows, wave2), lambda r: (r, 0)),
@@ -181,7 +200,7 @@
         ],
         scratch_shapes=scratch,
         compiler_params=pltpu.CompilerParams(dimension_semantics=("arbitrary",)),
-    )(lat_points[:, None], atmos_fields, table, column_weight.astype(jnp.float32), slot_rows, scale)
+    )(lat_points[:, None], atmos_fields, *table, column_weight.astype(jnp.float32), slot_rows, scale)
 
 
 def surface_kernel(slot_ref, base_ref, limit_ref, tiles_ref, out_ref):

time: 123 us -> 127 us (1.033)
  other arithmetic: 12.8 us -> 14.6 us
  local copies, waits for them, and re-layouts: 7.81 us -> 9.21 us
    convert_element_type x0 -> x1, other arithmetic: none -> 4.69 us  [fourier_table(): (-jnp.sin(angle)).astype(jnp.bfloat16)]
    another operation x1 -> x0, other arithmetic: 4.04 us -> none
  transfers between devices with their start and end apart: 13 -> 13, of which waited for: 8 -> 8; matrix products, arithmetic and copies ran while one was open for 17% -> 19% of each run, Pallas kernels for 34% -> 33%
where the time goes in v15:
time: 127 us; the launch traced here: 125 us
  Pallas kernels  41 us (32%)
  starting transfers between devices  30.9 us (24%)
  waiting for transfers between devices  22.2 us (17%)
  other arithmetic  14.6 us (11%)
  local copies, waits for them, and re-layouts  9.21 us (7%)
  matrix products  6.14 us (5%)
    pallas_call x1, Pallas kernels, fused_transform(): pl.pallas_call(transform_kernel, grid=(steps,), in_specs=[pl.BlockSpec((r...  35.6 us
    ppermute x2, starting transfers between devices, with_halo(): lax.ppermute(tail, axis, [(i, (i + 1) % count) for i in range(ends)])  7.6 us
    ppermute x2, waiting for transfers between devices, lev_sum(): lax.ppermute(values, 'lev', [(i, i ^ stride) for i in range(count)])  7.42 us
    ppermute x2, starting transfers between devices, with_halo(): lax.ppermute(head, axis, [((i + 1) % count, i) for i in range(ends)])  7.23 us
    ppermute x4, waiting for transfers between devices, lev_gather(): other = lax.ppermute(values, 'lev', [(i, i ^ stride) for i in range(count)])  6.77 us
    dot_general x1, matrix products, body(): jnp.einsum('srj,sjd->srd', lev_gather(regrouped, 1), legendre, preferred_...  6.14 us
    pallas_call x1, Pallas kernels, surface_gather(): pl.pallas_call(surface_kernel, in_specs=[pl.BlockSpec(memory_space=pltpu....  5.48 us
    all_to_all x1, starting transfers between devices, body(): lax.all_to_all(coeffs.transpose(4, 1, 0, 3, 2).reshape(wave_count, lev_de...  5.38 us
  transfers between devices with their start and end apart: 13, of which 8 were waited for; matrix products, arithmetic and copies ran while one was open for 19% of the time, Pallas kernels for 33%

profile of v15, /device:TPU:4, one launch (start us, length us, event | category | flops | bytes accessed | tf_op | source)
XLA Modules:
  0.0 125.1 jit_solution(13849382642929093802)
XLA Ops:
  0.7 1.6 %fusion.28 = (f32[2,1,2176]{2,1,0:T(1,128)}, f32[2,1,2176]{2,1,0:T(1,128)}) fusion(f32[1,16,2176]{2,1,0:T(8,128)} %bitcast.43, f32[1,16,2176]{2,1,0:T(8,128)} %bitcast.47), kind=kLoop, calls=%fused_computation.71 | loop fusion | flops 8704 | bytes 313344 | tf_op jit(solution)/shard_map/stack | solution.py:318
  2.3 3.5 %collective-permute-start.5 = (f32[2,1,2176]{2,1,0:T(1,128)}, f32[2,1,2176]{2,1,0:T(1,128)}, u32[]{:S(2)}, u32[]{:S(2)}) collective-permute-start(f32[2,1,2176]{2,1,0:T(1,128)} %get-tuple-element.17), channel_id=1, source_target_pairs={{0,1},{1,2},{2,3},{3,16},{16,17},{17,18},{18,19},{4,5},{5,6},{6,7}... | collective-permute-start | bytes 52232 | tf_op jit(solution)/shard_map/ppermute | solution.py:27
  5.8 5.1 %collective-permute-start.4 = (f32[2,1,2176]{2,1,0:T(1,128)}, f32[2,1,2176]{2,1,0:T(1,128)}, u32[]{:S(2)}, u32[]{:S(2)}) collective-permute-start(f32[2,1,2176]{2,1,0:T(1,128)} %get-tuple-element.16), channel_id=1, source_target_pairs={{1,0},{2,1},{3,2},{16,3},{17,16},{18,17},{19,18},{5,4},{6,5},{7,6}... | collective-permute-start | bytes 52232 | tf_op jit(solution)/shard_map/ppermute | solution.py:29
  10.9 4.7 %negate_convert_fusion = (bf16[32,5632]{1,0:T(8,128)(2,1)}, bf16[32,5632]{1,0:T(8,128)(2,1)}) fusion(s32[32]{0:T(128)} %param.11), kind=kLoop, calls=%fused_computation.12 | loop fusion | flops 2162688 | bytes 721024 | tf_op jit(solution)/shard_map/convert_element_type | solution.py:40
  16.9 0.8 compare_select_fusion
  18.5 1.5 %broadcast_in_dim.32.points_ref.limit_ref = s32[320,1]{1,0:T(8,128)} reshape(s32[320]{0:T(512)} %param.10) | data formatting | bytes 2560 | tf_op jit(solution)/shard_map/broadcast_in_dim | solution.py:203
  20.0 0.8 concatenate.63
  20.8 1.2 convert_element_type.27.weight_ref
  22.0 0.8 add_select_fusion.5
  22.9 1.6 %collective-permute-start.1 = (s32[320,22]{0,1:T(8,128)S(1)}, s32[320,22]{0,1:T(8,128)S(1)}, u32[]{:S(2)}, u32[]{:S(2)}) collective-permute-start(s32[320,22]{0,1:T(8,128)S(1)} %add_select_fusion.5), channel_id=1, source_target_pairs={{0,8},{4,12},{8,0},{12,4},{1,9},{5,13},{9,1},{13,5},{2,10},{6,14},... | collective-permute-start | bytes 84488 | tf_op jit(solution)/shard_map/ppermute | solution.py:62
  24.5 2.4 %collective-permute-done.1 = s32[320,22]{0,1:T(8,128)S(1)} collective-permute-done((s32[320,22]{0,1:T(8,128)S(1)}, s32[320,22]{0,1:T(8,128)S(1)}, u32[]{:S(2)}, u32[]{:S(2)}) %collective-permute-start.1) | collective-permute-done | bytes 28192 | tf_op jit(solution)/shard_map/ppermute | solution.py:62
  28.0 35.6 %shard_map.120 = (bf16[2,6,320,64]{3,2,1,0:T(8,128)(2,1)}, f32[3,272,256]{2,1,0:T(8,128)}) custom-call(s32[320,1]{1,0:T(8,128)} %broadcast_in_dim.32.points_ref.limit_ref, bf16[2,6,320,5632]{3,2,1,0:T(8,128)(2,1)} %cells_ref.1, bf16[32,5632]{1,0:T(8,128)(2,1)} %get-tuple-element.21.cos_ref, bf16[32,5632]{1,0:T(8,128)(2,1)} %get-tuple-element.20.sin_ref, ...), custom_call_target="tpu_custom_call" | custom-call | tf_op jit(solution)/shard_map/pallas_call | solution.py:181
  63.5 1.2 slice_bitcast_fusion.1
  64.7 2.8 %collective-permute-start.7 = (f32[272,256]{1,0:T(8,128)S(1)}, f32[272,256]{1,0:T(8,128)S(1)}, u32[]{:S(2)}, u32[]{:S(2)}) collective-permute-start(f32[272,256]{1,0:T(8,128)S(1)} %get-tuple-element.9), channel_id=1, source_target_pairs={{1,0},{2,1},{3,2},{16,3},{17,16},{18,17},{19,18},{5,4},{6,5},{7,6}... | collective-permute-start | bytes 835592 | tf_op jit(solution)/shard_map/ppermute | solution.py:303
  67.5 3.1 %collective-permute-start.6 = (f32[272,256]{1,0:T(8,128)S(1)}, f32[272,256]{1,0:T(8,128)S(1)}, u32[]{:S(2)}, u32[]{:S(2)}) collective-permute-start(f32[272,256]{1,0:T(8,128)S(1)} %get-tuple-element.8), channel_id=1, source_target_pairs={{0,1},{1,2},{2,3},{3,16},{16,17},{17,18},{18,19},{4,5},{5,6},{6,7}... | collective-permute-start | bytes 835592 | tf_op jit(solution)/shard_map/ppermute | solution.py:300
  71.2 1.0 copy.45
  72.2 5.4 %all-to-all-start = ((bf16[32,24,320]{2,1,0:T(8,128)(2,1)}), bf16[32,24,320]{2,1,0:T(8,128)(2,1)S(1)}, u32[]{:S(2)}, u32[]{:S(2)}) async-start(bf16[32,24,320]{2,1,0:T(8,128)(2,1)} %copy.45), calls=%async_computation | async-start | bytes 1179648 | tf_op jit(solution)/shard_map/all_to_all | solution.py:286
  77.6 3.0 %collective-permute-done.6 = f32[272,256]{1,0:T(8,128)S(1)} collective-permute-done((f32[272,256]{1,0:T(8,128)S(1)}, f32[272,256]{1,0:T(8,128)S(1)}, u32[]{:S(2)}, u32[]{:S(2)}) %collective-permute-start.6) | collective-permute-done | bytes 278560 | tf_op jit(solution)/shard_map/ppermute | solution.py:300
  80.6 1.0 fusion.21
  81.7 1.5 %collective-permute-done.8 = f32[272,256]{1,0:T(8,128)S(1)} collective-permute-done((f32[272,256]{1,0:T(8,128)S(1)}, f32[272,256]{1,0:T(8,128)S(1)}, u32[]{:S(2)}, u32[]{:S(2)}) %collective-permute-start.8) | collective-permute-done | bytes 278560 | tf_op jit(solution)/shard_map/ppermute | solution.py:50
  83.3 1.6 %collective-permute-start.9 = (f32[272,256]{1,0:T(8,128)S(1)}, f32[272,256]{1,0:T(8,128)S(1)}, u32[]{:S(2)}, u32[]{:S(2)}) collective-permute-start(f32[272,256]{1,0:T(8,128)S(1)} %add.92), channel_id=1, source_target_pairs={{0,8},{4,12},{8,0},{12,4},{1,9},{5,13},{9,1},{13,5},{2,10},{6,14},... | collective-permute-start | bytes 835592 | tf_op jit(solution)/shard_map/ppermute | solution.py:50
  86.1 5.9 %collective-permute-done.9 = f32[272,256]{1,0:T(8,128)S(1)} collective-permute-done((f32[272,256]{1,0:T(8,128)S(1)}, f32[272,256]{1,0:T(8,128)S(1)}, u32[]{:S(2)}, u32[]{:S(2)}) %collective-permute-start.9) | collective-permute-done | bytes 278560 | tf_op jit(solution)/shard_map/ppermute | solution.py:50
  93.0 0.9 fusion.20
  93.9 0.9 collective-permute-done.2
  95.0 1.6 %collective-permute-start.3 = (bf16[4,48,2560]{2,1,0:T(8,128)(2,1)S(1)}, bf16[4,48,2560]{2,1,0:T(8,128)(2,1)}, u32[]{:S(2)}, u32[]{:S(2)}) collective-permute-start(bf16[4,48,2560]{2,1,0:T(8,128)(2,1)S(1)} %maximum_select_fusion.2), channel_id=1, source_target_pairs={{0,8},{4,12},{8,0},{12,4},{1,9},{5,13},{9,1},{13,5},{2,10},{6,14},... | collective-permute-start | bytes 2949128 | tf_op jit(solution)/shard_map/ppermute | solution.py:62
  97.2 2.2 %collective-permute-start.11 = (f32[16,2176]{1,0:T(8,128)S(1)}, f32[16,2176]{1,0:T(8,128)S(1)}, u32[]{:S(2)}, u32[]{:S(2)}) collective-permute-start(f32[16,2176]{1,0:T(8,128)S(1)} %get-tuple-element.11), channel_id=1, source_target_pairs={{1,0},{2,1},{3,2},{16,3},{17,16},{18,17},{19,18},{5,4},{6,5},{7,6}... | collective-permute-start | bytes 417800 | tf_op jit(solution)/shard_map/ppermute | solution.py:29
  99.4 4.1 %collective-permute-start.10 = (f32[16,2176]{1,0:T(8,128)S(1)}, f32[16,2176]{1,0:T(8,128)S(1)}, u32[]{:S(2)}, u32[]{:S(2)}) collective-permute-start(f32[16,2176]{1,0:T(8,128)S(1)} %get-tuple-element.11), channel_id=1, source_target_pairs={{0,1},{1,2},{2,3},{3,16},{16,17},{17,18},{18,19},{4,5},{5,6},{6,7}... | collective-permute-start | bytes 417800 | tf_op jit(solution)/shard_map/ppermute | solution.py:27
  104.2 1.1 collective-permute-done.11
  105.3 3.9 %collective-permute-done.10 = f32[16,2176]{1,0:T(8,128)S(1)} collective-permute-done((f32[16,2176]{1,0:T(8,128)S(1)}, f32[16,2176]{1,0:T(8,128)S(1)}, u32[]{:S(2)}, u32[]{:S(2)}) %collective-permute-start.10) | collective-permute-done | bytes 139296 | tf_op jit(solution)/shard_map/ppermute | solution.py:27
  110.0 5.5 %shard_map.121 = f32[320,1408]{1,0:T(8,128)} custom-call(s32[3520]{0:T(1024)} %fusion.35.slot_ref, s32[1]{0:T(128)} %bitcast.15.base_ref, s32[320,1]{1,0:T(8,128)} %broadcast_in_dim.32.points_ref.limit_ref, f32[816,128]{1,0:T(8,128)} %reshape.69.tiles_ref), custom_call_target="tpu_custom_call" | custom-call | tf_op jit(solution)/shard_map/pallas_call | solution.py:230
  115.5 3.5 %collective-permute-done.3 = bf16[4,48,2560]{2,1,0:T(8,128)(2,1)} collective-permute-done((bf16[4,48,2560]{2,1,0:T(8,128)(2,1)S(1)}, bf16[4,48,2560]{2,1,0:T(8,128)(2,1)}, u32[]{:S(2)}, u32[]{:S(2)}) %collective-permute-start.3) | collective-permute-done | bytes 983072 | tf_op jit(solution)/shard_map/ppermute | solution.py:62
  119.0 6.1 %fusion = f32[4,96,384]{2,1,0:T(8,128)} fusion(bf16[4,2560,384]{2,1,0:T(8,128)(2,1)} %param.12, bf16[4,48,2560]{2,1,0:T(8,128)(2,1)S(1)} %maximum_select_fusion.2, bf16[4,48,2560]{2,1,0:T(8,128)(2,1)} %collective-permute-done.3, pred[]{:T(512)S(6)} %eq.19), kind=kOutput, calls=%fused_computation.1 | convolution fusion | flops 763822080 | bytes 10420225 | tf_op jit(solution)/shard_map/srj,sjd->srd/dot_general | solution.py:293
  (55 shorter events, 8.5 us)
Async XLA Ops:
  0.6 21.4 %collective-permute-start = (s32[320,11]{0,1:T(8,128)}, s32[320,11]{0,1:T(8,128)S(1)}, u32[]{:S(2)}, u32[]{:S(2)}) collective-permute-start(s32[320,11]{0,1:T(8,128)} %param.14), channel_id=1, source_target_pairs={{0,4},{4,0},{8,12},{12,8},{1,5},{5,1},{9,13},{13,9},{2,6},{6,2},{1... | collective-permute-start | bytes 42248 | tf_op jit(solution)/shard_map/ppermute | solution.py:62
  2.3 90.6 %collective-permute-start.5 = (f32[2,1,2176]{2,1,0:T(1,128)}, f32[2,1,2176]{2,1,0:T(1,128)}, u32[]{:S(2)}, u32[]{:S(2)}) collective-permute-start(f32[2,1,2176]{2,1,0:T(1,128)} %get-tuple-element.17), channel_id=1, source_target_pairs={{0,1},{1,2},{2,3},{3,16},{16,17},{17,18},{18,19},{4,5},{5,6},{6,7}... | collective-permute-start | bytes 52232 | tf_op jit(solution)/shard_map/ppermute | solution.py:27
  5.8 87.2 %collective-permute-start.4 = (f32[2,1,2176]{2,1,0:T(1,128)}, f32[2,1,2176]{2,1,0:T(1,128)}, u32[]{:S(2)}, u32[]{:S(2)}) collective-permute-start(f32[2,1,2176]{2,1,0:T(1,128)} %get-tuple-element.16), channel_id=1, source_target_pairs={{1,0},{2,1},{3,2},{16,3},{17,16},{18,17},{19,18},{5,4},{6,5},{7,6}... | collective-permute-start | bytes 52232 | tf_op jit(solution)/shard_map/ppermute | solution.py:29
  22.9 4.0 %collective-permute-start.1 = (s32[320,22]{0,1:T(8,128)S(1)}, s32[320,22]{0,1:T(8,128)S(1)}, u32[]{:S(2)}, u32[]{:S(2)}) collective-permute-start(s32[320,22]{0,1:T(8,128)S(1)} %add_select_fusion.5), channel_id=1, source_target_pairs={{0,8},{4,12},{8,0},{12,4},{1,9},{5,13},{9,1},{13,5},{2,10},{6,14},... | collective-permute-start | bytes 84488 | tf_op jit(solution)/shard_map/ppermute | solution.py:62
  28.0 42.6 %copy-start = (f32[16,2176]{1,0:T(8,128)S(1)}, f32[16,2176]{1,0:T(8,128)}, u32[]{:S(2)}) copy-start(f32[16,2176]{1,0:T(8,128)} %param.15) | copy-start | bytes 417796
  28.0 42.6 %copy-start.1 = (f32[16,2176]{1,0:T(8,128)S(1)}, f32[16,2176]{1,0:T(8,128)}, u32[]{:S(2)}) copy-start(f32[16,2176]{1,0:T(8,128)} %param.16) | copy-start | bytes 417796
  63.5 7.2 %copy-start.2 = (bf16[2,6,320,64]{3,2,1,0:T(8,128)(2,1)S(1)}, bf16[2,6,320,64]{3,2,1,0:T(8,128)(2,1)}, u32[]{:S(2)}) copy-start(bf16[2,6,320,64]{3,2,1,0:T(8,128)(2,1)} %get-tuple-element.6) | copy-start | bytes 1474564
  64.7 12.9 %collective-permute-start.7 = (f32[272,256]{1,0:T(8,128)S(1)}, f32[272,256]{1,0:T(8,128)S(1)}, u32[]{:S(2)}, u32[]{:S(2)}) collective-permute-start(f32[272,256]{1,0:T(8,128)S(1)} %get-tuple-element.9), channel_id=1, source_target_pairs={{1,0},{2,1},{3,2},{16,3},{17,16},{18,17},{19,18},{5,4},{6,5},{7,6}... | collective-permute-start | bytes 835592 | tf_op jit(solution)/shard_map/ppermute | solution.py:303
  67.5 13.1 %collective-permute-start.6 = (f32[272,256]{1,0:T(8,128)S(1)}, f32[272,256]{1,0:T(8,128)S(1)}, u32[]{:S(2)}, u32[]{:S(2)}) collective-permute-start(f32[272,256]{1,0:T(8,128)S(1)} %get-tuple-element.8), channel_id=1, source_target_pairs={{0,1},{1,2},{2,3},{3,16},{16,17},{17,18},{18,19},{4,5},{5,6},{6,7}... | collective-permute-start | bytes 835592 | tf_op jit(solution)/shard_map/ppermute | solution.py:300
  71.2 10.5 %copy-start.4 = (s32[320,11]{0,1:T(8,128)S(1)}, s32[320,11]{0,1:T(8,128)}, u32[]{:S(2)}) copy-start(s32[320,11]{0,1:T(8,128)} %param.14) | copy-start | bytes 42244
  71.2 13.6 %copy-start.5 = (s32[16,17]{1,0:T(8,128)S(1)}, s32[16,17]{1,0:T(8,128)}, u32[]{:S(2)}) copy-start(s32[16,17]{1,0:T(8,128)} %param.17) | copy-start | bytes 3268
  72.2 20.1 %all-to-all-start = ((bf16[32,24,320]{2,1,0:T(8,128)(2,1)}), bf16[32,24,320]{2,1,0:T(8,128)(2,1)S(1)}, u32[]{:S(2)}, u32[]{:S(2)}) async-start(bf16[32,24,320]{2,1,0:T(8,128)(2,1)} %copy.45), calls=%async_computation | async-start | bytes 1179648 | tf_op jit(solution)/shard_map/all_to_all | solution.py:286
  81.6 1.6 %collective-permute-start.8 = (f32[272,256]{1,0:T(8,128)S(1)}, f32[272,256]{1,0:T(8,128)S(1)}, u32[]{:S(2)}, u32[]{:S(2)}) collective-permute-start(f32[272,256]{1,0:T(8,128)S(1)} %fusion.21), channel_id=1, source_target_pairs={{0,4},{4,0},{8,12},{12,8},{1,5},{5,1},{9,13},{13,9},{2,6},{6,2},{1... | collective-permute-start | bytes 835592 | tf_op jit(solution)/shard_map/ppermute | solution.py:50
  83.3 8.8 %collective-permute-start.9 = (f32[272,256]{1,0:T(8,128)S(1)}, f32[272,256]{1,0:T(8,128)S(1)}, u32[]{:S(2)}, u32[]{:S(2)}) collective-permute-start(f32[272,256]{1,0:T(8,128)S(1)} %add.92), channel_id=1, source_target_pairs={{0,8},{4,12},{8,0},{12,4},{1,9},{5,13},{9,1},{13,5},{2,10},{6,14},... | collective-permute-start | bytes 835592 | tf_op jit(solution)/shard_map/ppermute | solution.py:50
  92.9 1.9 %collective-permute-start.2 = (bf16[4,24,2560]{2,1,0:T(8,128)(2,1)S(1)}, bf16[4,24,2560]{2,1,0:T(8,128)(2,1)S(1)}, u32[]{:S(2)}, u32[]{:S(2)}) collective-permute-start(bf16[4,24,2560]{2,1,0:T(8,128)(2,1)S(1)} %all_to_all.16), channel_id=1, source_target_pairs={{0,4},{4,0},{8,12},{12,8},{1,5},{5,1},{9,13},{13,9},{2,6},{6,2},{1... | collective-permute-start | bytes 1474568 | tf_op jit(solution)/shard_map/ppermute | solution.py:62
  95.0 24.0 %collective-permute-start.3 = (bf16[4,48,2560]{2,1,0:T(8,128)(2,1)S(1)}, bf16[4,48,2560]{2,1,0:T(8,128)(2,1)}, u32[]{:S(2)}, u32[]{:S(2)}) collective-permute-start(bf16[4,48,2560]{2,1,0:T(8,128)(2,1)S(1)} %maximum_select_fusion.2), channel_id=1, source_target_pairs={{0,8},{4,12},{8,0},{12,4},{1,9},{5,13},{9,1},{13,5},{2,10},{6,14},... | collective-permute-start | bytes 2949128 | tf_op jit(solution)/shard_map/ppermute | solution.py:62
  97.2 18.2 %copy-start.3 = (f32[16,2176]{1,0:T(8,128)}, f32[16,2176]{1,0:T(8,128)S(1)}, u32[]{:S(2)}) copy-start(f32[16,2176]{1,0:T(8,128)S(1)} %get-tuple-element.11) | copy-start | bytes 417796
  97.2 8.1 %collective-permute-start.11 = (f32[16,2176]{1,0:T(8,128)S(1)}, f32[16,2176]{1,0:T(8,128)S(1)}, u32[]{:S(2)}, u32[]{:S(2)}) collective-permute-start(f32[16,2176]{1,0:T(8,128)S(1)} %get-tuple-element.11), channel_id=1, source_target_pairs={{1,0},{2,1},{3,2},{16,3},{17,16},{18,17},{19,18},{5,4},{6,5},{7,6}... | collective-permute-start | bytes 417800 | tf_op jit(solution)/shard_map/ppermute | solution.py:29
  99.4 9.8 %collective-permute-start.10 = (f32[16,2176]{1,0:T(8,128)S(1)}, f32[16,2176]{1,0:T(8,128)S(1)}, u32[]{:S(2)}, u32[]{:S(2)}) collective-permute-start(f32[16,2176]{1,0:T(8,128)S(1)} %get-tuple-element.11), channel_id=1, source_target_pairs={{0,1},{1,2},{2,3},{3,16},{16,17},{17,18},{18,19},{4,5},{5,6},{6,7}... | collective-permute-start | bytes 417800 | tf_op jit(solution)/shard_map/ppermute | solution.py:27

commit v16 on v14

--- a/solution.py
+++ b/solution.py
@@ -71,7 +71,7 @@
 
 
 def row_block(rows):
-    for size in (64, 32, 16):
+    for size in (32, 16):
         if rows % size == 0:
             return size
     return rows

time: 123 us -> 125 us (1.016)
  Pallas kernels: 41 us -> 42.5 us
    pallas_call x1, Pallas kernels: 35.5 us -> 37.1 us  [fused_transform(): pl.pallas_call(transform_kernel, grid=(steps,), in_specs=[pl.BlockSpec((r...]
  transfers between devices with their start and end apart: 13 -> 13, of which waited for: 8 -> 8; matrix products, arithmetic and copies ran while one was open for 17% -> 17% of each run, Pallas kernels for 34% -> 35%
where the time goes in v16:
time: 125 us; the launch traced here: 123 us
  Pallas kernels  42.5 us (34%)
  starting transfers between devices  30.9 us (25%)
  waiting for transfers between devices  21.9 us (18%)
  other arithmetic  12.9 us (10%)
  local copies, waits for them, and re-layouts  8.18 us (7%)
  matrix products  5.53 us (4%)
    pallas_call x1, Pallas kernels, fused_transform(): pl.pallas_call(transform_kernel, grid=(steps,), in_specs=[pl.BlockSpec((r...  37.1 us
    ppermute x2, starting transfers between devices, with_halo(): lax.ppermute(tail, axis, [(i, (i + 1) % count) for i in range(ends)])  7.61 us
    ppermute x2, waiting for transfers between devices, lev_sum(): lax.ppermute(values, 'lev', [(i, i ^ stride) for i in range(count)])  7.42 us
    ppermute x2, starting transfers between devices, with_halo(): lax.ppermute(head, axis, [((i + 1) % count, i) for i in range(ends)])  7.22 us
    ppermute x4, waiting for transfers between devices, lev_gather(): other = lax.ppermute(values, 'lev', [(i, i ^ stride) for i in range(count)])  6.48 us
    dot_general x1, matrix products, body(): jnp.einsum('srj,sjd->srd', lev_gather(regrouped, 1), legendre, preferred_...  5.53 us
    pallas_call x1, Pallas kernels, surface_gather(): pl.pallas_call(surface_kernel, in_specs=[pl.BlockSpec(memory_space=pltpu....  5.48 us
    all_to_all x1, starting transfers between devices, body(): lax.all_to_all(coeffs.transpose(4, 1, 0, 3, 2).reshape(wave_count, lev_de...  5.38 us
  transfers between devices with their start and end apart: 13, of which 8 were waited for; matrix products, arithmetic and copies ran while one was open for 17% of the time, Pallas kernels for 35%

profile of v16, /device:TPU:4, one launch (start us, length us, event | category | flops | bytes accessed | tf_op | source)
XLA Modules:
  0.0 123.0 jit_solution(12339401798693573109)
XLA Ops:
  0.7 1.6 %fusion.28 = (f32[2,1,2176]{2,1,0:T(1,128)}, f32[2,1,2176]{2,1,0:T(1,128)}) fusion(f32[1,16,2176]{2,1,0:T(8,128)} %bitcast.42, f32[1,16,2176]{2,1,0:T(8,128)} %bitcast.46), kind=kLoop, calls=%fused_computation.72 | loop fusion | flops 8704 | bytes 313344 | tf_op jit(solution)/shard_map/stack | solution.py:299
  2.4 3.5 %collective-permute-start.5 = (f32[2,1,2176]{2,1,0:T(1,128)}, f32[2,1,2176]{2,1,0:T(1,128)}, u32[]{:S(2)}, u32[]{:S(2)}) collective-permute-start(f32[2,1,2176]{2,1,0:T(1,128)} %get-tuple-element.17), channel_id=1, source_target_pairs={{0,1},{1,2},{2,3},{3,16},{16,17},{17,18},{18,19},{4,5},{5,6},{6,7}... | collective-permute-start | bytes 52232 | tf_op jit(solution)/shard_map/ppermute | solution.py:27
  5.8 5.1 %collective-permute-start.4 = (f32[2,1,2176]{2,1,0:T(1,128)}, f32[2,1,2176]{2,1,0:T(1,128)}, u32[]{:S(2)}, u32[]{:S(2)}) collective-permute-start(f32[2,1,2176]{2,1,0:T(1,128)} %get-tuple-element.16), channel_id=1, source_target_pairs={{1,0},{2,1},{3,2},{16,3},{17,16},{18,17},{19,18},{5,4},{6,5},{7,6}... | collective-permute-start | bytes 52232 | tf_op jit(solution)/shard_map/ppermute | solution.py:29
  10.9 4.0 %cosine_convert_fusion = (bf16[32,5632]{1,0:T(8,128)(2,1)S(1)}, bf16[32,5632]{1,0:T(8,128)(2,1)S(1)}) fusion(s32[32]{0:T(128)} %param.11), kind=kLoop, calls=%fused_computation.14 | loop fusion | flops 2162688 | bytes 721024 | tf_op jit(solution)/shard_map/convert
  16.3 0.9 pad_maximum_fusion.table_ref
  17.4 0.8 pad_maximum_fusion.7.scale_ref
  18.2 0.8 broadcast_in_dim.32.points_ref.limit_ref
  19.7 1.6 %collective-permute-start.1 = (s32[320,22]{0,1:T(8,128)S(1)}, s32[320,22]{0,1:T(8,128)S(1)}, u32[]{:S(2)}, u32[]{:S(2)}) collective-permute-start(s32[320,22]{0,1:T(8,128)S(1)} %add_select_fusion.5), channel_id=1, source_target_pairs={{0,8},{4,12},{8,0},{12,4},{1,9},{5,13},{9,1},{13,5},{2,10},{6,14},... | collective-permute-start | bytes 84488 | tf_op jit(solution)/shard_map/ppermute | solution.py:62
  21.5 2.2 %collective-permute-done.1 = s32[320,22]{0,1:T(8,128)S(1)} collective-permute-done((s32[320,22]{0,1:T(8,128)S(1)}, s32[320,22]{0,1:T(8,128)S(1)}, u32[]{:S(2)}, u32[]{:S(2)}) %collective-permute-start.1) | collective-permute-done | bytes 28192 | tf_op jit(solution)/shard_map/ppermute | solution.py:62
  24.3 0.8 reshape.70.slot_ref
  25.1 37.1 %shard_map.120 = (bf16[2,6,320,64]{3,2,1,0:T(8,128)(2,1)}, f32[3,272,256]{2,1,0:T(8,128)}) custom-call(s32[320,1]{1,0:T(8,128)} %broadcast_in_dim.32.points_ref.limit_ref, bf16[2,6,320,5632]{3,2,1,0:T(8,128)(2,1)} %cells_ref.1, bf16[64,5632]{1,0:T(8,128)(2,1)} %pad_maximum_fusion.table_ref, f32[2,6]{1,0:T(2,128)} %convert_element_type.20.weight_ref, ...), custom_call_target="tpu_custom_call" | custom-call | tf_op jit(solution)/shard_map/pallas_call | solution.py:163
  62.2 1.2 slice_bitcast_fusion.1
  63.3 2.8 %collective-permute-start.7 = (f32[272,256]{1,0:T(8,128)S(1)}, f32[272,256]{1,0:T(8,128)S(1)}, u32[]{:S(2)}, u32[]{:S(2)}) collective-permute-start(f32[272,256]{1,0:T(8,128)S(1)} %get-tuple-element.9), channel_id=1, source_target_pairs={{1,0},{2,1},{3,2},{16,3},{17,16},{18,17},{19,18},{5,4},{6,5},{7,6}... | collective-permute-start | bytes 835592 | tf_op jit(solution)/shard_map/ppermute | solution.py:284
  66.1 3.1 %collective-permute-start.6 = (f32[272,256]{1,0:T(8,128)S(1)}, f32[272,256]{1,0:T(8,128)S(1)}, u32[]{:S(2)}, u32[]{:S(2)}) collective-permute-start(f32[272,256]{1,0:T(8,128)S(1)} %get-tuple-element.8), channel_id=1, source_target_pairs={{0,1},{1,2},{2,3},{3,16},{16,17},{17,18},{18,19},{4,5},{5,6},{6,7}... | collective-permute-start | bytes 835592 | tf_op jit(solution)/shard_map/ppermute | solution.py:281
  69.8 1.0 copy.52
  70.8 5.4 %all-to-all-start = ((bf16[32,24,320]{2,1,0:T(8,128)(2,1)}), bf16[32,24,320]{2,1,0:T(8,128)(2,1)S(1)}, u32[]{:S(2)}, u32[]{:S(2)}) async-start(bf16[32,24,320]{2,1,0:T(8,128)(2,1)} %copy.52), calls=%async_computation | async-start | bytes 1179648 | tf_op jit(solution)/shard_map/all_to_all | solution.py:267
  76.2 3.0 %collective-permute-done.6 = f32[272,256]{1,0:T(8,128)S(1)} collective-permute-done((f32[272,256]{1,0:T(8,128)S(1)}, f32[272,256]{1,0:T(8,128)S(1)}, u32[]{:S(2)}, u32[]{:S(2)}) %collective-permute-start.6) | collective-permute-done | bytes 278560 | tf_op jit(solution)/shard_map/ppermute | solution.py:281
  79.2 1.0 fusion.21
  80.3 1.5 %collective-permute-done.8 = f32[272,256]{1,0:T(8,128)S(1)} collective-permute-done((f32[272,256]{1,0:T(8,128)S(1)}, f32[272,256]{1,0:T(8,128)S(1)}, u32[]{:S(2)}, u32[]{:S(2)}) %collective-permute-start.8) | collective-permute-done | bytes 278560 | tf_op jit(solution)/shard_map/ppermute | solution.py:50
  81.9 1.6 %collective-permute-start.9 = (f32[272,256]{1,0:T(8,128)S(1)}, f32[272,256]{1,0:T(8,128)S(1)}, u32[]{:S(2)}, u32[]{:S(2)}) collective-permute-start(f32[272,256]{1,0:T(8,128)S(1)} %add.92), channel_id=1, source_target_pairs={{0,8},{4,12},{8,0},{12,4},{1,9},{5,13},{9,1},{13,5},{2,10},{6,14},... | collective-permute-start | bytes 835592 | tf_op jit(solution)/shard_map/ppermute | solution.py:50
  84.7 5.9 %collective-permute-done.9 = f32[272,256]{1,0:T(8,128)S(1)} collective-permute-done((f32[272,256]{1,0:T(8,128)S(1)}, f32[272,256]{1,0:T(8,128)S(1)}, u32[]{:S(2)}, u32[]{:S(2)}) %collective-permute-start.9) | collective-permute-done | bytes 278560 | tf_op jit(solution)/shard_map/ppermute | solution.py:50
  91.6 0.9 fusion.20
  92.6 0.9 collective-permute-done.2
  93.6 1.6 %collective-permute-start.3 = (bf16[4,48,2560]{2,1,0:T(8,128)(2,1)S(1)}, bf16[4,48,2560]{2,1,0:T(8,128)(2,1)S(1)}, u32[]{:S(2)}, u32[]{:S(2)}) collective-permute-start(bf16[4,48,2560]{2,1,0:T(8,128)(2,1)S(1)} %maximum_select_fusion.2), channel_id=1, source_target_pairs={{0,8},{4,12},{8,0},{12,4},{1,9},{5,13},{9,1},{13,5},{2,10},{6,14},... | collective-permute-start | bytes 2949128 | tf_op jit(solution)/shard_map/ppermute | solution.py:62
  95.9 2.2 %collective-permute-start.11 = (f32[16,2176]{1,0:T(8,128)S(1)}, f32[16,2176]{1,0:T(8,128)S(1)}, u32[]{:S(2)}, u32[]{:S(2)}) collective-permute-start(f32[16,2176]{1,0:T(8,128)S(1)} %get-tuple-element.11), channel_id=1, source_target_pairs={{1,0},{2,1},{3,2},{16,3},{17,16},{18,17},{19,18},{5,4},{6,5},{7,6}... | collective-permute-start | bytes 417800 | tf_op jit(solution)/shard_map/ppermute | solution.py:29
  98.0 4.1 %collective-permute-start.10 = (f32[16,2176]{1,0:T(8,128)S(1)}, f32[16,2176]{1,0:T(8,128)S(1)}, u32[]{:S(2)}, u32[]{:S(2)}) collective-permute-start(f32[16,2176]{1,0:T(8,128)S(1)} %get-tuple-element.11), channel_id=1, source_target_pairs={{0,1},{1,2},{2,3},{3,16},{16,17},{17,18},{18,19},{4,5},{5,6},{6,7}... | collective-permute-start | bytes 417800 | tf_op jit(solution)/shard_map/ppermute | solution.py:27
  102.8 1.1 collective-permute-done.11
  103.9 3.9 %collective-permute-done.10 = f32[16,2176]{1,0:T(8,128)S(1)} collective-permute-done((f32[16,2176]{1,0:T(8,128)S(1)}, f32[16,2176]{1,0:T(8,128)S(1)}, u32[]{:S(2)}, u32[]{:S(2)}) %collective-permute-start.10) | collective-permute-done | bytes 139296 | tf_op jit(solution)/shard_map/ppermute | solution.py:27
  107.8 0.8 reshape.69.tiles_ref
  108.6 5.5 %shard_map.121 = f32[320,1408]{1,0:T(8,128)} custom-call(s32[3520]{0:T(1024)} %fusion.35.slot_ref, s32[1]{0:T(128)} %bitcast.15.base_ref, s32[320,1]{1,0:T(8,128)} %broadcast_in_dim.32.points_ref.limit_ref, f32[816,128]{1,0:T(8,128)} %reshape.69.tiles_ref), custom_call_target="tpu_custom_call" | custom-call | tf_op jit(solution)/shard_map/pallas_call | solution.py:211
  114.1 3.4 %collective-permute-done.3 = bf16[4,48,2560]{2,1,0:T(8,128)(2,1)S(1)} collective-permute-done((bf16[4,48,2560]{2,1,0:T(8,128)(2,1)S(1)}, bf16[4,48,2560]{2,1,0:T(8,128)(2,1)S(1)}, u32[]{:S(2)}, u32[]{:S(2)}) %collective-permute-start.3) | collective-permute-done | bytes 983072 | tf_op jit(solution)/shard_map/ppermute | solution.py:62
  117.5 5.5 %fusion = f32[4,96,384]{2,1,0:T(8,128)} fusion(bf16[4,2560,384]{2,1,0:T(8,128)(2,1)} %param.12, bf16[4,48,2560]{2,1,0:T(8,128)(2,1)S(1)} %maximum_select_fusion.2, bf16[4,48,2560]{2,1,0:T(8,128)(2,1)S(1)} %collective-permute-done.3, pred[]{:T(512)S(6)} %eq.19), kind=kOutput, calls=%fused_computation.1 | convolution fusion | flops 763822080 | bytes 10420225 | tf_op jit(solution)/shard_map/srj,sjd->srd/dot_general | solution.py:274
  (61 shorter events, 7.4 us)
Async XLA Ops:
  0.6 18.3 %copy-start.4 = (s32[320,11]{0,1:T(8,128)S(1)}, s32[320,11]{0,1:T(8,128)}, u32[]{:S(2)}) copy-start(s32[320,11]{0,1:T(8,128)} %param.14) | copy-start | bytes 42244
  0.6 16.6 %copy-start.5 = (s32[320]{0:T(512)S(1)}, s32[320]{0:T(512)}, u32[]{:S(2)}) copy-start(s32[320]{0:T(512)} %param.10) | copy-start | bytes 3844
  0.7 18.4 %copy-start.7 = (bf16[2,6]{1,0:T(2,128)(2,1)S(1)}, bf16[2,6]{1,0:T(2,128)(2,1)}, u32[]{:S(2)}) copy-start(bf16[2,6]{1,0:T(2,128)(2,1)} %param.13) | copy-start | bytes 76
  0.7 19.0 %collective-permute-start = (s32[320,11]{0,1:T(8,128)}, s32[320,11]{0,1:T(8,128)S(1)}, u32[]{:S(2)}, u32[]{:S(2)}) collective-permute-start(s32[320,11]{0,1:T(8,128)} %param.14), channel_id=1, source_target_pairs={{0,4},{4,0},{8,12},{12,8},{1,5},{5,1},{9,13},{13,9},{2,6},{6,2},{1... | collective-permute-start | bytes 42248 | tf_op jit(solution)/shard_map/ppermute | solution.py:62
  2.4 89.2 %collective-permute-start.5 = (f32[2,1,2176]{2,1,0:T(1,128)}, f32[2,1,2176]{2,1,0:T(1,128)}, u32[]{:S(2)}, u32[]{:S(2)}) collective-permute-start(f32[2,1,2176]{2,1,0:T(1,128)} %get-tuple-element.17), channel_id=1, source_target_pairs={{0,1},{1,2},{2,3},{3,16},{16,17},{17,18},{18,19},{4,5},{5,6},{6,7}... | collective-permute-start | bytes 52232 | tf_op jit(solution)/shard_map/ppermute | solution.py:27
  5.8 85.8 %collective-permute-start.4 = (f32[2,1,2176]{2,1,0:T(1,128)}, f32[2,1,2176]{2,1,0:T(1,128)}, u32[]{:S(2)}, u32[]{:S(2)}) collective-permute-start(f32[2,1,2176]{2,1,0:T(1,128)} %get-tuple-element.16), channel_id=1, source_target_pairs={{1,0},{2,1},{3,2},{16,3},{17,16},{18,17},{19,18},{5,4},{6,5},{7,6}... | collective-permute-start | bytes 52232 | tf_op jit(solution)/shard_map/ppermute | solution.py:29
  19.7 4.0 %collective-permute-start.1 = (s32[320,22]{0,1:T(8,128)S(1)}, s32[320,22]{0,1:T(8,128)S(1)}, u32[]{:S(2)}, u32[]{:S(2)}) collective-permute-start(s32[320,22]{0,1:T(8,128)S(1)} %add_select_fusion.5), channel_id=1, source_target_pairs={{0,8},{4,12},{8,0},{12,4},{1,9},{5,13},{9,1},{13,5},{2,10},{6,14},... | collective-permute-start | bytes 84488 | tf_op jit(solution)/shard_map/ppermute | solution.py:62
  25.1 44.1 %copy-start = (f32[16,2176]{1,0:T(8,128)S(1)}, f32[16,2176]{1,0:T(8,128)}, u32[]{:S(2)}) copy-start(f32[16,2176]{1,0:T(8,128)} %param.15) | copy-start | bytes 417796
  25.1 44.1 %copy-start.1 = (f32[16,2176]{1,0:T(8,128)S(1)}, f32[16,2176]{1,0:T(8,128)}, u32[]{:S(2)}) copy-start(f32[16,2176]{1,0:T(8,128)} %param.16) | copy-start | bytes 417796
  62.1 7.2 %copy-start.2 = (bf16[2,6,320,64]{3,2,1,0:T(8,128)(2,1)S(1)}, bf16[2,6,320,64]{3,2,1,0:T(8,128)(2,1)}, u32[]{:S(2)}) copy-start(bf16[2,6,320,64]{3,2,1,0:T(8,128)(2,1)} %get-tuple-element.6) | copy-start | bytes 1474564
  63.3 12.9 %collective-permute-start.7 = (f32[272,256]{1,0:T(8,128)S(1)}, f32[272,256]{1,0:T(8,128)S(1)}, u32[]{:S(2)}, u32[]{:S(2)}) collective-permute-start(f32[272,256]{1,0:T(8,128)S(1)} %get-tuple-element.9), channel_id=1, source_target_pairs={{1,0},{2,1},{3,2},{16,3},{17,16},{18,17},{19,18},{5,4},{6,5},{7,6}... | collective-permute-start | bytes 835592 | tf_op jit(solution)/shard_map/ppermute | solution.py:284
  66.1 13.1 %collective-permute-start.6 = (f32[272,256]{1,0:T(8,128)S(1)}, f32[272,256]{1,0:T(8,128)S(1)}, u32[]{:S(2)}, u32[]{:S(2)}) collective-permute-start(f32[272,256]{1,0:T(8,128)S(1)} %get-tuple-element.8), channel_id=1, source_target_pairs={{0,1},{1,2},{2,3},{3,16},{16,17},{17,18},{18,19},{4,5},{5,6},{6,7}... | collective-permute-start | bytes 835592 | tf_op jit(solution)/shard_map/ppermute | solution.py:281
  69.8 13.7 %copy-start.6 = (s32[16,17]{1,0:T(8,128)S(1)}, s32[16,17]{1,0:T(8,128)}, u32[]{:S(2)}) copy-start(s32[16,17]{1,0:T(8,128)} %param.17) | copy-start | bytes 3268
  70.8 20.1 %all-to-all-start = ((bf16[32,24,320]{2,1,0:T(8,128)(2,1)}), bf16[32,24,320]{2,1,0:T(8,128)(2,1)S(1)}, u32[]{:S(2)}, u32[]{:S(2)}) async-start(bf16[32,24,320]{2,1,0:T(8,128)(2,1)} %copy.52), calls=%async_computation | async-start | bytes 1179648 | tf_op jit(solution)/shard_map/all_to_all | solution.py:267
  80.2 1.6 %collective-permute-start.8 = (f32[272,256]{1,0:T(8,128)S(1)}, f32[272,256]{1,0:T(8,128)S(1)}, u32[]{:S(2)}, u32[]{:S(2)}) collective-permute-start(f32[272,256]{1,0:T(8,128)S(1)} %fusion.21), channel_id=1, source_target_pairs={{0,4},{4,0},{8,12},{12,8},{1,5},{5,1},{9,13},{13,9},{2,6},{6,2},{1... | collective-permute-start | bytes 835592 | tf_op jit(solution)/shard_map/ppermute | solution.py:50
  81.9 8.8 %collective-permute-start.9 = (f32[272,256]{1,0:T(8,128)S(1)}, f32[272,256]{1,0:T(8,128)S(1)}, u32[]{:S(2)}, u32[]{:S(2)}) collective-permute-start(f32[272,256]{1,0:T(8,128)S(1)} %add.92), channel_id=1, source_target_pairs={{0,8},{4,12},{8,0},{12,4},{1,9},{5,13},{9,1},{13,5},{2,10},{6,14},... | collective-permute-start | bytes 835592 | tf_op jit(solution)/shard_map/ppermute | solution.py:50
  91.5 1.9 %collective-permute-start.2 = (bf16[4,24,2560]{2,1,0:T(8,128)(2,1)S(1)}, bf16[4,24,2560]{2,1,0:T(8,128)(2,1)S(1)}, u32[]{:S(2)}, u32[]{:S(2)}) collective-permute-start(bf16[4,24,2560]{2,1,0:T(8,128)(2,1)S(1)} %all_to_all.16), channel_id=1, source_target_pairs={{0,4},{4,0},{8,12},{12,8},{1,5},{5,1},{9,13},{13,9},{2,6},{6,2},{1... | collective-permute-start | bytes 1474568 | tf_op jit(solution)/shard_map/ppermute | solution.py:62
  93.6 23.9 %collective-permute-start.3 = (bf16[4,48,2560]{2,1,0:T(8,128)(2,1)S(1)}, bf16[4,48,2560]{2,1,0:T(8,128)(2,1)S(1)}, u32[]{:S(2)}, u32[]{:S(2)}) collective-permute-start(bf16[4,48,2560]{2,1,0:T(8,128)(2,1)S(1)} %maximum_select_fusion.2), channel_id=1, source_target_pairs={{0,8},{4,12},{8,0},{12,4},{1,9},{5,13},{9,1},{13,5},{2,10},{6,14},... | collective-permute-start | bytes 2949128 | tf_op jit(solution)/shard_map/ppermute | solution.py:62
  95.9 18.2 %copy-start.3 = (f32[16,2176]{1,0:T(8,128)}, f32[16,2176]{1,0:T(8,128)S(1)}, u32[]{:S(2)}) copy-start(f32[16,2176]{1,0:T(8,128)S(1)} %get-tuple-element.11) | copy-start | bytes 417796
  95.9 8.1 %collective-permute-start.11 = (f32[16,2176]{1,0:T(8,128)S(1)}, f32[16,2176]{1,0:T(8,128)S(1)}, u32[]{:S(2)}, u32[]{:S(2)}) collective-permute-start(f32[16,2176]{1,0:T(8,128)S(1)} %get-tuple-element.11), channel_id=1, source_target_pairs={{1,0},{2,1},{3,2},{16,3},{17,16},{18,17},{19,18},{5,4},{6,5},{7,6}... | collective-permute-start | bytes 417800 | tf_op jit(solution)/shard_map/ppermute | solution.py:29
  98.0 9.8 %collective-permute-start.10 = (f32[16,2176]{1,0:T(8,128)S(1)}, f32[16,2176]{1,0:T(8,128)S(1)}, u32[]{:S(2)}, u32[]{:S(2)}) collective-permute-start(f32[16,2176]{1,0:T(8,128)S(1)} %get-tuple-element.11), channel_id=1, source_target_pairs={{0,1},{1,2},{2,3},{3,16},{16,17},{17,18},{18,19},{4,5},{5,6},{6,7}... | collective-permute-start | bytes 417800 | tf_op jit(solution)/shard_map/ppermute | solution.py:27
